TPU v7x, 32 devices: a whole 2x2x4 slice. The times are simulated.
32 devices in a mesh: mem: 4 (over z), tile: 8 (over y, x, core).
Axes of the slice: x: 2, y: 2, z: 4, core: 2. Of those that a mesh axis runs over, the one named last changes fastest.
Arguments:
- source_blocks: bfloat16 [1024, 8, 2, 256], P('tile', 'mem'), may hold values from -6 to 6
- send_blocks: int32 [8, 8, 24], P('tile'), may hold values from 0 to 127
- recv_slot: int32 [8, 8, 24], P('tile'), may hold values from 0 to 95
- recv_weight: float32 [8, 8, 24], P('tile'), may hold values from 0.25 to 2
- recv_count: int32 [8, 8], P('tile'), may hold values from 0 to 24, as said below
- regional: bfloat16 [8, 2, 512, 384], P('mem', None, 'tile'), may hold values from -6 to 6
- x_operator: bfloat16 [512, 512], P(('mem', 'tile'))
- y_operator: bfloat16 [384, 384], P(('mem', 'tile'))
Outputs:
- blended: bfloat16 [8, 2, 512, 384], P('mem', None, 'tile')
Inputs may be any that keep to these rules, and one draw needn't show every extreme that they name: `recv_count`: live entries of one pair of tiles number at most 24; some pairs in every draw have 24.
All inputs are finite; a program needn't handle non-finite values.
Results may differ from a plain program's by a relative error of at most 0.0055.
Values may be sent and summed in bfloat16 or wider, within the bound.
No kernel may reach another device: no remote copies, remote signals or barrier semaphores. Data moves between devices by JAX's collectives and lax.ppermute only.
A program may use at most 128 MiB of HBM per device.

v0:
```python
import math

import jax
import jax.numpy as jnp
from jax import lax
from jax.sharding import PartitionSpec as P


def body(
    source_blocks, send_blocks, recv_slot, recv_weight, recv_count, regional, x_operator, y_operator
):
    tile_count = lax.axis_size("tile")
    member_count, level_count, columns, y_cells = regional.shape
    capacity = send_blocks.shape[2]
    block_cells = source_blocks.shape[3]
    block_side = math.isqrt(block_cells)
    picked = send_blocks[0].reshape(-1)
    packed = jnp.take(source_blocks, picked, axis=0).reshape(
        tile_count, capacity, member_count, level_count, block_cells
    )
    arrived = lax.all_to_all(packed, "tile", split_axis=0, concat_axis=0, tiled=True)
    slot_count = columns // block_side * (y_cells // block_side)
    live_mask = lax.broadcasted_iota(jnp.int32, (tile_count, capacity), 1) < recv_count[0][:, None]
    weights = jnp.where(live_mask, recv_weight[0], 0.0).reshape(-1)
    slot_match = recv_slot[0].reshape(-1)[None, :] == lax.broadcasted_iota(
        jnp.int32, (slot_count, tile_count * capacity), 0
    )
    remap_weights = jnp.where(slot_match, weights[None, :], 0.0).astype(jnp.bfloat16)
    remapped = jnp.dot(
        remap_weights,
        arrived.reshape(tile_count * capacity, -1),
        preferred_element_type=jnp.float32,
    )
    remapped = remapped.reshape(
        columns // block_side,
        y_cells // block_side,
        member_count,
        level_count,
        block_side,
        block_side,
    )
    remapped = remapped.transpose(2, 3, 0, 4, 1, 5).reshape(
        member_count, level_count, columns, y_cells
    )
    difference = (remapped - regional.astype(jnp.float32)).astype(jnp.bfloat16)
    x_lines = lax.all_to_all(difference, "tile", split_axis=3, concat_axis=2, tiled=True)
    after_first = jnp.einsum(
        "ax,mlxy->mlay",
        lax.all_gather(x_operator, ("mem", "tile"), axis=0, tiled=True),
        x_lines,
        preferred_element_type=jnp.float32,
    ).astype(jnp.bfloat16)
    tile_back = lax.all_to_all(after_first, "tile", split_axis=2, concat_axis=3, tiled=True)
    after_second = jnp.einsum(
        "by,mlxy->mlxb",
        lax.all_gather(y_operator, ("mem", "tile"), axis=0, tiled=True),
        tile_back,
        preferred_element_type=jnp.float32,
    )
    return (regional.astype(jnp.float32) + after_second).astype(jnp.bfloat16)


def solution(mesh):
    placed = (
        P("tile", "mem", None, None),
        P("tile", None, None),
        P("tile", None, None),
        P("tile", None, None),
        P("tile", None),
        P("mem", None, "tile", None),
        P(("mem", "tile"), None),
        P(("mem", "tile"), None),
    )
    return jax.shard_map(
        body, mesh=mesh, in_specs=placed, out_specs=P("mem", None, "tile", None), check_vma=False
    )
```

profile of v0, /device:TPU:0, one launch (start us, length us, event | category | flops | bytes accessed | tf_op | source)
XLA Modules:
  0.0 121.7 jit_solution(16398745087015653898)
XLA Ops:
  0.0 0.0 copy-start
  0.0 0.0 copy-start.6
  0.0 0.0 copy-start.5
  0.0 0.0 copy-start.4
  0.0 0.8 reshape_squeeze.6
  0.8 0.7 compare_and_fusion
  1.5 0.0 copy-done
  1.5 1.4 %gather_fusion = bf16[192,2,2,256]{3,2,1,0:T(2,128)(2,1)S(1)} fusion(bf16[128,2,2,256]{3,2,1,0:T(2,128)(2,1)S(1)} %copy-done, s32[1024]{0:T(1024)S(1)} %pad_clamp_fusion), kind=kCustom, calls=%fused_computation | custom fusion | bytes 787200 | tf_op jit(solution)/shard_map/jit(_take)/gather | solution.py:18
  3.0 1.2 broadcast_select_fusion
  4.2 5.2 %all-to-all-start = ((bf16[8,24,2,2,256]{4,3,2,1,0:T(2,128)(2,1)}), bf16[8,24,2,2,256]{4,3,2,1,0:T(2,128)(2,1)S(1)}, u32[]{:S(2)}, u32[]{:S(2)}) async-start(bf16[8,24,2,2,256]{4,3,2,1,0:T(2,128)(2,1)} %broadcast_select_fusion), calls=%async_computation | async-start | bytes 786432 | tf_op jit(solution)/shard_map/all_to_all | solution.py:21
  9.4 0.0 copy-done.6
  9.4 0.1 iota_compare_fusion
  9.4 0.1 lt.42
  9.5 0.0 copy-done.5
  9.5 0.1 squeeze.3
  9.6 0.0 copy-done.4
  9.6 0.1 eq.15
  9.7 8.0 %all-to-all-done = bf16[8,24,2,2,256]{4,3,2,1,0:T(2,128)(2,1)S(1)} async-done(((bf16[8,24,2,2,256]{4,3,2,1,0:T(2,128)(2,1)}), bf16[8,24,2,2,256]{4,3,2,1,0:T(2,128)(2,1)S(1)}, u32[]{:S(2)}, u32[]{:S(2)}) %all-to-all-start) | async-done | bytes 393248 | tf_op jit(solution)/shard_map/all_to_all | solution.py:21
  17.7 0.3 reshape.92
  18.0 0.2 copy.16
  18.2 1.9 %convolution_bitcast_fusion = f32[2,2,4,16,24,16]{4,5,3,1,0,2:T(8,128)} fusion(bf16[2,2,16,16,192,1]{4,3,2,1,0,5:T(8,128)(2,1)S(1)} %bitcast.53, bf16[192]{0:T(256)(128)(2,1)S(1)} %broadcast_select_fusion.1, s32[4,24]{1,0:T(4,128)S(1)} %multiply_add_fusion, s32[192]{0:T(256)S(1)} %eq.15), kind=kOutput, calls=%fused_computation.1 | convolution fusion | flops 37785600 | bytes 787968 | tf_op jit(solution)/shard_map/dot_general | solution.py:29
  20.0 2.2 %copy.17 = f32[2,2,4,16,24,16]{5,4,3,2,1,0:T(8,128)S(1)} copy(f32[2,2,4,16,24,16]{4,5,3,1,0,2:T(8,128)} %convolution_bitcast_fusion) | data formatting | bytes 786432 | tf_op jit(solution)/shard_map/transpose | solution.py:42
  22.3 0.0 copy-start.2
  22.3 1.6 %reshape.93 = f32[2,2,64,384]{3,2,1,0:T(8,128)} reshape(f32[2,2,4,16,24,16]{5,4,3,2,1,0:T(8,128)S(1)} %copy.17) | data formatting | bytes 786432 | tf_op jit(solution)/shard_map/reshape | solution.py:42
  23.9 1.1 fusion.3
  25.0 0.6 copy.18
  25.6 1.0 reshape.109
  26.6 3.4 %all-to-all-start.1 = ((bf16[8,2,6144]{2,1,0:T(2,128)(2,1)}), bf16[8,2,6144]{2,1,0:T(2,128)(2,1)S(1)}, u32[]{:S(2)}, u32[]{:S(2)}) async-start(bf16[8,2,6144]{2,1,0:T(2,128)(2,1)} %reshape.109), calls=%async_computation.1 | async-start | bytes 393216 | tf_op jit(solution)/shard_map/all_to_all | solution.py:46
  30.0 0.0 copy-done.2
  30.0 43.6 %all_gather.6 = bf16[512,512]{1,0:T(8,128)(2,1)S(1)} all-gather(bf16[16,512]{1,0:T(8,128)(2,1)S(1)} %copy-done.2), channel_id=1, replica_groups=mesh['mem'=4,'tile'=8] {'mem','tile'}, dimensions={0}, use_global_device_ids=true | all-gather | bytes 540672 | tf_op jit(solution)/shard_map/all_gather | solution.py:49
  73.6 0.0 all-to-all-done.1
  73.6 0.3 reshape.110
  73.9 0.0 copy-start.3
  73.9 0.3 copy.31
  74.2 0.3 all_to_all.33
  74.4 0.3 fusion.1
  74.8 0.4 copy.21
  75.2 1.4 %reshape.111 = bf16[8,2,6144]{2,1,0:T(2,128)(2,1)} reshape(bf16[512,2,2,48]{3,2,1,0:T(2,128)(2,1)S(1)} %bitcast.54) | data formatting | bytes 393216
  76.6 3.5 %all-to-all-start.2 = ((bf16[8,2,6144]{2,1,0:T(2,128)(2,1)}), bf16[8,2,6144]{2,1,0:T(2,128)(2,1)S(1)}, u32[]{:S(2)}, u32[]{:S(2)}) async-start(bf16[8,2,6144]{2,1,0:T(2,128)(2,1)} %reshape.111), calls=%async_computation.2 | async-start | bytes 393216 | tf_op jit(solution)/shard_map/all_to_all | solution.py:53
  80.1 0.0 copy-done.3
  80.1 39.3 %all-gather = bf16[32,12,384]{2,1,0:T(8,128)(2,1)S(1)} all-gather(bf16[1,12,384]{2,1,0:T(8,128)(2,1)S(1)} %bitcast.62), channel_id=1, replica_groups=mesh['mem'=4,'tile'=8] {'mem','tile'}, dimensions={0}, use_global_device_ids=true | all-gather | bytes 304128 | tf_op jit(solution)/shard_map/all_gather | solution.py:56
  119.4 0.1 reshape.107
  119.5 0.0 all-to-all-done.2
  119.5 0.5 reshape.112
  120.0 0.3 copy.30
  120.4 0.4 all_to_all.37
  120.8 0.0 copy-done.1
  120.8 1.0 fusion
  (5 shorter events, 0.0 us)
Async XLA Ops:
  0.0 1.5 %copy-start = (bf16[128,2,2,256]{3,2,1,0:T(2,128)(2,1)S(1)}, bf16[128,2,2,256]{3,2,1,0:T(2,128)(2,1)}, u32[]{:S(2)}) copy-start(bf16[128,2,2,256]{3,2,1,0:T(2,128)(2,1)} %param.8) | copy-start | bytes 786436
  0.0 9.4 %copy-start.6 = (s32[1,8]{1,0:T(1,128)S(1)}, s32[1,8]{1,0:T(1,128)}, u32[]{:S(2)}) copy-start(s32[1,8]{1,0:T(1,128)} %param.12) | copy-start | bytes 100
  0.0 9.5 %copy-start.5 = (f32[1,8,24]{2,1,0:T(8,128)S(1)}, f32[1,8,24]{2,1,0:T(8,128)}, u32[]{:S(2)}) copy-start(f32[1,8,24]{2,1,0:T(8,128)} %param.11) | copy-start | bytes 2308
  0.0 9.6 %copy-start.4 = (s32[1,8,24]{2,1,0:T(8,128)S(1)}, s32[1,8,24]{2,1,0:T(8,128)}, u32[]{:S(2)}) copy-start(s32[1,8,24]{2,1,0:T(8,128)} %param.10) | copy-start | bytes 2308
  4.2 13.5 %all-to-all-start = ((bf16[8,24,2,2,256]{4,3,2,1,0:T(2,128)(2,1)}), bf16[8,24,2,2,256]{4,3,2,1,0:T(2,128)(2,1)S(1)}, u32[]{:S(2)}, u32[]{:S(2)}) async-start(bf16[8,24,2,2,256]{4,3,2,1,0:T(2,128)(2,1)} %broadcast_select_fusion), calls=%async_computation | async-start | bytes 786432 | tf_op jit(solution)/shard_map/all_to_all | solution.py:21
  22.3 7.7 %copy-start.2 = (bf16[16,512]{1,0:T(8,128)(2,1)S(1)}, bf16[16,512]{1,0:T(8,128)(2,1)}, u32[]{:S(2)}) copy-start(bf16[16,512]{1,0:T(8,128)(2,1)} %param.14) | copy-start | bytes 49156
  26.6 47.0 %all-to-all-start.1 = ((bf16[8,2,6144]{2,1,0:T(2,128)(2,1)}), bf16[8,2,6144]{2,1,0:T(2,128)(2,1)S(1)}, u32[]{:S(2)}, u32[]{:S(2)}) async-start(bf16[8,2,6144]{2,1,0:T(2,128)(2,1)} %reshape.109), calls=%async_computation.1 | async-start | bytes 393216 | tf_op jit(solution)/shard_map/all_to_all | solution.py:46
  73.9 6.2 %copy-start.3 = (bf16[12,384]{1,0:T(8,128)(2,1)S(1)}, bf16[12,384]{1,0:T(8,128)(2,1)}, u32[]{:S(2)}) copy-start(bf16[12,384]{1,0:T(8,128)(2,1)} %param.15) | copy-start | bytes 27652
  76.6 44.2 %copy-start.1 = (bf16[2,2,64,384]{3,2,1,0:T(8,128)(2,1)S(1)}, bf16[2,2,64,384]{3,2,1,0:T(8,128)(2,1)}, u32[]{:S(2)}) copy-start(bf16[2,2,64,384]{3,2,1,0:T(8,128)(2,1)} %param.13) | copy-start | bytes 589828
  76.6 42.9 %all-to-all-start.2 = ((bf16[8,2,6144]{2,1,0:T(2,128)(2,1)}), bf16[8,2,6144]{2,1,0:T(2,128)(2,1)S(1)}, u32[]{:S(2)}, u32[]{:S(2)}) async-start(bf16[8,2,6144]{2,1,0:T(2,128)(2,1)} %reshape.111), calls=%async_computation.2 | async-start | bytes 393216 | tf_op jit(solution)/shard_map/all_to_all | solution.py:53
where the time goes:
time: 122 us
  blocking collectives  82.9 us (68%)
  local copies, waits for them, and re-layouts  12.4 us (10%)
  starting transfers between devices  12.1 us (10%)
  waiting for transfers between devices  7.98 us (7%)
  matrix products  3.14 us (3%)
  other arithmetic  3.08 us (3%)
    all_gather x1, blocking collectives, body(): lax.all_gather(x_operator, ('mem', 'tile'), axis=0, tiled=True)  43.6 us
    all_gather x1, blocking collectives, body(): lax.all_gather(y_operator, ('mem', 'tile'), axis=0, tiled=True)  39.3 us
    all_to_all x1, waiting for transfers between devices, body(): lax.all_to_all(packed, 'tile', split_axis=0, concat_axis=0, tiled=True)  7.98 us
    all_to_all x1, starting transfers between devices, body(): lax.all_to_all(packed, 'tile', split_axis=0, concat_axis=0, tiled=True)  5.18 us
    all_to_all x1, starting transfers between devices, body(): lax.all_to_all(after_first, 'tile', split_axis=2, concat_axis=3, tiled=True)  3.52 us
    all_to_all x1, starting transfers between devices, body(): lax.all_to_all(difference, 'tile', split_axis=3, concat_axis=2, tiled=True)  3.39 us
    unnamed x19, local copies, waits for them, and re-layouts  3.32 us
  transfers between devices with their start and end apart: 3, of which 1 were waited for; matrix products, arithmetic and copies ran while one was open for 0% of the time, Pallas kernels for 0%

commit v1 on v0

--- a/solution.py
+++ b/solution.py
@@ -4,6 +4,26 @@
 import jax.numpy as jnp
 from jax import lax
 from jax.sharding import PartitionSpec as P
+
+
+def gather_rows(shard, axis_name):
+    count = lax.axis_size(axis_name)
+    copies = jnp.broadcast_to(shard[None], (count,) + shard.shape)
+    return lax.all_to_all(copies, axis_name, split_axis=0, concat_axis=0, tiled=True)
+
+
+def gather_operators(x_operator, y_operator):
+    mem_count = lax.axis_size("mem")
+    tile_count = lax.axis_size("tile")
+    x_rows, x_cols = x_operator.shape
+    y_rows, y_cols = y_operator.shape
+    x_size = x_rows * x_cols
+    both = jnp.concatenate([x_operator.reshape(-1), y_operator.reshape(-1)])
+    both = gather_rows(gather_rows(both[None], "mem"), "tile")
+    both = both.reshape(tile_count, mem_count, -1).transpose(1, 0, 2)
+    x_full = both[:, :, :x_size].reshape(mem_count * tile_count * x_rows, x_cols)
+    y_full = both[:, :, x_size:].reshape(mem_count * tile_count * y_rows, y_cols)
+    return x_full, y_full
 
 
 def body(
@@ -14,6 +34,7 @@
     capacity = send_blocks.shape[2]
     block_cells = source_blocks.shape[3]
     block_side = math.isqrt(block_cells)
+    x_full, y_full = gather_operators(x_operator, y_operator)
     picked = send_blocks[0].reshape(-1)
     packed = jnp.take(source_blocks, picked, axis=0).reshape(
         tile_count, capacity, member_count, level_count, block_cells
@@ -46,14 +67,14 @@
     x_lines = lax.all_to_all(difference, "tile", split_axis=3, concat_axis=2, tiled=True)
     after_first = jnp.einsum(
         "ax,mlxy->mlay",
-        lax.all_gather(x_operator, ("mem", "tile"), axis=0, tiled=True),
+        x_full,
         x_lines,
         preferred_element_type=jnp.float32,
     ).astype(jnp.bfloat16)
     tile_back = lax.all_to_all(after_first, "tile", split_axis=2, concat_axis=3, tiled=True)
     after_second = jnp.einsum(
         "by,mlxy->mlxb",
-        lax.all_gather(y_operator, ("mem", "tile"), axis=0, tiled=True),
+        y_full,
         tile_back,
         preferred_element_type=jnp.float32,
     )

time: 122 us -> 74 us (0.61)
  blocking collectives: 82.9 us -> 0 us
  waiting for transfers between devices: 7.98 us -> 29 us
  starting transfers between devices: 12.1 us -> 20.4 us
  local copies, waits for them, and re-layouts: 12.4 us -> 16.1 us
  other arithmetic: 3.08 us -> 4.35 us
    all_gather x2 -> x0, blocking collectives: 82.9 us -> none  [the longest x1 43.6 us: body(): lax.all_gather(x_operator, ('mem', 'tile'), axis=0, tiled=True)]
    all_to_all x0 -> x2, waiting for transfers between devices: none -> 12.1 us  [gather_rows(): lax.all_to_all(copies, axis_name, split_axis=0, concat_axis=0, tiled=True)]
    all_to_all x0 -> x2, starting transfers between devices: none -> 8.42 us  [gather_rows(): lax.all_to_all(copies, axis_name, split_axis=0, concat_axis=0, tiled=True)]
    all_to_all x1, waiting for transfers between devices: 0.01 us -> 6.02 us  [body(): lax.all_to_all(difference, 'tile', split_axis=3, concat_axis=2, tiled=True)]
    all_to_all x1, waiting for transfers between devices: 0.01 us -> 5.61 us  [body(): lax.all_to_all(after_first, 'tile', split_axis=2, concat_axis=3, tiled=True)]
    all_to_all x1, waiting for transfers between devices: 7.98 us -> 5.34 us  [body(): lax.all_to_all(packed, 'tile', split_axis=0, concat_axis=0, tiled=True)]
    broadcast_in_dim x0 -> x3, local copies, waits for them, and re-layouts: none -> 1.75 us  [gather_rows(): copies = jnp.broadcast_to(shard[None], (count,) + shard.shape)]
    broadcast_in_dim x0 -> x1, other arithmetic: none -> 1.26 us  [gather_rows(): copies = jnp.broadcast_to(shard[None], (count,) + shard.shape)]
  transfers between devices with their start and end apart: 3 -> 5, of which waited for: 1 -> 4; matrix products, arithmetic and copies ran while one was open for 0% -> 18% of each run, Pallas kernels for 0% -> 0%
where the time goes in v1:
time: 74 us; the launch traced here: 73.3 us
  waiting for transfers between devices  29 us (39%)
  starting transfers between devices  20.4 us (28%)
  local copies, waits for them, and re-layouts  16.1 us (22%)
  other arithmetic  4.35 us (6%)
  matrix products  3.15 us (4%)
    all_to_all x2, waiting for transfers between devices, gather_rows(): lax.all_to_all(copies, axis_name, split_axis=0, concat_axis=0, tiled=True)  12.1 us
    all_to_all x2, starting transfers between devices, gather_rows(): lax.all_to_all(copies, axis_name, split_axis=0, concat_axis=0, tiled=True)  8.42 us
    all_to_all x1, waiting for transfers between devices, body(): lax.all_to_all(difference, 'tile', split_axis=3, concat_axis=2, tiled=True)  6.02 us
    all_to_all x1, waiting for transfers between devices, body(): lax.all_to_all(after_first, 'tile', split_axis=2, concat_axis=3, tiled=True)  5.61 us
    all_to_all x1, waiting for transfers between devices, body(): lax.all_to_all(packed, 'tile', split_axis=0, concat_axis=0, tiled=True)  5.34 us
    all_to_all x1, starting transfers between devices, body(): lax.all_to_all(packed, 'tile', split_axis=0, concat_axis=0, tiled=True)  5.18 us
    unnamed x22, local copies, waits for them, and re-layouts  4.07 us
    all_to_all x1, starting transfers between devices, body(): lax.all_to_all(difference, 'tile', split_axis=3, concat_axis=2, tiled=True)  3.39 us
  transfers between devices with their start and end apart: 5, of which 4 were waited for; matrix products, arithmetic and copies ran while one was open for 18% of the time, Pallas kernels for 0%

profile of v1, /device:TPU:0, one launch (start us, length us, event | category | flops | bytes accessed | tf_op | source)
XLA Modules:
  0.0 73.3 jit_solution(1774075096843622021)
XLA Ops:
  0.0 0.8 %reshape_squeeze.6 = s32[192,1]{0,1:T(1,128)S(1)} reshape(s32[1,8,24]{2,1,0:T(8,128)} %param.9) | data formatting | bytes 1536 | tf_op jit(solution)/shard_map/reshape;squeeze | solution.py:38
  0.8 0.7 compare_and_fusion
  1.6 1.4 %gather_fusion = bf16[192,2,2,256]{3,2,1,0:T(2,128)(2,1)S(1)} fusion(bf16[128,2,2,256]{3,2,1,0:T(2,128)(2,1)S(1)} %copy-done, s32[1024]{0:T(1024)S(1)} %pad_clamp_fusion), kind=kCustom, calls=%fused_computation | custom fusion | bytes 787200 | tf_op jit(solution)/shard_map/jit(_take)/gather | solution.py:39
  3.0 1.2 %broadcast_select_fusion = bf16[8,24,2,2,256]{4,3,2,1,0:T(2,128)(2,1)} fusion(bf16[8,24,2,2,256]{4,3,2,1,0:T(2,128)(2,1)S(1)} %bitcast.64, pred[8,24]{1,0:T(8,128)(4,1)S(1)} %compare_and_fusion), kind=kLoop, calls=%fused_computation.6 | loop fusion | flops 196608 | bytes 786624 | tf_op jit(solution)/shard_map/jit(_take)/select_n | solution.py:39
  4.2 5.2 %all-to-all-start = ((bf16[8,24,2,2,256]{4,3,2,1,0:T(2,128)(2,1)}), bf16[8,24,2,2,256]{4,3,2,1,0:T(2,128)(2,1)S(1)}, u32[]{:S(2)}, u32[]{:S(2)}) async-start(bf16[8,24,2,2,256]{4,3,2,1,0:T(2,128)(2,1)} %broadcast_select_fusion), calls=%async_computation | async-start | bytes 786432 | tf_op jit(solution)/shard_map/all_to_all | solution.py:42
  9.5 0.1 iota_compare_fusion
  9.5 0.1 lt.42
  9.6 0.1 squeeze.3
  9.7 0.1 eq.15
  9.8 0.1 broadcast_in_dim.44
  9.9 0.5 broadcast.78
  10.4 1.3 %reduce = bf16[4,12800]{1,0:T(4,128)(2,1)S(1)} reduce(bf16[4,1,12800]{2,1,0:T(2,128)(2,1)S(1)} %broadcast_in_dim.44, bf16[]{:T(256)} %broadcast.78), dimensions={1}, to_apply=%broadcast_in_dim.44.reduce_sub_computation | reduce | bytes 204802 | tf_op jit(solution)/shard_map/broadcast_in_dim | solution.py:11
  11.7 0.7 reshape.136
  12.4 5.3 %all-to-all-done = bf16[8,24,2,2,256]{4,3,2,1,0:T(2,128)(2,1)S(1)} async-done(((bf16[8,24,2,2,256]{4,3,2,1,0:T(2,128)(2,1)}), bf16[8,24,2,2,256]{4,3,2,1,0:T(2,128)(2,1)S(1)}, u32[]{:S(2)}, u32[]{:S(2)}) %all-to-all-start) | async-done | bytes 393248 | tf_op jit(solution)/shard_map/all_to_all | solution.py:42
  17.7 4.9 %all-to-all-start.2 = ((bf16[4,2,6400]{2,1,0:T(2,128)(2,1)}), bf16[4,2,6400]{2,1,0:T(2,128)(2,1)S(1)}, u32[]{:S(2)}, u32[]{:S(2)}) async-start(bf16[4,2,6400]{2,1,0:T(2,128)(2,1)} %reshape.136), calls=%async_computation.2 | async-start | bytes 204800 | tf_op jit(solution)/shard_map/all_to_all | solution.py:12
  22.6 0.3 reshape.113
  22.9 0.2 copy.25
  23.1 1.9 %convolution_bitcast_fusion = f32[2,2,4,16,24,16]{4,5,3,1,0,2:T(8,128)} fusion(bf16[2,2,16,16,192,1]{4,3,2,1,0,5:T(8,128)(2,1)S(1)} %bitcast.60, bf16[192]{0:T(256)(128)(2,1)S(1)} %broadcast_select_fusion.1, s32[4,24]{1,0:T(4,128)S(1)} %multiply_add_fusion, s32[192]{0:T(256)S(1)} %eq.15), kind=kOutput, calls=%fused_computation.1 | convolution fusion | flops 37785600 | bytes 787968 | tf_op jit(solution)/shard_map/dot_general | solution.py:50
  24.9 2.2 %copy.26 = f32[2,2,4,16,24,16]{5,4,3,2,1,0:T(8,128)S(1)} copy(f32[2,2,4,16,24,16]{4,5,3,1,0,2:T(8,128)} %convolution_bitcast_fusion) | data formatting | bytes 786432 | tf_op jit(solution)/shard_map/transpose | solution.py:63
  27.2 1.6 %reshape.114 = f32[2,2,64,384]{3,2,1,0:T(8,128)} reshape(f32[2,2,4,16,24,16]{5,4,3,2,1,0:T(8,128)S(1)} %copy.26) | data formatting | bytes 786432 | tf_op jit(solution)/shard_map/reshape | solution.py:63
  28.8 1.1 %fusion.3 = bf16[2,2,64,384]{3,2,1,0:T(8,128)(2,1)S(1)} fusion(f32[2,2,64,384]{3,2,1,0:T(8,128)} %reshape.114, bf16[2,2,64,384]{3,2,1,0:T(8,128)(2,1)} %param.13), kind=kLoop, calls=%fused_computation.10 | loop fusion | flops 294912 | bytes 786432 | tf_op jit(solution)/shard_map/convert_element_type | solution.py:66
  29.9 0.6 copy.27
  30.5 1.0 %reshape.134 = bf16[8,2,6144]{2,1,0:T(2,128)(2,1)} reshape(bf16[384,2,2,64]{3,2,1,0:T(2,128)(2,1)S(1)} %bitcast.66) | data formatting | bytes 393216
  31.5 3.4 %all-to-all-start.1 = ((bf16[8,2,6144]{2,1,0:T(2,128)(2,1)}), bf16[8,2,6144]{2,1,0:T(2,128)(2,1)S(1)}, u32[]{:S(2)}, u32[]{:S(2)}) async-start(bf16[8,2,6144]{2,1,0:T(2,128)(2,1)} %reshape.134), calls=%async_computation.1 | async-start | bytes 393216 | tf_op jit(solution)/shard_map/all_to_all | solution.py:67
  34.9 0.1 reshape.137
  35.0 0.1 copy.46
  35.0 6.0 %all-to-all-done.1 = bf16[8,2,6144]{2,1,0:T(2,128)(2,1)S(1)} async-done(((bf16[8,2,6144]{2,1,0:T(2,128)(2,1)}), bf16[8,2,6144]{2,1,0:T(2,128)(2,1)S(1)}, u32[]{:S(2)}, u32[]{:S(2)}) %all-to-all-start.1) | async-done | bytes 196640 | tf_op jit(solution)/shard_map/all_to_all | solution.py:67
  41.0 1.1 %broadcast_in_dim.46 = bf16[8,4,1,12800]{3,1,2,0:T(4,128)(2,1)} broadcast(bf16[4,12800]{1,0:T(4,128)(2,1)S(1)} %bitcast.69), dimensions={1,3} | broadcast | bytes 921600 | tf_op jit(solution)/shard_map/broadcast_in_dim | solution.py:11
  42.2 3.5 %all-to-all-start.3 = ((bf16[8,4,1,12800]{3,1,2,0:T(4,128)(2,1)}), bf16[8,4,1,12800]{3,1,2,0:T(4,128)(2,1)S(1)}, u32[]{:S(2)}, u32[]{:S(2)}) async-start(bf16[8,4,1,12800]{3,1,2,0:T(4,128)(2,1)} %broadcast_in_dim.46), calls=%async_computation.3 | async-start | bytes 1638400 | tf_op jit(solution)/shard_map/all_to_all | solution.py:12
  45.7 0.3 reshape.135
  46.0 0.3 copy.45
  46.3 0.3 all_to_all.39
  46.5 12.1 %all-to-all-done.3 = bf16[8,4,1,12800]{3,1,2,0:T(4,128)(2,1)S(1)} async-done(((bf16[8,4,1,12800]{3,1,2,0:T(4,128)(2,1)}), bf16[8,4,1,12800]{3,1,2,0:T(4,128)(2,1)S(1)}, u32[]{:S(2)}, u32[]{:S(2)}) %all-to-all-start.3) | async-done | bytes 819232 | tf_op jit(solution)/shard_map/all_to_all | solution.py:12
  58.6 0.2 slice.10
  58.8 0.3 copy.30
  59.1 0.2 reshape.130
  59.3 0.3 fusion.1
  59.7 0.4 copy.31
  60.1 1.4 %reshape.138 = bf16[8,2,6144]{2,1,0:T(2,128)(2,1)} reshape(bf16[512,2,2,48]{3,2,1,0:T(2,128)(2,1)S(1)} %bitcast.61) | data formatting | bytes 393216
  61.5 3.4 %all-to-all-start.4 = ((bf16[8,2,6144]{2,1,0:T(2,128)(2,1)}), bf16[8,2,6144]{2,1,0:T(2,128)(2,1)S(1)}, u32[]{:S(2)}, u32[]{:S(2)}) async-start(bf16[8,2,6144]{2,1,0:T(2,128)(2,1)} %reshape.138), calls=%async_computation.4 | async-start | bytes 393216 | tf_op jit(solution)/shard_map/all_to_all | solution.py:74
  64.9 0.1 slice.11
  65.0 0.1 copy.33
  65.1 0.4 reshape.131
  65.5 5.6 %all-to-all-done.4 = bf16[8,2,6144]{2,1,0:T(2,128)(2,1)S(1)} async-done(((bf16[8,2,6144]{2,1,0:T(2,128)(2,1)}), bf16[8,2,6144]{2,1,0:T(2,128)(2,1)S(1)}, u32[]{:S(2)}, u32[]{:S(2)}) %all-to-all-start.4) | async-done | bytes 196640 | tf_op jit(solution)/shard_map/all_to_all | solution.py:74
  71.1 0.5 reshape.139
  71.6 0.3 copy.44
  71.9 0.4 all_to_all.45
  72.3 1.0 %fusion = bf16[2,2,64,384]{3,2,1,0:T(8,128)(2,1)} fusion(bf16[2,2,64,384]{3,2,1,0:T(8,128)(2,1)S(1)} %all_to_all.45, bf16[2,2,64,384]{3,2,1,0:T(8,128)(2,1)S(1)} %copy-done.1, bf16[384,384,1,1]{1,0,2,3:T(8,128)(2,1)S(1)} %reshape.131), kind=kOutput, calls=%fused_computation.4 | convolution fusion | flops 75792384 | bytes 884736 | tf_op jit(solution)/shard_map/by,mlxy->mlxb/dot_general | solution.py:75
  (22 shorter events, 0.1 us)
Async XLA Ops:
  0.0 1.5 %copy-start = (bf16[128,2,2,256]{3,2,1,0:T(2,128)(2,1)S(1)}, bf16[128,2,2,256]{3,2,1,0:T(2,128)(2,1)}, u32[]{:S(2)}) copy-start(bf16[128,2,2,256]{3,2,1,0:T(2,128)(2,1)} %param.8) | copy-start | bytes 786436
  0.0 9.4 %copy-start.3 = (bf16[12,384]{1,0:T(8,128)(2,1)S(1)}, bf16[12,384]{1,0:T(8,128)(2,1)}, u32[]{:S(2)}) copy-start(bf16[12,384]{1,0:T(8,128)(2,1)} %param.15) | copy-start | bytes 27652
  0.0 9.4 %copy-start.2 = (bf16[16,512]{1,0:T(8,128)(2,1)S(1)}, bf16[16,512]{1,0:T(8,128)(2,1)}, u32[]{:S(2)}) copy-start(bf16[16,512]{1,0:T(8,128)(2,1)} %param.14) | copy-start | bytes 49156
  0.0 9.4 %copy-start.6 = (s32[1,8]{1,0:T(1,128)S(1)}, s32[1,8]{1,0:T(1,128)}, u32[]{:S(2)}) copy-start(s32[1,8]{1,0:T(1,128)} %param.12) | copy-start | bytes 100
  0.0 9.6 %copy-start.5 = (f32[1,8,24]{2,1,0:T(8,128)S(1)}, f32[1,8,24]{2,1,0:T(8,128)}, u32[]{:S(2)}) copy-start(f32[1,8,24]{2,1,0:T(8,128)} %param.11) | copy-start | bytes 2308
  0.0 9.7 %copy-start.4 = (s32[1,8,24]{2,1,0:T(8,128)S(1)}, s32[1,8,24]{2,1,0:T(8,128)}, u32[]{:S(2)}) copy-start(s32[1,8,24]{2,1,0:T(8,128)} %param.10) | copy-start | bytes 2308
  4.2 13.5 %all-to-all-start = ((bf16[8,24,2,2,256]{4,3,2,1,0:T(2,128)(2,1)}), bf16[8,24,2,2,256]{4,3,2,1,0:T(2,128)(2,1)S(1)}, u32[]{:S(2)}, u32[]{:S(2)}) async-start(bf16[8,24,2,2,256]{4,3,2,1,0:T(2,128)(2,1)} %broadcast_select_fusion), calls=%async_computation | async-start | bytes 786432 | tf_op jit(solution)/shard_map/all_to_all | solution.py:42
  17.7 13.8 %all-to-all-start.2 = ((bf16[4,2,6400]{2,1,0:T(2,128)(2,1)}), bf16[4,2,6400]{2,1,0:T(2,128)(2,1)S(1)}, u32[]{:S(2)}, u32[]{:S(2)}) async-start(bf16[4,2,6400]{2,1,0:T(2,128)(2,1)} %reshape.136), calls=%async_computation.2 | async-start | bytes 204800 | tf_op jit(solution)/shard_map/all_to_all | solution.py:12
  31.5 9.6 %all-to-all-start.1 = ((bf16[8,2,6144]{2,1,0:T(2,128)(2,1)}), bf16[8,2,6144]{2,1,0:T(2,128)(2,1)S(1)}, u32[]{:S(2)}, u32[]{:S(2)}) async-start(bf16[8,2,6144]{2,1,0:T(2,128)(2,1)} %reshape.134), calls=%async_computation.1 | async-start | bytes 393216 | tf_op jit(solution)/shard_map/all_to_all | solution.py:67
  42.2 16.4 %all-to-all-start.3 = ((bf16[8,4,1,12800]{3,1,2,0:T(4,128)(2,1)}), bf16[8,4,1,12800]{3,1,2,0:T(4,128)(2,1)S(1)}, u32[]{:S(2)}, u32[]{:S(2)}) async-start(bf16[8,4,1,12800]{3,1,2,0:T(4,128)(2,1)} %broadcast_in_dim.46), calls=%async_computation.3 | async-start | bytes 1638400 | tf_op jit(solution)/shard_map/all_to_all | solution.py:12
  61.5 9.6 %all-to-all-start.4 = ((bf16[8,2,6144]{2,1,0:T(2,128)(2,1)}), bf16[8,2,6144]{2,1,0:T(2,128)(2,1)S(1)}, u32[]{:S(2)}, u32[]{:S(2)}) async-start(bf16[8,2,6144]{2,1,0:T(2,128)(2,1)} %reshape.138), calls=%async_computation.4 | async-start | bytes 393216 | tf_op jit(solution)/shard_map/all_to_all | solution.py:74
  64.9 7.4 %copy-start.1 = (bf16[2,2,64,384]{3,2,1,0:T(8,128)(2,1)S(1)}, bf16[2,2,64,384]{3,2,1,0:T(8,128)(2,1)}, u32[]{:S(2)}) copy-start(bf16[2,2,64,384]{3,2,1,0:T(8,128)(2,1)} %param.13) | copy-start | bytes 589828

commit v2 on v0

--- a/solution.py
+++ b/solution.py
@@ -6,14 +6,48 @@
 from jax.sharding import PartitionSpec as P
 
 
+def gather_rows(shard, axis_name):
+    count = lax.axis_size(axis_name)
+    copies = jnp.broadcast_to(shard[None], (count,) + shard.shape)
+    return lax.all_to_all(copies, axis_name, split_axis=0, concat_axis=0, tiled=True)
+
+
+def exchange(data, extra):
+    tile_count = data.shape[0]
+    flat = data.reshape(tile_count, -1)
+    size = flat.shape[1]
+    payload = jnp.concatenate(
+        [flat, jnp.broadcast_to(extra[None], (tile_count,) + extra.shape)], axis=1
+    )
+    got = lax.all_to_all(payload, "tile", split_axis=0, concat_axis=0, tiled=True)
+    return got[:, :size].reshape(data.shape), got[:, size:]
+
+
+def rows_in_order(got, rows, cols):
+    tile_count, mem_count = got.shape[0], got.shape[1]
+    return got.reshape(tile_count, mem_count, rows, cols).transpose(1, 0, 2, 3).reshape(
+        mem_count * tile_count * rows, cols
+    )
+
+
 def body(
     source_blocks, send_blocks, recv_slot, recv_weight, recv_count, regional, x_operator, y_operator
 ):
     tile_count = lax.axis_size("tile")
+    mem_count = lax.axis_size("mem")
     member_count, level_count, columns, y_cells = regional.shape
     capacity = send_blocks.shape[2]
     block_cells = source_blocks.shape[3]
     block_side = math.isqrt(block_cells)
+    x_rows, x_cols = x_operator.shape
+    y_rows, y_cols = y_operator.shape
+    x_size = x_rows * x_cols
+
+    both = jnp.concatenate([x_operator.reshape(-1), y_operator.reshape(-1)])
+    both = gather_rows(both[None], "mem").reshape(mem_count, -1)
+    x_part = both[:, :x_size].reshape(-1)
+    y_part = both[:, x_size:].reshape(-1)
+
     picked = send_blocks[0].reshape(-1)
     packed = jnp.take(source_blocks, picked, axis=0).reshape(
         tile_count, capacity, member_count, level_count, block_cells
@@ -43,19 +77,24 @@
         member_count, level_count, columns, y_cells
     )
     difference = (remapped - regional.astype(jnp.float32)).astype(jnp.bfloat16)
-    x_lines = lax.all_to_all(difference, "tile", split_axis=3, concat_axis=2, tiled=True)
+
+    y_chunk = y_cells // tile_count
+    outgoing = difference.reshape(member_count, level_count, columns, tile_count, y_chunk)
+    got, x_got = exchange(outgoing.transpose(3, 0, 1, 2, 4), x_part)
+    x_lines = got.transpose(1, 2, 0, 3, 4).reshape(
+        member_count, level_count, tile_count * columns, y_chunk
+    )
+    x_full = rows_in_order(x_got.reshape(tile_count, mem_count, -1), x_rows, x_cols)
     after_first = jnp.einsum(
-        "ax,mlxy->mlay",
-        lax.all_gather(x_operator, ("mem", "tile"), axis=0, tiled=True),
-        x_lines,
-        preferred_element_type=jnp.float32,
+        "ax,mlxy->mlay", x_full, x_lines, preferred_element_type=jnp.float32
     ).astype(jnp.bfloat16)
-    tile_back = lax.all_to_all(after_first, "tile", split_axis=2, concat_axis=3, tiled=True)
+
+    back = after_first.reshape(member_count, level_count, tile_count, columns, y_chunk)
+    got, y_got = exchange(back.transpose(2, 0, 1, 3, 4), y_part)
+    tile_back = got.transpose(1, 2, 3, 0, 4).reshape(member_count, level_count, columns, y_cells)
+    y_full = rows_in_order(y_got.reshape(tile_count, mem_count, -1), y_rows, y_cols)
     after_second = jnp.einsum(
-        "by,mlxy->mlxb",
-        lax.all_gather(y_operator, ("mem", "tile"), axis=0, tiled=True),
-        tile_back,
-        preferred_element_type=jnp.float32,
+        "by,mlxy->mlxb", y_full, tile_back, preferred_element_type=jnp.float32
     )
     return (regional.astype(jnp.float32) + after_second).astype(jnp.bfloat16)
 

time: 122 us -> 76.8 us (0.63)
  blocking collectives: 82.9 us -> 11.8 us
  waiting for transfers between devices: 7.98 us -> 19.3 us
  local copies, waits for them, and re-layouts: 12.4 us -> 20.7 us
  other arithmetic: 3.08 us -> 7.27 us
  starting transfers between devices: 12.1 us -> 13.6 us
    all_gather x2 -> x0, blocking collectives: 82.9 us -> none  [the longest x1 43.6 us: body(): lax.all_gather(x_operator, ('mem', 'tile'), axis=0, tiled=True)]
    all_to_all x2, waiting for transfers between devices: 0.01 us -> 11.9 us  [the longest x1 11.8 us: exchange(): lax.all_to_all(payload, 'tile', split_axis=0, concat_axis=0, tiled=True)]
    all_to_all x0 -> x1, blocking collectives: none -> 11.8 us  [exchange(): lax.all_to_all(payload, 'tile', split_axis=0, concat_axis=0, tiled=True)]
    reshape x0 -> x11, local copies, waits for them, and re-layouts: none -> 5.16 us  [the longest x2 1.59 us: exchange(): flat = data.reshape(tile_count, -1)]
    all_to_all x2, starting transfers between devices: 6.92 us -> 9.86 us  [the longest x1 6.32 us: gather_rows(): lax.all_to_all(copies, axis_name, split_axis=0, concat_axis=0, tiled=True)]
    unnamed x19 -> x20, local copies, waits for them, and re-layouts: 3.32 us -> 5.68 us
    all_to_all x0 -> x4, other arithmetic: none -> 2.29 us  [exchange(): lax.all_to_all(payload, 'tile', split_axis=0, concat_axis=0, tiled=True)]
    all_to_all x1, starting transfers between devices: 5.18 us -> 3.72 us  [body(): lax.all_to_all(packed, 'tile', split_axis=0, concat_axis=0, tiled=True)]
  transfers between devices with their start and end apart: 3 -> 3, of which waited for: 1 -> 3; matrix products, arithmetic and copies ran while one was open for 0% -> 9% of each run, Pallas kernels for 0% -> 0%
where the time goes in v2:
time: 76.8 us; the launch traced here: 76.1 us
  local copies, waits for them, and re-layouts  20.7 us (27%)
  waiting for transfers between devices  19.3 us (25%)
  starting transfers between devices  13.6 us (18%)
  blocking collectives  11.8 us (15%)
  other arithmetic  7.27 us (9%)
  matrix products  3.15 us (4%)
    all_to_all x1, blocking collectives, exchange(): lax.all_to_all(payload, 'tile', split_axis=0, concat_axis=0, tiled=True)  11.8 us
    all_to_all x1, waiting for transfers between devices, exchange(): lax.all_to_all(payload, 'tile', split_axis=0, concat_axis=0, tiled=True)  11.8 us
    all_to_all x1, waiting for transfers between devices, body(): lax.all_to_all(packed, 'tile', split_axis=0, concat_axis=0, tiled=True)  7.39 us
    all_to_all x1, starting transfers between devices, gather_rows(): lax.all_to_all(copies, axis_name, split_axis=0, concat_axis=0, tiled=True)  6.32 us
    unnamed x20, local copies, waits for them, and re-layouts  5.68 us
    all_to_all x1, starting transfers between devices, body(): lax.all_to_all(packed, 'tile', split_axis=0, concat_axis=0, tiled=True)  3.72 us
    all_to_all x1, starting transfers between devices, exchange(): lax.all_to_all(payload, 'tile', split_axis=0, concat_axis=0, tiled=True)  3.54 us
    all_to_all x4, other arithmetic, exchange(): lax.all_to_all(payload, 'tile', split_axis=0, concat_axis=0, tiled=True)  2.29 us
  transfers between devices with their start and end apart: 3, of which 3 were waited for; matrix products, arithmetic and copies ran while one was open for 9% of the time, Pallas kernels for 0%

profile of v2, /device:TPU:0, one launch (start us, length us, event | category | flops | bytes accessed | tf_op | source)
XLA Modules:
  0.0 76.1 jit_solution(15492173306189883397)
XLA Ops:
  0.0 0.8 %reshape.145 = bf16[4608]{0:T(1024)(128)(2,1)S(1)} reshape(bf16[12,384]{1,0:T(8,128)(2,1)} %param.15) | data formatting | bytes 18432 | tf_op jit(solution)/shard_map/reshape | solution.py:46
  0.8 0.7 copy.42
  1.6 0.5 broadcast.81
  2.1 1.2 %reduce = bf16[4,12800]{1,0:T(4,128)(2,1)S(1)} reduce(bf16[4,1,12800]{2,1,0:T(2,128)(2,1)S(1)} %broadcast_in_dim.50, bf16[]{:T(256)} %broadcast.81), dimensions={1}, to_apply=%broadcast_in_dim.50.reduce_sub_computation | reduce | bytes 204802 | tf_op jit(solution)/shard_map/broadcast_in_dim | solution.py:11
  3.4 0.7 reshape.170
  4.1 6.3 %all-to-all-start.1 = ((bf16[4,2,6400]{2,1,0:T(2,128)(2,1)}), bf16[4,2,6400]{2,1,0:T(2,128)(2,1)S(1)}, u32[]{:S(2)}, u32[]{:S(2)}) async-start(bf16[4,2,6400]{2,1,0:T(2,128)(2,1)} %reshape.170), calls=%async_computation.1 | async-start | bytes 204800 | tf_op jit(solution)/shard_map/all_to_all | solution.py:12
  10.4 0.8 reshape_squeeze.6
  11.2 0.7 compare_and_fusion
  11.9 0.7 iota_compare_fusion
  12.7 0.8 %squeeze.3 = bf16[192]{0:T(256)(128)(2,1)S(1)} reshape(f32[1,8,24]{2,1,0:T(8,128)} %param.11) | data formatting | bytes 1152 | tf_op jit(solution)/shard_map/squeeze | solution.py:58
  13.5 1.4 %gather_fusion = bf16[192,2,2,256]{3,2,1,0:T(2,128)(2,1)S(1)} fusion(bf16[128,2,2,256]{3,2,1,0:T(2,128)(2,1)S(1)} %copy-done, s32[1024]{0:T(1024)S(1)} %pad_clamp_fusion), kind=kCustom, calls=%fused_computation | custom fusion | bytes 787200 | tf_op jit(solution)/shard_map/jit(_take)/gather | solution.py:52
  14.9 1.2 %broadcast_select_fusion = bf16[8,24,2,2,256]{4,3,2,1,0:T(2,128)(2,1)} fusion(bf16[8,24,2,2,256]{4,3,2,1,0:T(2,128)(2,1)S(1)} %bitcast.93, pred[8,24]{1,0:T(8,128)(4,1)S(1)} %compare_and_fusion), kind=kLoop, calls=%fused_computation.6 | loop fusion | flops 196608 | bytes 786624 | tf_op jit(solution)/shard_map/jit(_take)/select_n | solution.py:52
  16.1 0.1 all-to-all-done.1
  16.2 3.7 %all-to-all-start = ((bf16[8,24,2,2,256]{4,3,2,1,0:T(2,128)(2,1)}), bf16[8,24,2,2,256]{4,3,2,1,0:T(2,128)(2,1)S(1)}, u32[]{:S(2)}, u32[]{:S(2)}) async-start(bf16[8,24,2,2,256]{4,3,2,1,0:T(2,128)(2,1)} %broadcast_select_fusion), calls=%async_computation | async-start | bytes 786432 | tf_op jit(solution)/shard_map/all_to_all | solution.py:55
  20.3 0.6 pad.3.clone
  20.9 7.4 %all-to-all-done = bf16[8,24,2,2,256]{4,3,2,1,0:T(2,128)(2,1)S(1)} async-done(((bf16[8,24,2,2,256]{4,3,2,1,0:T(2,128)(2,1)}), bf16[8,24,2,2,256]{4,3,2,1,0:T(2,128)(2,1)S(1)}, u32[]{:S(2)}, u32[]{:S(2)}) %all-to-all-start) | async-done | bytes 393248 | tf_op jit(solution)/shard_map/all_to_all | solution.py:55
  28.3 0.3 reshape.140
  28.6 0.2 copy.26
  28.8 1.9 %convolution_bitcast_fusion = f32[2,2,4,16,24,16]{4,5,3,1,0,2:T(8,128)} fusion(bf16[2,2,16,16,192,1]{4,3,2,1,0,5:T(8,128)(2,1)S(1)} %bitcast.88, bf16[192]{0:T(256)(128)(2,1)S(1)} %broadcast_select_fusion.1, s32[4,24]{1,0:T(4,128)S(1)} %multiply_add_fusion, s32[192]{0:T(256)S(1)} %eq.15), kind=kOutput, calls=%fused_computation.1 | convolution fusion | flops 37785600 | bytes 787968 | tf_op jit(solution)/shard_map/dot_general | solution.py:63
  30.7 2.2 %copy.27 = f32[2,2,4,16,24,16]{5,4,3,2,1,0:T(8,128)S(1)} copy(f32[2,2,4,16,24,16]{4,5,3,1,0,2:T(8,128)} %convolution_bitcast_fusion) | data formatting | bytes 786432 | tf_op jit(solution)/shard_map/transpose | solution.py:76
  32.9 1.6 %reshape.141 = f32[2,2,64,384]{3,2,1,0:T(8,128)} reshape(f32[2,2,4,16,24,16]{5,4,3,2,1,0:T(8,128)S(1)} %copy.27) | data formatting | bytes 786432 | tf_op jit(solution)/shard_map/reshape | solution.py:76
  34.5 1.1 %fusion.2 = bf16[2,2,64,384]{3,2,1,0:T(8,128)(2,1)S(1)} fusion(f32[2,2,64,384]{3,2,1,0:T(8,128)} %reshape.141, bf16[2,2,64,384]{3,2,1,0:T(8,128)(2,1)} %param.13), kind=kLoop, calls=%fused_computation.12 | loop fusion | flops 294912 | bytes 786432 | tf_op jit(solution)/shard_map/convert_element_type | solution.py:79
  35.6 0.4 reshape.142
  36.1 0.1 copy.28
  36.2 0.8 %reshape.143 = bf16[8,12288]{1,0:T(8,128)(2,1)S(1)} reshape(bf16[8,2,2,64,48]{4,3,2,1,0:T(8,128)(2,1)S(1)} %copy.28) | data formatting | bytes 393216 | tf_op jit(solution)/shard_map/reshape | solution.py:17
  37.1 1.2 %reduce.1 = bf16[8,45056]{1,0:T(8,128)(2,1)S(1)} reduce(bf16[8,1,45056]{2,0,1:T(8,128)(2,1)S(1)} %maximum_bitcast_fusion, bf16[]{:T(256)} %broadcast.81), dimensions={1}, to_apply=%copy.29.reduce_sub_computation | reduce | bytes 1441794 | tf_op jit(solution)/shard_map/all_to_all | solution.py:22
  38.3 1.4 %reshape.172 = bf16[8,2,22528]{2,1,0:T(2,128)(2,1)} reshape(bf16[8,45056]{1,0:T(8,128)(2,1)S(1)} %reduce.1) | data formatting | bytes 1441792
  39.7 3.5 %all-to-all-start.2 = ((bf16[8,2,22528]{2,1,0:T(2,128)(2,1)}), bf16[8,2,22528]{2,1,0:T(2,128)(2,1)S(1)}, u32[]{:S(2)}, u32[]{:S(2)}) async-start(bf16[8,2,22528]{2,1,0:T(2,128)(2,1)} %reshape.172), calls=%async_computation.2 | async-start | bytes 1441792 | tf_op jit(solution)/shard_map/all_to_all | solution.py:22
  43.3 11.8 %all-to-all-done.2 = bf16[8,2,22528]{2,1,0:T(2,128)(2,1)S(1)} async-done(((bf16[8,2,22528]{2,1,0:T(2,128)(2,1)}), bf16[8,2,22528]{2,1,0:T(2,128)(2,1)S(1)}, u32[]{:S(2)}, u32[]{:S(2)}) %all-to-all-start.2) | async-done | bytes 720928 | tf_op jit(solution)/shard_map/all_to_all | solution.py:22
  55.1 0.7 reshape.173
  55.8 0.8 %copy.49 = bf16[8,1,45056]{2,0,1:T(8,128)(2,1)S(1)} copy(bf16[8,1,45056]{2,1,0:T(2,128)(2,1)S(1)} %reshape.173) | data formatting | bytes 1441792
  56.7 0.5 reshape.147
  57.2 0.3 copy.30
  57.5 0.3 reshape.148
  57.8 0.2 copy.31
  58.0 0.3 fusion.1
  58.3 0.2 reshape.150
  58.5 0.4 copy.32
  58.9 0.8 %reshape.151 = bf16[8,12288]{1,0:T(8,128)(2,1)S(1)} reshape(bf16[8,2,2,64,48]{4,3,2,1,0:T(8,128)(2,1)S(1)} %bitcast.86) | data formatting | bytes 393216 | tf_op jit(solution)/shard_map/reshape | solution.py:17
  59.8 1.0 %reduce.2 = bf16[8,30720]{1,0:T(8,128)(2,1)S(1)} reduce(bf16[8,1,30720]{2,0,1:T(8,128)(2,1)S(1)} %maximum_bitcast_fusion.1, bf16[]{:T(256)} %broadcast.81), dimensions={1}, to_apply=%copy.33.reduce_sub_computation | reduce | bytes 983042 | tf_op jit(solution)/shard_map/all_to_all | solution.py:22
  60.7 0.4 reshape.174
  61.1 11.8 %all_to_all.34 = bf16[8,2,15360]{2,1,0:T(2,128)(2,1)S(1)} all-to-all(bf16[8,2,15360]{2,1,0:T(2,128)(2,1)S(1)} %reshape.174), channel_id=1, replica_groups=mesh['mem'=4,'tile'=8] {'tile'}, dimensions={0} | all-to-all | bytes 983040 | tf_op jit(solution)/shard_map/all_to_all | solution.py:22
  72.9 0.4 reshape.175
  73.3 0.3 copy.50
  73.7 0.5 reshape.152
  74.2 0.3 copy.34
  74.6 0.4 reshape.153
  75.1 1.0 %fusion = bf16[2,2,64,384]{3,2,1,0:T(8,128)(2,1)} fusion(bf16[2,2,64,384]{3,2,1,0:T(8,128)(2,1)S(1)} %reshape.153, bf16[2,2,64,384]{3,2,1,0:T(8,128)(2,1)S(1)} %copy-done.1, bf16[384,384,1,1]{1,0,2,3:T(8,128)(2,1)S(1)} %reshape.166), kind=kOutput, calls=%fused_computation.4 | convolution fusion | flops 75792384 | bytes 884736 | tf_op jit(solution)/shard_map/by,mlxy->mlxb/dot_general | solution.py:96
  (31 shorter events, 1.0 us)
Async XLA Ops:
  0.0 13.5 %copy-start = (bf16[128,2,2,256]{3,2,1,0:T(2,128)(2,1)S(1)}, bf16[128,2,2,256]{3,2,1,0:T(2,128)(2,1)}, u32[]{:S(2)}) copy-start(bf16[128,2,2,256]{3,2,1,0:T(2,128)(2,1)} %param.8) | copy-start | bytes 786436
  3.4 16.6 %copy-start.3 = (s32[1,8,24]{2,1,0:T(8,128)S(1)}, s32[1,8,24]{2,1,0:T(8,128)}, u32[]{:S(2)}) copy-start(s32[1,8,24]{2,1,0:T(8,128)} %param.10) | copy-start | bytes 2308
  4.1 12.2 %all-to-all-start.1 = ((bf16[4,2,6400]{2,1,0:T(2,128)(2,1)}), bf16[4,2,6400]{2,1,0:T(2,128)(2,1)S(1)}, u32[]{:S(2)}, u32[]{:S(2)}) async-start(bf16[4,2,6400]{2,1,0:T(2,128)(2,1)} %reshape.170), calls=%async_computation.1 | async-start | bytes 204800 | tf_op jit(solution)/shard_map/all_to_all | solution.py:12
  16.2 12.1 %all-to-all-start = ((bf16[8,24,2,2,256]{4,3,2,1,0:T(2,128)(2,1)}), bf16[8,24,2,2,256]{4,3,2,1,0:T(2,128)(2,1)S(1)}, u32[]{:S(2)}, u32[]{:S(2)}) async-start(bf16[8,24,2,2,256]{4,3,2,1,0:T(2,128)(2,1)} %broadcast_select_fusion), calls=%async_computation | async-start | bytes 786432 | tf_op jit(solution)/shard_map/all_to_all | solution.py:55
  35.6 1.4 %copy-start.2 = (bf16[45056]{0:T(1024)(128)(2,1)S(1)}, bf16[45056]{0:T(1024)(128)(2,1)}, u32[]{:S(2)}) copy-start(bf16[45056]{0:T(1024)(128)(2,1)} %pad.3.clone) | copy-start | bytes 270340
  39.7 15.4 %all-to-all-start.2 = ((bf16[8,2,22528]{2,1,0:T(2,128)(2,1)}), bf16[8,2,22528]{2,1,0:T(2,128)(2,1)S(1)}, u32[]{:S(2)}, u32[]{:S(2)}) async-start(bf16[8,2,22528]{2,1,0:T(2,128)(2,1)} %reshape.172), calls=%async_computation.2 | async-start | bytes 1441792 | tf_op jit(solution)/shard_map/all_to_all | solution.py:22
  74.2 0.9 %copy-start.1 = (bf16[2,2,64,384]{3,2,1,0:T(8,128)(2,1)S(1)}, bf16[2,2,64,384]{3,2,1,0:T(8,128)(2,1)}, u32[]{:S(2)}) copy-start(bf16[2,2,64,384]{3,2,1,0:T(8,128)(2,1)} %param.13) | copy-start | bytes 589828

commit v3 on v1

--- a/solution.py
+++ b/solution.py
@@ -6,10 +6,19 @@
 from jax.sharding import PartitionSpec as P
 
 
-def gather_rows(shard, axis_name):
+def doubling_gather(data, axis_name, bits):
     count = lax.axis_size(axis_name)
-    copies = jnp.broadcast_to(shard[None], (count,) + shard.shape)
-    return lax.all_to_all(copies, axis_name, split_axis=0, concat_axis=0, tiled=True)
+    index = lax.axis_index(axis_name)
+    for bit in bits:
+        received = lax.ppermute(data, axis_name, [(j, j ^ bit) for j in range(count)])
+        high = (index // bit) % 2 == 1
+        data = jnp.stack([jnp.where(high, received, data), jnp.where(high, data, received)])
+    return data
+
+
+def bit_order(count, bits):
+    stacked = list(reversed(bits))
+    return [stacked.index(bit) for bit in sorted(bits, reverse=True)]
 
 
 def gather_operators(x_operator, y_operator):
@@ -19,10 +28,17 @@
     y_rows, y_cols = y_operator.shape
     x_size = x_rows * x_cols
     both = jnp.concatenate([x_operator.reshape(-1), y_operator.reshape(-1)])
-    both = gather_rows(gather_rows(both[None], "mem"), "tile")
-    both = both.reshape(tile_count, mem_count, -1).transpose(1, 0, 2)
-    x_full = both[:, :, :x_size].reshape(mem_count * tile_count * x_rows, x_cols)
-    y_full = both[:, :, x_size:].reshape(mem_count * tile_count * y_rows, y_cols)
+    mem_bits = [1 << k for k in range(mem_count.bit_length() - 1)]
+    tile_bits = [1 << k for k in range(1, tile_count.bit_length() - 1)] + [1]
+    both = doubling_gather(both, "mem", mem_bits)
+    both = doubling_gather(both, "tile", tile_bits)
+    tile_axes = bit_order(tile_count, tile_bits)
+    mem_axes = [len(tile_bits) + k for k in bit_order(mem_count, mem_bits)]
+    both = both.transpose(mem_axes + tile_axes + [both.ndim - 1]).reshape(
+        mem_count * tile_count, -1
+    )
+    x_full = both[:, :x_size].reshape(mem_count * tile_count * x_rows, x_cols)
+    y_full = both[:, x_size:].reshape(mem_count * tile_count * y_rows, y_cols)
     return x_full, y_full
 
 

time: 74 us -> 66.6 us (0.90)
  waiting for transfers between devices: 29 us -> 19.2 us
  other arithmetic: 4.35 us -> 8.9 us
  local copies, waits for them, and re-layouts: 16.1 us -> 14.2 us
    all_to_all x2 -> x0, waiting for transfers between devices: 12.1 us -> none  [gather_rows(): lax.all_to_all(copies, axis_name, split_axis=0, concat_axis=0, tiled=True)]
    all_to_all x2 -> x0, starting transfers between devices: 8.42 us -> none  [gather_rows(): lax.all_to_all(copies, axis_name, split_axis=0, concat_axis=0, tiled=True)]
    ppermute x0 -> x5, starting transfers between devices: none -> 7.99 us  [doubling_gather(): lax.ppermute(data, axis_name, [(j, j ^ bit) for j in range(count)])]
    ppermute x0 -> x5, waiting for transfers between devices: none -> 7.47 us  [doubling_gather(): lax.ppermute(data, axis_name, [(j, j ^ bit) for j in range(count)])]
    all_to_all x1, waiting for transfers between devices: 5.34 us -> 0.01 us  [body(): lax.all_to_all(packed, 'tile', split_axis=0, concat_axis=0, tiled=True)]
    another operation x0 -> x8, other arithmetic: none -> 4.65 us  [doubling_gather(): jnp.stack([jnp.where(high, received, data), jnp.where(high, data, receive...]
    broadcast_in_dim x3 -> x0, local copies, waits for them, and re-layouts: 1.75 us -> none  [gather_rows(): copies = jnp.broadcast_to(shard[None], (count,) + shard.shape)]
    broadcast_in_dim x1 -> x0, other arithmetic: 1.26 us -> none  [gather_rows(): copies = jnp.broadcast_to(shard[None], (count,) + shard.shape)]
  transfers between devices with their start and end apart: 5 -> 8, of which waited for: 4 -> 5; matrix products, arithmetic and copies ran while one was open for 18% -> 18% of each run, Pallas kernels for 0% -> 0%
where the time goes in v3:
time: 66.6 us; the launch traced here: 66.1 us
  starting transfers between devices  20.3 us (30%)
  waiting for transfers between devices  19.2 us (29%)
  local copies, waits for them, and re-layouts  14.2 us (21%)
  other arithmetic  8.9 us (13%)
  matrix products  3.13 us (5%)
    ppermute x5, starting transfers between devices, doubling_gather(): lax.ppermute(data, axis_name, [(j, j ^ bit) for j in range(count)])  7.99 us
    ppermute x5, waiting for transfers between devices, doubling_gather(): lax.ppermute(data, axis_name, [(j, j ^ bit) for j in range(count)])  7.47 us
    all_to_all x1, waiting for transfers between devices, body(): lax.all_to_all(difference, 'tile', split_axis=3, concat_axis=2, tiled=True)  5.97 us
    all_to_all x1, waiting for transfers between devices, body(): lax.all_to_all(after_first, 'tile', split_axis=2, concat_axis=3, tiled=True)  5.77 us
    all_to_all x1, starting transfers between devices, body(): lax.all_to_all(packed, 'tile', split_axis=0, concat_axis=0, tiled=True)  5.18 us
    another operation x8, other arithmetic, doubling_gather(): jnp.stack([jnp.where(high, received, data), jnp.where(high, data, receive...  4.65 us
    all_to_all x1, starting transfers between devices, body(): lax.all_to_all(difference, 'tile', split_axis=3, concat_axis=2, tiled=True)  3.57 us
    all_to_all x1, starting transfers between devices, body(): lax.all_to_all(after_first, 'tile', split_axis=2, concat_axis=3, tiled=True)  3.52 us
  transfers between devices with their start and end apart: 8, of which 5 were waited for; matrix products, arithmetic and copies ran while one was open for 18% of the time, Pallas kernels for 0%

profile of v3, /device:TPU:0, one launch (start us, length us, event | category | flops | bytes accessed | tf_op | source)
XLA Modules:
  0.0 66.1 jit_solution(17107505966029430035)
XLA Ops:
  0.0 0.8 %reshape_squeeze.6 = s32[192,1]{0,1:T(1,128)S(1)} reshape(s32[1,8,24]{2,1,0:T(8,128)} %param.9) | data formatting | bytes 1536 | tf_op jit(solution)/shard_map/reshape;squeeze | solution.py:54
  0.8 0.7 %compare_and_fusion = pred[8,24]{1,0:T(8,128)(4,1)S(1)} fusion(s32[1,8,24]{2,1,0:T(8,128)} %param.9), kind=kLoop, calls=%fused_computation.47 | loop fusion | flops 1152 | bytes 960 | tf_op jit(solution)/shard_map/jit(_take)/and | solution.py:55
  1.6 1.4 %gather_fusion = bf16[192,2,2,256]{3,2,1,0:T(2,128)(2,1)S(1)} fusion(bf16[128,2,2,256]{3,2,1,0:T(2,128)(2,1)S(1)} %copy-done, s32[1024]{0:T(1024)S(1)} %pad_clamp_fusion), kind=kCustom, calls=%fused_computation | custom fusion | bytes 787200 | tf_op jit(solution)/shard_map/jit(_take)/gather | solution.py:55
  3.0 1.2 %broadcast_select_fusion.2 = bf16[8,24,2,2,256]{4,3,2,1,0:T(2,128)(2,1)} fusion(bf16[8,24,2,2,256]{4,3,2,1,0:T(2,128)(2,1)S(1)} %bitcast.74, pred[8,24]{1,0:T(8,128)(4,1)S(1)} %compare_and_fusion), kind=kLoop, calls=%fused_computation.9 | loop fusion | flops 196608 | bytes 786624 | tf_op jit(solution)/shard_map/jit(_take)/select_n | solution.py:55
  4.2 5.2 %all-to-all-start = ((bf16[8,24,2,2,256]{4,3,2,1,0:T(2,128)(2,1)}), bf16[8,24,2,2,256]{4,3,2,1,0:T(2,128)(2,1)S(1)}, u32[]{:S(2)}, u32[]{:S(2)}) async-start(bf16[8,24,2,2,256]{4,3,2,1,0:T(2,128)(2,1)} %broadcast_select_fusion.2), calls=%async_computation | async-start | bytes 786432 | tf_op jit(solution)/shard_map/all_to_all | solution.py:58
  9.5 1.6 %collective-permute-start = (bf16[12800]{0:T(1024)(128)(2,1)S(1)}, bf16[12800]{0:T(1024)(128)(2,1)S(1)}, u32[]{:S(2)}, u32[]{:S(2)}) collective-permute-start(bf16[12800]{0:T(1024)(128)(2,1)S(1)} %constant_dynamic-update-slice_fusion), channel_id=1, source_target_pairs={{0,8},{8,0},{16,24},{24,16},{1,9},{9,1},{17,25},{25,17},{2,10},{10... | collective-permute-start | bytes 76808 | tf_op jit(solution)/shard_map/ppermute | solution.py:13
  11.2 0.1 lt.64
  11.4 2.0 %collective-permute-done = bf16[12800]{0:T(1024)(128)(2,1)S(1)} collective-permute-done((bf16[12800]{0:T(1024)(128)(2,1)S(1)}, bf16[12800]{0:T(1024)(128)(2,1)S(1)}, u32[]{:S(2)}, u32[]{:S(2)}) %collective-permute-start) | collective-permute-done | bytes 25632 | tf_op jit(solution)/shard_map/ppermute | solution.py:13
  13.5 0.1 pad_maximum_fusion.3
  13.6 2.7 %collective-permute-start.1 = (bf16[2,12800]{1,0:T(2,128)(2,1)S(1)}, bf16[2,12800]{1,0:T(2,128)(2,1)S(1)}, u32[]{:S(2)}, u32[]{:S(2)}) collective-permute-start(bf16[2,12800]{1,0:T(2,128)(2,1)S(1)} %pad_maximum_fusion.3), channel_id=1, source_target_pairs={{0,16},{8,24},{16,0},{24,8},{1,17},{9,25},{17,1},{25,9},{2,18},{10... | collective-permute-start | bytes 153608 | tf_op jit(solution)/shard_map/ppermute | solution.py:13
  16.3 2.6 %collective-permute-done.1 = bf16[2,12800]{1,0:T(2,128)(2,1)S(1)} collective-permute-done((bf16[2,12800]{1,0:T(2,128)(2,1)S(1)}, bf16[2,12800]{1,0:T(2,128)(2,1)S(1)}, u32[]{:S(2)}, u32[]{:S(2)}) %collective-permute-start.1) | collective-permute-done | bytes 51232 | tf_op jit(solution)/shard_map/ppermute | solution.py:13
  18.9 0.2 fusion.11
  19.1 0.1 pad_maximum_fusion.2
  19.2 1.8 %collective-permute-start.2 = (bf16[2,2,12800]{2,1,0:T(2,128)(2,1)S(1)}, bf16[2,2,12800]{2,1,0:T(2,128)(2,1)S(1)}, u32[]{:S(2)}, u32[]{:S(2)}) collective-permute-start(bf16[2,2,12800]{2,1,0:T(2,128)(2,1)S(1)} %pad_maximum_fusion.2), channel_id=1, source_target_pairs={{0,2},{1,3},{2,0},{3,1},{4,6},{5,7},{6,4},{7,5},{8,10},{9,11},{10,... | collective-permute-start | bytes 307208 | tf_op jit(solution)/shard_map/ppermute | solution.py:13
  21.1 2.9 %collective-permute-done.2 = bf16[2,2,12800]{2,1,0:T(2,128)(2,1)S(1)} collective-permute-done((bf16[2,2,12800]{2,1,0:T(2,128)(2,1)S(1)}, bf16[2,2,12800]{2,1,0:T(2,128)(2,1)S(1)}, u32[]{:S(2)}, u32[]{:S(2)}) %collective-permute-start.2) | collective-permute-done | bytes 102432 | tf_op jit(solution)/shard_map/ppermute | solution.py:13
  23.9 0.2 fusion.9
  24.2 1.0 %pad_maximum_fusion.1 = bf16[2,2,2,12800]{3,2,1,0:T(2,128)(2,1)} fusion(bf16[1,2,2,12800]{3,2,1,0:T(2,128)(2,1)S(1)} %get-tuple-element.10, bf16[1,2,2,12800]{3,2,1,0:T(2,128)(2,1)S(1)} %get-tuple-element.9), kind=kLoop, calls=%fused_computation.23 | loop fusion | flops 102400 | bytes 409600 | tf_op jit(solution)/shard_map/stack | solution.py:15
  25.2 1.8 %collective-permute-start.3 = (bf16[2,2,2,12800]{3,2,1,0:T(2,128)(2,1)}, bf16[2,2,2,12800]{3,2,1,0:T(2,128)(2,1)}, u32[]{:S(2)}, u32[]{:S(2)}) collective-permute-start(bf16[2,2,2,12800]{3,2,1,0:T(2,128)(2,1)} %pad_maximum_fusion.1), channel_id=1, source_target_pairs={{0,4},{1,5},{2,6},{3,7},{4,0},{5,1},{6,2},{7,3},{8,12},{9,13},{10,... | collective-permute-start | bytes 614408 | tf_op jit(solution)/shard_map/ppermute | solution.py:13
  27.0 0.3 reshape.107
  27.2 0.2 copy.24
  27.4 1.8 %convolution_bitcast_fusion = f32[2,2,4,16,24,16]{4,5,3,1,0,2:T(8,128)} fusion(bf16[2,2,16,16,192,1]{4,3,2,1,0,5:T(8,128)(2,1)S(1)} %bitcast.70, bf16[192]{0:T(256)(128)(2,1)S(1)} %broadcast_select_fusion.11, s32[4,24]{1,0:T(4,128)S(1)} %multiply_add_fusion, s32[192]{0:T(256)S(1)} %eq.36), kind=kOutput, calls=%fused_computation.1 | convolution fusion | flops 37785600 | bytes 787968 | tf_op jit(solution)/shard_map/dot_general | solution.py:66
  29.3 2.2 %copy.25 = f32[2,2,4,16,24,16]{5,4,3,2,1,0:T(8,128)S(1)} copy(f32[2,2,4,16,24,16]{4,5,3,1,0,2:T(8,128)} %convolution_bitcast_fusion) | data formatting | bytes 786432 | tf_op jit(solution)/shard_map/transpose | solution.py:79
  31.5 1.6 %reshape.108 = f32[2,2,64,384]{3,2,1,0:T(8,128)} reshape(f32[2,2,4,16,24,16]{5,4,3,2,1,0:T(8,128)S(1)} %copy.25) | data formatting | bytes 786432 | tf_op jit(solution)/shard_map/reshape | solution.py:79
  33.2 1.5 %fusion.7 = (bf16[1,2,2,2,12800]{4,3,2,1,0:T(2,128)(2,1)S(1)}, bf16[1,2,2,2,12800]{4,3,2,1,0:T(2,128)(2,1)S(1)}) fusion(bf16[2,2,2,12800]{3,2,1,0:T(2,128)(2,1)} %collective-permute-done.3, pred[]{:T(512)S(6)} %eq.40, bf16[1,2,2,12800]{3,2,1,0:T(2,128)(2,1)} %copy-done.1, bf16[1,2,2,12800]{3,2,1,0:T(2,128)(2,1)S(1)} %get-tuple-element.9), kind=kLoop, calls=%fused_computation.21 | loop fusion | flops 307200 | bytes 819201 | tf_op jit(solution)/shard_map/stack | solution.py:15
  34.6 0.6 pad_maximum_fusion
  35.3 1.1 %fusion.5 = bf16[2,2,64,384]{3,2,1,0:T(8,128)(2,1)S(1)} fusion(f32[2,2,64,384]{3,2,1,0:T(8,128)} %reshape.108, bf16[2,2,64,384]{3,2,1,0:T(8,128)(2,1)} %param.13), kind=kLoop, calls=%fused_computation.18 | loop fusion | flops 294912 | bytes 786432 | tf_op jit(solution)/shard_map/convert_element_type | solution.py:82
  36.4 0.6 copy.26
  37.0 1.0 %reshape.128 = bf16[8,2,6144]{2,1,0:T(2,128)(2,1)} reshape(bf16[384,2,2,64]{3,2,1,0:T(2,128)(2,1)S(1)} %bitcast.76) | data formatting | bytes 393216
  38.0 3.6 %all-to-all-start.1 = ((bf16[8,2,6144]{2,1,0:T(2,128)(2,1)}), bf16[8,2,6144]{2,1,0:T(2,128)(2,1)S(1)}, u32[]{:S(2)}, u32[]{:S(2)}) async-start(bf16[8,2,6144]{2,1,0:T(2,128)(2,1)} %reshape.128), calls=%async_computation.1 | async-start | bytes 393216 | tf_op jit(solution)/shard_map/all_to_all | solution.py:83
  41.6 6.0 %all-to-all-done.1 = bf16[8,2,6144]{2,1,0:T(2,128)(2,1)S(1)} async-done(((bf16[8,2,6144]{2,1,0:T(2,128)(2,1)}), bf16[8,2,6144]{2,1,0:T(2,128)(2,1)S(1)}, u32[]{:S(2)}, u32[]{:S(2)}) %all-to-all-start.1) | async-done | bytes 196640 | tf_op jit(solution)/shard_map/all_to_all | solution.py:83
  47.6 0.3 reshape.129
  47.8 0.3 copy.41
  48.1 0.3 all_to_all.33
  48.4 1.0 %fusion.3 = (bf16[1,2,2,2,2,12800]{5,4,3,2,1,0:T(2,128)(2,1)S(1)}, bf16[1,2,2,2,2,12800]{5,4,3,2,1,0:T(2,128)(2,1)S(1)}) fusion(bf16[2,2,2,2,12800]{4,3,2,1,0:T(2,128)(2,1)S(1)} %collective-permute-done.4, pred[]{:T(512)S(6)} %eq.39, bf16[1,2,2,2,12800]{4,3,2,1,0:T(2,128)(2,1)S(1)} %get-tuple-element.8, bf16[1,2,2,2,12800]{4,3,2,1,0:T(2,128)(2,1)S(1)} %get-tuple-element.7), kind=kLoop, calls=%fused_computation.13 | loop fusion | flops 614400 | bytes 1638401 | tf_op jit(solution)/shard_map/stack | solution.py:15
  49.4 1.2 %maximum_bitcast_fusion = bf16[2,2,2,2,2,12800]{5,1,0,3,2,4:T(2,128)(2,1)S(1)} fusion(bf16[1,2,2,2,2,12800]{5,4,3,2,1,0:T(2,128)(2,1)S(1)} %get-tuple-element.6, bf16[1,2,2,2,2,12800]{5,4,3,2,1,0:T(2,128)(2,1)S(1)} %get-tuple-element.5), kind=kLoop, calls=%fused_computation.6 | loop fusion | flops 409600 | bytes 1638400 | tf_op jit(solution)/shard_map/transpose | solution.py:37
  50.5 0.8 %copy.29 = bf16[2,2,2,2,2,12800]{5,4,3,2,1,0:T(2,128)(2,1)S(1)} copy(bf16[2,2,2,2,2,12800]{5,1,0,3,2,4:T(2,128)(2,1)S(1)} %maximum_bitcast_fusion) | data formatting | bytes 1638400 | tf_op jit(solution)/shard_map/transpose | solution.py:37
  51.4 0.3 reshape.111
  51.7 0.2 reshape.124
  52.0 0.3 fusion.1
  52.3 0.4 copy.30
  52.7 1.4 %reshape.130 = bf16[8,2,6144]{2,1,0:T(2,128)(2,1)} reshape(bf16[512,2,2,48]{3,2,1,0:T(2,128)(2,1)S(1)} %bitcast.71) | data formatting | bytes 393216
  54.2 3.5 %all-to-all-start.2 = ((bf16[8,2,6144]{2,1,0:T(2,128)(2,1)}), bf16[8,2,6144]{2,1,0:T(2,128)(2,1)S(1)}, u32[]{:S(2)}, u32[]{:S(2)}) async-start(bf16[8,2,6144]{2,1,0:T(2,128)(2,1)} %reshape.130), calls=%async_computation.2 | async-start | bytes 393216 | tf_op jit(solution)/shard_map/all_to_all | solution.py:90
  57.7 0.4 reshape.125
  58.1 5.8 %all-to-all-done.2 = bf16[8,2,6144]{2,1,0:T(2,128)(2,1)S(1)} async-done(((bf16[8,2,6144]{2,1,0:T(2,128)(2,1)}), bf16[8,2,6144]{2,1,0:T(2,128)(2,1)S(1)}, u32[]{:S(2)}, u32[]{:S(2)}) %all-to-all-start.2) | async-done | bytes 196640 | tf_op jit(solution)/shard_map/all_to_all | solution.py:90
  63.9 0.5 reshape.131
  64.4 0.3 copy.40
  64.7 0.4 all_to_all.37
  65.1 1.0 %fusion = bf16[2,2,64,384]{3,2,1,0:T(8,128)(2,1)} fusion(bf16[2,2,64,384]{3,2,1,0:T(8,128)(2,1)S(1)} %all_to_all.37, bf16[2,2,64,384]{3,2,1,0:T(8,128)(2,1)S(1)} %copy-done.2, bf16[384,384,1,1]{1,0,2,3:T(8,128)(2,1)S(1)} %reshape.125), kind=kOutput, calls=%fused_computation.4 | convolution fusion | flops 75792384 | bytes 884736 | tf_op jit(solution)/shard_map/by,mlxy->mlxb/dot_general | solution.py:91
  (36 shorter events, 0.5 us)
Async XLA Ops:
  0.0 1.5 %copy-start = (bf16[128,2,2,256]{3,2,1,0:T(2,128)(2,1)S(1)}, bf16[128,2,2,256]{3,2,1,0:T(2,128)(2,1)}, u32[]{:S(2)}) copy-start(bf16[128,2,2,256]{3,2,1,0:T(2,128)(2,1)} %param.8) | copy-start | bytes 786436
  0.0 9.4 %copy-start.3 = (bf16[16,512]{1,0:T(8,128)(2,1)S(1)}, bf16[16,512]{1,0:T(8,128)(2,1)}, u32[]{:S(2)}) copy-start(bf16[16,512]{1,0:T(8,128)(2,1)} %param.14) | copy-start | bytes 49156
  0.0 9.4 %copy-start.4 = (bf16[12,384]{1,0:T(8,128)(2,1)S(1)}, bf16[12,384]{1,0:T(8,128)(2,1)}, u32[]{:S(2)}) copy-start(bf16[12,384]{1,0:T(8,128)(2,1)} %param.15) | copy-start | bytes 27652
  0.0 11.1 %copy-start.7 = (s32[1,8]{1,0:T(1,128)S(1)}, s32[1,8]{1,0:T(1,128)}, u32[]{:S(2)}) copy-start(s32[1,8]{1,0:T(1,128)} %param.12) | copy-start | bytes 100
  0.0 11.3 %copy-start.6 = (f32[1,8,24]{2,1,0:T(8,128)S(1)}, f32[1,8,24]{2,1,0:T(8,128)}, u32[]{:S(2)}) copy-start(f32[1,8,24]{2,1,0:T(8,128)} %param.11) | copy-start | bytes 2308
  0.0 16.2 %copy-start.5 = (s32[1,8,24]{2,1,0:T(8,128)S(1)}, s32[1,8,24]{2,1,0:T(8,128)}, u32[]{:S(2)}) copy-start(s32[1,8,24]{2,1,0:T(8,128)} %param.10) | copy-start | bytes 2308
  4.2 22.7 %all-to-all-start = ((bf16[8,24,2,2,256]{4,3,2,1,0:T(2,128)(2,1)}), bf16[8,24,2,2,256]{4,3,2,1,0:T(2,128)(2,1)S(1)}, u32[]{:S(2)}, u32[]{:S(2)}) async-start(bf16[8,24,2,2,256]{4,3,2,1,0:T(2,128)(2,1)} %broadcast_select_fusion.2), calls=%async_computation | async-start | bytes 786432 | tf_op jit(solution)/shard_map/all_to_all | solution.py:58
  9.5 3.9 %collective-permute-start = (bf16[12800]{0:T(1024)(128)(2,1)S(1)}, bf16[12800]{0:T(1024)(128)(2,1)S(1)}, u32[]{:S(2)}, u32[]{:S(2)}) collective-permute-start(bf16[12800]{0:T(1024)(128)(2,1)S(1)} %constant_dynamic-update-slice_fusion), channel_id=1, source_target_pairs={{0,8},{8,0},{16,24},{24,16},{1,9},{9,1},{17,25},{25,17},{2,10},{10... | collective-permute-start | bytes 76808 | tf_op jit(solution)/shard_map/ppermute | solution.py:13
  13.6 5.3 %collective-permute-start.1 = (bf16[2,12800]{1,0:T(2,128)(2,1)S(1)}, bf16[2,12800]{1,0:T(2,128)(2,1)S(1)}, u32[]{:S(2)}, u32[]{:S(2)}) collective-permute-start(bf16[2,12800]{1,0:T(2,128)(2,1)S(1)} %pad_maximum_fusion.3), channel_id=1, source_target_pairs={{0,16},{8,24},{16,0},{24,8},{1,17},{9,25},{17,1},{25,9},{2,18},{10... | collective-permute-start | bytes 153608 | tf_op jit(solution)/shard_map/ppermute | solution.py:13
  19.2 4.7 %collective-permute-start.2 = (bf16[2,2,12800]{2,1,0:T(2,128)(2,1)S(1)}, bf16[2,2,12800]{2,1,0:T(2,128)(2,1)S(1)}, u32[]{:S(2)}, u32[]{:S(2)}) collective-permute-start(bf16[2,2,12800]{2,1,0:T(2,128)(2,1)S(1)} %pad_maximum_fusion.2), channel_id=1, source_target_pairs={{0,2},{1,3},{2,0},{3,1},{4,6},{5,7},{6,4},{7,5},{8,10},{9,11},{10,... | collective-permute-start | bytes 307208 | tf_op jit(solution)/shard_map/ppermute | solution.py:13
  24.2 3.0 %copy-start.1 = (bf16[1,2,2,12800]{3,2,1,0:T(2,128)(2,1)}, bf16[1,2,2,12800]{3,2,1,0:T(2,128)(2,1)S(1)}, u32[]{:S(2)}) copy-start(bf16[1,2,2,12800]{3,2,1,0:T(2,128)(2,1)S(1)} %get-tuple-element.10) | copy-start | bytes 307204
  25.2 8.0 %collective-permute-start.3 = (bf16[2,2,2,12800]{3,2,1,0:T(2,128)(2,1)}, bf16[2,2,2,12800]{3,2,1,0:T(2,128)(2,1)}, u32[]{:S(2)}, u32[]{:S(2)}) collective-permute-start(bf16[2,2,2,12800]{3,2,1,0:T(2,128)(2,1)} %pad_maximum_fusion.1), channel_id=1, source_target_pairs={{0,4},{1,5},{2,6},{3,7},{4,0},{5,1},{6,2},{7,3},{8,12},{9,13},{10,... | collective-permute-start | bytes 614408 | tf_op jit(solution)/shard_map/ppermute | solution.py:13
  35.2 13.2 %collective-permute-start.4 = (bf16[2,2,2,2,12800]{4,3,2,1,0:T(2,128)(2,1)S(1)}, bf16[2,2,2,2,12800]{4,3,2,1,0:T(2,128)(2,1)S(1)}, u32[]{:S(2)}, u32[]{:S(2)}) collective-permute-start(bf16[2,2,2,2,12800]{4,3,2,1,0:T(2,128)(2,1)S(1)} %pad_maximum_fusion), channel_id=1, source_target_pairs={{0,1},{1,0},{2,3},{3,2},{4,5},{5,4},{6,7},{7,6},{8,9},{9,8},{10,11... | collective-permute-start | bytes 1228808 | tf_op jit(solution)/shard_map/ppermute | solution.py:13
  38.0 9.6 %all-to-all-start.1 = ((bf16[8,2,6144]{2,1,0:T(2,128)(2,1)}), bf16[8,2,6144]{2,1,0:T(2,128)(2,1)S(1)}, u32[]{:S(2)}, u32[]{:S(2)}) async-start(bf16[8,2,6144]{2,1,0:T(2,128)(2,1)} %reshape.128), calls=%async_computation.1 | async-start | bytes 393216 | tf_op jit(solution)/shard_map/all_to_all | solution.py:83
  54.2 10.9 %copy-start.2 = (bf16[2,2,64,384]{3,2,1,0:T(8,128)(2,1)S(1)}, bf16[2,2,64,384]{3,2,1,0:T(8,128)(2,1)}, u32[]{:S(2)}) copy-start(bf16[2,2,64,384]{3,2,1,0:T(8,128)(2,1)} %param.13) | copy-start | bytes 589828
  54.2 9.7 %all-to-all-start.2 = ((bf16[8,2,6144]{2,1,0:T(2,128)(2,1)}), bf16[8,2,6144]{2,1,0:T(2,128)(2,1)S(1)}, u32[]{:S(2)}, u32[]{:S(2)}) async-start(bf16[8,2,6144]{2,1,0:T(2,128)(2,1)} %reshape.130), calls=%async_computation.2 | async-start | bytes 393216 | tf_op jit(solution)/shard_map/all_to_all | solution.py:90

commit v4 on v3

--- a/solution.py
+++ b/solution.py
@@ -21,7 +21,7 @@
     return [stacked.index(bit) for bit in sorted(bits, reverse=True)]
 
 
-def gather_operators(x_operator, y_operator):
+def gather_operators(x_operator, y_operator, after):
     mem_count = lax.axis_size("mem")
     tile_count = lax.axis_size("tile")
     x_rows, x_cols = x_operator.shape
@@ -31,6 +31,7 @@
     mem_bits = [1 << k for k in range(mem_count.bit_length() - 1)]
     tile_bits = [1 << k for k in range(1, tile_count.bit_length() - 1)] + [1]
     both = doubling_gather(both, "mem", mem_bits)
+    both, after = lax.optimization_barrier((both, after))
     both = doubling_gather(both, "tile", tile_bits)
     tile_axes = bit_order(tile_count, tile_bits)
     mem_axes = [len(tile_bits) + k for k in bit_order(mem_count, mem_bits)]
@@ -39,7 +40,7 @@
     )
     x_full = both[:, :x_size].reshape(mem_count * tile_count * x_rows, x_cols)
     y_full = both[:, x_size:].reshape(mem_count * tile_count * y_rows, y_cols)
-    return x_full, y_full
+    return x_full, y_full, after
 
 
 def body(
@@ -50,12 +51,12 @@
     capacity = send_blocks.shape[2]
     block_cells = source_blocks.shape[3]
     block_side = math.isqrt(block_cells)
-    x_full, y_full = gather_operators(x_operator, y_operator)
     picked = send_blocks[0].reshape(-1)
     packed = jnp.take(source_blocks, picked, axis=0).reshape(
         tile_count, capacity, member_count, level_count, block_cells
     )
     arrived = lax.all_to_all(packed, "tile", split_axis=0, concat_axis=0, tiled=True)
+    x_full, y_full, arrived = gather_operators(x_operator, y_operator, arrived)
     slot_count = columns // block_side * (y_cells // block_side)
     live_mask = lax.broadcasted_iota(jnp.int32, (tile_count, capacity), 1) < recv_count[0][:, None]
     weights = jnp.where(live_mask, recv_weight[0], 0.0).reshape(-1)

time: 66.6 us -> 66.4 us (level)
  starting transfers between devices: 20.3 us -> 17.8 us
  local copies, waits for them, and re-layouts: 14.2 us -> 15.6 us
  waiting for transfers between devices: 19.2 us -> 20.2 us
    all_to_all x1, starting transfers between devices: 5.18 us -> 3.72 us  [body(): lax.all_to_all(packed, 'tile', split_axis=0, concat_axis=0, tiled=True)]
    all_to_all x1, waiting for transfers between devices: 0.01 us -> 1.4 us  [body(): lax.all_to_all(packed, 'tile', split_axis=0, concat_axis=0, tiled=True)]
    ppermute x5, starting transfers between devices: 7.99 us -> 6.94 us  [doubling_gather(): lax.ppermute(data, axis_name, [(j, j ^ bit) for j in range(count)])]
    unnamed x22 -> x18, local copies, waits for them, and re-layouts: 3.26 us -> 4.01 us
    reshape x1, local copies, waits for them, and re-layouts: 0.02 us -> 0.73 us  [gather_operators(): both = jnp.concatenate([x_operator.reshape(-1), y_operator.reshape(-1)])]
  transfers between devices with their start and end apart: 8 -> 8, of which waited for: 5 -> 5; matrix products, arithmetic and copies ran while one was open for 18% -> 22% of each run, Pallas kernels for 0% -> 0%
where the time goes in v4:
time: 66.4 us; the launch traced here: 65.9 us
  waiting for transfers between devices  20.2 us (30%)
  starting transfers between devices  17.8 us (27%)
  local copies, waits for them, and re-layouts  15.6 us (23%)
  other arithmetic  8.85 us (13%)
  matrix products  3.14 us (5%)
    ppermute x5, waiting for transfers between devices, doubling_gather(): lax.ppermute(data, axis_name, [(j, j ^ bit) for j in range(count)])  7.02 us
    ppermute x5, starting transfers between devices, doubling_gather(): lax.ppermute(data, axis_name, [(j, j ^ bit) for j in range(count)])  6.94 us
    all_to_all x1, waiting for transfers between devices, body(): lax.all_to_all(difference, 'tile', split_axis=3, concat_axis=2, tiled=True)  5.97 us
    all_to_all x1, waiting for transfers between devices, body(): lax.all_to_all(after_first, 'tile', split_axis=2, concat_axis=3, tiled=True)  5.77 us
    another operation x8, other arithmetic, doubling_gather(): jnp.stack([jnp.where(high, received, data), jnp.where(high, data, receive...  4.59 us
    unnamed x18, local copies, waits for them, and re-layouts  4.01 us
    all_to_all x1, starting transfers between devices, body(): lax.all_to_all(packed, 'tile', split_axis=0, concat_axis=0, tiled=True)  3.72 us
    all_to_all x1, starting transfers between devices, body(): lax.all_to_all(difference, 'tile', split_axis=3, concat_axis=2, tiled=True)  3.57 us
  transfers between devices with their start and end apart: 8, of which 5 were waited for; matrix products, arithmetic and copies ran while one was open for 22% of the time, Pallas kernels for 0%

profile of v4, /device:TPU:0, one launch (start us, length us, event | category | flops | bytes accessed | tf_op | source)
XLA Modules:
  0.0 65.9 jit_solution(2088553613350863666)
XLA Ops:
  0.0 0.8 %copy.37 = bf16[2,4,8,128]{3,1,2,0:T(4,128)(2,1)S(1)} copy(bf16[2,4,8,128]{3,2,1,0:T(8,128)(2,1)} %bitcast.80) | data formatting | bytes 32768
  0.8 0.7 %reshape.108 = bf16[4608]{0:T(1024)(128)(2,1)S(1)} reshape(bf16[12,384]{1,0:T(8,128)(2,1)} %param.15) | data formatting | bytes 18432 | tf_op jit(solution)/shard_map/reshape | solution.py:30
  1.5 3.1 %collective-permute-start = (bf16[12800]{0:T(1024)(128)(2,1)S(1)}, bf16[12800]{0:T(1024)(128)(2,1)S(1)}, u32[]{:S(2)}, u32[]{:S(2)}) collective-permute-start(bf16[12800]{0:T(1024)(128)(2,1)S(1)} %constant_dynamic-update-slice_fusion), channel_id=1, source_target_pairs={{0,8},{8,0},{16,24},{24,16},{1,9},{9,1},{17,25},{25,17},{2,10},{10... | collective-permute-start | bytes 76808 | tf_op jit(solution)/shard_map/ppermute | solution.py:13
  4.6 0.8 %reshape_squeeze.6 = s32[192,1]{0,1:T(1,128)S(1)} reshape(s32[1,8,24]{2,1,0:T(8,128)} %param.9) | data formatting | bytes 1536 | tf_op jit(solution)/shard_map/reshape;squeeze | solution.py:54
  5.4 0.7 %compare_and_fusion = pred[8,24]{1,0:T(8,128)(4,1)S(1)} fusion(s32[1,8,24]{2,1,0:T(8,128)} %param.9), kind=kLoop, calls=%fused_computation.47 | loop fusion | flops 1152 | bytes 960 | tf_op jit(solution)/shard_map/jit(_take)/and | solution.py:55
  6.1 1.4 %gather_fusion = bf16[192,2,2,256]{3,2,1,0:T(2,128)(2,1)S(1)} fusion(bf16[128,2,2,256]{3,2,1,0:T(2,128)(2,1)S(1)} %copy-done, s32[1024]{0:T(1024)S(1)} %pad_clamp_fusion), kind=kCustom, calls=%fused_computation | custom fusion | bytes 787200 | tf_op jit(solution)/shard_map/jit(_take)/gather | solution.py:55
  7.5 1.2 %broadcast_select_fusion.2 = bf16[8,24,2,2,256]{4,3,2,1,0:T(2,128)(2,1)} fusion(bf16[8,24,2,2,256]{4,3,2,1,0:T(2,128)(2,1)S(1)} %bitcast.75, pred[8,24]{1,0:T(8,128)(4,1)S(1)} %compare_and_fusion), kind=kLoop, calls=%fused_computation.9 | loop fusion | flops 196608 | bytes 786624 | tf_op jit(solution)/shard_map/jit(_take)/select_n | solution.py:55
  8.8 3.7 %all-to-all-start = ((bf16[8,24,2,2,256]{4,3,2,1,0:T(2,128)(2,1)}), bf16[8,24,2,2,256]{4,3,2,1,0:T(2,128)(2,1)S(1)}, u32[]{:S(2)}, u32[]{:S(2)}) async-start(bf16[8,24,2,2,256]{4,3,2,1,0:T(2,128)(2,1)} %broadcast_select_fusion.2), calls=%async_computation | async-start | bytes 786432 | tf_op jit(solution)/shard_map/all_to_all | solution.py:58
  13.0 2.7 %collective-permute-start.1 = (bf16[2,12800]{1,0:T(2,128)(2,1)S(1)}, bf16[2,12800]{1,0:T(2,128)(2,1)S(1)}, u32[]{:S(2)}, u32[]{:S(2)}) collective-permute-start(bf16[2,12800]{1,0:T(2,128)(2,1)S(1)} %pad_maximum_fusion.3), channel_id=1, source_target_pairs={{0,16},{8,24},{16,0},{24,8},{1,17},{9,25},{17,1},{25,9},{2,18},{10... | collective-permute-start | bytes 153608 | tf_op jit(solution)/shard_map/ppermute | solution.py:13
  15.7 3.4 %collective-permute-done.1 = bf16[2,12800]{1,0:T(2,128)(2,1)S(1)} collective-permute-done((bf16[2,12800]{1,0:T(2,128)(2,1)S(1)}, bf16[2,12800]{1,0:T(2,128)(2,1)S(1)}, u32[]{:S(2)}, u32[]{:S(2)}) %collective-permute-start.1) | collective-permute-done | bytes 51232 | tf_op jit(solution)/shard_map/ppermute | solution.py:13
  19.1 0.2 fusion.11
  19.3 0.1 pad_maximum_fusion.2
  19.4 1.4 %all-to-all-done = bf16[8,24,2,2,256]{4,3,2,1,0:T(2,128)(2,1)S(1)} async-done(((bf16[8,24,2,2,256]{4,3,2,1,0:T(2,128)(2,1)}), bf16[8,24,2,2,256]{4,3,2,1,0:T(2,128)(2,1)S(1)}, u32[]{:S(2)}, u32[]{:S(2)}) %all-to-all-start) | async-done | bytes 393248 | tf_op jit(solution)/shard_map/all_to_all | solution.py:58
  20.8 0.6 collective-permute-start.2
  21.4 0.3 reshape.109
  21.7 0.2 copy.24
  21.9 3.6 %collective-permute-done.2 = bf16[2,2,12800]{2,1,0:T(2,128)(2,1)S(1)} collective-permute-done((bf16[2,2,12800]{2,1,0:T(2,128)(2,1)S(1)}, bf16[2,2,12800]{2,1,0:T(2,128)(2,1)S(1)}, u32[]{:S(2)}, u32[]{:S(2)}) %collective-permute-start.2) | collective-permute-done | bytes 102432 | tf_op jit(solution)/shard_map/ppermute | solution.py:13
  25.5 0.2 fusion.9
  25.7 1.0 %pad_maximum_fusion.1 = bf16[2,2,2,12800]{3,2,1,0:T(2,128)(2,1)} fusion(bf16[1,2,2,12800]{3,2,1,0:T(2,128)(2,1)S(1)} %get-tuple-element.14, bf16[1,2,2,12800]{3,2,1,0:T(2,128)(2,1)S(1)} %get-tuple-element.13), kind=kLoop, calls=%fused_computation.23 | loop fusion | flops 102400 | bytes 409600 | tf_op jit(solution)/shard_map/stack | solution.py:15
  26.6 0.6 collective-permute-start.3
  27.2 1.9 %convolution_bitcast_fusion = f32[2,2,4,16,24,16]{4,5,3,1,0,2:T(8,128)} fusion(bf16[2,2,16,16,192,1]{4,3,2,1,0,5:T(8,128)(2,1)S(1)} %bitcast.71, bf16[192]{0:T(256)(128)(2,1)S(1)} %broadcast_select_fusion.11, s32[4,24]{1,0:T(4,128)S(1)} %multiply_add_fusion, s32[192]{0:T(256)S(1)} %eq.36), kind=kOutput, calls=%fused_computation.1 | convolution fusion | flops 37785600 | bytes 787968 | tf_op jit(solution)/shard_map/dot_general | solution.py:67
  29.1 2.2 %copy.25 = f32[2,2,4,16,24,16]{5,4,3,2,1,0:T(8,128)S(1)} copy(f32[2,2,4,16,24,16]{4,5,3,1,0,2:T(8,128)} %convolution_bitcast_fusion) | data formatting | bytes 786432 | tf_op jit(solution)/shard_map/transpose | solution.py:80
  31.3 1.6 %reshape.110 = f32[2,2,64,384]{3,2,1,0:T(8,128)} reshape(f32[2,2,4,16,24,16]{5,4,3,2,1,0:T(8,128)S(1)} %copy.25) | data formatting | bytes 786432 | tf_op jit(solution)/shard_map/reshape | solution.py:80
  32.9 1.5 %fusion.7 = (bf16[1,2,2,2,12800]{4,3,2,1,0:T(2,128)(2,1)S(1)}, bf16[1,2,2,2,12800]{4,3,2,1,0:T(2,128)(2,1)S(1)}) fusion(bf16[2,2,2,12800]{3,2,1,0:T(2,128)(2,1)} %collective-permute-done.3, pred[]{:T(512)S(6)} %eq.42, bf16[1,2,2,12800]{3,2,1,0:T(2,128)(2,1)} %copy-done.1, bf16[1,2,2,12800]{3,2,1,0:T(2,128)(2,1)S(1)} %get-tuple-element.13), kind=kLoop, calls=%fused_computation.21 | loop fusion | flops 307200 | bytes 819201 | tf_op jit(solution)/shard_map/stack | solution.py:15
  34.4 0.6 pad_maximum_fusion
  35.1 1.1 %fusion.5 = bf16[2,2,64,384]{3,2,1,0:T(8,128)(2,1)S(1)} fusion(f32[2,2,64,384]{3,2,1,0:T(8,128)} %reshape.110, bf16[2,2,64,384]{3,2,1,0:T(8,128)(2,1)} %param.13), kind=kLoop, calls=%fused_computation.18 | loop fusion | flops 294912 | bytes 786432 | tf_op jit(solution)/shard_map/convert_element_type | solution.py:83
  36.2 0.6 copy.26
  36.8 1.0 %reshape.128 = bf16[8,2,6144]{2,1,0:T(2,128)(2,1)} reshape(bf16[384,2,2,64]{3,2,1,0:T(2,128)(2,1)S(1)} %bitcast.76) | data formatting | bytes 393216
  37.8 3.6 %all-to-all-start.1 = ((bf16[8,2,6144]{2,1,0:T(2,128)(2,1)}), bf16[8,2,6144]{2,1,0:T(2,128)(2,1)S(1)}, u32[]{:S(2)}, u32[]{:S(2)}) async-start(bf16[8,2,6144]{2,1,0:T(2,128)(2,1)} %reshape.128), calls=%async_computation.1 | async-start | bytes 393216 | tf_op jit(solution)/shard_map/all_to_all | solution.py:84
  41.4 6.0 %all-to-all-done.1 = bf16[8,2,6144]{2,1,0:T(2,128)(2,1)S(1)} async-done(((bf16[8,2,6144]{2,1,0:T(2,128)(2,1)}), bf16[8,2,6144]{2,1,0:T(2,128)(2,1)S(1)}, u32[]{:S(2)}, u32[]{:S(2)}) %all-to-all-start.1) | async-done | bytes 196640 | tf_op jit(solution)/shard_map/all_to_all | solution.py:84
  47.3 0.3 reshape.129
  47.6 0.3 copy.41
  47.9 0.3 all_to_all.33
  48.2 1.0 %fusion.3 = (bf16[1,2,2,2,2,12800]{5,4,3,2,1,0:T(2,128)(2,1)S(1)}, bf16[1,2,2,2,2,12800]{5,4,3,2,1,0:T(2,128)(2,1)S(1)}) fusion(bf16[2,2,2,2,12800]{4,3,2,1,0:T(2,128)(2,1)S(1)} %collective-permute-done.4, pred[]{:T(512)S(6)} %eq.41, bf16[1,2,2,2,12800]{4,3,2,1,0:T(2,128)(2,1)S(1)} %get-tuple-element.12, bf16[1,2,2,2,12800]{4,3,2,1,0:T(2,128)(2,1)S(1)} %get-tuple-element.11), kind=kLoop, calls=%fused_computation.13 | loop fusion | flops 614400 | bytes 1638401 | tf_op jit(solution)/shard_map/stack | solution.py:15
  49.1 1.2 %maximum_bitcast_fusion = bf16[2,2,2,2,2,12800]{5,1,0,3,2,4:T(2,128)(2,1)S(1)} fusion(bf16[1,2,2,2,2,12800]{5,4,3,2,1,0:T(2,128)(2,1)S(1)} %get-tuple-element.10, bf16[1,2,2,2,2,12800]{5,4,3,2,1,0:T(2,128)(2,1)S(1)} %get-tuple-element.9), kind=kLoop, calls=%fused_computation.6 | loop fusion | flops 409600 | bytes 1638400 | tf_op jit(solution)/shard_map/transpose | solution.py:38
  50.3 0.8 %copy.29 = bf16[2,2,2,2,2,12800]{5,4,3,2,1,0:T(2,128)(2,1)S(1)} copy(bf16[2,2,2,2,2,12800]{5,1,0,3,2,4:T(2,128)(2,1)S(1)} %maximum_bitcast_fusion) | data formatting | bytes 1638400 | tf_op jit(solution)/shard_map/transpose | solution.py:38
  51.2 0.3 reshape.111
  51.5 0.2 reshape.124
  51.8 0.3 fusion.1
  52.1 0.4 copy.30
  52.5 1.4 %reshape.130 = bf16[8,2,6144]{2,1,0:T(2,128)(2,1)} reshape(bf16[512,2,2,48]{3,2,1,0:T(2,128)(2,1)S(1)} %bitcast.72) | data formatting | bytes 393216
  53.9 3.5 %all-to-all-start.2 = ((bf16[8,2,6144]{2,1,0:T(2,128)(2,1)}), bf16[8,2,6144]{2,1,0:T(2,128)(2,1)S(1)}, u32[]{:S(2)}, u32[]{:S(2)}) async-start(bf16[8,2,6144]{2,1,0:T(2,128)(2,1)} %reshape.130), calls=%async_computation.2 | async-start | bytes 393216 | tf_op jit(solution)/shard_map/all_to_all | solution.py:91
  57.5 0.4 reshape.125
  57.9 5.8 %all-to-all-done.2 = bf16[8,2,6144]{2,1,0:T(2,128)(2,1)S(1)} async-done(((bf16[8,2,6144]{2,1,0:T(2,128)(2,1)}), bf16[8,2,6144]{2,1,0:T(2,128)(2,1)S(1)}, u32[]{:S(2)}, u32[]{:S(2)}) %all-to-all-start.2) | async-done | bytes 196640 | tf_op jit(solution)/shard_map/all_to_all | solution.py:91
  63.6 0.5 reshape.131
  64.1 0.3 copy.40
  64.5 0.4 all_to_all.37
  64.9 1.0 %fusion = bf16[2,2,64,384]{3,2,1,0:T(8,128)(2,1)} fusion(bf16[2,2,64,384]{3,2,1,0:T(8,128)(2,1)S(1)} %all_to_all.37, bf16[2,2,64,384]{3,2,1,0:T(8,128)(2,1)S(1)} %copy-done.2, bf16[384,384,1,1]{1,0,2,3:T(8,128)(2,1)S(1)} %reshape.125), kind=kOutput, calls=%fused_computation.4 | convolution fusion | flops 75792384 | bytes 884736 | tf_op jit(solution)/shard_map/by,mlxy->mlxb/dot_general | solution.py:92
  (32 shorter events, 0.7 us)
Async XLA Ops:
  0.0 6.1 %copy-start = (bf16[128,2,2,256]{3,2,1,0:T(2,128)(2,1)S(1)}, bf16[128,2,2,256]{3,2,1,0:T(2,128)(2,1)}, u32[]{:S(2)}) copy-start(bf16[128,2,2,256]{3,2,1,0:T(2,128)(2,1)} %param.8) | copy-start | bytes 786436
  0.0 12.5 %copy-start.5 = (s32[1,8]{1,0:T(1,128)S(1)}, s32[1,8]{1,0:T(1,128)}, u32[]{:S(2)}) copy-start(s32[1,8]{1,0:T(1,128)} %param.12) | copy-start | bytes 100
  0.0 12.6 %copy-start.4 = (f32[1,8,24]{2,1,0:T(8,128)S(1)}, f32[1,8,24]{2,1,0:T(8,128)}, u32[]{:S(2)}) copy-start(f32[1,8,24]{2,1,0:T(8,128)} %param.11) | copy-start | bytes 2308
  0.0 15.6 %copy-start.3 = (s32[1,8,24]{2,1,0:T(8,128)S(1)}, s32[1,8,24]{2,1,0:T(8,128)}, u32[]{:S(2)}) copy-start(s32[1,8,24]{2,1,0:T(8,128)} %param.10) | copy-start | bytes 2308
  1.5 11.2 %collective-permute-start = (bf16[12800]{0:T(1024)(128)(2,1)S(1)}, bf16[12800]{0:T(1024)(128)(2,1)S(1)}, u32[]{:S(2)}, u32[]{:S(2)}) collective-permute-start(bf16[12800]{0:T(1024)(128)(2,1)S(1)} %constant_dynamic-update-slice_fusion), channel_id=1, source_target_pairs={{0,8},{8,0},{16,24},{24,16},{1,9},{9,1},{17,25},{25,17},{2,10},{10... | collective-permute-start | bytes 76808 | tf_op jit(solution)/shard_map/ppermute | solution.py:13
  8.8 12.1 %all-to-all-start = ((bf16[8,24,2,2,256]{4,3,2,1,0:T(2,128)(2,1)}), bf16[8,24,2,2,256]{4,3,2,1,0:T(2,128)(2,1)S(1)}, u32[]{:S(2)}, u32[]{:S(2)}) async-start(bf16[8,24,2,2,256]{4,3,2,1,0:T(2,128)(2,1)} %broadcast_select_fusion.2), calls=%async_computation | async-start | bytes 786432 | tf_op jit(solution)/shard_map/all_to_all | solution.py:58
  13.0 6.1 %collective-permute-start.1 = (bf16[2,12800]{1,0:T(2,128)(2,1)S(1)}, bf16[2,12800]{1,0:T(2,128)(2,1)S(1)}, u32[]{:S(2)}, u32[]{:S(2)}) collective-permute-start(bf16[2,12800]{1,0:T(2,128)(2,1)S(1)} %pad_maximum_fusion.3), channel_id=1, source_target_pairs={{0,16},{8,24},{16,0},{24,8},{1,17},{9,25},{17,1},{25,9},{2,18},{10... | collective-permute-start | bytes 153608 | tf_op jit(solution)/shard_map/ppermute | solution.py:13
  20.8 4.7 %collective-permute-start.2 = (bf16[2,2,12800]{2,1,0:T(2,128)(2,1)S(1)}, bf16[2,2,12800]{2,1,0:T(2,128)(2,1)S(1)}, u32[]{:S(2)}, u32[]{:S(2)}) collective-permute-start(bf16[2,2,12800]{2,1,0:T(2,128)(2,1)S(1)} %pad_maximum_fusion.2), channel_id=1, source_target_pairs={{0,2},{1,3},{2,0},{3,1},{4,6},{5,7},{6,4},{7,5},{8,10},{9,11},{10,... | collective-permute-start | bytes 307208 | tf_op jit(solution)/shard_map/ppermute | solution.py:13
  25.7 1.6 %copy-start.1 = (bf16[1,2,2,12800]{3,2,1,0:T(2,128)(2,1)}, bf16[1,2,2,12800]{3,2,1,0:T(2,128)(2,1)S(1)}, u32[]{:S(2)}) copy-start(bf16[1,2,2,12800]{3,2,1,0:T(2,128)(2,1)S(1)} %get-tuple-element.14) | copy-start | bytes 307204
  26.6 6.3 %collective-permute-start.3 = (bf16[2,2,2,12800]{3,2,1,0:T(2,128)(2,1)}, bf16[2,2,2,12800]{3,2,1,0:T(2,128)(2,1)}, u32[]{:S(2)}, u32[]{:S(2)}) collective-permute-start(bf16[2,2,2,12800]{3,2,1,0:T(2,128)(2,1)} %pad_maximum_fusion.1), channel_id=1, source_target_pairs={{0,4},{1,5},{2,6},{3,7},{4,0},{5,1},{6,2},{7,3},{8,12},{9,13},{10,... | collective-permute-start | bytes 614408 | tf_op jit(solution)/shard_map/ppermute | solution.py:13
  35.0 13.2 %collective-permute-start.4 = (bf16[2,2,2,2,12800]{4,3,2,1,0:T(2,128)(2,1)S(1)}, bf16[2,2,2,2,12800]{4,3,2,1,0:T(2,128)(2,1)S(1)}, u32[]{:S(2)}, u32[]{:S(2)}) collective-permute-start(bf16[2,2,2,2,12800]{4,3,2,1,0:T(2,128)(2,1)S(1)} %pad_maximum_fusion), channel_id=1, source_target_pairs={{0,1},{1,0},{2,3},{3,2},{4,5},{5,4},{6,7},{7,6},{8,9},{9,8},{10,11... | collective-permute-start | bytes 1228808 | tf_op jit(solution)/shard_map/ppermute | solution.py:13
  37.8 9.6 %all-to-all-start.1 = ((bf16[8,2,6144]{2,1,0:T(2,128)(2,1)}), bf16[8,2,6144]{2,1,0:T(2,128)(2,1)S(1)}, u32[]{:S(2)}, u32[]{:S(2)}) async-start(bf16[8,2,6144]{2,1,0:T(2,128)(2,1)} %reshape.128), calls=%async_computation.1 | async-start | bytes 393216 | tf_op jit(solution)/shard_map/all_to_all | solution.py:84
  53.9 10.9 %copy-start.2 = (bf16[2,2,64,384]{3,2,1,0:T(8,128)(2,1)S(1)}, bf16[2,2,64,384]{3,2,1,0:T(8,128)(2,1)}, u32[]{:S(2)}) copy-start(bf16[2,2,64,384]{3,2,1,0:T(8,128)(2,1)} %param.13) | copy-start | bytes 589828
  53.9 9.7 %all-to-all-start.2 = ((bf16[8,2,6144]{2,1,0:T(2,128)(2,1)}), bf16[8,2,6144]{2,1,0:T(2,128)(2,1)S(1)}, u32[]{:S(2)}, u32[]{:S(2)}) async-start(bf16[8,2,6144]{2,1,0:T(2,128)(2,1)} %reshape.130), calls=%async_computation.2 | async-start | bytes 393216 | tf_op jit(solution)/shard_map/all_to_all | solution.py:91

commit v5 on v4

--- a/solution.py
+++ b/solution.py
@@ -57,12 +57,16 @@
     )
     arrived = lax.all_to_all(packed, "tile", split_axis=0, concat_axis=0, tiled=True)
     x_full, y_full, arrived = gather_operators(x_operator, y_operator, arrived)
-    slot_count = columns // block_side * (y_cells // block_side)
+    sx_count = columns // block_side
+    y_blocks = y_cells // block_side
+    j_count = y_blocks // tile_count
+    y_chunk = y_cells // tile_count
     live_mask = lax.broadcasted_iota(jnp.int32, (tile_count, capacity), 1) < recv_count[0][:, None]
     weights = jnp.where(live_mask, recv_weight[0], 0.0).reshape(-1)
-    slot_match = recv_slot[0].reshape(-1)[None, :] == lax.broadcasted_iota(
-        jnp.int32, (slot_count, tile_count * capacity), 0
-    )
+    row = lax.broadcasted_iota(jnp.int32, (tile_count, sx_count, j_count), 0) * j_count
+    row = row + lax.broadcasted_iota(jnp.int32, (tile_count, sx_count, j_count), 1) * y_blocks
+    row = row + lax.broadcasted_iota(jnp.int32, (tile_count, sx_count, j_count), 2)
+    slot_match = recv_slot[0].reshape(-1)[None, :] == row.reshape(-1)[:, None]
     remap_weights = jnp.where(slot_match, weights[None, :], 0.0).astype(jnp.bfloat16)
     remapped = jnp.dot(
         remap_weights,
@@ -70,24 +74,21 @@
         preferred_element_type=jnp.float32,
     )
     remapped = remapped.reshape(
-        columns // block_side,
-        y_cells // block_side,
-        member_count,
-        level_count,
-        block_side,
-        block_side,
+        tile_count, sx_count, j_count, member_count, level_count, block_side, block_side
+    ).transpose(0, 1, 5, 3, 4, 2, 6)
+    local_regional = regional.reshape(
+        member_count, level_count, sx_count, block_side, tile_count, j_count, block_side
+    ).transpose(4, 2, 3, 0, 1, 5, 6)
+    difference = (remapped - local_regional.astype(jnp.float32)).astype(jnp.bfloat16)
+    x_lines = lax.all_to_all(
+        difference.reshape(tile_count, columns, -1), "tile", split_axis=0, concat_axis=0, tiled=True
     )
-    remapped = remapped.transpose(2, 3, 0, 4, 1, 5).reshape(
-        member_count, level_count, columns, y_cells
-    )
-    difference = (remapped - regional.astype(jnp.float32)).astype(jnp.bfloat16)
-    x_lines = lax.all_to_all(difference, "tile", split_axis=3, concat_axis=2, tiled=True)
-    after_first = jnp.einsum(
-        "ax,mlxy->mlay",
-        x_full,
-        x_lines,
-        preferred_element_type=jnp.float32,
+    after_first = jnp.dot(
+        x_full, x_lines.reshape(tile_count * columns, -1), preferred_element_type=jnp.float32
     ).astype(jnp.bfloat16)
+    after_first = after_first.reshape(
+        tile_count * columns, member_count, level_count, y_chunk
+    ).transpose(1, 2, 0, 3)
     tile_back = lax.all_to_all(after_first, "tile", split_axis=2, concat_axis=3, tiled=True)
     after_second = jnp.einsum(
         "by,mlxy->mlxb",

time: 66.4 us -> 70.4 us (1.060)
  local copies, waits for them, and re-layouts: 15.6 us -> 18.2 us
  matrix products: 3.14 us -> 4.43 us
    ppermute x5, waiting for transfers between devices: 7.02 us -> 11.4 us  [doubling_gather(): lax.ppermute(data, axis_name, [(j, j ^ bit) for j in range(count)])]
    all_to_all x1, waiting for transfers between devices: 5.97 us -> 2.08 us  [body(): lax.all_to_all(difference.reshape(tile_count, columns, -1), 'tile', split...]
    convert_element_type x2 -> x1, local copies, waits for them, and re-layouts: 0.99 us -> 3.99 us  [body(): local_regional.astype(jnp.float32)]
    reshape x1 -> x3, local copies, waits for them, and re-layouts: 1.62 us -> 4.22 us  [the longest x2 3.83 us: body(): difference.reshape(tile_count, columns, -1)]
    transpose x1 -> x0, local copies, waits for them, and re-layouts: 2.25 us -> none  [body(): remapped.transpose(2, 3, 0, 4, 1, 5)]
    dot_general x1, matrix products: 1.85 us -> 3.13 us  [body(): jnp.dot(remap_weights, arrived.reshape(tile_count * capacity, -1), prefer...]
    convert_element_type x1 -> x0, other arithmetic: 1.09 us -> none  [body(): difference = (remapped - regional.astype(jnp.float32)).astype(jnp.bfloat16)]
    unnamed x18 -> x11, local copies, waits for them, and re-layouts: 4.01 us -> 3.11 us
  transfers between devices with their start and end apart: 8 -> 8, of which waited for: 5 -> 6; matrix products, arithmetic and copies ran while one was open for 22% -> 33% of each run, Pallas kernels for 0% -> 0%
where the time goes in v5:
time: 70.4 us; the launch traced here: 69.8 us
  waiting for transfers between devices  20.1 us (29%)
  local copies, waits for them, and re-layouts  18.2 us (26%)
  starting transfers between devices  18.1 us (26%)
  other arithmetic  8.58 us (12%)
  matrix products  4.43 us (6%)
    ppermute x5, waiting for transfers between devices, doubling_gather(): lax.ppermute(data, axis_name, [(j, j ^ bit) for j in range(count)])  11.4 us
    ppermute x5, starting transfers between devices, doubling_gather(): lax.ppermute(data, axis_name, [(j, j ^ bit) for j in range(count)])  7.43 us
    all_to_all x1, waiting for transfers between devices, body(): lax.all_to_all(after_first, 'tile', split_axis=2, concat_axis=3, tiled=True)  5.77 us
    another operation x8, other arithmetic, doubling_gather(): jnp.stack([jnp.where(high, received, data), jnp.where(high, data, receive...  4.68 us
    convert_element_type x1, local copies, waits for them, and re-layouts, body(): local_regional.astype(jnp.float32)  3.99 us
    reshape x2, local copies, waits for them, and re-layouts, body(): difference.reshape(tile_count, columns, -1)  3.83 us
    all_to_all x1, starting transfers between devices, body(): lax.all_to_all(packed, 'tile', split_axis=0, concat_axis=0, tiled=True)  3.72 us
    all_to_all x1, starting transfers between devices, body(): lax.all_to_all(difference.reshape(tile_count, columns, -1), 'tile', split...  3.59 us
  transfers between devices with their start and end apart: 8, of which 6 were waited for; matrix products, arithmetic and copies ran while one was open for 33% of the time, Pallas kernels for 0%

profile of v5, /device:TPU:0, one launch (start us, length us, event | category | flops | bytes accessed | tf_op | source)
XLA Modules:
  0.0 69.8 jit_solution(6242076988192731624)
XLA Ops:
  0.0 0.8 %copy.43 = bf16[2,4,8,128]{3,1,2,0:T(4,128)(2,1)S(1)} copy(bf16[2,4,8,128]{3,2,1,0:T(8,128)(2,1)} %bitcast.75) | data formatting | bytes 32768
  0.8 0.7 %reshape.130 = bf16[4608]{0:T(1024)(128)(2,1)S(1)} reshape(bf16[12,384]{1,0:T(8,128)(2,1)} %param.15) | data formatting | bytes 18432 | tf_op jit(solution)/shard_map/reshape | solution.py:30
  1.5 3.1 %collective-permute-start = (bf16[12800]{0:T(1024)(128)(2,1)S(1)}, bf16[12800]{0:T(1024)(128)(2,1)S(1)}, u32[]{:S(2)}, u32[]{:S(2)}) collective-permute-start(bf16[12800]{0:T(1024)(128)(2,1)S(1)} %constant_dynamic-update-slice_fusion), channel_id=1, source_target_pairs={{0,8},{8,0},{16,24},{24,16},{1,9},{9,1},{17,25},{25,17},{2,10},{10... | collective-permute-start | bytes 76808 | tf_op jit(solution)/shard_map/ppermute | solution.py:13
  4.6 0.8 %reshape_squeeze.6 = s32[192,1]{0,1:T(1,128)S(1)} reshape(s32[1,8,24]{2,1,0:T(8,128)} %param.9) | data formatting | bytes 1536 | tf_op jit(solution)/shard_map/reshape;squeeze | solution.py:54
  5.4 0.7 %compare_and_fusion = pred[8,24]{1,0:T(8,128)(4,1)S(1)} fusion(s32[1,8,24]{2,1,0:T(8,128)} %param.9), kind=kLoop, calls=%fused_computation.44 | loop fusion | flops 1152 | bytes 960 | tf_op jit(solution)/shard_map/jit(_take)/and | solution.py:55
  6.1 1.4 %gather_fusion = bf16[192,2,2,256]{3,2,1,0:T(2,128)(2,1)S(1)} fusion(bf16[128,2,2,256]{3,2,1,0:T(2,128)(2,1)S(1)} %copy-done, s32[1024]{0:T(1024)S(1)} %pad_clamp_fusion), kind=kCustom, calls=%fused_computation | custom fusion | bytes 787200 | tf_op jit(solution)/shard_map/jit(_take)/gather | solution.py:55
  7.5 1.2 %broadcast_select_fusion.2 = bf16[8,24,2,2,256]{4,3,2,1,0:T(2,128)(2,1)} fusion(bf16[8,24,2,2,256]{4,3,2,1,0:T(2,128)(2,1)S(1)} %bitcast.71, pred[8,24]{1,0:T(8,128)(4,1)S(1)} %compare_and_fusion), kind=kLoop, calls=%fused_computation.9 | loop fusion | flops 196608 | bytes 786624 | tf_op jit(solution)/shard_map/jit(_take)/select_n | solution.py:55
  8.8 3.7 %all-to-all-start = ((bf16[8,24,2,2,256]{4,3,2,1,0:T(2,128)(2,1)}), bf16[8,24,2,2,256]{4,3,2,1,0:T(2,128)(2,1)S(1)}, u32[]{:S(2)}, u32[]{:S(2)}) async-start(bf16[8,24,2,2,256]{4,3,2,1,0:T(2,128)(2,1)} %broadcast_select_fusion.2), calls=%async_computation | async-start | bytes 786432 | tf_op jit(solution)/shard_map/all_to_all | solution.py:58
  12.5 0.7 %iota_compare_fusion = pred[8,24]{1,0:T(8,128)(4,1)S(1)} fusion(s32[8]{0:T(128)} %bitcast.77), kind=kLoop, calls=%fused_computation.43 | loop fusion | flops 192 | bytes 224 | tf_op jit(solution)/shard_map/lt | solution.py:64
  13.3 0.1 pad_maximum_fusion.3
  13.4 2.7 %collective-permute-start.1 = (bf16[2,12800]{1,0:T(2,128)(2,1)S(1)}, bf16[2,12800]{1,0:T(2,128)(2,1)S(1)}, u32[]{:S(2)}, u32[]{:S(2)}) collective-permute-start(bf16[2,12800]{1,0:T(2,128)(2,1)S(1)} %pad_maximum_fusion.3), channel_id=1, source_target_pairs={{0,16},{8,24},{16,0},{24,8},{1,17},{9,25},{17,1},{25,9},{2,18},{10... | collective-permute-start | bytes 153608 | tf_op jit(solution)/shard_map/ppermute | solution.py:13
  16.2 0.8 %squeeze.3 = bf16[192]{0:T(256)(128)(2,1)S(1)} reshape(f32[1,8,24]{2,1,0:T(8,128)} %param.11) | data formatting | bytes 1152 | tf_op jit(solution)/shard_map/squeeze | solution.py:65
  16.9 2.6 %collective-permute-done.1 = bf16[2,12800]{1,0:T(2,128)(2,1)S(1)} collective-permute-done((bf16[2,12800]{1,0:T(2,128)(2,1)S(1)}, bf16[2,12800]{1,0:T(2,128)(2,1)S(1)}, u32[]{:S(2)}, u32[]{:S(2)}) %collective-permute-start.1) | collective-permute-done | bytes 51232 | tf_op jit(solution)/shard_map/ppermute | solution.py:13
  19.6 0.2 fusion.9
  19.7 0.1 pad_maximum_fusion.2
  19.9 0.9 %all-to-all-done = bf16[8,24,2,2,256]{4,3,2,1,0:T(2,128)(2,1)S(1)} async-done(((bf16[8,24,2,2,256]{4,3,2,1,0:T(2,128)(2,1)}), bf16[8,24,2,2,256]{4,3,2,1,0:T(2,128)(2,1)S(1)}, u32[]{:S(2)}, u32[]{:S(2)}) %all-to-all-start) | async-done | bytes 393248 | tf_op jit(solution)/shard_map/all_to_all | solution.py:58
  20.8 0.8 %collective-permute-start.2 = (bf16[2,2,12800]{2,1,0:T(2,128)(2,1)S(1)}, bf16[2,2,12800]{2,1,0:T(2,128)(2,1)S(1)}, u32[]{:S(2)}, u32[]{:S(2)}) collective-permute-start(bf16[2,2,12800]{2,1,0:T(2,128)(2,1)S(1)} %pad_maximum_fusion.2), channel_id=1, source_target_pairs={{0,2},{1,3},{2,0},{3,1},{4,6},{5,7},{6,4},{7,5},{8,10},{9,11},{10,... | collective-permute-start | bytes 307208 | tf_op jit(solution)/shard_map/ppermute | solution.py:13
  21.6 3.8 %collective-permute-done.2 = bf16[2,2,12800]{2,1,0:T(2,128)(2,1)S(1)} collective-permute-done((bf16[2,2,12800]{2,1,0:T(2,128)(2,1)S(1)}, bf16[2,2,12800]{2,1,0:T(2,128)(2,1)S(1)}, u32[]{:S(2)}, u32[]{:S(2)}) %collective-permute-start.2) | collective-permute-done | bytes 102432 | tf_op jit(solution)/shard_map/ppermute | solution.py:13
  25.5 0.2 fusion.7
  25.7 0.3 pad_maximum_fusion.1
  26.0 0.9 %collective-permute-start.3 = (bf16[2,2,2,12800]{3,2,1,0:T(2,128)(2,1)S(1)}, bf16[2,2,2,12800]{3,2,1,0:T(2,128)(2,1)S(1)}, u32[]{:S(2)}, u32[]{:S(2)}) collective-permute-start(bf16[2,2,2,12800]{3,2,1,0:T(2,128)(2,1)S(1)} %pad_maximum_fusion.1), channel_id=1, source_target_pairs={{0,4},{1,5},{2,6},{3,7},{4,0},{5,1},{6,2},{7,3},{8,12},{9,13},{10,... | collective-permute-start | bytes 614408 | tf_op jit(solution)/shard_map/ppermute | solution.py:13
  26.9 4.9 %collective-permute-done.3 = bf16[2,2,2,12800]{3,2,1,0:T(2,128)(2,1)S(1)} collective-permute-done((bf16[2,2,2,12800]{3,2,1,0:T(2,128)(2,1)S(1)}, bf16[2,2,2,12800]{3,2,1,0:T(2,128)(2,1)S(1)}, u32[]{:S(2)}, u32[]{:S(2)}) %collective-permute-start.3) | collective-permute-done | bytes 204832 | tf_op jit(solution)/shard_map/ppermute | solution.py:13
  31.8 0.5 fusion.5
  32.3 1.4 %pad_maximum_fusion = bf16[2,2,2,2,12800]{4,3,2,1,0:T(2,128)(2,1)} fusion(bf16[1,2,2,2,12800]{4,3,2,1,0:T(2,128)(2,1)S(1)} %get-tuple-element.12, bf16[1,2,2,2,12800]{4,3,2,1,0:T(2,128)(2,1)S(1)} %get-tuple-element.11), kind=kLoop, calls=%fused_computation.13 | loop fusion | flops 204800 | bytes 819200 | tf_op jit(solution)/shard_map/stack | solution.py:15
  33.6 4.0 %reshape.150 = f32[2,2,4,16,8,3,16]{6,5,4,3,2,1,0:T(4,128)} reshape(bf16[2,2,64,384]{3,2,1,0:T(8,128)(2,1)S(1)} %copy-done.1) | data formatting | bytes 589824 | tf_op jit(solution)/shard_map/convert_element_type | solution.py:82
  37.7 0.3 reshape.133
  38.0 0.2 copy.26
  38.2 3.1 %fusion = bf16[8,4,16,2,2,3,16]{6,0,2,4,3,5,1:T(8,128)(2,1)S(1)} fusion(f32[2,2,4,16,8,3,16]{6,5,4,3,2,1,0:T(4,128)} %reshape.150, bf16[2,2,16,16,192,1,1]{4,3,2,1,0,6,5:T(8,128)(2,1)S(1)} %bitcast.70, bf16[192]{0:T(256)(128)(2,1)S(1)} %broadcast_select_fusion.11, s32[8,4,3]{0,2,1:T(4,128)S(1)} %iota_add_fusion, s32[192]{0:T(256)S(1)} %eq.46), kind=kOutput, calls=%fused_computation.2 | convolution fusion | flops 37982208 | bytes 984576 | tf_op jit(solution)/shard_map/dot_general | solution.py:71
  41.3 1.4 %copy.39 = bf16[8,4,16,2,2,3,16]{6,5,4,3,2,1,0:T(4,128)(2,1)S(1)} copy(bf16[8,4,16,2,2,3,16]{6,0,2,4,3,5,1:T(8,128)(2,1)S(1)} %fusion) | data formatting | bytes 393216 | tf_op jit(solution)/shard_map/reshape | solution.py:84
  42.7 2.5 %reshape.151 = bf16[8,64,192]{2,1,0:T(8,128)(2,1)} reshape(bf16[8,4,16,2,2,3,16]{6,5,4,3,2,1,0:T(4,128)(2,1)S(1)} %copy.39) | data formatting | bytes 393216 | tf_op jit(solution)/shard_map/reshape | solution.py:84
  45.2 3.6 %all-to-all-start.1 = ((bf16[8,64,192]{2,1,0:T(8,128)(2,1)}), bf16[8,64,192]{2,1,0:T(8,128)(2,1)S(1)}, u32[]{:S(2)}, u32[]{:S(2)}) async-start(bf16[8,64,192]{2,1,0:T(8,128)(2,1)} %reshape.151), calls=%async_computation.1 | async-start | bytes 524288 | tf_op jit(solution)/shard_map/all_to_all | solution.py:83
  48.8 2.0 %fusion.2 = (bf16[1,2,2,2,2,12800]{5,4,3,2,1,0:T(2,128)(2,1)S(1)}, bf16[1,2,2,2,2,12800]{5,4,3,2,1,0:T(2,128)(2,1)S(1)}) fusion(bf16[2,2,2,2,12800]{4,3,2,1,0:T(2,128)(2,1)} %collective-permute-done.4, pred[]{:T(512)S(6)} %eq.41, bf16[1,2,2,2,12800]{4,3,2,1,0:T(2,128)(2,1)S(1)} %get-tuple-element.12, bf16[1,2,2,2,12800]{4,3,2,1,0:T(2,128)(2,1)S(1)} %get-tuple-element.11), kind=kLoop, calls=%fused_computation.11 | loop fusion | flops 614400 | bytes 1638401 | tf_op jit(solution)/shard_map/stack | solution.py:15
  50.7 1.2 %maximum_bitcast_fusion = bf16[2,2,2,2,2,12800]{5,1,0,3,2,4:T(2,128)(2,1)S(1)} fusion(bf16[1,2,2,2,2,12800]{5,4,3,2,1,0:T(2,128)(2,1)S(1)} %get-tuple-element.10, bf16[1,2,2,2,2,12800]{5,4,3,2,1,0:T(2,128)(2,1)S(1)} %get-tuple-element.9), kind=kLoop, calls=%fused_computation.6 | loop fusion | flops 409600 | bytes 1638400 | tf_op jit(solution)/shard_map/transpose | solution.py:38
  51.9 0.8 %copy.25 = bf16[2,2,2,2,2,12800]{5,4,3,2,1,0:T(2,128)(2,1)S(1)} copy(bf16[2,2,2,2,2,12800]{5,1,0,3,2,4:T(2,128)(2,1)S(1)} %maximum_bitcast_fusion) | data formatting | bytes 1638400 | tf_op jit(solution)/shard_map/transpose | solution.py:38
  52.8 0.3 reshape.131
  53.1 0.2 reshape.132
  53.4 2.1 %all-to-all-done.1 = bf16[8,64,192]{2,1,0:T(8,128)(2,1)S(1)} async-done(((bf16[8,64,192]{2,1,0:T(8,128)(2,1)}), bf16[8,64,192]{2,1,0:T(8,128)(2,1)S(1)}, u32[]{:S(2)}, u32[]{:S(2)}) %all-to-all-start.1) | async-done | bytes 196640 | tf_op jit(solution)/shard_map/all_to_all | solution.py:83
  55.5 0.3 convolution_convert_fusion
  55.8 0.4 copy.31
  56.2 0.4 bitcast_bitcast_fusion
  56.6 1.4 %reshape.153 = bf16[8,2,6144]{2,1,0:T(2,128)(2,1)} reshape(bf16[512,2,2,48]{3,2,1,0:T(2,128)(2,1)S(1)} %bitcast_bitcast_fusion) | data formatting | bytes 393216
  58.0 3.4 %all-to-all-start.2 = ((bf16[8,2,6144]{2,1,0:T(2,128)(2,1)}), bf16[8,2,6144]{2,1,0:T(2,128)(2,1)S(1)}, u32[]{:S(2)}, u32[]{:S(2)}) async-start(bf16[8,2,6144]{2,1,0:T(2,128)(2,1)} %reshape.153), calls=%async_computation.2 | async-start | bytes 393216 | tf_op jit(solution)/shard_map/all_to_all | solution.py:92
  61.4 0.4 reshape.149
  61.8 5.8 %all-to-all-done.2 = bf16[8,2,6144]{2,1,0:T(2,128)(2,1)S(1)} async-done(((bf16[8,2,6144]{2,1,0:T(2,128)(2,1)}), bf16[8,2,6144]{2,1,0:T(2,128)(2,1)S(1)}, u32[]{:S(2)}, u32[]{:S(2)}) %all-to-all-start.2) | async-done | bytes 196640 | tf_op jit(solution)/shard_map/all_to_all | solution.py:92
  67.6 0.5 reshape.154
  68.1 0.3 copy.46
  68.4 0.4 all_to_all.24
  68.8 1.0 %fusion.1 = bf16[2,2,64,384]{3,2,1,0:T(8,128)(2,1)} fusion(bf16[2,2,64,384]{3,2,1,0:T(8,128)(2,1)S(1)} %all_to_all.24, bf16[384,384,1,1]{1,0,2,3:T(8,128)(2,1)S(1)} %reshape.149, bf16[2,2,64,384]{3,2,1,0:T(8,128)(2,1)S(1)} %copy-done.1), kind=kOutput, calls=%fused_computation.5 | convolution fusion | flops 75792384 | bytes 884736 | tf_op jit(solution)/shard_map/by,mlxy->mlxb/dot_general | solution.py:93
  (24 shorter events, 0.4 us)
Async XLA Ops:
  0.0 6.1 %copy-start = (bf16[128,2,2,256]{3,2,1,0:T(2,128)(2,1)S(1)}, bf16[128,2,2,256]{3,2,1,0:T(2,128)(2,1)}, u32[]{:S(2)}) copy-start(bf16[128,2,2,256]{3,2,1,0:T(2,128)(2,1)} %param.8) | copy-start | bytes 786436
  0.0 33.6 %copy-start.1 = (bf16[2,2,64,384]{3,2,1,0:T(8,128)(2,1)S(1)}, bf16[2,2,64,384]{3,2,1,0:T(8,128)(2,1)}, u32[]{:S(2)}) copy-start(bf16[2,2,64,384]{3,2,1,0:T(8,128)(2,1)} %param.13) | copy-start | bytes 589828
  1.5 11.7 %collective-permute-start = (bf16[12800]{0:T(1024)(128)(2,1)S(1)}, bf16[12800]{0:T(1024)(128)(2,1)S(1)}, u32[]{:S(2)}, u32[]{:S(2)}) collective-permute-start(bf16[12800]{0:T(1024)(128)(2,1)S(1)} %constant_dynamic-update-slice_fusion), channel_id=1, source_target_pairs={{0,8},{8,0},{16,24},{24,16},{1,9},{9,1},{17,25},{25,17},{2,10},{10... | collective-permute-start | bytes 76808 | tf_op jit(solution)/shard_map/ppermute | solution.py:13
  8.8 12.1 %all-to-all-start = ((bf16[8,24,2,2,256]{4,3,2,1,0:T(2,128)(2,1)}), bf16[8,24,2,2,256]{4,3,2,1,0:T(2,128)(2,1)S(1)}, u32[]{:S(2)}, u32[]{:S(2)}) async-start(bf16[8,24,2,2,256]{4,3,2,1,0:T(2,128)(2,1)} %broadcast_select_fusion.2), calls=%async_computation | async-start | bytes 786432 | tf_op jit(solution)/shard_map/all_to_all | solution.py:58
  13.4 6.1 %collective-permute-start.1 = (bf16[2,12800]{1,0:T(2,128)(2,1)S(1)}, bf16[2,12800]{1,0:T(2,128)(2,1)S(1)}, u32[]{:S(2)}, u32[]{:S(2)}) collective-permute-start(bf16[2,12800]{1,0:T(2,128)(2,1)S(1)} %pad_maximum_fusion.3), channel_id=1, source_target_pairs={{0,16},{8,24},{16,0},{24,8},{1,17},{9,25},{17,1},{25,9},{2,18},{10... | collective-permute-start | bytes 153608 | tf_op jit(solution)/shard_map/ppermute | solution.py:13
  20.8 4.7 %collective-permute-start.2 = (bf16[2,2,12800]{2,1,0:T(2,128)(2,1)S(1)}, bf16[2,2,12800]{2,1,0:T(2,128)(2,1)S(1)}, u32[]{:S(2)}, u32[]{:S(2)}) collective-permute-start(bf16[2,2,12800]{2,1,0:T(2,128)(2,1)S(1)} %pad_maximum_fusion.2), channel_id=1, source_target_pairs={{0,2},{1,3},{2,0},{3,1},{4,6},{5,7},{6,4},{7,5},{8,10},{9,11},{10,... | collective-permute-start | bytes 307208 | tf_op jit(solution)/shard_map/ppermute | solution.py:13
  25.6 12.0 %copy-start.2 = (s32[1,8,24]{2,1,0:T(8,128)S(1)}, s32[1,8,24]{2,1,0:T(8,128)}, u32[]{:S(2)}) copy-start(s32[1,8,24]{2,1,0:T(8,128)} %param.10) | copy-start | bytes 2308
  26.0 5.8 %collective-permute-start.3 = (bf16[2,2,2,12800]{3,2,1,0:T(2,128)(2,1)S(1)}, bf16[2,2,2,12800]{3,2,1,0:T(2,128)(2,1)S(1)}, u32[]{:S(2)}, u32[]{:S(2)}) collective-permute-start(bf16[2,2,2,12800]{3,2,1,0:T(2,128)(2,1)S(1)} %pad_maximum_fusion.1), channel_id=1, source_target_pairs={{0,4},{1,5},{2,6},{3,7},{4,0},{5,1},{6,2},{7,3},{8,12},{9,13},{10,... | collective-permute-start | bytes 614408 | tf_op jit(solution)/shard_map/ppermute | solution.py:13
  33.6 15.1 %collective-permute-start.4 = (bf16[2,2,2,2,12800]{4,3,2,1,0:T(2,128)(2,1)}, bf16[2,2,2,2,12800]{4,3,2,1,0:T(2,128)(2,1)}, u32[]{:S(2)}, u32[]{:S(2)}) collective-permute-start(bf16[2,2,2,2,12800]{4,3,2,1,0:T(2,128)(2,1)} %pad_maximum_fusion), channel_id=1, source_target_pairs={{0,1},{1,0},{2,3},{3,2},{4,5},{5,4},{6,7},{7,6},{8,9},{9,8},{10,11... | collective-permute-start | bytes 1228808 | tf_op jit(solution)/shard_map/ppermute | solution.py:13
  45.2 10.3 %all-to-all-start.1 = ((bf16[8,64,192]{2,1,0:T(8,128)(2,1)}), bf16[8,64,192]{2,1,0:T(8,128)(2,1)S(1)}, u32[]{:S(2)}, u32[]{:S(2)}) async-start(bf16[8,64,192]{2,1,0:T(8,128)(2,1)} %reshape.151), calls=%async_computation.1 | async-start | bytes 524288 | tf_op jit(solution)/shard_map/all_to_all | solution.py:83
  58.0 9.6 %all-to-all-start.2 = ((bf16[8,2,6144]{2,1,0:T(2,128)(2,1)}), bf16[8,2,6144]{2,1,0:T(2,128)(2,1)S(1)}, u32[]{:S(2)}, u32[]{:S(2)}) async-start(bf16[8,2,6144]{2,1,0:T(2,128)(2,1)} %reshape.153), calls=%async_computation.2 | async-start | bytes 393216 | tf_op jit(solution)/shard_map/all_to_all | solution.py:92

commit v6 on v4

--- a/solution.py
+++ b/solution.py
@@ -8,17 +8,17 @@
 
 def doubling_gather(data, axis_name, bits):
     count = lax.axis_size(axis_name)
-    index = lax.axis_index(axis_name)
     for bit in bits:
         received = lax.ppermute(data, axis_name, [(j, j ^ bit) for j in range(count)])
-        high = (index // bit) % 2 == 1
-        data = jnp.stack([jnp.where(high, received, data), jnp.where(high, data, received)])
+        data = jnp.stack([data, received])
     return data
 
 
-def bit_order(count, bits):
-    stacked = list(reversed(bits))
-    return [stacked.index(bit) for bit in sorted(bits, reverse=True)]
+def stacked_position(offset, bits):
+    position = jnp.zeros_like(offset)
+    for bit in reversed(bits):
+        position = position * 2 + (offset // bit) % 2
+    return position
 
 
 def gather_operators(x_operator, y_operator, after):
@@ -32,14 +32,16 @@
     tile_bits = [1 << k for k in range(1, tile_count.bit_length() - 1)] + [1]
     both = doubling_gather(both, "mem", mem_bits)
     both, after = lax.optimization_barrier((both, after))
-    both = doubling_gather(both, "tile", tile_bits)
-    tile_axes = bit_order(tile_count, tile_bits)
-    mem_axes = [len(tile_bits) + k for k in bit_order(mem_count, mem_bits)]
-    both = both.transpose(mem_axes + tile_axes + [both.ndim - 1]).reshape(
-        mem_count * tile_count, -1
-    )
-    x_full = both[:, :x_size].reshape(mem_count * tile_count * x_rows, x_cols)
-    y_full = both[:, x_size:].reshape(mem_count * tile_count * y_rows, y_cols)
+    both = doubling_gather(both, "tile", tile_bits).reshape(mem_count * tile_count, -1)
+    mem_of = lax.broadcasted_iota(jnp.int32, (mem_count, tile_count), 0)
+    tile_of = lax.broadcasted_iota(jnp.int32, (mem_count, tile_count), 1)
+    position = stacked_position(tile_of ^ lax.axis_index("tile"), tile_bits) * mem_count
+    position = position + stacked_position(mem_of ^ lax.axis_index("mem"), mem_bits)
+    position = position.reshape(-1)
+    x_full = jnp.take(both[:, :x_size], position, axis=0, mode="clip")
+    y_full = jnp.take(both[:, x_size:], position, axis=0, mode="clip")
+    x_full = x_full.reshape(mem_count * tile_count * x_rows, x_cols)
+    y_full = y_full.reshape(mem_count * tile_count * y_rows, y_cols)
     return x_full, y_full, after
 
 
@@ -52,7 +54,7 @@
     block_cells = source_blocks.shape[3]
     block_side = math.isqrt(block_cells)
     picked = send_blocks[0].reshape(-1)
-    packed = jnp.take(source_blocks, picked, axis=0).reshape(
+    packed = jnp.take(source_blocks, picked, axis=0, mode="clip").reshape(
         tile_count, capacity, member_count, level_count, block_cells
     )
     arrived = lax.all_to_all(packed, "tile", split_axis=0, concat_axis=0, tiled=True)

time: 66.4 us -> 64.2 us (0.967)
  waiting for transfers between devices: 20.2 us -> 15.8 us
  other arithmetic: 8.85 us -> 5.29 us
  local copies, waits for them, and re-layouts: 15.6 us -> 19.1 us
  starting transfers between devices: 17.8 us -> 20 us
    ppermute x5, starting transfers between devices: 6.94 us -> 9.47 us  [doubling_gather(): lax.ppermute(data, axis_name, [(j, j ^ bit) for j in range(count)])]
    gather x1 -> x3, local copies, waits for them, and re-layouts: 1.44 us -> 3.86 us  [the longest x1 2.26 us: body(): jnp.take(source_blocks, picked, axis=0, mode='clip')]
    all_to_all x1, waiting for transfers between devices: 5.97 us -> 3.6 us  [body(): lax.all_to_all(difference, 'tile', split_axis=3, concat_axis=2, tiled=True)]
    all_to_all x1, waiting for transfers between devices: 1.4 us -> 0.01 us  [body(): lax.all_to_all(packed, 'tile', split_axis=0, concat_axis=0, tiled=True)]
    another operation x8, other arithmetic: 4.59 us -> 3.27 us  [doubling_gather(): data = jnp.stack([data, received])]
    transpose x1 -> x0, other arithmetic: 1.16 us -> none  [gather_operators(): both.transpose(mem_axes + tile_axes + [both.ndim - 1])]
    select_n x3, other arithmetic: 1.22 us -> 0.08 us  [stacked_position(): position = position * 2 + offset // bit % 2]
    transpose x1 -> x0, local copies, waits for them, and re-layouts: 0.84 us -> none  [gather_operators(): both.transpose(mem_axes + tile_axes + [both.ndim - 1])]
  transfers between devices with their start and end apart: 8 -> 8, of which waited for: 5 -> 5; matrix products, arithmetic and copies ran while one was open for 22% -> 19% of each run, Pallas kernels for 0% -> 0%
where the time goes in v6:
time: 64.2 us; the launch traced here: 63.6 us
  starting transfers between devices  20 us (31%)
  local copies, waits for them, and re-layouts  19.1 us (30%)
  waiting for transfers between devices  15.8 us (25%)
  other arithmetic  5.29 us (8%)
  matrix products  3.15 us (5%)
    ppermute x5, starting transfers between devices, doubling_gather(): lax.ppermute(data, axis_name, [(j, j ^ bit) for j in range(count)])  9.47 us
    ppermute x5, waiting for transfers between devices, doubling_gather(): lax.ppermute(data, axis_name, [(j, j ^ bit) for j in range(count)])  7.13 us
    all_to_all x1, waiting for transfers between devices, body(): lax.all_to_all(after_first, 'tile', split_axis=2, concat_axis=3, tiled=True)  5.02 us
    unnamed x10, local copies, waits for them, and re-layouts  4 us
    all_to_all x1, starting transfers between devices, body(): lax.all_to_all(packed, 'tile', split_axis=0, concat_axis=0, tiled=True)  3.72 us
    all_to_all x1, waiting for transfers between devices, body(): lax.all_to_all(difference, 'tile', split_axis=3, concat_axis=2, tiled=True)  3.6 us
    all_to_all x1, starting transfers between devices, body(): lax.all_to_all(difference, 'tile', split_axis=3, concat_axis=2, tiled=True)  3.39 us
    all_to_all x1, starting transfers between devices, body(): lax.all_to_all(after_first, 'tile', split_axis=2, concat_axis=3, tiled=True)  3.39 us
  transfers between devices with their start and end apart: 8, of which 5 were waited for; matrix products, arithmetic and copies ran while one was open for 19% of the time, Pallas kernels for 0%

profile of v6, /device:TPU:0, one launch (start us, length us, event | category | flops | bytes accessed | tf_op | source)
XLA Modules:
  0.0 63.6 jit_solution(7167859729569573145)
XLA Ops:
  0.0 0.8 %copy.28 = bf16[2,4,8,128]{3,1,2,0:T(4,128)(2,1)S(1)} copy(bf16[2,4,8,128]{3,2,1,0:T(8,128)(2,1)} %bitcast.77) | data formatting | bytes 32768
  0.8 0.7 %reshape.464 = bf16[4608]{0:T(1024)(128)(2,1)S(1)} reshape(bf16[12,384]{1,0:T(8,128)(2,1)} %param.15) | data formatting | bytes 18432 | tf_op jit(solution)/shard_map/reshape | solution.py:30
  1.5 3.1 %collective-permute-start = (bf16[12800]{0:T(1024)(128)(2,1)S(1)}, bf16[12800]{0:T(1024)(128)(2,1)S(1)}, u32[]{:S(2)}, u32[]{:S(2)}) collective-permute-start(bf16[12800]{0:T(1024)(128)(2,1)S(1)} %constant_dynamic-update-slice_fusion), channel_id=1, source_target_pairs={{0,8},{8,0},{16,24},{24,16},{1,9},{9,1},{17,25},{25,17},{2,10},{10... | collective-permute-start | bytes 76808 | tf_op jit(solution)/shard_map/ppermute | solution.py:12
  4.6 0.8 %reshape.473 = s32[192]{0:T(256)S(1)} reshape(s32[1,8,24]{2,1,0:T(8,128)} %param.9) | data formatting | bytes 1536 | tf_op jit(solution)/shard_map/jit(_take)/broadcast_in_dim | solution.py:57
  5.4 2.3 %gather_fusion = bf16[192,2,2,256]{3,2,1,0:T(2,128)(2,1)} fusion(bf16[128,2,2,256]{3,2,1,0:T(2,128)(2,1)S(1)} %copy-done, s32[1024]{0:T(1024)S(1)} %pad_clamp_fusion.1), kind=kCustom, calls=%fused_computation | custom fusion | bytes 787200 | tf_op jit(solution)/shard_map/jit(_take)/gather | solution.py:57
  7.7 3.7 %all-to-all-start = ((bf16[8,24,2,2,256]{4,3,2,1,0:T(2,128)(2,1)}), bf16[8,24,2,2,256]{4,3,2,1,0:T(2,128)(2,1)S(1)}, u32[]{:S(2)}, u32[]{:S(2)}) async-start(bf16[8,24,2,2,256]{4,3,2,1,0:T(2,128)(2,1)} %bitcast.5), calls=%async_computation | async-start | bytes 786432 | tf_op jit(solution)/shard_map/all_to_all | solution.py:60
  11.5 0.7 %iota_compare_fusion = pred[8,24]{1,0:T(8,128)(4,1)S(1)} fusion(s32[8]{0:T(128)} %bitcast.78), kind=kLoop, calls=%fused_computation.28 | loop fusion | flops 192 | bytes 224 | tf_op jit(solution)/shard_map/lt | solution.py:63
  12.3 0.8 %squeeze.3 = bf16[192]{0:T(256)(128)(2,1)S(1)} reshape(f32[1,8,24]{2,1,0:T(8,128)} %param.11) | data formatting | bytes 1152 | tf_op jit(solution)/shard_map/squeeze | solution.py:64
  13.8 0.8 %eq.21 = s32[192]{0:T(256)S(1)} reshape(s32[1,8,24]{2,1,0:T(8,128)} %param.10) | data formatting | bytes 1536 | tf_op jit(solution)/shard_map/eq | solution.py:65
  14.7 2.7 %collective-permute-start.1 = (bf16[2,12800]{1,0:T(2,128)(2,1)S(1)}, bf16[2,12800]{1,0:T(2,128)(2,1)S(1)}, u32[]{:S(2)}, u32[]{:S(2)}) collective-permute-start(bf16[2,12800]{1,0:T(2,128)(2,1)S(1)} %pad_maximum_fusion.4), channel_id=1, source_target_pairs={{0,16},{8,24},{16,0},{24,8},{1,17},{9,25},{17,1},{25,9},{2,18},{10... | collective-permute-start | bytes 153608 | tf_op jit(solution)/shard_map/ppermute | solution.py:12
  17.5 3.4 %collective-permute-done.1 = bf16[2,12800]{1,0:T(2,128)(2,1)S(1)} collective-permute-done((bf16[2,12800]{1,0:T(2,128)(2,1)S(1)}, bf16[2,12800]{1,0:T(2,128)(2,1)S(1)}, u32[]{:S(2)}, u32[]{:S(2)}) %collective-permute-start.1) | collective-permute-done | bytes 51232 | tf_op jit(solution)/shard_map/ppermute | solution.py:12
  20.8 0.1 pad_maximum_fusion.3
  21.0 0.3 reshape.466
  21.3 0.2 copy.16
  21.5 1.8 %convolution_bitcast_fusion = f32[2,2,4,16,24,16]{4,5,3,1,0,2:T(8,128)} fusion(bf16[2,2,16,16,192,1]{4,3,2,1,0,5:T(8,128)(2,1)S(1)} %bitcast.61, bf16[192]{0:T(256)(128)(2,1)S(1)} %broadcast_select_fusion.3, s32[4,24]{1,0:T(4,128)S(1)} %multiply_add_fusion, s32[192]{0:T(256)S(1)} %eq.21), kind=kOutput, calls=%fused_computation.3 | convolution fusion | flops 37785600 | bytes 787968 | tf_op jit(solution)/shard_map/dot_general | solution.py:69
  23.3 2.2 %copy.17 = f32[2,2,4,16,24,16]{5,4,3,2,1,0:T(8,128)S(1)} copy(f32[2,2,4,16,24,16]{4,5,3,1,0,2:T(8,128)} %convolution_bitcast_fusion) | data formatting | bytes 786432 | tf_op jit(solution)/shard_map/transpose | solution.py:82
  25.6 1.6 %reshape.467 = f32[2,2,64,384]{3,2,1,0:T(8,128)} reshape(f32[2,2,4,16,24,16]{5,4,3,2,1,0:T(8,128)S(1)} %copy.17) | data formatting | bytes 786432 | tf_op jit(solution)/shard_map/reshape | solution.py:82
  27.2 1.7 %collective-permute-start.2 = (bf16[2,2,12800]{2,1,0:T(2,128)(2,1)S(1)}, bf16[2,2,12800]{2,1,0:T(2,128)(2,1)S(1)}, u32[]{:S(2)}, u32[]{:S(2)}) collective-permute-start(bf16[2,2,12800]{2,1,0:T(2,128)(2,1)S(1)} %pad_maximum_fusion.3), channel_id=1, source_target_pairs={{0,2},{1,3},{2,0},{3,1},{4,6},{5,7},{6,4},{7,5},{8,10},{9,11},{10,... | collective-permute-start | bytes 307208 | tf_op jit(solution)/shard_map/ppermute | solution.py:12
  28.9 1.1 %fusion.3 = bf16[2,2,64,384]{3,2,1,0:T(8,128)(2,1)S(1)} fusion(f32[2,2,64,384]{3,2,1,0:T(8,128)} %reshape.467, bf16[2,2,64,384]{3,2,1,0:T(8,128)(2,1)} %param.13), kind=kLoop, calls=%fused_computation.13 | loop fusion | flops 294912 | bytes 786432 | tf_op jit(solution)/shard_map/convert_element_type | solution.py:85
  30.0 0.6 copy.18
  30.6 1.0 %reshape.502 = bf16[8,2,6144]{2,1,0:T(2,128)(2,1)} reshape(bf16[384,2,2,64]{3,2,1,0:T(2,128)(2,1)S(1)} %bitcast.65) | data formatting | bytes 393216
  31.6 3.4 %all-to-all-start.1 = ((bf16[8,2,6144]{2,1,0:T(2,128)(2,1)}), bf16[8,2,6144]{2,1,0:T(2,128)(2,1)S(1)}, u32[]{:S(2)}, u32[]{:S(2)}) async-start(bf16[8,2,6144]{2,1,0:T(2,128)(2,1)} %reshape.502), calls=%async_computation.1 | async-start | bytes 393216 | tf_op jit(solution)/shard_map/all_to_all | solution.py:86
  35.0 0.3 pad_maximum_fusion.2
  35.3 2.0 %collective-permute-start.3 = (bf16[2,2,2,12800]{3,2,1,0:T(2,128)(2,1)S(1)}, bf16[2,2,2,12800]{3,2,1,0:T(2,128)(2,1)S(1)}, u32[]{:S(2)}, u32[]{:S(2)}) collective-permute-start(bf16[2,2,2,12800]{3,2,1,0:T(2,128)(2,1)S(1)} %pad_maximum_fusion.2), channel_id=1, source_target_pairs={{0,4},{1,5},{2,6},{3,7},{4,0},{5,1},{6,2},{7,3},{8,12},{9,13},{10,... | collective-permute-start | bytes 614408 | tf_op jit(solution)/shard_map/ppermute | solution.py:12
  37.3 0.3 fusion.28
  37.6 3.6 %all-to-all-done.1 = bf16[8,2,6144]{2,1,0:T(2,128)(2,1)S(1)} async-done(((bf16[8,2,6144]{2,1,0:T(2,128)(2,1)}), bf16[8,2,6144]{2,1,0:T(2,128)(2,1)S(1)}, u32[]{:S(2)}, u32[]{:S(2)}) %all-to-all-start.1) | async-done | bytes 196640 | tf_op jit(solution)/shard_map/all_to_all | solution.py:86
  41.2 0.3 reshape.503
  41.5 0.3 copy.32
  41.7 0.3 all_to_all.33
  42.0 2.6 %collective-permute-done.3 = bf16[2,2,2,12800]{3,2,1,0:T(2,128)(2,1)S(1)} collective-permute-done((bf16[2,2,2,12800]{3,2,1,0:T(2,128)(2,1)S(1)}, bf16[2,2,2,12800]{3,2,1,0:T(2,128)(2,1)S(1)}, u32[]{:S(2)}, u32[]{:S(2)}) %collective-permute-start.3) | collective-permute-done | bytes 204832 | tf_op jit(solution)/shard_map/ppermute | solution.py:12
  44.6 0.6 pad_maximum_fusion.1
  45.3 0.6 fusion.27
  45.9 1.1 %collective-permute-done.4 = bf16[2,2,2,2,12800]{4,3,2,1,0:T(2,128)(2,1)S(1)} collective-permute-done((bf16[2,2,2,2,12800]{4,3,2,1,0:T(2,128)(2,1)S(1)}, bf16[2,2,2,2,12800]{4,3,2,1,0:T(2,128)(2,1)S(1)}, u32[]{:S(2)}, u32[]{:S(2)}) %collective-permute-start.4) | collective-permute-done | bytes 409632 | tf_op jit(solution)/shard_map/ppermute | solution.py:12
  47.0 1.2 %pad_maximum_fusion = bf16[2,2,2,2,2,12800]{5,4,3,2,1,0:T(2,128)(2,1)S(1)} fusion(bf16[1,2,2,2,2,12800]{5,4,3,2,1,0:T(2,128)(2,1)S(1)} %bitcast.72, bf16[1,2,2,2,2,12800]{5,4,3,2,1,0:T(2,128)(2,1)S(1)} %fusion.27), kind=kLoop, calls=%fused_computation.8 | loop fusion | flops 409600 | bytes 1638400 | tf_op jit(solution)/shard_map/stack | solution.py:13
  48.2 0.3 reshape.468
  48.5 0.9 %gather_fusion.1 = bf16[32,8192]{1,0:T(8,128)(2,1)S(1)} fusion(bf16[32,8192]{1,0:T(8,128)(2,1)S(1)} %slice.14, s32[1024]{0:T(1024)S(1)} %pad_clamp_fusion), kind=kCustom, calls=%fused_computation.1 | custom fusion | bytes 1048704 | tf_op jit(solution)/shard_map/jit(_take)/gather | solution.py:41
  49.4 0.2 reshape.498
  49.7 0.3 fusion.1
  50.0 0.4 copy.21
  50.4 1.4 %reshape.504 = bf16[8,2,6144]{2,1,0:T(2,128)(2,1)} reshape(bf16[512,2,2,48]{3,2,1,0:T(2,128)(2,1)S(1)} %bitcast.62) | data formatting | bytes 393216
  51.8 3.4 %all-to-all-start.2 = ((bf16[8,2,6144]{2,1,0:T(2,128)(2,1)}), bf16[8,2,6144]{2,1,0:T(2,128)(2,1)S(1)}, u32[]{:S(2)}, u32[]{:S(2)}) async-start(bf16[8,2,6144]{2,1,0:T(2,128)(2,1)} %reshape.504), calls=%async_computation.2 | async-start | bytes 393216 | tf_op jit(solution)/shard_map/all_to_all | solution.py:93
  55.3 0.7 %gather_fusion.2 = bf16[32,4608]{1,0:T(8,128)(2,1)S(1)} fusion(bf16[32,4608]{1,0:T(8,128)(2,1)S(1)} %slice.15, s32[1024]{0:T(1024)S(1)} %pad_clamp_fusion), kind=kCustom, calls=%fused_computation.2 | custom fusion | bytes 589952 | tf_op jit(solution)/shard_map/jit(_take)/gather | solution.py:42
  56.0 0.4 reshape.499
  56.4 5.0 %all-to-all-done.2 = bf16[8,2,6144]{2,1,0:T(2,128)(2,1)S(1)} async-done(((bf16[8,2,6144]{2,1,0:T(2,128)(2,1)}), bf16[8,2,6144]{2,1,0:T(2,128)(2,1)S(1)}, u32[]{:S(2)}, u32[]{:S(2)}) %all-to-all-start.2) | async-done | bytes 196640 | tf_op jit(solution)/shard_map/all_to_all | solution.py:93
  61.4 0.5 reshape.505
  61.9 0.3 copy.31
  62.3 0.4 all_to_all.37
  62.7 1.0 %fusion = bf16[2,2,64,384]{3,2,1,0:T(8,128)(2,1)} fusion(bf16[2,2,64,384]{3,2,1,0:T(8,128)(2,1)S(1)} %all_to_all.37, bf16[2,2,64,384]{3,2,1,0:T(8,128)(2,1)S(1)} %copy-done.1, bf16[384,384,1,1]{1,0,2,3:T(8,128)(2,1)S(1)} %reshape.499), kind=kOutput, calls=%fused_computation.6 | convolution fusion | flops 75792384 | bytes 884736 | tf_op jit(solution)/shard_map/by,mlxy->mlxb/dot_general | solution.py:94
  (39 shorter events, 1.3 us)
Async XLA Ops:
  0.0 5.4 %copy-start = (bf16[128,2,2,256]{3,2,1,0:T(2,128)(2,1)S(1)}, bf16[128,2,2,256]{3,2,1,0:T(2,128)(2,1)}, u32[]{:S(2)}) copy-start(bf16[128,2,2,256]{3,2,1,0:T(2,128)(2,1)} %param.8) | copy-start | bytes 786436
  1.5 13.0 %collective-permute-start = (bf16[12800]{0:T(1024)(128)(2,1)S(1)}, bf16[12800]{0:T(1024)(128)(2,1)S(1)}, u32[]{:S(2)}, u32[]{:S(2)}) collective-permute-start(bf16[12800]{0:T(1024)(128)(2,1)S(1)} %constant_dynamic-update-slice_fusion), channel_id=1, source_target_pairs={{0,8},{8,0},{16,24},{24,16},{1,9},{9,1},{17,25},{25,17},{2,10},{10... | collective-permute-start | bytes 76808 | tf_op jit(solution)/shard_map/ppermute | solution.py:12
  7.7 13.3 %all-to-all-start = ((bf16[8,24,2,2,256]{4,3,2,1,0:T(2,128)(2,1)}), bf16[8,24,2,2,256]{4,3,2,1,0:T(2,128)(2,1)S(1)}, u32[]{:S(2)}, u32[]{:S(2)}) async-start(bf16[8,24,2,2,256]{4,3,2,1,0:T(2,128)(2,1)} %bitcast.5), calls=%async_computation | async-start | bytes 786432 | tf_op jit(solution)/shard_map/all_to_all | solution.py:60
  14.7 6.1 %collective-permute-start.1 = (bf16[2,12800]{1,0:T(2,128)(2,1)S(1)}, bf16[2,12800]{1,0:T(2,128)(2,1)S(1)}, u32[]{:S(2)}, u32[]{:S(2)}) collective-permute-start(bf16[2,12800]{1,0:T(2,128)(2,1)S(1)} %pad_maximum_fusion.4), channel_id=1, source_target_pairs={{0,16},{8,24},{16,0},{24,8},{1,17},{9,25},{17,1},{25,9},{2,18},{10... | collective-permute-start | bytes 153608 | tf_op jit(solution)/shard_map/ppermute | solution.py:12
  27.2 7.8 %collective-permute-start.2 = (bf16[2,2,12800]{2,1,0:T(2,128)(2,1)S(1)}, bf16[2,2,12800]{2,1,0:T(2,128)(2,1)S(1)}, u32[]{:S(2)}, u32[]{:S(2)}) collective-permute-start(bf16[2,2,12800]{2,1,0:T(2,128)(2,1)S(1)} %pad_maximum_fusion.3), channel_id=1, source_target_pairs={{0,2},{1,3},{2,0},{3,1},{4,6},{5,7},{6,4},{7,5},{8,10},{9,11},{10,... | collective-permute-start | bytes 307208 | tf_op jit(solution)/shard_map/ppermute | solution.py:12
  31.6 9.6 %all-to-all-start.1 = ((bf16[8,2,6144]{2,1,0:T(2,128)(2,1)}), bf16[8,2,6144]{2,1,0:T(2,128)(2,1)S(1)}, u32[]{:S(2)}, u32[]{:S(2)}) async-start(bf16[8,2,6144]{2,1,0:T(2,128)(2,1)} %reshape.502), calls=%async_computation.1 | async-start | bytes 393216 | tf_op jit(solution)/shard_map/all_to_all | solution.py:86
  35.3 9.3 %collective-permute-start.3 = (bf16[2,2,2,12800]{3,2,1,0:T(2,128)(2,1)S(1)}, bf16[2,2,2,12800]{3,2,1,0:T(2,128)(2,1)S(1)}, u32[]{:S(2)}, u32[]{:S(2)}) collective-permute-start(bf16[2,2,2,12800]{3,2,1,0:T(2,128)(2,1)S(1)} %pad_maximum_fusion.2), channel_id=1, source_target_pairs={{0,4},{1,5},{2,6},{3,7},{4,0},{5,1},{6,2},{7,3},{8,12},{9,13},{10,... | collective-permute-start | bytes 614408 | tf_op jit(solution)/shard_map/ppermute | solution.py:12
  45.2 1.8 %collective-permute-start.4 = (bf16[2,2,2,2,12800]{4,3,2,1,0:T(2,128)(2,1)S(1)}, bf16[2,2,2,2,12800]{4,3,2,1,0:T(2,128)(2,1)S(1)}, u32[]{:S(2)}, u32[]{:S(2)}) collective-permute-start(bf16[2,2,2,2,12800]{4,3,2,1,0:T(2,128)(2,1)S(1)} %pad_maximum_fusion.1), channel_id=1, source_target_pairs={{0,1},{1,0},{2,3},{3,2},{4,5},{5,4},{6,7},{7,6},{8,9},{9,8},{10,11... | collective-permute-start | bytes 1228808 | tf_op jit(solution)/shard_map/ppermute | solution.py:12
  51.8 9.6 %all-to-all-start.2 = ((bf16[8,2,6144]{2,1,0:T(2,128)(2,1)}), bf16[8,2,6144]{2,1,0:T(2,128)(2,1)S(1)}, u32[]{:S(2)}, u32[]{:S(2)}) async-start(bf16[8,2,6144]{2,1,0:T(2,128)(2,1)} %reshape.504), calls=%async_computation.2 | async-start | bytes 393216 | tf_op jit(solution)/shard_map/all_to_all | solution.py:93
  56.0 6.7 %copy-start.1 = (bf16[2,2,64,384]{3,2,1,0:T(8,128)(2,1)S(1)}, bf16[2,2,64,384]{3,2,1,0:T(8,128)(2,1)}, u32[]{:S(2)}) copy-start(bf16[2,2,64,384]{3,2,1,0:T(8,128)(2,1)} %param.13) | copy-start | bytes 589828

commit v7 on v6

--- a/solution.py
+++ b/solution.py
@@ -28,15 +28,15 @@
     y_rows, y_cols = y_operator.shape
     x_size = x_rows * x_cols
     both = jnp.concatenate([x_operator.reshape(-1), y_operator.reshape(-1)])
-    mem_bits = [1 << k for k in range(mem_count.bit_length() - 1)]
     tile_bits = [1 << k for k in range(1, tile_count.bit_length() - 1)] + [1]
-    both = doubling_gather(both, "mem", mem_bits)
+    copies = jnp.broadcast_to(both[None], (mem_count,) + both.shape)
+    both = lax.all_to_all(copies, "mem", split_axis=0, concat_axis=0, tiled=True)
     both, after = lax.optimization_barrier((both, after))
     both = doubling_gather(both, "tile", tile_bits).reshape(mem_count * tile_count, -1)
     mem_of = lax.broadcasted_iota(jnp.int32, (mem_count, tile_count), 0)
     tile_of = lax.broadcasted_iota(jnp.int32, (mem_count, tile_count), 1)
     position = stacked_position(tile_of ^ lax.axis_index("tile"), tile_bits) * mem_count
-    position = position + stacked_position(mem_of ^ lax.axis_index("mem"), mem_bits)
+    position = position + mem_of
     position = position.reshape(-1)
     x_full = jnp.take(both[:, :x_size], position, axis=0, mode="clip")
     y_full = jnp.take(both[:, x_size:], position, axis=0, mode="clip")

time: 64.2 us -> 71.4 us (1.11)
  waiting for transfers between devices: 15.8 us -> 23 us
  starting transfers between devices: 20 us -> 18 us
  local copies, waits for them, and re-layouts: 19.1 us -> 20.2 us
  other arithmetic: 5.29 us -> 6.03 us
    ppermute x5 -> x3, starting transfers between devices: 9.47 us -> 1.19 us  [doubling_gather(): lax.ppermute(data, axis_name, [(j, j ^ bit) for j in range(count)])]
    all_to_all x1, waiting for transfers between devices: 0.01 us -> 8.01 us  [body(): lax.all_to_all(packed, 'tile', split_axis=0, concat_axis=0, tiled=True)]
    all_to_all x0 -> x1, starting transfers between devices: none -> 6.32 us  [gather_operators(): lax.all_to_all(copies, 'mem', split_axis=0, concat_axis=0, tiled=True)]
    ppermute x5 -> x3, waiting for transfers between devices: 7.13 us -> 3.62 us  [doubling_gather(): lax.ppermute(data, axis_name, [(j, j ^ bit) for j in range(count)])]
    all_to_all x1, waiting for transfers between devices: 3.6 us -> 6.13 us  [body(): lax.all_to_all(difference, 'tile', split_axis=3, concat_axis=2, tiled=True)]
    broadcast_in_dim x0 -> x1, other arithmetic: none -> 1.26 us  [gather_operators(): copies = jnp.broadcast_to(both[None], (mem_count,) + both.shape)]
    unnamed x10 -> x12, local copies, waits for them, and re-layouts: 4 us -> 4.77 us
    another operation x8 -> x3, other arithmetic: 3.27 us -> 2.85 us  [doubling_gather(): data = jnp.stack([data, received])]
  transfers between devices with their start and end apart: 8 -> 7, of which waited for: 5 -> 5; matrix products, arithmetic and copies ran while one was open for 19% -> 23% of each run, Pallas kernels for 0% -> 0%
where the time goes in v7:
time: 71.4 us; the launch traced here: 70.6 us
  waiting for transfers between devices  23 us (32%)
  local copies, waits for them, and re-layouts  20.2 us (28%)
  starting transfers between devices  18 us (25%)
  other arithmetic  6.03 us (8%)
  matrix products  3.14 us (4%)
    all_to_all x1, waiting for transfers between devices, body(): lax.all_to_all(packed, 'tile', split_axis=0, concat_axis=0, tiled=True)  8.01 us
    all_to_all x1, starting transfers between devices, gather_operators(): lax.all_to_all(copies, 'mem', split_axis=0, concat_axis=0, tiled=True)  6.32 us
    all_to_all x1, waiting for transfers between devices, body(): lax.all_to_all(difference, 'tile', split_axis=3, concat_axis=2, tiled=True)  6.13 us
    all_to_all x1, waiting for transfers between devices, body(): lax.all_to_all(after_first, 'tile', split_axis=2, concat_axis=3, tiled=True)  5.02 us
    unnamed x12, local copies, waits for them, and re-layouts  4.77 us
    all_to_all x1, starting transfers between devices, body(): lax.all_to_all(packed, 'tile', split_axis=0, concat_axis=0, tiled=True)  3.72 us
    ppermute x3, waiting for transfers between devices, doubling_gather(): lax.ppermute(data, axis_name, [(j, j ^ bit) for j in range(count)])  3.62 us
    all_to_all x1, starting transfers between devices, body(): lax.all_to_all(after_first, 'tile', split_axis=2, concat_axis=3, tiled=True)  3.39 us
  transfers between devices with their start and end apart: 7, of which 5 were waited for; matrix products, arithmetic and copies ran while one was open for 23% of the time, Pallas kernels for 0%

profile of v7, /device:TPU:0, one launch (start us, length us, event | category | flops | bytes accessed | tf_op | source)
XLA Modules:
  0.0 70.6 jit_solution(4695090069868034646)
XLA Ops:
  0.0 0.8 %reshape.328 = bf16[4608]{0:T(1024)(128)(2,1)S(1)} reshape(bf16[12,384]{1,0:T(8,128)(2,1)} %param.15) | data formatting | bytes 18432 | tf_op jit(solution)/shard_map/reshape | solution.py:30
  0.8 0.7 %copy.36 = bf16[2,4,8,128]{3,1,2,0:T(4,128)(2,1)S(1)} copy(bf16[2,4,8,128]{3,2,1,0:T(8,128)(2,1)} %bitcast.73) | data formatting | bytes 32768
  1.5 0.1 broadcast_in_dim.33
  1.6 0.5 broadcast.285
  2.1 1.3 %reduce = bf16[4,12800]{1,0:T(4,128)(2,1)S(1)} reduce(bf16[4,1,12800]{2,1,0:T(2,128)(2,1)S(1)} %broadcast_in_dim.33, bf16[]{:T(256)} %broadcast.285), dimensions={1}, to_apply=%broadcast_in_dim.33.reduce_sub_computation | reduce | bytes 204802 | tf_op jit(solution)/shard_map/broadcast_in_dim | solution.py:32
  3.4 0.7 reshape.366
  4.1 6.3 %all-to-all-start = ((bf16[4,2,6400]{2,1,0:T(2,128)(2,1)}), bf16[4,2,6400]{2,1,0:T(2,128)(2,1)S(1)}, u32[]{:S(2)}, u32[]{:S(2)}) async-start(bf16[4,2,6400]{2,1,0:T(2,128)(2,1)} %reshape.366), calls=%async_computation | async-start | bytes 204800 | tf_op jit(solution)/shard_map/all_to_all | solution.py:33
  10.5 0.8 %reshape.337 = s32[192]{0:T(256)S(1)} reshape(s32[1,8,24]{2,1,0:T(8,128)} %param.9) | data formatting | bytes 1536 | tf_op jit(solution)/shard_map/jit(_take)/broadcast_in_dim | solution.py:57
  11.2 0.7 %iota_compare_fusion = pred[8,24]{1,0:T(8,128)(4,1)S(1)} fusion(s32[8]{0:T(128)} %bitcast.74), kind=kLoop, calls=%fused_computation.27 | loop fusion | flops 192 | bytes 224 | tf_op jit(solution)/shard_map/lt | solution.py:63
  12.0 0.8 %squeeze.3 = bf16[192]{0:T(256)(128)(2,1)S(1)} reshape(f32[1,8,24]{2,1,0:T(8,128)} %param.11) | data formatting | bytes 1152 | tf_op jit(solution)/shard_map/squeeze | solution.py:64
  12.8 0.8 %eq.19 = s32[192]{0:T(256)S(1)} reshape(s32[1,8,24]{2,1,0:T(8,128)} %param.10) | data formatting | bytes 1536 | tf_op jit(solution)/shard_map/eq | solution.py:65
  13.8 2.3 %gather_fusion = bf16[192,2,2,256]{3,2,1,0:T(2,128)(2,1)} fusion(bf16[128,2,2,256]{3,2,1,0:T(2,128)(2,1)S(1)} %copy-done, s32[1024]{0:T(1024)S(1)} %pad_clamp_fusion.1), kind=kCustom, calls=%fused_computation | custom fusion | bytes 787200 | tf_op jit(solution)/shard_map/jit(_take)/gather | solution.py:57
  16.0 0.2 all-to-all-done
  16.3 3.7 %all-to-all-start.1 = ((bf16[8,24,2,2,256]{4,3,2,1,0:T(2,128)(2,1)}), bf16[8,24,2,2,256]{4,3,2,1,0:T(2,128)(2,1)S(1)}, u32[]{:S(2)}, u32[]{:S(2)}) async-start(bf16[8,24,2,2,256]{4,3,2,1,0:T(2,128)(2,1)} %bitcast.3), calls=%async_computation.1 | async-start | bytes 786432 | tf_op jit(solution)/shard_map/all_to_all | solution.py:60
  20.3 8.0 %all-to-all-done.1 = bf16[8,24,2,2,256]{4,3,2,1,0:T(2,128)(2,1)S(1)} async-done(((bf16[8,24,2,2,256]{4,3,2,1,0:T(2,128)(2,1)}), bf16[8,24,2,2,256]{4,3,2,1,0:T(2,128)(2,1)S(1)}, u32[]{:S(2)}, u32[]{:S(2)}) %all-to-all-start.1) | async-done | bytes 393248 | tf_op jit(solution)/shard_map/all_to_all | solution.py:60
  28.3 0.6 collective-permute-start
  28.9 0.3 reshape.330
  29.2 0.2 copy.23
  29.4 3.6 %collective-permute-done = bf16[4,12800]{1,0:T(4,128)(2,1)S(1)} collective-permute-done((bf16[4,12800]{1,0:T(4,128)(2,1)S(1)}, bf16[4,12800]{1,0:T(4,128)(2,1)S(1)}, u32[]{:S(2)}, u32[]{:S(2)}) %collective-permute-start) | collective-permute-done | bytes 102432 | tf_op jit(solution)/shard_map/ppermute | solution.py:12
  33.0 0.9 %fusion.18 = (bf16[1,2,4,12800]{3,2,1,0:T(4,128)(2,1)}, bf16[2,4,12800]{2,1,0:T(4,128)(2,1)}) fusion(bf16[1,4,12800]{2,1,0:T(4,128)(2,1)S(1)} %bitcast.71, bf16[1,4,12800]{2,1,0:T(4,128)(2,1)S(1)} %bitcast.69), kind=kLoop, calls=%fused_computation.60 | loop fusion | flops 102400 | bytes 614400 | tf_op jit(solution)/shard_map/stack | solution.py:13
  33.9 0.6 collective-permute-start.1
  34.5 1.9 %convolution_bitcast_fusion = f32[2,2,4,16,24,16]{4,5,3,1,0,2:T(8,128)} fusion(bf16[2,2,16,16,192,1]{4,3,2,1,0,5:T(8,128)(2,1)S(1)} %bitcast.61, bf16[192]{0:T(256)(128)(2,1)S(1)} %broadcast_select_fusion.2, s32[4,24]{1,0:T(4,128)S(1)} %multiply_add_fusion, s32[192]{0:T(256)S(1)} %eq.19), kind=kOutput, calls=%fused_computation.3 | convolution fusion | flops 37785600 | bytes 787968 | tf_op jit(solution)/shard_map/dot_general | solution.py:69
  36.3 2.2 %copy.24 = f32[2,2,4,16,24,16]{5,4,3,2,1,0:T(8,128)S(1)} copy(f32[2,2,4,16,24,16]{4,5,3,1,0,2:T(8,128)} %convolution_bitcast_fusion) | data formatting | bytes 786432 | tf_op jit(solution)/shard_map/transpose | solution.py:82
  38.6 1.6 %reshape.331 = f32[2,2,64,384]{3,2,1,0:T(8,128)} reshape(f32[2,2,4,16,24,16]{5,4,3,2,1,0:T(8,128)S(1)} %copy.24) | data formatting | bytes 786432 | tf_op jit(solution)/shard_map/reshape | solution.py:82
  40.2 1.4 %fusion.19 = (bf16[1,2,2,4,12800]{4,3,2,1,0:T(4,128)(2,1)S(1)}, bf16[2,2,4,12800]{3,2,1,0:T(4,128)(2,1)S(1)}) fusion(bf16[1,2,4,12800]{3,2,1,0:T(4,128)(2,1)} %bitcast.14, bf16[1,2,4,12800]{3,2,1,0:T(4,128)(2,1)} %get-tuple-element.11), kind=kLoop, calls=%fused_computation.61 | loop fusion | flops 204800 | bytes 1228800 | tf_op jit(solution)/shard_map/stack | solution.py:13
  41.6 1.1 %fusion.3 = bf16[2,2,64,384]{3,2,1,0:T(8,128)(2,1)S(1)} fusion(f32[2,2,64,384]{3,2,1,0:T(8,128)} %reshape.331, bf16[2,2,64,384]{3,2,1,0:T(8,128)(2,1)} %param.13), kind=kLoop, calls=%fused_computation.13 | loop fusion | flops 294912 | bytes 786432 | tf_op jit(solution)/shard_map/convert_element_type | solution.py:85
  42.7 0.6 copy.25
  43.3 1.0 %reshape.368 = bf16[8,2,6144]{2,1,0:T(2,128)(2,1)} reshape(bf16[384,2,2,64]{3,2,1,0:T(2,128)(2,1)S(1)} %bitcast.65) | data formatting | bytes 393216
  44.3 3.4 %all-to-all-start.2 = ((bf16[8,2,6144]{2,1,0:T(2,128)(2,1)}), bf16[8,2,6144]{2,1,0:T(2,128)(2,1)S(1)}, u32[]{:S(2)}, u32[]{:S(2)}) async-start(bf16[8,2,6144]{2,1,0:T(2,128)(2,1)} %reshape.368), calls=%async_computation.2 | async-start | bytes 393216 | tf_op jit(solution)/shard_map/all_to_all | solution.py:86
  47.7 6.1 %all-to-all-done.2 = bf16[8,2,6144]{2,1,0:T(2,128)(2,1)S(1)} async-done(((bf16[8,2,6144]{2,1,0:T(2,128)(2,1)}), bf16[8,2,6144]{2,1,0:T(2,128)(2,1)S(1)}, u32[]{:S(2)}, u32[]{:S(2)}) %all-to-all-start.2) | async-done | bytes 196640 | tf_op jit(solution)/shard_map/all_to_all | solution.py:86
  53.9 0.3 reshape.369
  54.2 0.3 copy.41
  54.4 0.3 all_to_all.41
  54.7 0.6 pad_maximum_fusion
  55.3 0.2 reshape.332
  55.5 0.9 %gather_fusion.1 = bf16[32,8192]{1,0:T(8,128)(2,1)S(1)} fusion(bf16[32,8192]{1,0:T(8,128)(2,1)S(1)} %slice.14, s32[1024]{0:T(1024)S(1)} %pad_clamp_fusion), kind=kCustom, calls=%fused_computation.1 | custom fusion | bytes 1048704 | tf_op jit(solution)/shard_map/jit(_take)/gather | solution.py:41
  56.4 0.2 reshape.362
  56.7 0.3 fusion.1
  57.0 0.4 copy.28
  57.4 1.4 %reshape.370 = bf16[8,2,6144]{2,1,0:T(2,128)(2,1)} reshape(bf16[512,2,2,48]{3,2,1,0:T(2,128)(2,1)S(1)} %bitcast.62) | data formatting | bytes 393216
  58.8 3.4 %all-to-all-start.3 = ((bf16[8,2,6144]{2,1,0:T(2,128)(2,1)}), bf16[8,2,6144]{2,1,0:T(2,128)(2,1)S(1)}, u32[]{:S(2)}, u32[]{:S(2)}) async-start(bf16[8,2,6144]{2,1,0:T(2,128)(2,1)} %reshape.370), calls=%async_computation.3 | async-start | bytes 393216 | tf_op jit(solution)/shard_map/all_to_all | solution.py:93
  62.3 0.7 %gather_fusion.2 = bf16[32,4608]{1,0:T(8,128)(2,1)S(1)} fusion(bf16[32,4608]{1,0:T(8,128)(2,1)S(1)} %slice.15, s32[1024]{0:T(1024)S(1)} %pad_clamp_fusion), kind=kCustom, calls=%fused_computation.2 | custom fusion | bytes 589952 | tf_op jit(solution)/shard_map/jit(_take)/gather | solution.py:42
  63.0 0.4 reshape.363
  63.4 5.0 %all-to-all-done.3 = bf16[8,2,6144]{2,1,0:T(2,128)(2,1)S(1)} async-done(((bf16[8,2,6144]{2,1,0:T(2,128)(2,1)}), bf16[8,2,6144]{2,1,0:T(2,128)(2,1)S(1)}, u32[]{:S(2)}, u32[]{:S(2)}) %all-to-all-start.3) | async-done | bytes 196640 | tf_op jit(solution)/shard_map/all_to_all | solution.py:93
  68.4 0.5 reshape.371
  68.9 0.3 copy.40
  69.3 0.4 all_to_all.45
  69.7 1.0 %fusion = bf16[2,2,64,384]{3,2,1,0:T(8,128)(2,1)} fusion(bf16[2,2,64,384]{3,2,1,0:T(8,128)(2,1)S(1)} %all_to_all.45, bf16[2,2,64,384]{3,2,1,0:T(8,128)(2,1)S(1)} %copy-done.1, bf16[384,384,1,1]{1,0,2,3:T(8,128)(2,1)S(1)} %reshape.363), kind=kOutput, calls=%fused_computation.6 | convolution fusion | flops 75792384 | bytes 884736 | tf_op jit(solution)/shard_map/by,mlxy->mlxb/dot_general | solution.py:94
  (30 shorter events, 0.8 us)
Async XLA Ops:
  0.0 13.8 %copy-start = (bf16[128,2,2,256]{3,2,1,0:T(2,128)(2,1)S(1)}, bf16[128,2,2,256]{3,2,1,0:T(2,128)(2,1)}, u32[]{:S(2)}) copy-start(bf16[128,2,2,256]{3,2,1,0:T(2,128)(2,1)} %param.8) | copy-start | bytes 786436
  4.1 12.2 %all-to-all-start = ((bf16[4,2,6400]{2,1,0:T(2,128)(2,1)}), bf16[4,2,6400]{2,1,0:T(2,128)(2,1)S(1)}, u32[]{:S(2)}, u32[]{:S(2)}) async-start(bf16[4,2,6400]{2,1,0:T(2,128)(2,1)} %reshape.366), calls=%async_computation | async-start | bytes 204800 | tf_op jit(solution)/shard_map/all_to_all | solution.py:33
  16.3 12.1 %all-to-all-start.1 = ((bf16[8,24,2,2,256]{4,3,2,1,0:T(2,128)(2,1)}), bf16[8,24,2,2,256]{4,3,2,1,0:T(2,128)(2,1)S(1)}, u32[]{:S(2)}, u32[]{:S(2)}) async-start(bf16[8,24,2,2,256]{4,3,2,1,0:T(2,128)(2,1)} %bitcast.3), calls=%async_computation.1 | async-start | bytes 786432 | tf_op jit(solution)/shard_map/all_to_all | solution.py:60
  28.3 4.7 %collective-permute-start = (bf16[4,12800]{1,0:T(4,128)(2,1)S(1)}, bf16[4,12800]{1,0:T(4,128)(2,1)S(1)}, u32[]{:S(2)}, u32[]{:S(2)}) collective-permute-start(bf16[4,12800]{1,0:T(4,128)(2,1)S(1)} %bitcast.68), channel_id=1, source_target_pairs={{0,2},{1,3},{2,0},{3,1},{4,6},{5,7},{6,4},{7,5},{8,10},{9,11},{10,... | collective-permute-start | bytes 307208 | tf_op jit(solution)/shard_map/ppermute | solution.py:12
  33.9 6.3 %collective-permute-start.1 = (bf16[2,4,12800]{2,1,0:T(4,128)(2,1)}, bf16[2,4,12800]{2,1,0:T(4,128)(2,1)}, u32[]{:S(2)}, u32[]{:S(2)}) collective-permute-start(bf16[2,4,12800]{2,1,0:T(4,128)(2,1)} %get-tuple-element.12), channel_id=1, source_target_pairs={{0,4},{1,5},{2,6},{3,7},{4,0},{5,1},{6,2},{7,3},{8,12},{9,13},{10,... | collective-permute-start | bytes 614408 | tf_op jit(solution)/shard_map/ppermute | solution.py:12
  41.5 13.2 %collective-permute-start.2 = (bf16[2,2,4,12800]{3,2,1,0:T(4,128)(2,1)S(1)}, bf16[2,2,4,12800]{3,2,1,0:T(4,128)(2,1)S(1)}, u32[]{:S(2)}, u32[]{:S(2)}) collective-permute-start(bf16[2,2,4,12800]{3,2,1,0:T(4,128)(2,1)S(1)} %get-tuple-element.10), channel_id=1, source_target_pairs={{0,1},{1,0},{2,3},{3,2},{4,5},{5,4},{6,7},{7,6},{8,9},{9,8},{10,11... | collective-permute-start | bytes 1228808 | tf_op jit(solution)/shard_map/ppermute | solution.py:12
  44.3 9.6 %all-to-all-start.2 = ((bf16[8,2,6144]{2,1,0:T(2,128)(2,1)}), bf16[8,2,6144]{2,1,0:T(2,128)(2,1)S(1)}, u32[]{:S(2)}, u32[]{:S(2)}) async-start(bf16[8,2,6144]{2,1,0:T(2,128)(2,1)} %reshape.368), calls=%async_computation.2 | async-start | bytes 393216 | tf_op jit(solution)/shard_map/all_to_all | solution.py:86
  58.8 9.6 %all-to-all-start.3 = ((bf16[8,2,6144]{2,1,0:T(2,128)(2,1)}), bf16[8,2,6144]{2,1,0:T(2,128)(2,1)S(1)}, u32[]{:S(2)}, u32[]{:S(2)}) async-start(bf16[8,2,6144]{2,1,0:T(2,128)(2,1)} %reshape.370), calls=%async_computation.3 | async-start | bytes 393216 | tf_op jit(solution)/shard_map/all_to_all | solution.py:93
  63.0 6.7 %copy-start.1 = (bf16[2,2,64,384]{3,2,1,0:T(8,128)(2,1)S(1)}, bf16[2,2,64,384]{3,2,1,0:T(8,128)(2,1)}, u32[]{:S(2)}) copy-start(bf16[2,2,64,384]{3,2,1,0:T(8,128)(2,1)} %param.13) | copy-start | bytes 589828

commit v8 on v6

--- a/solution.py
+++ b/solution.py
@@ -59,37 +59,40 @@
     )
     arrived = lax.all_to_all(packed, "tile", split_axis=0, concat_axis=0, tiled=True)
     x_full, y_full, arrived = gather_operators(x_operator, y_operator, arrived)
-    slot_count = columns // block_side * (y_cells // block_side)
+    sx_count = columns // block_side
+    y_blocks = y_cells // block_side
+    j_count = y_blocks // tile_count
+    y_chunk = y_cells // tile_count
     live_mask = lax.broadcasted_iota(jnp.int32, (tile_count, capacity), 1) < recv_count[0][:, None]
     weights = jnp.where(live_mask, recv_weight[0], 0.0).reshape(-1)
-    slot_match = recv_slot[0].reshape(-1)[None, :] == lax.broadcasted_iota(
-        jnp.int32, (slot_count, tile_count * capacity), 0
-    )
+    row = lax.broadcasted_iota(jnp.int32, (tile_count, sx_count, j_count), 0) * j_count
+    row = row + lax.broadcasted_iota(jnp.int32, (tile_count, sx_count, j_count), 1) * y_blocks
+    row = row + lax.broadcasted_iota(jnp.int32, (tile_count, sx_count, j_count), 2)
+    slot_match = recv_slot[0].reshape(-1)[None, :] == row.reshape(-1)[:, None]
     remap_weights = jnp.where(slot_match, weights[None, :], 0.0).astype(jnp.bfloat16)
     remapped = jnp.dot(
         remap_weights,
         arrived.reshape(tile_count * capacity, -1),
         preferred_element_type=jnp.float32,
     )
-    remapped = remapped.reshape(
-        columns // block_side,
-        y_cells // block_side,
-        member_count,
-        level_count,
-        block_side,
-        block_side,
+    local_regional = regional.reshape(
+        member_count, level_count, sx_count, block_side, tile_count, j_count, block_side
+    ).transpose(4, 2, 5, 0, 1, 3, 6).reshape(remapped.shape)
+    difference = (remapped - local_regional.astype(jnp.float32)).astype(jnp.bfloat16)
+    lines = lax.all_to_all(
+        difference.reshape(tile_count, sx_count * j_count, -1),
+        "tile",
+        split_axis=0,
+        concat_axis=0,
+        tiled=True,
     )
-    remapped = remapped.transpose(2, 3, 0, 4, 1, 5).reshape(
-        member_count, level_count, columns, y_cells
-    )
-    difference = (remapped - regional.astype(jnp.float32)).astype(jnp.bfloat16)
-    x_lines = lax.all_to_all(difference, "tile", split_axis=3, concat_axis=2, tiled=True)
-    after_first = jnp.einsum(
-        "ax,mlxy->mlay",
-        x_full,
-        x_lines,
-        preferred_element_type=jnp.float32,
-    ).astype(jnp.bfloat16)
+    x_lines = lines.reshape(
+        tile_count, sx_count, j_count, member_count, level_count, block_side, block_side
+    ).transpose(0, 1, 5, 3, 4, 2, 6).reshape(tile_count * columns, -1)
+    after_first = jnp.dot(x_full, x_lines, preferred_element_type=jnp.float32).astype(jnp.bfloat16)
+    after_first = after_first.reshape(
+        tile_count * columns, member_count, level_count, y_chunk
+    ).transpose(1, 2, 0, 3)
     tile_back = lax.all_to_all(after_first, "tile", split_axis=2, concat_axis=3, tiled=True)
     after_second = jnp.einsum(
         "by,mlxy->mlxb",

time: 64.2 us -> 76 us (1.18)
  local copies, waits for them, and re-layouts: 19.1 us -> 32.8 us
  waiting for transfers between devices: 15.8 us -> 11.3 us
  other arithmetic: 5.29 us -> 7.78 us
    convert_element_type x2 -> x4, local copies, waits for them, and re-layouts: 0.99 us -> 10.5 us  [the longest x3 9.36 us: body(): local_regional.astype(jnp.float32)]
    reshape x1 -> x4, local copies, waits for them, and re-layouts: 1.63 us -> 5.89 us  [the longest x1 3.48 us: body(): x_lines = lines.reshape(tile_count, sx_count, j_count, member_count, leve...]
    ppermute x5, waiting for transfers between devices: 7.13 us -> 3.26 us  [doubling_gather(): lax.ppermute(data, axis_name, [(j, j ^ bit) for j in range(count)])]
    another operation x8, other arithmetic: 3.27 us -> 6.76 us  [doubling_gather(): data = jnp.stack([data, received])]
    convert_element_type x1 -> x0, other arithmetic: 1.09 us -> none  [body(): difference = (remapped - regional.astype(jnp.float32)).astype(jnp.bfloat16)]
    unnamed x10 -> x11, local copies, waits for them, and re-layouts: 4 us -> 3.06 us
    reshape x2 -> x1, local copies, waits for them, and re-layouts: 0.47 us -> 1.26 us  [body(): arrived.reshape(tile_count * capacity, -1)]
  transfers between devices with their start and end apart: 8 -> 8, of which waited for: 5 -> 4; matrix products, arithmetic and copies ran while one was open for 19% -> 42% of each run, Pallas kernels for 0% -> 0%
where the time goes in v8:
time: 76 us; the launch traced here: 75.2 us
  local copies, waits for them, and re-layouts  32.8 us (43%)
  starting transfers between devices  20.4 us (27%)
  waiting for transfers between devices  11.3 us (15%)
  other arithmetic  7.78 us (10%)
  matrix products  2.53 us (3%)
    convert_element_type x3, local copies, waits for them, and re-layouts, body(): local_regional.astype(jnp.float32)  9.36 us
    ppermute x5, starting transfers between devices, doubling_gather(): lax.ppermute(data, axis_name, [(j, j ^ bit) for j in range(count)])  9.32 us
    another operation x8, other arithmetic, doubling_gather(): data = jnp.stack([data, received])  6.76 us
    all_to_all x1, waiting for transfers between devices, body(): lax.all_to_all(after_first, 'tile', split_axis=2, concat_axis=3, tiled=True)  5.02 us
    all_to_all x1, starting transfers between devices, body(): lax.all_to_all(packed, 'tile', split_axis=0, concat_axis=0, tiled=True)  4.1 us
    all_to_all x1, starting transfers between devices, body(): lax.all_to_all(difference.reshape(tile_count, sx_count * j_count, -1), 't...  3.59 us
    reshape x1, local copies, waits for them, and re-layouts, body(): x_lines = lines.reshape(tile_count, sx_count, j_count, member_count, leve...  3.48 us
    all_to_all x1, starting transfers between devices, body(): lax.all_to_all(after_first, 'tile', split_axis=2, concat_axis=3, tiled=True)  3.39 us
  transfers between devices with their start and end apart: 8, of which 4 were waited for; matrix products, arithmetic and copies ran while one was open for 42% of the time, Pallas kernels for 0%

profile of v8, /device:TPU:0, one launch (start us, length us, event | category | flops | bytes accessed | tf_op | source)
XLA Modules:
  0.0 75.2 jit_solution(7309290156862629098)
XLA Ops:
  0.0 0.8 %reshape.474 = bf16[4608]{0:T(1024)(128)(2,1)S(1)} reshape(bf16[12,384]{1,0:T(8,128)(2,1)} %param.15) | data formatting | bytes 18432 | tf_op jit(solution)/shard_map/reshape | solution.py:30
  0.8 0.7 copy.30
  1.5 3.1 %collective-permute-start = (bf16[12800]{0:T(1024)(128)(2,1)S(1)}, bf16[12800]{0:T(1024)(128)(2,1)S(1)}, u32[]{:S(2)}, u32[]{:S(2)}) collective-permute-start(bf16[12800]{0:T(1024)(128)(2,1)S(1)} %constant_dynamic-update-slice_fusion), channel_id=1, source_target_pairs={{0,8},{8,0},{16,24},{24,16},{1,9},{9,1},{17,25},{25,17},{2,10},{10... | collective-permute-start | bytes 76808 | tf_op jit(solution)/shard_map/ppermute | solution.py:12
  4.6 0.8 %reshape.488 = s32[192]{0:T(256)S(1)} reshape(s32[1,8,24]{2,1,0:T(8,128)} %param.9) | data formatting | bytes 1536 | tf_op jit(solution)/shard_map/jit(_take)/broadcast_in_dim | solution.py:57
  5.4 2.3 %gather_fusion = bf16[192,2,2,256]{3,2,1,0:T(2,128)(2,1)} fusion(bf16[128,2,2,256]{3,2,1,0:T(2,128)(2,1)S(1)} %copy-done, s32[1024]{0:T(1024)S(1)} %pad_clamp_fusion.1), kind=kCustom, calls=%fused_computation | custom fusion | bytes 787200 | tf_op jit(solution)/shard_map/jit(_take)/gather | solution.py:57
  7.6 4.1 %all-to-all-start = ((bf16[8,24,2,2,256]{4,3,2,1,0:T(2,128)(2,1)}), bf16[8,24,2,2,256]{4,3,2,1,0:T(2,128)(2,1)}, u32[]{:S(2)}, u32[]{:S(2)}) async-start(bf16[8,24,2,2,256]{4,3,2,1,0:T(2,128)(2,1)} %bitcast.2), calls=%async_computation | async-start | bytes 786432 | tf_op jit(solution)/shard_map/all_to_all | solution.py:60
  11.9 0.8 %squeeze.3 = bf16[192]{0:T(256)(128)(2,1)S(1)} reshape(f32[1,8,24]{2,1,0:T(8,128)} %param.11) | data formatting | bytes 1152 | tf_op jit(solution)/shard_map/squeeze | solution.py:67
  12.8 0.7 iota_compare_fusion
  14.2 0.8 %eq.21 = s32[192]{0:T(256)S(1)} reshape(s32[1,8,24]{2,1,0:T(8,128)} %param.10) | data formatting | bytes 1536 | tf_op jit(solution)/shard_map/eq | solution.py:71
  15.1 1.1 %copy.20 = f32[2,2,64,384]{2,3,1,0:T(8,128)S(1)} copy(bf16[2,2,64,384]{3,2,1,0:T(8,128)(2,1)} %param.13) | data formatting | bytes 589824 | tf_op jit(solution)/shard_map/convert_element_type | solution.py:103
  16.2 2.9 %reshape.485 = f32[2,2,4,16,8,3,16]{3,2,6,5,4,1,0:T(4,128)} reshape(f32[2,2,64,384]{2,3,1,0:T(8,128)S(1)} %copy.20) | data formatting | bytes 786432 | tf_op jit(solution)/shard_map/convert_element_type | solution.py:81
  19.2 3.2 %copy.21 = f32[8,4,3,2,2,16,16]{6,5,4,3,2,1,0:T(8,128)S(1)} copy(f32[8,4,3,2,2,16,16]{5,1,6,2,0,4,3:T(4,128)} %bitcast.49) | data formatting | bytes 786432 | tf_op jit(solution)/shard_map/convert_element_type | solution.py:81
  22.3 3.3 %reshape.484 = f32[96,1024]{1,0:T(8,128)} reshape(f32[8,4,3,2,2,16,16]{6,5,4,3,2,1,0:T(8,128)S(1)} %copy.21) | data formatting | bytes 786432 | tf_op jit(solution)/shard_map/convert_element_type | solution.py:81
  25.6 0.1 pad_maximum_fusion.4
  25.8 2.7 %collective-permute-start.1 = (bf16[2,12800]{1,0:T(2,128)(2,1)S(1)}, bf16[2,12800]{1,0:T(2,128)(2,1)S(1)}, u32[]{:S(2)}, u32[]{:S(2)}) collective-permute-start(bf16[2,12800]{1,0:T(2,128)(2,1)S(1)} %pad_maximum_fusion.4), channel_id=1, source_target_pairs={{0,16},{8,24},{16,0},{24,8},{1,17},{9,25},{17,1},{25,9},{2,18},{10... | collective-permute-start | bytes 153608 | tf_op jit(solution)/shard_map/ppermute | solution.py:12
  28.4 0.1 fusion.26
  28.5 3.2 %collective-permute-done.1 = bf16[2,12800]{1,0:T(2,128)(2,1)S(1)} collective-permute-done((bf16[2,12800]{1,0:T(2,128)(2,1)S(1)}, bf16[2,12800]{1,0:T(2,128)(2,1)S(1)}, u32[]{:S(2)}, u32[]{:S(2)}) %collective-permute-start.1) | collective-permute-done | bytes 51232 | tf_op jit(solution)/shard_map/ppermute | solution.py:12
  31.7 0.1 pad_maximum_fusion.3
  31.9 1.3 %reshape.478 = bf16[192,1024]{1,0:T(8,128)(2,1)S(1)} reshape(bf16[8,24,2,2,256]{4,3,2,1,0:T(2,128)(2,1)} %all-to-all-done) | data formatting | bytes 786432 | tf_op jit(solution)/shard_map/reshape | solution.py:75
  33.1 1.7 %collective-permute-start.2 = (bf16[2,2,12800]{2,1,0:T(2,128)(2,1)S(1)}, bf16[2,2,12800]{2,1,0:T(2,128)(2,1)S(1)}, u32[]{:S(2)}, u32[]{:S(2)}) collective-permute-start(bf16[2,2,12800]{2,1,0:T(2,128)(2,1)S(1)} %pad_maximum_fusion.3), channel_id=1, source_target_pairs={{0,2},{1,3},{2,0},{3,1},{4,6},{5,7},{6,4},{7,5},{8,10},{9,11},{10,... | collective-permute-start | bytes 307208 | tf_op jit(solution)/shard_map/ppermute | solution.py:12
  34.9 1.2 %fusion = bf16[96,1024]{1,0:T(8,128)(2,1)S(1)} fusion(f32[96,1024]{1,0:T(8,128)} %reshape.484, bf16[192,1024]{1,0:T(8,128)(2,1)S(1)} %reshape.478, bf16[192]{0:T(256)(128)(2,1)S(1)} %broadcast_select_fusion.3, s32[192]{0:T(256)S(1)} %eq.21, s32[96]{0:T(128)S(1)} %add.139), kind=kOutput, calls=%fused_computation.5 | convolution fusion | flops 37982208 | bytes 984576 | tf_op jit(solution)/shard_map/dot_general | solution.py:73
  36.1 0.7 reshape.479
  36.9 3.6 %all-to-all-start.1 = ((bf16[8,12,1024]{2,1,0:T(8,128)(2,1)}), bf16[8,12,1024]{2,1,0:T(8,128)(2,1)S(1)}, u32[]{:S(2)}, u32[]{:S(2)}) async-start(bf16[8,12,1024]{2,1,0:T(8,128)(2,1)} %reshape.479), calls=%async_computation.1 | async-start | bytes 524288 | tf_op jit(solution)/shard_map/all_to_all | solution.py:82
  40.5 1.0 %pad_maximum_fusion.2 = bf16[2,2,2,12800]{3,2,1,0:T(2,128)(2,1)} fusion(bf16[1,2,2,12800]{3,2,1,0:T(2,128)(2,1)S(1)} %bitcast.57, bf16[1,2,2,12800]{3,2,1,0:T(2,128)(2,1)S(1)} %bitcast.53), kind=kLoop, calls=%fused_computation.12 | loop fusion | flops 102400 | bytes 409600 | tf_op jit(solution)/shard_map/stack | solution.py:13
  41.4 1.8 %collective-permute-start.3 = (bf16[2,2,2,12800]{3,2,1,0:T(2,128)(2,1)}, bf16[2,2,2,12800]{3,2,1,0:T(2,128)(2,1)}, u32[]{:S(2)}, u32[]{:S(2)}) collective-permute-start(bf16[2,2,2,12800]{3,2,1,0:T(2,128)(2,1)} %pad_maximum_fusion.2), channel_id=1, source_target_pairs={{0,4},{1,5},{2,6},{3,7},{4,0},{5,1},{6,2},{7,3},{8,12},{9,13},{10,... | collective-permute-start | bytes 614408 | tf_op jit(solution)/shard_map/ppermute | solution.py:12
  43.2 1.0 %fusion.25 = bf16[1,2,2,2,12800]{4,3,2,1,0:T(2,128)(2,1)} fusion(bf16[1,2,2,12800]{3,2,1,0:T(2,128)(2,1)S(1)} %bitcast.58, bf16[1,2,2,12800]{3,2,1,0:T(2,128)(2,1)S(1)} %bitcast.54), kind=kLoop, calls=%fused_computation.79 | loop fusion | flops 102400 | bytes 409600 | tf_op jit(solution)/shard_map/stack | solution.py:13
  44.2 3.0 %all-to-all-done.1 = bf16[8,12,1024]{2,1,0:T(8,128)(2,1)S(1)} async-done(((bf16[8,12,1024]{2,1,0:T(8,128)(2,1)}), bf16[8,12,1024]{2,1,0:T(8,128)(2,1)S(1)}, u32[]{:S(2)}, u32[]{:S(2)}) %all-to-all-start.1) | async-done | bytes 196640 | tf_op jit(solution)/shard_map/all_to_all | solution.py:82
  47.3 1.3 %reshape.480 = bf16[8,4,3,2,2,16,16]{6,5,4,3,0,2,1:T(8,128)(2,1)S(1)} reshape(bf16[8,12,1024]{2,0,1:T(8,128)(2,1)S(1)} %copy.22) | data formatting | bytes 393216 | tf_op jit(solution)/shard_map/reshape | solution.py:89
  48.6 2.7 %copy.23 = bf16[8,4,16,2,2,3,16]{2,1,0,6,5,4,3:T(4,128)(2,1)S(1)} copy(bf16[8,4,16,2,2,3,16]{6,2,4,3,0,5,1:T(8,128)(2,1)S(1)} %bitcast.50) | data formatting | bytes 393216 | tf_op jit(solution)/shard_map/transpose | solution.py:91
  51.3 3.5 %reshape.481 = bf16[512,192]{0,1:T(8,128)(2,1)} reshape(bf16[8,4,16,2,2,3,16]{2,1,0,6,5,4,3:T(4,128)(2,1)S(1)} %copy.23) | data formatting | bytes 393216 | tf_op jit(solution)/shard_map/reshape | solution.py:91
  54.7 1.6 %pad_maximum_fusion.1 = bf16[2,2,2,2,12800]{4,3,2,1,0:T(2,128)(2,1)S(1)} fusion(bf16[1,2,2,2,12800]{4,3,2,1,0:T(2,128)(2,1)} %bitcast.6, bf16[1,2,2,2,12800]{4,3,2,1,0:T(2,128)(2,1)} %fusion.25), kind=kLoop, calls=%fused_computation.10 | loop fusion | flops 204800 | bytes 819200 | tf_op jit(solution)/shard_map/stack | solution.py:13
  56.5 1.6 %fusion.24 = bf16[1,2,2,2,2,12800]{5,4,3,2,1,0:T(2,128)(2,1)S(1)} fusion(bf16[1,2,2,2,12800]{4,3,2,1,0:T(2,128)(2,1)} %bitcast.6, bf16[1,2,2,2,12800]{4,3,2,1,0:T(2,128)(2,1)} %fusion.25), kind=kLoop, calls=%fused_computation.78 | loop fusion | flops 204800 | bytes 819200 | tf_op jit(solution)/shard_map/stack | solution.py:13
  58.2 1.2 %pad_maximum_fusion = bf16[2,2,2,2,2,12800]{5,4,3,2,1,0:T(2,128)(2,1)S(1)} fusion(bf16[1,2,2,2,2,12800]{5,4,3,2,1,0:T(2,128)(2,1)S(1)} %bitcast.56, bf16[1,2,2,2,2,12800]{5,4,3,2,1,0:T(2,128)(2,1)S(1)} %fusion.24), kind=kLoop, calls=%fused_computation.8 | loop fusion | flops 409600 | bytes 1638400 | tf_op jit(solution)/shard_map/stack | solution.py:13
  59.4 0.3 reshape.476
  59.7 0.9 %gather_fusion.1 = bf16[32,8192]{1,0:T(8,128)(2,1)S(1)} fusion(bf16[32,8192]{1,0:T(8,128)(2,1)S(1)} %slice.14, s32[1024]{0:T(1024)S(1)} %pad_clamp_fusion), kind=kCustom, calls=%fused_computation.1 | custom fusion | bytes 1048704 | tf_op jit(solution)/shard_map/jit(_take)/gather | solution.py:41
  60.6 0.2 reshape.477
  60.9 0.3 convolution_convert_fusion
  61.2 0.4 copy.24
  61.6 0.4 bitcast_bitcast_fusion
  62.0 1.4 %reshape.513 = bf16[8,2,6144]{2,1,0:T(2,128)(2,1)} reshape(bf16[512,2,2,48]{3,2,1,0:T(2,128)(2,1)S(1)} %bitcast_bitcast_fusion) | data formatting | bytes 393216
  63.4 3.4 %all-to-all-start.2 = ((bf16[8,2,6144]{2,1,0:T(2,128)(2,1)}), bf16[8,2,6144]{2,1,0:T(2,128)(2,1)S(1)}, u32[]{:S(2)}, u32[]{:S(2)}) async-start(bf16[8,2,6144]{2,1,0:T(2,128)(2,1)} %reshape.513), calls=%async_computation.2 | async-start | bytes 393216 | tf_op jit(solution)/shard_map/all_to_all | solution.py:96
  66.9 0.7 gather_fusion.2
  67.6 0.4 reshape.511
  68.0 5.0 %all-to-all-done.2 = bf16[8,2,6144]{2,1,0:T(2,128)(2,1)S(1)} async-done(((bf16[8,2,6144]{2,1,0:T(2,128)(2,1)}), bf16[8,2,6144]{2,1,0:T(2,128)(2,1)S(1)}, u32[]{:S(2)}, u32[]{:S(2)}) %all-to-all-start.2) | async-done | bytes 196640 | tf_op jit(solution)/shard_map/all_to_all | solution.py:96
  73.0 0.5 reshape.514
  73.5 0.3 copy.32
  73.9 0.4 all_to_all.24
  74.2 1.0 %fusion.1 = bf16[2,2,64,384]{3,2,1,0:T(8,128)(2,1)} fusion(bf16[2,2,64,384]{3,2,1,0:T(8,128)(2,1)S(1)} %all_to_all.24, bf16[384,384,1,1]{1,0,2,3:T(8,128)(2,1)S(1)} %reshape.511, bf16[2,2,64,384]{3,2,1,0:T(8,128)(2,1)S(1)} %copy-done.2), kind=kOutput, calls=%fused_computation.7 | convolution fusion | flops 75792384 | bytes 884736 | tf_op jit(solution)/shard_map/by,mlxy->mlxb/dot_general | solution.py:97
  (45 shorter events, 1.4 us)
Async XLA Ops:
  0.0 5.4 %copy-start = (bf16[128,2,2,256]{3,2,1,0:T(2,128)(2,1)S(1)}, bf16[128,2,2,256]{3,2,1,0:T(2,128)(2,1)}, u32[]{:S(2)}) copy-start(bf16[128,2,2,256]{3,2,1,0:T(2,128)(2,1)} %param.8) | copy-start | bytes 786436
  1.5 24.1 %collective-permute-start = (bf16[12800]{0:T(1024)(128)(2,1)S(1)}, bf16[12800]{0:T(1024)(128)(2,1)S(1)}, u32[]{:S(2)}, u32[]{:S(2)}) collective-permute-start(bf16[12800]{0:T(1024)(128)(2,1)S(1)} %constant_dynamic-update-slice_fusion), channel_id=1, source_target_pairs={{0,8},{8,0},{16,24},{24,16},{1,9},{9,1},{17,25},{25,17},{2,10},{10... | collective-permute-start | bytes 76808 | tf_op jit(solution)/shard_map/ppermute | solution.py:12
  7.6 24.2 %all-to-all-start = ((bf16[8,24,2,2,256]{4,3,2,1,0:T(2,128)(2,1)}), bf16[8,24,2,2,256]{4,3,2,1,0:T(2,128)(2,1)}, u32[]{:S(2)}, u32[]{:S(2)}) async-start(bf16[8,24,2,2,256]{4,3,2,1,0:T(2,128)(2,1)} %bitcast.2), calls=%async_computation | async-start | bytes 786432 | tf_op jit(solution)/shard_map/all_to_all | solution.py:60
  25.8 6.0 %collective-permute-start.1 = (bf16[2,12800]{1,0:T(2,128)(2,1)S(1)}, bf16[2,12800]{1,0:T(2,128)(2,1)S(1)}, u32[]{:S(2)}, u32[]{:S(2)}) collective-permute-start(bf16[2,12800]{1,0:T(2,128)(2,1)S(1)} %pad_maximum_fusion.4), channel_id=1, source_target_pairs={{0,16},{8,24},{16,0},{24,8},{1,17},{9,25},{17,1},{25,9},{2,18},{10... | collective-permute-start | bytes 153608 | tf_op jit(solution)/shard_map/ppermute | solution.py:12
  33.1 7.3 %collective-permute-start.2 = (bf16[2,2,12800]{2,1,0:T(2,128)(2,1)S(1)}, bf16[2,2,12800]{2,1,0:T(2,128)(2,1)S(1)}, u32[]{:S(2)}, u32[]{:S(2)}) collective-permute-start(bf16[2,2,12800]{2,1,0:T(2,128)(2,1)S(1)} %pad_maximum_fusion.3), channel_id=1, source_target_pairs={{0,2},{1,3},{2,0},{3,1},{4,6},{5,7},{6,4},{7,5},{8,10},{9,11},{10,... | collective-permute-start | bytes 307208 | tf_op jit(solution)/shard_map/ppermute | solution.py:12
  36.9 10.3 %all-to-all-start.1 = ((bf16[8,12,1024]{2,1,0:T(8,128)(2,1)}), bf16[8,12,1024]{2,1,0:T(8,128)(2,1)S(1)}, u32[]{:S(2)}, u32[]{:S(2)}) async-start(bf16[8,12,1024]{2,1,0:T(8,128)(2,1)} %reshape.479), calls=%async_computation.1 | async-start | bytes 524288 | tf_op jit(solution)/shard_map/all_to_all | solution.py:82
  41.4 13.3 %collective-permute-start.3 = (bf16[2,2,2,12800]{3,2,1,0:T(2,128)(2,1)}, bf16[2,2,2,12800]{3,2,1,0:T(2,128)(2,1)}, u32[]{:S(2)}, u32[]{:S(2)}) collective-permute-start(bf16[2,2,2,12800]{3,2,1,0:T(2,128)(2,1)} %pad_maximum_fusion.2), channel_id=1, source_target_pairs={{0,4},{1,5},{2,6},{3,7},{4,0},{5,1},{6,2},{7,3},{8,12},{9,13},{10,... | collective-permute-start | bytes 614408 | tf_op jit(solution)/shard_map/ppermute | solution.py:12
  56.4 1.8 %collective-permute-start.4 = (bf16[2,2,2,2,12800]{4,3,2,1,0:T(2,128)(2,1)S(1)}, bf16[2,2,2,2,12800]{4,3,2,1,0:T(2,128)(2,1)S(1)}, u32[]{:S(2)}, u32[]{:S(2)}) collective-permute-start(bf16[2,2,2,2,12800]{4,3,2,1,0:T(2,128)(2,1)S(1)} %pad_maximum_fusion.1), channel_id=1, source_target_pairs={{0,1},{1,0},{2,3},{3,2},{4,5},{5,4},{6,7},{7,6},{8,9},{9,8},{10,11... | collective-permute-start | bytes 1228808 | tf_op jit(solution)/shard_map/ppermute | solution.py:12
  59.7 1.1 %copy-start.1 = (bf16[512,192]{0,1:T(8,128)(2,1)S(1)}, bf16[512,192]{0,1:T(8,128)(2,1)}, u32[]{:S(2)}) copy-start(bf16[512,192]{0,1:T(8,128)(2,1)} %reshape.481) | copy-start | bytes 589828
  63.4 9.6 %all-to-all-start.2 = ((bf16[8,2,6144]{2,1,0:T(2,128)(2,1)}), bf16[8,2,6144]{2,1,0:T(2,128)(2,1)S(1)}, u32[]{:S(2)}, u32[]{:S(2)}) async-start(bf16[8,2,6144]{2,1,0:T(2,128)(2,1)} %reshape.513), calls=%async_computation.2 | async-start | bytes 393216 | tf_op jit(solution)/shard_map/all_to_all | solution.py:96
  66.8 7.4 %copy-start.2 = (bf16[2,2,64,384]{3,2,1,0:T(8,128)(2,1)S(1)}, bf16[2,2,64,384]{3,2,1,0:T(8,128)(2,1)}, u32[]{:S(2)}) copy-start(bf16[2,2,64,384]{3,2,1,0:T(8,128)(2,1)} %param.13) | copy-start | bytes 589828

commit v9 on v6

--- a/solution.py
+++ b/solution.py
@@ -6,19 +6,27 @@
 from jax.sharding import PartitionSpec as P
 
 
-def doubling_gather(data, axis_name, bits):
+def xor_gather(data, axis_name, groups):
     count = lax.axis_size(axis_name)
-    for bit in bits:
-        received = lax.ppermute(data, axis_name, [(j, j ^ bit) for j in range(count)])
-        data = jnp.stack([data, received])
+    for group in groups:
+        parts = [data]
+        for code in range(1, 1 << len(group)):
+            offset = sum(bit for k, bit in enumerate(group) if code >> k & 1)
+            parts.append(lax.ppermute(data, axis_name, [(j, j ^ offset) for j in range(count)]))
+        data = jnp.stack(parts)
     return data
 
 
-def stacked_position(offset, bits):
+def stacked_position(offset, groups):
     position = jnp.zeros_like(offset)
-    for bit in reversed(bits):
-        position = position * 2 + (offset // bit) % 2
+    for group in reversed(groups):
+        digit = sum(((offset // bit) % 2) << k for k, bit in enumerate(group))
+        position = position * (1 << len(group)) + digit
     return position
+
+
+def bit_groups(bits):
+    return [bits[k : k + 2] for k in range(0, len(bits), 2)]
 
 
 def gather_operators(x_operator, y_operator, after):
@@ -28,11 +36,11 @@
     y_rows, y_cols = y_operator.shape
     x_size = x_rows * x_cols
     both = jnp.concatenate([x_operator.reshape(-1), y_operator.reshape(-1)])
-    mem_bits = [1 << k for k in range(mem_count.bit_length() - 1)]
-    tile_bits = [1 << k for k in range(1, tile_count.bit_length() - 1)] + [1]
-    both = doubling_gather(both, "mem", mem_bits)
+    mem_bits = bit_groups([1 << k for k in range(mem_count.bit_length() - 1)])
+    tile_bits = bit_groups([1 << k for k in range(1, tile_count.bit_length() - 1)]) + [[1]]
+    both = xor_gather(both, "mem", mem_bits)
     both, after = lax.optimization_barrier((both, after))
-    both = doubling_gather(both, "tile", tile_bits).reshape(mem_count * tile_count, -1)
+    both = xor_gather(both, "tile", tile_bits).reshape(mem_count * tile_count, -1)
     mem_of = lax.broadcasted_iota(jnp.int32, (mem_count, tile_count), 0)
     tile_of = lax.broadcasted_iota(jnp.int32, (mem_count, tile_count), 1)
     position = stacked_position(tile_of ^ lax.axis_index("tile"), tile_bits) * mem_count

time: 64.2 us -> 61.9 us (0.964)
  waiting for transfers between devices: 15.8 us -> 12.8 us
    ppermute x5 -> x7, waiting for transfers between devices: 7.13 us -> 0.02 us  [xor_gather(): lax.ppermute(data, axis_name, [(j, j ^ offset) for j in range(count)])]
    all_to_all x1, waiting for transfers between devices: 0.01 us -> 4.79 us  [body(): lax.all_to_all(packed, 'tile', split_axis=0, concat_axis=0, tiled=True)]
    all_to_all x1, waiting for transfers between devices: 3.6 us -> 2.95 us  [body(): lax.all_to_all(difference, 'tile', split_axis=3, concat_axis=2, tiled=True)]
    another operation x8 -> x4, other arithmetic: 3.27 us -> 3.54 us  [xor_gather(): data = jnp.stack(parts)]
    ppermute x5 -> x7, starting transfers between devices: 9.47 us -> 9.7 us  [xor_gather(): lax.ppermute(data, axis_name, [(j, j ^ offset) for j in range(count)])]
  transfers between devices with their start and end apart: 8 -> 10, of which waited for: 5 -> 3; matrix products, arithmetic and copies ran while one was open for 19% -> 32% of each run, Pallas kernels for 0% -> 0%
where the time goes in v9:
time: 61.9 us; the launch traced here: 61.2 us
  starting transfers between devices  20.4 us (33%)
  local copies, waits for them, and re-layouts  19 us (31%)
  waiting for transfers between devices  12.8 us (21%)
  other arithmetic  5.56 us (9%)
  matrix products  3.16 us (5%)
    ppermute x7, starting transfers between devices, xor_gather(): lax.ppermute(data, axis_name, [(j, j ^ offset) for j in range(count)])  9.7 us
    all_to_all x1, waiting for transfers between devices, body(): lax.all_to_all(after_first, 'tile', split_axis=2, concat_axis=3, tiled=True)  5.02 us
    all_to_all x1, waiting for transfers between devices, body(): lax.all_to_all(packed, 'tile', split_axis=0, concat_axis=0, tiled=True)  4.79 us
    unnamed x10, local copies, waits for them, and re-layouts  4 us
    all_to_all x1, starting transfers between devices, body(): lax.all_to_all(packed, 'tile', split_axis=0, concat_axis=0, tiled=True)  3.87 us
    another operation x4, other arithmetic, xor_gather(): data = jnp.stack(parts)  3.54 us
    all_to_all x1, starting transfers between devices, body(): lax.all_to_all(difference, 'tile', split_axis=3, concat_axis=2, tiled=True)  3.39 us
    all_to_all x1, starting transfers between devices, body(): lax.all_to_all(after_first, 'tile', split_axis=2, concat_axis=3, tiled=True)  3.39 us
  transfers between devices with their start and end apart: 10, of which 3 were waited for; matrix products, arithmetic and copies ran while one was open for 32% of the time, Pallas kernels for 0%

profile of v9, /device:TPU:0, one launch (start us, length us, event | category | flops | bytes accessed | tf_op | source)
XLA Modules:
  0.0 61.2 jit_solution(10935352648912647601)
XLA Ops:
  0.0 0.8 %copy.28 = bf16[2,4,8,128]{3,1,2,0:T(4,128)(2,1)S(1)} copy(bf16[2,4,8,128]{3,2,1,0:T(8,128)(2,1)} %bitcast.68) | data formatting | bytes 32768
  0.8 0.7 %reshape.471 = bf16[4608]{0:T(1024)(128)(2,1)S(1)} reshape(bf16[12,384]{1,0:T(8,128)(2,1)} %param.15) | data formatting | bytes 18432 | tf_op jit(solution)/shard_map/reshape | solution.py:38
  1.5 5.1 %collective-permute-start.2 = (bf16[12800]{0:T(1024)(128)(2,1)S(1)}, bf16[12800]{0:T(1024)(128)(2,1)S(1)}, u32[]{:S(2)}, u32[]{:S(2)}) collective-permute-start(bf16[12800]{0:T(1024)(128)(2,1)S(1)} %constant_dynamic-update-slice_fusion), channel_id=1, source_target_pairs={{0,24},{8,16},{16,8},{24,0},{1,25},{9,17},{17,9},{25,1},{2,26},{10... | collective-permute-start | bytes 76808 | tf_op jit(solution)/shard_map/ppermute | solution.py:15
  6.6 0.6 %collective-permute-start = (bf16[12800]{0:T(1024)(128)(2,1)S(1)}, bf16[12800]{0:T(1024)(128)(2,1)S(1)}, u32[]{:S(2)}, u32[]{:S(2)}) collective-permute-start(bf16[12800]{0:T(1024)(128)(2,1)S(1)} %constant_dynamic-update-slice_fusion), channel_id=1, source_target_pairs={{0,8},{8,0},{16,24},{24,16},{1,9},{9,1},{17,25},{25,17},{2,10},{10... | collective-permute-start | bytes 76808 | tf_op jit(solution)/shard_map/ppermute | solution.py:15
  7.3 0.8 %reshape.480 = s32[192]{0:T(256)S(1)} reshape(s32[1,8,24]{2,1,0:T(8,128)} %param.9) | data formatting | bytes 1536 | tf_op jit(solution)/shard_map/jit(_take)/broadcast_in_dim | solution.py:65
  8.1 2.3 %gather_fusion = bf16[192,2,2,256]{3,2,1,0:T(2,128)(2,1)} fusion(bf16[128,2,2,256]{3,2,1,0:T(2,128)(2,1)S(1)} %copy-done, s32[1024]{0:T(1024)S(1)} %pad_clamp_fusion.1), kind=kCustom, calls=%fused_computation | custom fusion | bytes 787200 | tf_op jit(solution)/shard_map/jit(_take)/gather | solution.py:65
  10.3 3.9 %all-to-all-start = ((bf16[8,24,2,2,256]{4,3,2,1,0:T(2,128)(2,1)}), bf16[8,24,2,2,256]{4,3,2,1,0:T(2,128)(2,1)S(1)}, u32[]{:S(2)}, u32[]{:S(2)}) async-start(bf16[8,24,2,2,256]{4,3,2,1,0:T(2,128)(2,1)} %bitcast.3), calls=%async_computation | async-start | bytes 786432 | tf_op jit(solution)/shard_map/all_to_all | solution.py:68
  14.3 0.7 %iota_compare_fusion = pred[8,24]{1,0:T(8,128)(4,1)S(1)} fusion(s32[8]{0:T(128)} %bitcast.69), kind=kLoop, calls=%fused_computation.26 | loop fusion | flops 192 | bytes 224 | tf_op jit(solution)/shard_map/lt | solution.py:71
  15.1 0.8 %squeeze.3 = bf16[192]{0:T(256)(128)(2,1)S(1)} reshape(f32[1,8,24]{2,1,0:T(8,128)} %param.11) | data formatting | bytes 1152 | tf_op jit(solution)/shard_map/squeeze | solution.py:72
  16.2 0.1 select_n.131
  16.3 0.1 select_n.128
  16.6 0.8 %eq.21 = s32[192]{0:T(256)S(1)} reshape(s32[1,8,24]{2,1,0:T(8,128)} %param.10) | data formatting | bytes 1536 | tf_op jit(solution)/shard_map/eq | solution.py:73
  17.5 0.2 pad_maximum_fusion.2
  17.7 4.8 %all-to-all-done = bf16[8,24,2,2,256]{4,3,2,1,0:T(2,128)(2,1)S(1)} async-done(((bf16[8,24,2,2,256]{4,3,2,1,0:T(2,128)(2,1)}), bf16[8,24,2,2,256]{4,3,2,1,0:T(2,128)(2,1)S(1)}, u32[]{:S(2)}, u32[]{:S(2)}) %all-to-all-start) | async-done | bytes 393248 | tf_op jit(solution)/shard_map/all_to_all | solution.py:68
  22.5 0.6 collective-permute-start.5
  23.1 1.5 %collective-permute-start.4 = (bf16[4,12800]{1,0:T(4,128)(2,1)S(1)}, bf16[4,12800]{1,0:T(4,128)(2,1)}, u32[]{:S(2)}, u32[]{:S(2)}) collective-permute-start(bf16[4,12800]{1,0:T(4,128)(2,1)S(1)} %pad_maximum_fusion.2), channel_id=1, source_target_pairs={{0,4},{1,5},{2,6},{3,7},{4,0},{5,1},{6,2},{7,3},{8,12},{9,13},{10,... | collective-permute-start | bytes 307208 | tf_op jit(solution)/shard_map/ppermute | solution.py:15
  24.5 1.5 %collective-permute-start.3 = (bf16[4,12800]{1,0:T(4,128)(2,1)S(1)}, bf16[4,12800]{1,0:T(4,128)(2,1)}, u32[]{:S(2)}, u32[]{:S(2)}) collective-permute-start(bf16[4,12800]{1,0:T(4,128)(2,1)S(1)} %pad_maximum_fusion.2), channel_id=1, source_target_pairs={{0,2},{1,3},{2,0},{3,1},{4,6},{5,7},{6,4},{7,5},{8,10},{9,11},{10,... | collective-permute-start | bytes 307208 | tf_op jit(solution)/shard_map/ppermute | solution.py:15
  26.0 0.3 reshape.473
  26.3 0.2 copy.16
  26.5 1.9 %convolution_bitcast_fusion = f32[2,2,4,16,24,16]{4,5,3,1,0,2:T(8,128)} fusion(bf16[2,2,16,16,192,1]{4,3,2,1,0,5:T(8,128)(2,1)S(1)} %bitcast.57, bf16[192]{0:T(256)(128)(2,1)S(1)} %broadcast_select_fusion.3, s32[4,24]{1,0:T(4,128)S(1)} %multiply_add_fusion, s32[192]{0:T(256)S(1)} %eq.21), kind=kOutput, calls=%fused_computation.3 | convolution fusion | flops 37785600 | bytes 787968 | tf_op jit(solution)/shard_map/dot_general | solution.py:77
  28.4 2.2 %copy.17 = f32[2,2,4,16,24,16]{5,4,3,2,1,0:T(8,128)S(1)} copy(f32[2,2,4,16,24,16]{4,5,3,1,0,2:T(8,128)} %convolution_bitcast_fusion) | data formatting | bytes 786432 | tf_op jit(solution)/shard_map/transpose | solution.py:90
  30.6 1.6 %reshape.474 = f32[2,2,64,384]{3,2,1,0:T(8,128)} reshape(f32[2,2,4,16,24,16]{5,4,3,2,1,0:T(8,128)S(1)} %copy.17) | data formatting | bytes 786432 | tf_op jit(solution)/shard_map/reshape | solution.py:90
  32.2 1.1 %fusion.3 = bf16[2,2,64,384]{3,2,1,0:T(8,128)(2,1)S(1)} fusion(f32[2,2,64,384]{3,2,1,0:T(8,128)} %reshape.474, bf16[2,2,64,384]{3,2,1,0:T(8,128)(2,1)} %param.13), kind=kLoop, calls=%fused_computation.13 | loop fusion | flops 294912 | bytes 786432 | tf_op jit(solution)/shard_map/convert_element_type | solution.py:93
  33.3 0.6 copy.18
  33.9 1.0 %reshape.509 = bf16[8,2,6144]{2,1,0:T(2,128)(2,1)} reshape(bf16[384,2,2,64]{3,2,1,0:T(2,128)(2,1)S(1)} %bitcast.61) | data formatting | bytes 393216
  34.9 3.4 %all-to-all-start.1 = ((bf16[8,2,6144]{2,1,0:T(2,128)(2,1)}), bf16[8,2,6144]{2,1,0:T(2,128)(2,1)S(1)}, u32[]{:S(2)}, u32[]{:S(2)}) async-start(bf16[8,2,6144]{2,1,0:T(2,128)(2,1)} %reshape.509), calls=%async_computation.1 | async-start | bytes 393216 | tf_op jit(solution)/shard_map/all_to_all | solution.py:94
  38.3 1.4 %pad_maximum_fusion.1 = bf16[4,4,12800]{2,1,0:T(4,128)(2,1)S(1)} fusion(bf16[1,4,12800]{2,1,0:T(4,128)(2,1)} %bitcast.14, bf16[1,4,12800]{2,1,0:T(4,128)(2,1)} %bitcast.13, bf16[1,4,12800]{2,1,0:T(4,128)(2,1)} %bitcast.12, bf16[1,4,12800]{2,1,0:T(4,128)(2,1)S(1)} %bitcast.64), kind=kLoop, calls=%fused_computation.12 | loop fusion | flops 614400 | bytes 819200 | tf_op jit(solution)/shard_map/stack | solution.py:16
  39.7 0.5 collective-permute-start.6
  40.2 1.4 %fusion.31 = bf16[1,4,4,12800]{3,2,1,0:T(4,128)(2,1)S(1)} fusion(bf16[1,4,12800]{2,1,0:T(4,128)(2,1)} %bitcast.14, bf16[1,4,12800]{2,1,0:T(4,128)(2,1)} %bitcast.13, bf16[1,4,12800]{2,1,0:T(4,128)(2,1)} %bitcast.12, bf16[1,4,12800]{2,1,0:T(4,128)(2,1)S(1)} %bitcast.65), kind=kLoop, calls=%fused_computation.82 | loop fusion | flops 614400 | bytes 819200 | tf_op jit(solution)/shard_map/stack | solution.py:16
  41.5 3.0 %all-to-all-done.1 = bf16[8,2,6144]{2,1,0:T(2,128)(2,1)S(1)} async-done(((bf16[8,2,6144]{2,1,0:T(2,128)(2,1)}), bf16[8,2,6144]{2,1,0:T(2,128)(2,1)S(1)}, u32[]{:S(2)}, u32[]{:S(2)}) %all-to-all-start.1) | async-done | bytes 196640 | tf_op jit(solution)/shard_map/all_to_all | solution.py:94
  44.5 0.3 reshape.510
  44.8 0.3 copy.32
  45.0 0.3 all_to_all.33
  45.3 0.6 pad_maximum_fusion
  45.9 0.2 reshape.475
  46.1 0.9 %gather_fusion.1 = bf16[32,8192]{1,0:T(8,128)(2,1)S(1)} fusion(bf16[32,8192]{1,0:T(8,128)(2,1)S(1)} %slice.14, s32[1024]{0:T(1024)S(1)} %pad_clamp_fusion), kind=kCustom, calls=%fused_computation.1 | custom fusion | bytes 1048704 | tf_op jit(solution)/shard_map/jit(_take)/gather | solution.py:49
  47.0 0.2 reshape.505
  47.3 0.3 fusion.1
  47.6 0.4 copy.21
  48.0 1.4 %reshape.511 = bf16[8,2,6144]{2,1,0:T(2,128)(2,1)} reshape(bf16[512,2,2,48]{3,2,1,0:T(2,128)(2,1)S(1)} %bitcast.58) | data formatting | bytes 393216
  49.4 3.4 %all-to-all-start.2 = ((bf16[8,2,6144]{2,1,0:T(2,128)(2,1)}), bf16[8,2,6144]{2,1,0:T(2,128)(2,1)S(1)}, u32[]{:S(2)}, u32[]{:S(2)}) async-start(bf16[8,2,6144]{2,1,0:T(2,128)(2,1)} %reshape.511), calls=%async_computation.2 | async-start | bytes 393216 | tf_op jit(solution)/shard_map/all_to_all | solution.py:101
  52.9 0.7 %gather_fusion.2 = bf16[32,4608]{1,0:T(8,128)(2,1)S(1)} fusion(bf16[32,4608]{1,0:T(8,128)(2,1)S(1)} %slice.15, s32[1024]{0:T(1024)S(1)} %pad_clamp_fusion), kind=kCustom, calls=%fused_computation.2 | custom fusion | bytes 589952 | tf_op jit(solution)/shard_map/jit(_take)/gather | solution.py:50
  53.6 0.4 reshape.506
  54.0 5.0 %all-to-all-done.2 = bf16[8,2,6144]{2,1,0:T(2,128)(2,1)S(1)} async-done(((bf16[8,2,6144]{2,1,0:T(2,128)(2,1)}), bf16[8,2,6144]{2,1,0:T(2,128)(2,1)S(1)}, u32[]{:S(2)}, u32[]{:S(2)}) %all-to-all-start.2) | async-done | bytes 196640 | tf_op jit(solution)/shard_map/all_to_all | solution.py:101
  59.0 0.5 reshape.512
  59.5 0.3 copy.31
  59.9 0.4 all_to_all.37
  60.3 1.0 %fusion = bf16[2,2,64,384]{3,2,1,0:T(8,128)(2,1)} fusion(bf16[2,2,64,384]{3,2,1,0:T(8,128)(2,1)S(1)} %all_to_all.37, bf16[2,2,64,384]{3,2,1,0:T(8,128)(2,1)S(1)} %copy-done.1, bf16[384,384,1,1]{1,0,2,3:T(8,128)(2,1)S(1)} %reshape.506), kind=kOutput, calls=%fused_computation.6 | convolution fusion | flops 75792384 | bytes 884736 | tf_op jit(solution)/shard_map/by,mlxy->mlxb/dot_general | solution.py:102
  (41 shorter events, 0.8 us)
Async XLA Ops:
  0.0 8.1 %copy-start = (bf16[128,2,2,256]{3,2,1,0:T(2,128)(2,1)S(1)}, bf16[128,2,2,256]{3,2,1,0:T(2,128)(2,1)}, u32[]{:S(2)}) copy-start(bf16[128,2,2,256]{3,2,1,0:T(2,128)(2,1)} %param.8) | copy-start | bytes 786436
  1.5 15.8 %collective-permute-start.2 = (bf16[12800]{0:T(1024)(128)(2,1)S(1)}, bf16[12800]{0:T(1024)(128)(2,1)S(1)}, u32[]{:S(2)}, u32[]{:S(2)}) collective-permute-start(bf16[12800]{0:T(1024)(128)(2,1)S(1)} %constant_dynamic-update-slice_fusion), channel_id=1, source_target_pairs={{0,24},{8,16},{16,8},{24,0},{1,25},{9,17},{17,9},{25,1},{2,26},{10... | collective-permute-start | bytes 76808 | tf_op jit(solution)/shard_map/ppermute | solution.py:15
  6.6 10.7 %collective-permute-start.1 = (bf16[12800]{0:T(1024)(128)(2,1)S(1)}, bf16[12800]{0:T(1024)(128)(2,1)S(1)}, u32[]{:S(2)}, u32[]{:S(2)}) collective-permute-start(bf16[12800]{0:T(1024)(128)(2,1)S(1)} %constant_dynamic-update-slice_fusion), channel_id=1, source_target_pairs={{0,16},{8,24},{16,0},{24,8},{1,17},{9,25},{17,1},{25,9},{2,18},{10... | collective-permute-start | bytes 76808 | tf_op jit(solution)/shard_map/ppermute | solution.py:15
  6.6 10.8 %collective-permute-start = (bf16[12800]{0:T(1024)(128)(2,1)S(1)}, bf16[12800]{0:T(1024)(128)(2,1)S(1)}, u32[]{:S(2)}, u32[]{:S(2)}) collective-permute-start(bf16[12800]{0:T(1024)(128)(2,1)S(1)} %constant_dynamic-update-slice_fusion), channel_id=1, source_target_pairs={{0,8},{8,0},{16,24},{24,16},{1,9},{9,1},{17,25},{25,17},{2,10},{10... | collective-permute-start | bytes 76808 | tf_op jit(solution)/shard_map/ppermute | solution.py:15
  10.3 12.2 %all-to-all-start = ((bf16[8,24,2,2,256]{4,3,2,1,0:T(2,128)(2,1)}), bf16[8,24,2,2,256]{4,3,2,1,0:T(2,128)(2,1)S(1)}, u32[]{:S(2)}, u32[]{:S(2)}) async-start(bf16[8,24,2,2,256]{4,3,2,1,0:T(2,128)(2,1)} %bitcast.3), calls=%async_computation | async-start | bytes 786432 | tf_op jit(solution)/shard_map/all_to_all | solution.py:68
  22.5 15.8 %collective-permute-start.5 = (bf16[4,12800]{1,0:T(4,128)(2,1)S(1)}, bf16[4,12800]{1,0:T(4,128)(2,1)}, u32[]{:S(2)}, u32[]{:S(2)}) collective-permute-start(bf16[4,12800]{1,0:T(4,128)(2,1)S(1)} %pad_maximum_fusion.2), channel_id=1, source_target_pairs={{0,6},{1,7},{2,4},{3,5},{4,2},{5,3},{6,0},{7,1},{8,14},{9,15},{10,... | collective-permute-start | bytes 307208 | tf_op jit(solution)/shard_map/ppermute | solution.py:15
  23.1 15.2 %collective-permute-start.4 = (bf16[4,12800]{1,0:T(4,128)(2,1)S(1)}, bf16[4,12800]{1,0:T(4,128)(2,1)}, u32[]{:S(2)}, u32[]{:S(2)}) collective-permute-start(bf16[4,12800]{1,0:T(4,128)(2,1)S(1)} %pad_maximum_fusion.2), channel_id=1, source_target_pairs={{0,4},{1,5},{2,6},{3,7},{4,0},{5,1},{6,2},{7,3},{8,12},{9,13},{10,... | collective-permute-start | bytes 307208 | tf_op jit(solution)/shard_map/ppermute | solution.py:15
  24.5 13.8 %collective-permute-start.3 = (bf16[4,12800]{1,0:T(4,128)(2,1)S(1)}, bf16[4,12800]{1,0:T(4,128)(2,1)}, u32[]{:S(2)}, u32[]{:S(2)}) collective-permute-start(bf16[4,12800]{1,0:T(4,128)(2,1)S(1)} %pad_maximum_fusion.2), channel_id=1, source_target_pairs={{0,2},{1,3},{2,0},{3,1},{4,6},{5,7},{6,4},{7,5},{8,10},{9,11},{10,... | collective-permute-start | bytes 307208 | tf_op jit(solution)/shard_map/ppermute | solution.py:15
  34.9 9.6 %all-to-all-start.1 = ((bf16[8,2,6144]{2,1,0:T(2,128)(2,1)}), bf16[8,2,6144]{2,1,0:T(2,128)(2,1)S(1)}, u32[]{:S(2)}, u32[]{:S(2)}) async-start(bf16[8,2,6144]{2,1,0:T(2,128)(2,1)} %reshape.509), calls=%async_computation.1 | async-start | bytes 393216 | tf_op jit(solution)/shard_map/all_to_all | solution.py:94
  39.7 5.6 %collective-permute-start.6 = (bf16[4,4,12800]{2,1,0:T(4,128)(2,1)S(1)}, bf16[4,4,12800]{2,1,0:T(4,128)(2,1)S(1)}, u32[]{:S(2)}, u32[]{:S(2)}) collective-permute-start(bf16[4,4,12800]{2,1,0:T(4,128)(2,1)S(1)} %pad_maximum_fusion.1), channel_id=1, source_target_pairs={{0,1},{1,0},{2,3},{3,2},{4,5},{5,4},{6,7},{7,6},{8,9},{9,8},{10,11... | collective-permute-start | bytes 1228808 | tf_op jit(solution)/shard_map/ppermute | solution.py:15
  49.4 9.6 %all-to-all-start.2 = ((bf16[8,2,6144]{2,1,0:T(2,128)(2,1)}), bf16[8,2,6144]{2,1,0:T(2,128)(2,1)S(1)}, u32[]{:S(2)}, u32[]{:S(2)}) async-start(bf16[8,2,6144]{2,1,0:T(2,128)(2,1)} %reshape.511), calls=%async_computation.2 | async-start | bytes 393216 | tf_op jit(solution)/shard_map/all_to_all | solution.py:101
  53.6 6.7 %copy-start.1 = (bf16[2,2,64,384]{3,2,1,0:T(8,128)(2,1)S(1)}, bf16[2,2,64,384]{3,2,1,0:T(8,128)(2,1)}, u32[]{:S(2)}) copy-start(bf16[2,2,64,384]{3,2,1,0:T(8,128)(2,1)} %param.13) | copy-start | bytes 589828

commit v10 on v9

--- a/solution.py
+++ b/solution.py
@@ -38,8 +38,8 @@
     both = jnp.concatenate([x_operator.reshape(-1), y_operator.reshape(-1)])
     mem_bits = bit_groups([1 << k for k in range(mem_count.bit_length() - 1)])
     tile_bits = bit_groups([1 << k for k in range(1, tile_count.bit_length() - 1)]) + [[1]]
+    both, after = lax.optimization_barrier((both, after))
     both = xor_gather(both, "mem", mem_bits)
-    both, after = lax.optimization_barrier((both, after))
     both = xor_gather(both, "tile", tile_bits).reshape(mem_count * tile_count, -1)
     mem_of = lax.broadcasted_iota(jnp.int32, (mem_count, tile_count), 0)
     tile_of = lax.broadcasted_iota(jnp.int32, (mem_count, tile_count), 1)
@@ -65,8 +65,8 @@
     packed = jnp.take(source_blocks, picked, axis=0, mode="clip").reshape(
         tile_count, capacity, member_count, level_count, block_cells
     )
+    x_full, y_full, packed = gather_operators(x_operator, y_operator, packed)
     arrived = lax.all_to_all(packed, "tile", split_axis=0, concat_axis=0, tiled=True)
-    x_full, y_full, arrived = gather_operators(x_operator, y_operator, arrived)
     slot_count = columns // block_side * (y_cells // block_side)
     live_mask = lax.broadcasted_iota(jnp.int32, (tile_count, capacity), 1) < recv_count[0][:, None]
     weights = jnp.where(live_mask, recv_weight[0], 0.0).reshape(-1)

time: 61.9 us -> 65 us (1.050)
  waiting for transfers between devices: 12.8 us -> 16.1 us
    ppermute x7, waiting for transfers between devices: 0.02 us -> 5.31 us  [xor_gather(): lax.ppermute(data, axis_name, [(j, j ^ offset) for j in range(count)])]
    all_to_all x1, waiting for transfers between devices: 4.79 us -> 0.01 us  [body(): lax.all_to_all(packed, 'tile', split_axis=0, concat_axis=0, tiled=True)]
    all_to_all x1, waiting for transfers between devices: 2.95 us -> 5.76 us  [body(): lax.all_to_all(difference, 'tile', split_axis=3, concat_axis=2, tiled=True)]
    another operation x4 -> x5, other arithmetic: 3.54 us -> 3.6 us  [xor_gather(): data = jnp.stack(parts)]
    unnamed x10 -> x21, local copies, waits for them, and re-layouts: 4 us -> 3.98 us
  transfers between devices with their start and end apart: 10 -> 10, of which waited for: 3 -> 4; matrix products, arithmetic and copies ran while one was open for 32% -> 24% of each run, Pallas kernels for 0% -> 0%
where the time goes in v10:
time: 65 us; the launch traced here: 64.3 us
  starting transfers between devices  20 us (31%)
  local copies, waits for them, and re-layouts  19 us (29%)
  waiting for transfers between devices  16.1 us (25%)
  other arithmetic  5.68 us (9%)
  matrix products  3.15 us (5%)
    ppermute x7, starting transfers between devices, xor_gather(): lax.ppermute(data, axis_name, [(j, j ^ offset) for j in range(count)])  9.31 us
    all_to_all x1, waiting for transfers between devices, body(): lax.all_to_all(difference, 'tile', split_axis=3, concat_axis=2, tiled=True)  5.76 us
    ppermute x7, waiting for transfers between devices, xor_gather(): lax.ppermute(data, axis_name, [(j, j ^ offset) for j in range(count)])  5.31 us
    all_to_all x1, waiting for transfers between devices, body(): lax.all_to_all(after_first, 'tile', split_axis=2, concat_axis=3, tiled=True)  5.02 us
    unnamed x21, local copies, waits for them, and re-layouts  3.98 us
    all_to_all x1, starting transfers between devices, body(): lax.all_to_all(packed, 'tile', split_axis=0, concat_axis=0, tiled=True)  3.94 us
    another operation x5, other arithmetic, xor_gather(): data = jnp.stack(parts)  3.6 us
    all_to_all x1, starting transfers between devices, body(): lax.all_to_all(difference, 'tile', split_axis=3, concat_axis=2, tiled=True)  3.39 us
  transfers between devices with their start and end apart: 10, of which 4 were waited for; matrix products, arithmetic and copies ran while one was open for 24% of the time, Pallas kernels for 0%

profile of v10, /device:TPU:0, one launch (start us, length us, event | category | flops | bytes accessed | tf_op | source)
XLA Modules:
  0.0 64.3 jit_solution(11121373186460434185)
XLA Ops:
  0.0 0.8 %reshape.471 = bf16[4608]{0:T(1024)(128)(2,1)S(1)} reshape(bf16[12,384]{1,0:T(8,128)(2,1)} %param.15) | data formatting | bytes 18432 | tf_op jit(solution)/shard_map/reshape | solution.py:38
  0.8 0.7 %copy.28 = bf16[2,4,8,128]{3,1,2,0:T(4,128)(2,1)S(1)} copy(bf16[2,4,8,128]{3,2,1,0:T(8,128)(2,1)} %bitcast.72) | data formatting | bytes 32768
  1.5 0.8 %reshape.480 = s32[192]{0:T(256)S(1)} reshape(s32[1,8,24]{2,1,0:T(8,128)} %param.9) | data formatting | bytes 1536 | tf_op jit(solution)/shard_map/jit(_take)/broadcast_in_dim | solution.py:65
  2.3 2.3 %gather_fusion = bf16[192,2,2,256]{3,2,1,0:T(2,128)(2,1)} fusion(bf16[128,2,2,256]{3,2,1,0:T(2,128)(2,1)S(1)} %copy-done, s32[1024]{0:T(1024)S(1)} %pad_clamp_fusion.1), kind=kCustom, calls=%fused_computation | custom fusion | bytes 787200 | tf_op jit(solution)/shard_map/jit(_take)/gather | solution.py:65
  4.5 5.0 %collective-permute-start.2 = (bf16[12800]{0:T(1024)(128)(2,1)S(1)}, bf16[12800]{0:T(1024)(128)(2,1)S(1)}, u32[]{:S(2)}, u32[]{:S(2)}) collective-permute-start(bf16[12800]{0:T(1024)(128)(2,1)S(1)} %pad_maximum_fusion.3), channel_id=1, source_target_pairs={{0,24},{8,16},{16,8},{24,0},{1,25},{9,17},{17,9},{25,1},{2,26},{10... | collective-permute-start | bytes 76808 | tf_op jit(solution)/shard_map/ppermute | solution.py:15
  9.6 0.6 collective-permute-start
  10.2 3.9 %all-to-all-start = ((bf16[8,24,2,2,256]{4,3,2,1,0:T(2,128)(2,1)}), bf16[8,24,2,2,256]{4,3,2,1,0:T(2,128)(2,1)S(1)}, u32[]{:S(2)}, u32[]{:S(2)}) async-start(bf16[8,24,2,2,256]{4,3,2,1,0:T(2,128)(2,1)} %bitcast.3), calls=%async_computation | async-start | bytes 786432 | tf_op jit(solution)/shard_map/all_to_all | solution.py:69
  14.2 0.7 %iota_compare_fusion = pred[8,24]{1,0:T(8,128)(4,1)S(1)} fusion(s32[8]{0:T(128)} %bitcast.73), kind=kLoop, calls=%fused_computation.26 | loop fusion | flops 192 | bytes 224 | tf_op jit(solution)/shard_map/lt | solution.py:71
  15.0 0.8 %squeeze.3 = bf16[192]{0:T(256)(128)(2,1)S(1)} reshape(f32[1,8,24]{2,1,0:T(8,128)} %param.11) | data formatting | bytes 1152 | tf_op jit(solution)/shard_map/squeeze | solution.py:72
  16.1 0.1 select_n.131
  16.2 0.1 select_n.128
  16.5 0.8 %eq.21 = s32[192]{0:T(256)S(1)} reshape(s32[1,8,24]{2,1,0:T(8,128)} %param.10) | data formatting | bytes 1536 | tf_op jit(solution)/shard_map/eq | solution.py:73
  17.4 0.2 pad_maximum_fusion.2
  17.7 3.0 %collective-permute-start.5 = (bf16[4,12800]{1,0:T(4,128)(2,1)S(1)}, bf16[4,12800]{1,0:T(4,128)(2,1)S(1)}, u32[]{:S(2)}, u32[]{:S(2)}) collective-permute-start(bf16[4,12800]{1,0:T(4,128)(2,1)S(1)} %pad_maximum_fusion.2), channel_id=1, source_target_pairs={{0,6},{1,7},{2,4},{3,5},{4,2},{5,3},{6,0},{7,1},{8,14},{9,15},{10,... | collective-permute-start | bytes 307208 | tf_op jit(solution)/shard_map/ppermute | solution.py:15
  20.6 0.6 collective-permute-start.4
  21.3 0.2 fusion.32
  21.5 3.4 %collective-permute-done.5 = bf16[4,12800]{1,0:T(4,128)(2,1)S(1)} collective-permute-done((bf16[4,12800]{1,0:T(4,128)(2,1)S(1)}, bf16[4,12800]{1,0:T(4,128)(2,1)S(1)}, u32[]{:S(2)}, u32[]{:S(2)}) %collective-permute-start.5) | collective-permute-done | bytes 102432 | tf_op jit(solution)/shard_map/ppermute | solution.py:15
  24.9 1.9 %collective-permute-done.4 = bf16[4,12800]{1,0:T(4,128)(2,1)S(1)} collective-permute-done((bf16[4,12800]{1,0:T(4,128)(2,1)S(1)}, bf16[4,12800]{1,0:T(4,128)(2,1)S(1)}, u32[]{:S(2)}, u32[]{:S(2)}) %collective-permute-start.4) | collective-permute-done | bytes 102432 | tf_op jit(solution)/shard_map/ppermute | solution.py:15
  26.8 1.1 %pad_maximum_fusion.1 = bf16[4,4,12800]{2,1,0:T(4,128)(2,1)} fusion(bf16[1,4,12800]{2,1,0:T(4,128)(2,1)S(1)} %bitcast.65, bf16[1,4,12800]{2,1,0:T(4,128)(2,1)S(1)} %bitcast.67, bf16[1,4,12800]{2,1,0:T(4,128)(2,1)S(1)} %bitcast.69, bf16[1,4,12800]{2,1,0:T(4,128)(2,1)S(1)} %fusion.32), kind=kLoop, calls=%fused_computation.12 | loop fusion | flops 614400 | bytes 819200 | tf_op jit(solution)/shard_map/stack | solution.py:16
  28.0 0.3 reshape.473
  28.3 0.2 copy.16
  28.5 1.9 %convolution_bitcast_fusion = f32[2,2,4,16,24,16]{4,5,3,1,0,2:T(8,128)} fusion(bf16[2,2,16,16,192,1]{4,3,2,1,0,5:T(8,128)(2,1)S(1)} %bitcast.57, bf16[192]{0:T(256)(128)(2,1)S(1)} %broadcast_select_fusion.3, s32[4,24]{1,0:T(4,128)S(1)} %multiply_add_fusion, s32[192]{0:T(256)S(1)} %eq.21), kind=kOutput, calls=%fused_computation.3 | convolution fusion | flops 37785600 | bytes 787968 | tf_op jit(solution)/shard_map/dot_general | solution.py:77
  30.4 2.2 %copy.17 = f32[2,2,4,16,24,16]{5,4,3,2,1,0:T(8,128)S(1)} copy(f32[2,2,4,16,24,16]{4,5,3,1,0,2:T(8,128)} %convolution_bitcast_fusion) | data formatting | bytes 786432 | tf_op jit(solution)/shard_map/transpose | solution.py:90
  32.6 1.6 %reshape.474 = f32[2,2,64,384]{3,2,1,0:T(8,128)} reshape(f32[2,2,4,16,24,16]{5,4,3,2,1,0:T(8,128)S(1)} %copy.17) | data formatting | bytes 786432 | tf_op jit(solution)/shard_map/reshape | solution.py:90
  34.3 1.1 %fusion.3 = bf16[2,2,64,384]{3,2,1,0:T(8,128)(2,1)S(1)} fusion(f32[2,2,64,384]{3,2,1,0:T(8,128)} %reshape.474, bf16[2,2,64,384]{3,2,1,0:T(8,128)(2,1)} %param.13), kind=kLoop, calls=%fused_computation.13 | loop fusion | flops 294912 | bytes 786432 | tf_op jit(solution)/shard_map/convert_element_type | solution.py:93
  35.4 0.6 copy.18
  36.0 1.0 %reshape.509 = bf16[8,2,6144]{2,1,0:T(2,128)(2,1)} reshape(bf16[384,2,2,64]{3,2,1,0:T(2,128)(2,1)S(1)} %bitcast.62) | data formatting | bytes 393216
  37.0 3.4 %all-to-all-start.1 = ((bf16[8,2,6144]{2,1,0:T(2,128)(2,1)}), bf16[8,2,6144]{2,1,0:T(2,128)(2,1)S(1)}, u32[]{:S(2)}, u32[]{:S(2)}) async-start(bf16[8,2,6144]{2,1,0:T(2,128)(2,1)} %reshape.509), calls=%async_computation.1 | async-start | bytes 393216 | tf_op jit(solution)/shard_map/all_to_all | solution.py:94
  40.4 0.4 fusion.31
  40.8 5.8 %all-to-all-done.1 = bf16[8,2,6144]{2,1,0:T(2,128)(2,1)S(1)} async-done(((bf16[8,2,6144]{2,1,0:T(2,128)(2,1)}), bf16[8,2,6144]{2,1,0:T(2,128)(2,1)S(1)}, u32[]{:S(2)}, u32[]{:S(2)}) %all-to-all-start.1) | async-done | bytes 196640 | tf_op jit(solution)/shard_map/all_to_all | solution.py:94
  46.6 0.3 reshape.510
  46.8 0.3 copy.32
  47.1 0.3 all_to_all.33
  47.4 1.6 %pad_maximum_fusion = bf16[2,4,4,12800]{3,2,1,0:T(4,128)(2,1)S(1)} fusion(bf16[1,4,4,12800]{3,2,1,0:T(4,128)(2,1)} %bitcast.16, bf16[1,4,4,12800]{3,2,1,0:T(4,128)(2,1)S(1)} %fusion.31), kind=kLoop, calls=%fused_computation.8 | loop fusion | flops 409600 | bytes 1638400 | tf_op jit(solution)/shard_map/stack | solution.py:16
  49.0 0.2 reshape.475
  49.2 0.9 %gather_fusion.1 = bf16[32,8192]{1,0:T(8,128)(2,1)S(1)} fusion(bf16[32,8192]{1,0:T(8,128)(2,1)S(1)} %slice.14, s32[1024]{0:T(1024)S(1)} %pad_clamp_fusion), kind=kCustom, calls=%fused_computation.1 | custom fusion | bytes 1048704 | tf_op jit(solution)/shard_map/jit(_take)/gather | solution.py:49
  50.1 0.2 reshape.505
  50.4 0.3 fusion.1
  50.7 0.4 copy.21
  51.1 1.4 %reshape.511 = bf16[8,2,6144]{2,1,0:T(2,128)(2,1)} reshape(bf16[512,2,2,48]{3,2,1,0:T(2,128)(2,1)S(1)} %bitcast.58) | data formatting | bytes 393216
  52.5 3.4 %all-to-all-start.2 = ((bf16[8,2,6144]{2,1,0:T(2,128)(2,1)}), bf16[8,2,6144]{2,1,0:T(2,128)(2,1)S(1)}, u32[]{:S(2)}, u32[]{:S(2)}) async-start(bf16[8,2,6144]{2,1,0:T(2,128)(2,1)} %reshape.511), calls=%async_computation.2 | async-start | bytes 393216 | tf_op jit(solution)/shard_map/all_to_all | solution.py:101
  56.0 0.7 %gather_fusion.2 = bf16[32,4608]{1,0:T(8,128)(2,1)S(1)} fusion(bf16[32,4608]{1,0:T(8,128)(2,1)S(1)} %slice.15, s32[1024]{0:T(1024)S(1)} %pad_clamp_fusion), kind=kCustom, calls=%fused_computation.2 | custom fusion | bytes 589952 | tf_op jit(solution)/shard_map/jit(_take)/gather | solution.py:50
  56.7 0.4 reshape.506
  57.1 5.0 %all-to-all-done.2 = bf16[8,2,6144]{2,1,0:T(2,128)(2,1)S(1)} async-done(((bf16[8,2,6144]{2,1,0:T(2,128)(2,1)}), bf16[8,2,6144]{2,1,0:T(2,128)(2,1)S(1)}, u32[]{:S(2)}, u32[]{:S(2)}) %all-to-all-start.2) | async-done | bytes 196640 | tf_op jit(solution)/shard_map/all_to_all | solution.py:101
  62.1 0.5 reshape.512
  62.6 0.3 copy.31
  63.0 0.4 all_to_all.37
  63.4 1.0 %fusion = bf16[2,2,64,384]{3,2,1,0:T(8,128)(2,1)} fusion(bf16[2,2,64,384]{3,2,1,0:T(8,128)(2,1)S(1)} %all_to_all.37, bf16[2,2,64,384]{3,2,1,0:T(8,128)(2,1)S(1)} %copy-done.1, bf16[384,384,1,1]{1,0,2,3:T(8,128)(2,1)S(1)} %reshape.506), kind=kOutput, calls=%fused_computation.6 | convolution fusion | flops 75792384 | bytes 884736 | tf_op jit(solution)/shard_map/by,mlxy->mlxb/dot_general | solution.py:102
  (53 shorter events, 1.0 us)
Async XLA Ops:
  0.0 2.3 %copy-start = (bf16[128,2,2,256]{3,2,1,0:T(2,128)(2,1)S(1)}, bf16[128,2,2,256]{3,2,1,0:T(2,128)(2,1)}, u32[]{:S(2)}) copy-start(bf16[128,2,2,256]{3,2,1,0:T(2,128)(2,1)} %param.8) | copy-start | bytes 786436
  4.5 12.7 %collective-permute-start.2 = (bf16[12800]{0:T(1024)(128)(2,1)S(1)}, bf16[12800]{0:T(1024)(128)(2,1)S(1)}, u32[]{:S(2)}, u32[]{:S(2)}) collective-permute-start(bf16[12800]{0:T(1024)(128)(2,1)S(1)} %pad_maximum_fusion.3), channel_id=1, source_target_pairs={{0,24},{8,16},{16,8},{24,0},{1,25},{9,17},{17,9},{25,1},{2,26},{10... | collective-permute-start | bytes 76808 | tf_op jit(solution)/shard_map/ppermute | solution.py:15
  9.6 7.7 %collective-permute-start.1 = (bf16[12800]{0:T(1024)(128)(2,1)S(1)}, bf16[12800]{0:T(1024)(128)(2,1)S(1)}, u32[]{:S(2)}, u32[]{:S(2)}) collective-permute-start(bf16[12800]{0:T(1024)(128)(2,1)S(1)} %pad_maximum_fusion.3), channel_id=1, source_target_pairs={{0,16},{8,24},{16,0},{24,8},{1,17},{9,25},{17,1},{25,9},{2,18},{10... | collective-permute-start | bytes 76808 | tf_op jit(solution)/shard_map/ppermute | solution.py:15
  9.6 7.8 %collective-permute-start = (bf16[12800]{0:T(1024)(128)(2,1)S(1)}, bf16[12800]{0:T(1024)(128)(2,1)S(1)}, u32[]{:S(2)}, u32[]{:S(2)}) collective-permute-start(bf16[12800]{0:T(1024)(128)(2,1)S(1)} %pad_maximum_fusion.3), channel_id=1, source_target_pairs={{0,8},{8,0},{16,24},{24,16},{1,9},{9,1},{17,25},{25,17},{2,10},{10... | collective-permute-start | bytes 76808 | tf_op jit(solution)/shard_map/ppermute | solution.py:15
  10.2 17.9 %all-to-all-start = ((bf16[8,24,2,2,256]{4,3,2,1,0:T(2,128)(2,1)}), bf16[8,24,2,2,256]{4,3,2,1,0:T(2,128)(2,1)S(1)}, u32[]{:S(2)}, u32[]{:S(2)}) async-start(bf16[8,24,2,2,256]{4,3,2,1,0:T(2,128)(2,1)} %bitcast.3), calls=%async_computation | async-start | bytes 786432 | tf_op jit(solution)/shard_map/all_to_all | solution.py:69
  17.7 7.3 %collective-permute-start.5 = (bf16[4,12800]{1,0:T(4,128)(2,1)S(1)}, bf16[4,12800]{1,0:T(4,128)(2,1)S(1)}, u32[]{:S(2)}, u32[]{:S(2)}) collective-permute-start(bf16[4,12800]{1,0:T(4,128)(2,1)S(1)} %pad_maximum_fusion.2), channel_id=1, source_target_pairs={{0,6},{1,7},{2,4},{3,5},{4,2},{5,3},{6,0},{7,1},{8,14},{9,15},{10,... | collective-permute-start | bytes 307208 | tf_op jit(solution)/shard_map/ppermute | solution.py:15
  20.6 6.2 %collective-permute-start.4 = (bf16[4,12800]{1,0:T(4,128)(2,1)S(1)}, bf16[4,12800]{1,0:T(4,128)(2,1)S(1)}, u32[]{:S(2)}, u32[]{:S(2)}) collective-permute-start(bf16[4,12800]{1,0:T(4,128)(2,1)S(1)} %pad_maximum_fusion.2), channel_id=1, source_target_pairs={{0,4},{1,5},{2,6},{3,7},{4,0},{5,1},{6,2},{7,3},{8,12},{9,13},{10,... | collective-permute-start | bytes 307208 | tf_op jit(solution)/shard_map/ppermute | solution.py:15
  21.2 5.6 %collective-permute-start.3 = (bf16[4,12800]{1,0:T(4,128)(2,1)S(1)}, bf16[4,12800]{1,0:T(4,128)(2,1)S(1)}, u32[]{:S(2)}, u32[]{:S(2)}) collective-permute-start(bf16[4,12800]{1,0:T(4,128)(2,1)S(1)} %pad_maximum_fusion.2), channel_id=1, source_target_pairs={{0,2},{1,3},{2,0},{3,1},{4,6},{5,7},{6,4},{7,5},{8,10},{9,11},{10,... | collective-permute-start | bytes 307208 | tf_op jit(solution)/shard_map/ppermute | solution.py:15
  24.9 3.1 %copy-start.2 = (bf16[4,12800]{1,0:T(4,128)(2,1)}, bf16[4,12800]{1,0:T(4,128)(2,1)S(1)}, u32[]{:S(2)}) copy-start(bf16[4,12800]{1,0:T(4,128)(2,1)S(1)} %collective-permute-done.5) | copy-start | bytes 307204
  26.8 1.2 %copy-start.4 = (bf16[4,12800]{1,0:T(4,128)(2,1)}, bf16[4,12800]{1,0:T(4,128)(2,1)S(1)}, u32[]{:S(2)}) copy-start(bf16[4,12800]{1,0:T(4,128)(2,1)S(1)} %collective-permute-done.4) | copy-start | bytes 307204
  26.8 1.2 %copy-start.6 = (bf16[4,12800]{1,0:T(4,128)(2,1)}, bf16[4,12800]{1,0:T(4,128)(2,1)S(1)}, u32[]{:S(2)}) copy-start(bf16[4,12800]{1,0:T(4,128)(2,1)S(1)} %collective-permute-done.3) | copy-start | bytes 307204
  28.0 19.4 %collective-permute-start.6 = (bf16[4,4,12800]{2,1,0:T(4,128)(2,1)}, bf16[4,4,12800]{2,1,0:T(4,128)(2,1)}, u32[]{:S(2)}, u32[]{:S(2)}) collective-permute-start(bf16[4,4,12800]{2,1,0:T(4,128)(2,1)} %pad_maximum_fusion.1), channel_id=1, source_target_pairs={{0,1},{1,0},{2,3},{3,2},{4,5},{5,4},{6,7},{7,6},{8,9},{9,8},{10,11... | collective-permute-start | bytes 1228808 | tf_op jit(solution)/shard_map/ppermute | solution.py:15
  34.3 6.1 %copy-start.3 = (bf16[4,12800]{1,0:T(4,128)(2,1)S(1)}, bf16[4,12800]{1,0:T(4,128)(2,1)}, u32[]{:S(2)}) copy-start(bf16[4,12800]{1,0:T(4,128)(2,1)} %copy-done.2) | copy-start | bytes 307204
  34.3 6.1 %copy-start.5 = (bf16[4,12800]{1,0:T(4,128)(2,1)S(1)}, bf16[4,12800]{1,0:T(4,128)(2,1)}, u32[]{:S(2)}) copy-start(bf16[4,12800]{1,0:T(4,128)(2,1)} %copy-done.4) | copy-start | bytes 307204
  34.3 6.2 %copy-start.7 = (bf16[4,12800]{1,0:T(4,128)(2,1)S(1)}, bf16[4,12800]{1,0:T(4,128)(2,1)}, u32[]{:S(2)}) copy-start(bf16[4,12800]{1,0:T(4,128)(2,1)} %copy-done.6) | copy-start | bytes 307204
  37.0 9.6 %all-to-all-start.1 = ((bf16[8,2,6144]{2,1,0:T(2,128)(2,1)}), bf16[8,2,6144]{2,1,0:T(2,128)(2,1)S(1)}, u32[]{:S(2)}, u32[]{:S(2)}) async-start(bf16[8,2,6144]{2,1,0:T(2,128)(2,1)} %reshape.509), calls=%async_computation.1 | async-start | bytes 393216 | tf_op jit(solution)/shard_map/all_to_all | solution.py:94
  52.5 9.6 %all-to-all-start.2 = ((bf16[8,2,6144]{2,1,0:T(2,128)(2,1)}), bf16[8,2,6144]{2,1,0:T(2,128)(2,1)S(1)}, u32[]{:S(2)}, u32[]{:S(2)}) async-start(bf16[8,2,6144]{2,1,0:T(2,128)(2,1)} %reshape.511), calls=%async_computation.2 | async-start | bytes 393216 | tf_op jit(solution)/shard_map/all_to_all | solution.py:101
  56.7 6.7 %copy-start.1 = (bf16[2,2,64,384]{3,2,1,0:T(8,128)(2,1)S(1)}, bf16[2,2,64,384]{3,2,1,0:T(8,128)(2,1)}, u32[]{:S(2)}) copy-start(bf16[2,2,64,384]{3,2,1,0:T(8,128)(2,1)} %param.13) | copy-start | bytes 589828

commit v11 on v9

--- a/solution.py
+++ b/solution.py
@@ -34,20 +34,25 @@
     tile_count = lax.axis_size("tile")
     x_rows, x_cols = x_operator.shape
     y_rows, y_cols = y_operator.shape
-    x_size = x_rows * x_cols
-    both = jnp.concatenate([x_operator.reshape(-1), y_operator.reshape(-1)])
+    width = max(x_cols, y_cols)
+    both = jnp.concatenate(
+        [
+            jnp.pad(x_operator, ((0, 0), (0, width - x_cols))),
+            jnp.pad(y_operator, ((0, 0), (0, width - y_cols))),
+        ]
+    )
     mem_bits = bit_groups([1 << k for k in range(mem_count.bit_length() - 1)])
     tile_bits = bit_groups([1 << k for k in range(1, tile_count.bit_length() - 1)]) + [[1]]
     both = xor_gather(both, "mem", mem_bits)
     both, after = lax.optimization_barrier((both, after))
-    both = xor_gather(both, "tile", tile_bits).reshape(mem_count * tile_count, -1)
+    both = xor_gather(both, "tile", tile_bits).reshape(mem_count * tile_count, x_rows + y_rows, width)
     mem_of = lax.broadcasted_iota(jnp.int32, (mem_count, tile_count), 0)
     tile_of = lax.broadcasted_iota(jnp.int32, (mem_count, tile_count), 1)
     position = stacked_position(tile_of ^ lax.axis_index("tile"), tile_bits) * mem_count
     position = position + stacked_position(mem_of ^ lax.axis_index("mem"), mem_bits)
     position = position.reshape(-1)
-    x_full = jnp.take(both[:, :x_size], position, axis=0, mode="clip")
-    y_full = jnp.take(both[:, x_size:], position, axis=0, mode="clip")
+    x_full = jnp.take(both[:, :x_rows, :x_cols], position, axis=0, mode="clip")
+    y_full = jnp.take(both[:, x_rows:, :y_cols], position, axis=0, mode="clip")
     x_full = x_full.reshape(mem_count * tile_count * x_rows, x_cols)
     y_full = y_full.reshape(mem_count * tile_count * y_rows, y_cols)
     return x_full, y_full, after
@@ -62,9 +67,14 @@
     block_cells = source_blocks.shape[3]
     block_side = math.isqrt(block_cells)
     picked = send_blocks[0].reshape(-1)
-    packed = jnp.take(source_blocks, picked, axis=0, mode="clip").reshape(
-        tile_count, capacity, member_count, level_count, block_cells
+    held = source_blocks.shape[0]
+    one_hot = (picked[:, None] == lax.broadcasted_iota(jnp.int32, (1, held), 1)).astype(
+        source_blocks.dtype
     )
+    packed = jnp.dot(
+        one_hot, source_blocks.reshape(held, -1), preferred_element_type=jnp.float32
+    ).astype(source_blocks.dtype)
+    packed = packed.reshape(tile_count, capacity, member_count, level_count, block_cells)
     arrived = lax.all_to_all(packed, "tile", split_axis=0, concat_axis=0, tiled=True)
     x_full, y_full, arrived = gather_operators(x_operator, y_operator, arrived)
     slot_count = columns // block_side * (y_cells // block_side)

time: 61.9 us -> 60.4 us (0.976)
  waiting for transfers between devices: 12.8 us -> 17.5 us
  local copies, waits for them, and re-layouts: 19 us -> 14.6 us
  other arithmetic: 5.56 us -> 3.99 us
    all_to_all x1, waiting for transfers between devices: 2.95 us -> 6.12 us  [body(): lax.all_to_all(difference, 'tile', split_axis=3, concat_axis=2, tiled=True)]
    gather x3 -> x2, local copies, waits for them, and re-layouts: 3.85 us -> 1.21 us  [the longest x1 0.63 us: gather_operators(): y_full = jnp.take(both[:, x_rows:, :y_cols], position, axis=0, mode='clip')]
    all_to_all x1, waiting for transfers between devices: 4.79 us -> 6.01 us  [body(): lax.all_to_all(packed, 'tile', split_axis=0, concat_axis=0, tiled=True)]
    reshape x3 -> x2, local copies, waits for them, and re-layouts: 1.15 us -> 2.14 us  [the longest x1 1.12 us: body(): source_blocks.reshape(held, -1)]
    another operation x4, other arithmetic: 3.54 us -> 2.75 us  [xor_gather(): data = jnp.stack(parts)]
    eq x0 -> x1, local copies, waits for them, and re-layouts: none -> 0.76 us  [body(): picked[:, None] == lax.broadcasted_iota(jnp.int32, (1, held), 1)]
    unnamed x10 -> x14, local copies, waits for them, and re-layouts: 4 us -> 3.24 us
    broadcast_in_dim x1 -> x0, local copies, waits for them, and re-layouts: 0.76 us -> none  [body(): jnp.take(source_blocks, picked, axis=0, mode='clip')]
  transfers between devices with their start and end apart: 10 -> 10, of which waited for: 3 -> 3; matrix products, arithmetic and copies ran while one was open for 32% -> 25% of each run, Pallas kernels for 0% -> 0%
where the time goes in v11:
time: 60.4 us; the launch traced here: 59.8 us
  starting transfers between devices  19.9 us (33%)
  waiting for transfers between devices  17.5 us (29%)
  local copies, waits for them, and re-layouts  14.6 us (24%)
  other arithmetic  3.99 us (7%)
  matrix products  3.45 us (6%)
    ppermute x7, starting transfers between devices, xor_gather(): lax.ppermute(data, axis_name, [(j, j ^ offset) for j in range(count)])  9.24 us
    all_to_all x1, waiting for transfers between devices, body(): lax.all_to_all(difference, 'tile', split_axis=3, concat_axis=2, tiled=True)  6.12 us
    all_to_all x1, waiting for transfers between devices, body(): lax.all_to_all(packed, 'tile', split_axis=0, concat_axis=0, tiled=True)  6.01 us
    all_to_all x1, waiting for transfers between devices, body(): lax.all_to_all(after_first, 'tile', split_axis=2, concat_axis=3, tiled=True)  5.39 us
    all_to_all x1, starting transfers between devices, body(): lax.all_to_all(packed, 'tile', split_axis=0, concat_axis=0, tiled=True)  3.87 us
    all_to_all x1, starting transfers between devices, body(): lax.all_to_all(difference, 'tile', split_axis=3, concat_axis=2, tiled=True)  3.39 us
    all_to_all x1, starting transfers between devices, body(): lax.all_to_all(after_first, 'tile', split_axis=2, concat_axis=3, tiled=True)  3.39 us
    unnamed x14, local copies, waits for them, and re-layouts  3.24 us
  transfers between devices with their start and end apart: 10, of which 3 were waited for; matrix products, arithmetic and copies ran while one was open for 25% of the time, Pallas kernels for 0%

profile of v11, /device:TPU:0, one launch (start us, length us, event | category | flops | bytes accessed | tf_op | source)
XLA Modules:
  0.0 59.8 jit_solution(16799143354014660392)
XLA Ops:
  0.0 0.8 %fusion.30 = (bf16[1,28,512]{2,1,0:T(8,128)(2,1)S(1)}, bf16[28,512]{1,0:T(8,128)(2,1)S(1)}) fusion(bf16[12,384]{1,0:T(8,128)(2,1)} %param.15, bf16[16,512]{1,0:T(8,128)(2,1)} %param.14), kind=kLoop, calls=%fused_computation.83 | loop fusion | flops 86016 | bytes 82944 | tf_op jit(solution)/shard_map/stack | solution.py:16
  0.8 5.0 %collective-permute-start.2 = (bf16[28,512]{1,0:T(8,128)(2,1)S(1)}, bf16[28,512]{1,0:T(8,128)(2,1)S(1)}, u32[]{:S(2)}, u32[]{:S(2)}) collective-permute-start(bf16[28,512]{1,0:T(8,128)(2,1)S(1)} %get-tuple-element.12), channel_id=1, source_target_pairs={{0,24},{8,16},{16,8},{24,0},{1,25},{9,17},{17,9},{25,1},{2,26},{10... | collective-permute-start | bytes 86024 | tf_op jit(solution)/shard_map/ppermute | solution.py:15
  5.8 0.6 %collective-permute-start = (bf16[28,512]{1,0:T(8,128)(2,1)S(1)}, bf16[28,512]{1,0:T(8,128)(2,1)S(1)}, u32[]{:S(2)}, u32[]{:S(2)}) collective-permute-start(bf16[28,512]{1,0:T(8,128)(2,1)S(1)} %get-tuple-element.12), channel_id=1, source_target_pairs={{0,8},{8,0},{16,24},{24,16},{1,9},{9,1},{17,25},{25,17},{2,10},{10... | collective-permute-start | bytes 86024 | tf_op jit(solution)/shard_map/ppermute | solution.py:15
  6.5 1.1 %reshape.467 = bf16[128,1024]{1,0:T(8,128)(2,1)S(1)} reshape(bf16[128,2,2,256]{3,2,1,0:T(2,128)(2,1)} %param.8) | data formatting | bytes 524288 | tf_op jit(solution)/shard_map/reshape | solution.py:75
  7.6 0.8 %eq.39 = s32[192]{0:T(256)S(1)} reshape(s32[1,8,24]{2,1,0:T(8,128)} %param.9) | data formatting | bytes 1536 | tf_op jit(solution)/shard_map/eq | solution.py:71
  8.4 0.3 convolution_convert_fusion
  8.7 1.0 %reshape.468 = bf16[8,24,2,2,256]{4,3,2,1,0:T(2,128)(2,1)} reshape(bf16[192,1024]{1,0:T(8,128)(2,1)S(1)} %convolution_convert_fusion) | data formatting | bytes 786432 | tf_op jit(solution)/shard_map/reshape | solution.py:77
  9.7 3.9 %all-to-all-start = ((bf16[8,24,2,2,256]{4,3,2,1,0:T(2,128)(2,1)}), bf16[8,24,2,2,256]{4,3,2,1,0:T(2,128)(2,1)S(1)}, u32[]{:S(2)}, u32[]{:S(2)}) async-start(bf16[8,24,2,2,256]{4,3,2,1,0:T(2,128)(2,1)} %reshape.468), calls=%async_computation | async-start | bytes 786432 | tf_op jit(solution)/shard_map/all_to_all | solution.py:78
  13.7 0.1 iota_compare_fusion.3
  13.8 0.1 lt.42
  13.9 0.1 squeeze.3
  14.1 0.1 eq.36
  14.1 0.1 select_n.135
  14.3 0.1 iota.84
  14.4 0.1 select_n.131
  14.5 0.1 select_n.128
  14.5 0.7 %iota.75 = s32[32,1]{0,1:T(1,128)} reshape(s32[4,8]{1,0:T(4,128)S(1)} %iota.74) | data formatting | bytes 256 | tf_op jit(solution)/shard_map/iota | solution.py:50
  15.2 0.7 %pad_maximum_fusion.2 = bf16[4,28,512]{2,1,0:T(8,128)(2,1)} fusion(bf16[1,28,512]{2,1,0:T(8,128)(2,1)S(1)} %bitcast.75, bf16[1,28,512]{2,1,0:T(8,128)(2,1)S(1)} %bitcast.76, bf16[1,28,512]{2,1,0:T(8,128)(2,1)S(1)} %bitcast.77, bf16[1,28,512]{2,1,0:T(8,128)(2,1)S(1)} %get-tuple-element.11), kind=kLoop, calls=%fused_computation.15 | loop fusion | flops 172032 | bytes 229376 | tf_op jit(solution)/shard_map/stack | solution.py:16
  15.9 6.0 %all-to-all-done = bf16[8,24,2,2,256]{4,3,2,1,0:T(2,128)(2,1)S(1)} async-done(((bf16[8,24,2,2,256]{4,3,2,1,0:T(2,128)(2,1)}), bf16[8,24,2,2,256]{4,3,2,1,0:T(2,128)(2,1)S(1)}, u32[]{:S(2)}, u32[]{:S(2)}) %all-to-all-start) | async-done | bytes 393248 | tf_op jit(solution)/shard_map/all_to_all | solution.py:78
  21.9 0.6 collective-permute-start.5
  22.5 1.5 %collective-permute-start.4 = (bf16[4,28,512]{2,1,0:T(8,128)(2,1)}, bf16[4,28,512]{2,1,0:T(8,128)(2,1)}, u32[]{:S(2)}, u32[]{:S(2)}) collective-permute-start(bf16[4,28,512]{2,1,0:T(8,128)(2,1)} %pad_maximum_fusion.2), channel_id=1, source_target_pairs={{0,4},{1,5},{2,6},{3,7},{4,0},{5,1},{6,2},{7,3},{8,12},{9,13},{10,... | collective-permute-start | bytes 344072 | tf_op jit(solution)/shard_map/ppermute | solution.py:15
  23.9 1.5 %collective-permute-start.3 = (bf16[4,28,512]{2,1,0:T(8,128)(2,1)}, bf16[4,28,512]{2,1,0:T(8,128)(2,1)}, u32[]{:S(2)}, u32[]{:S(2)}) collective-permute-start(bf16[4,28,512]{2,1,0:T(8,128)(2,1)} %pad_maximum_fusion.2), channel_id=1, source_target_pairs={{0,2},{1,3},{2,0},{3,1},{4,6},{5,7},{6,4},{7,5},{8,10},{9,11},{10,... | collective-permute-start | bytes 344072 | tf_op jit(solution)/shard_map/ppermute | solution.py:15
  25.4 0.3 reshape.469
  25.7 0.2 copy.16
  25.9 1.8 %convolution_bitcast_fusion = f32[2,2,4,16,24,16]{4,5,3,1,0,2:T(8,128)} fusion(bf16[2,2,16,16,192,1]{4,3,2,1,0,5:T(8,128)(2,1)S(1)} %bitcast.66, bf16[192]{0:T(256)(128)(2,1)S(1)} %broadcast_select_fusion.3, s32[4,24]{1,0:T(4,128)S(1)} %multiply_add_fusion, s32[192]{0:T(256)S(1)} %eq.36), kind=kOutput, calls=%fused_computation.2 | convolution fusion | flops 37785600 | bytes 787968 | tf_op jit(solution)/shard_map/dot_general | solution.py:87
  27.7 2.2 %copy.17 = f32[2,2,4,16,24,16]{5,4,3,2,1,0:T(8,128)S(1)} copy(f32[2,2,4,16,24,16]{4,5,3,1,0,2:T(8,128)} %convolution_bitcast_fusion) | data formatting | bytes 786432 | tf_op jit(solution)/shard_map/transpose | solution.py:100
  30.0 0.9 %reshape.470 = f32[2,2,64,384]{3,2,1,0:T(8,128)S(1)} reshape(f32[2,2,4,16,24,16]{5,4,3,2,1,0:T(8,128)S(1)} %copy.17) | data formatting | bytes 786432 | tf_op jit(solution)/shard_map/reshape | solution.py:100
  30.9 1.2 %fusion.31 = (bf16[1,4,4,28,512]{4,3,2,1,0:T(8,128)(2,1)S(1)}, bf16[4,4,28,512]{3,2,1,0:T(8,128)(2,1)S(1)}) fusion(bf16[1,4,28,512]{3,2,1,0:T(8,128)(2,1)} %bitcast.17, bf16[1,4,28,512]{3,2,1,0:T(8,128)(2,1)} %bitcast.16, bf16[1,4,28,512]{3,2,1,0:T(8,128)(2,1)} %bitcast.15, bf16[1,4,28,512]{3,2,1,0:T(8,128)(2,1)} %bitcast.14), kind=kLoop, calls=%fused_computation.84 | loop fusion | flops 688128 | bytes 1376256 | tf_op jit(solution)/shard_map/stack | solution.py:16
  32.2 1.0 %fusion.2 = bf16[2,2,64,384]{3,2,1,0:T(8,128)(2,1)S(1)} fusion(f32[2,2,64,384]{3,2,1,0:T(8,128)S(1)} %reshape.470, bf16[2,2,64,384]{3,2,1,0:T(8,128)(2,1)} %param.13), kind=kLoop, calls=%fused_computation.12 | loop fusion | flops 294912 | bytes 786432 | tf_op jit(solution)/shard_map/convert_element_type | solution.py:103
  33.1 0.6 %copy.18 = bf16[2,2,64,384]{2,1,0,3:T(2,128)(2,1)S(1)} copy(bf16[2,2,64,384]{3,2,1,0:T(8,128)(2,1)S(1)} %fusion.2) | data formatting | bytes 393216 | tf_op jit(solution)/shard_map/convert_element_type | solution.py:103
  33.8 1.0 %reshape.495 = bf16[8,2,6144]{2,1,0:T(2,128)(2,1)} reshape(bf16[384,2,2,64]{3,2,1,0:T(2,128)(2,1)S(1)} %bitcast.71) | data formatting | bytes 393216
  34.7 3.4 %all-to-all-start.1 = ((bf16[8,2,6144]{2,1,0:T(2,128)(2,1)}), bf16[8,2,6144]{2,1,0:T(2,128)(2,1)S(1)}, u32[]{:S(2)}, u32[]{:S(2)}) async-start(bf16[8,2,6144]{2,1,0:T(2,128)(2,1)} %reshape.495), calls=%async_computation.1 | async-start | bytes 393216 | tf_op jit(solution)/shard_map/all_to_all | solution.py:104
  38.2 6.1 %all-to-all-done.1 = bf16[8,2,6144]{2,1,0:T(2,128)(2,1)S(1)} async-done(((bf16[8,2,6144]{2,1,0:T(2,128)(2,1)}), bf16[8,2,6144]{2,1,0:T(2,128)(2,1)S(1)}, u32[]{:S(2)}, u32[]{:S(2)}) %all-to-all-start.1) | async-done | bytes 196640 | tf_op jit(solution)/shard_map/all_to_all | solution.py:104
  44.3 0.3 reshape.496
  44.6 0.3 copy.31
  44.9 0.3 all_to_all.33
  45.1 0.1 pad_maximum_fusion
  45.3 0.6 gather_fusion
  45.9 0.3 fusion.1
  46.2 0.4 copy.21
  46.6 1.4 %reshape.497 = bf16[8,2,6144]{2,1,0:T(2,128)(2,1)} reshape(bf16[512,2,2,48]{3,2,1,0:T(2,128)(2,1)S(1)} %bitcast.68) | data formatting | bytes 393216
  48.1 3.4 %all-to-all-start.2 = ((bf16[8,2,6144]{2,1,0:T(2,128)(2,1)}), bf16[8,2,6144]{2,1,0:T(2,128)(2,1)S(1)}, u32[]{:S(2)}, u32[]{:S(2)}) async-start(bf16[8,2,6144]{2,1,0:T(2,128)(2,1)} %reshape.497), calls=%async_computation.2 | async-start | bytes 393216 | tf_op jit(solution)/shard_map/all_to_all | solution.py:111
  51.5 0.6 %gather_fusion.1 = bf16[32,12,384]{2,1,0:T(8,128)(2,1)S(1)} fusion(bf16[32,12,384]{2,1,0:T(8,128)(2,1)S(1)} %slice.13, s32[1024]{0:T(1024)S(1)} %pad_clamp_fusion), kind=kCustom, calls=%fused_computation.1 | custom fusion | bytes 589952 | tf_op jit(solution)/shard_map/jit(_take)/gather | solution.py:55
  52.2 5.4 %all-to-all-done.2 = bf16[8,2,6144]{2,1,0:T(2,128)(2,1)S(1)} async-done(((bf16[8,2,6144]{2,1,0:T(2,128)(2,1)}), bf16[8,2,6144]{2,1,0:T(2,128)(2,1)S(1)}, u32[]{:S(2)}, u32[]{:S(2)}) %all-to-all-start.2) | async-done | bytes 196640 | tf_op jit(solution)/shard_map/all_to_all | solution.py:111
  57.6 0.5 reshape.498
  58.1 0.3 copy.30
  58.5 0.4 all_to_all.37
  58.9 1.0 %fusion = bf16[2,2,64,384]{3,2,1,0:T(8,128)(2,1)} fusion(bf16[2,2,64,384]{3,2,1,0:T(8,128)(2,1)S(1)} %all_to_all.37, bf16[2,2,64,384]{3,2,1,0:T(8,128)(2,1)S(1)} %copy-done, bf16[384,384,1,1]{1,0,2,3:T(8,128)(2,1)S(1)} %reshape.493), kind=kOutput, calls=%fused_computation.6 | convolution fusion | flops 75792384 | bytes 884736 | tf_op jit(solution)/shard_map/by,mlxy->mlxb/dot_general | solution.py:112
  (38 shorter events, 0.5 us)
Async XLA Ops:
  0.0 13.7 %copy-start.4 = (s32[1,8]{1,0:T(1,128)S(1)}, s32[1,8]{1,0:T(1,128)}, u32[]{:S(2)}) copy-start(s32[1,8]{1,0:T(1,128)} %param.12) | copy-start | bytes 100
  0.0 13.8 %copy-start.2 = (f32[1,8,24]{2,1,0:T(8,128)S(1)}, f32[1,8,24]{2,1,0:T(8,128)}, u32[]{:S(2)}) copy-start(f32[1,8,24]{2,1,0:T(8,128)} %param.11) | copy-start | bytes 2308
  0.0 14.1 %copy-start.1 = (s32[1,8,24]{2,1,0:T(8,128)S(1)}, s32[1,8,24]{2,1,0:T(8,128)}, u32[]{:S(2)}) copy-start(s32[1,8,24]{2,1,0:T(8,128)} %param.10) | copy-start | bytes 2308
  0.8 14.4 %collective-permute-start.2 = (bf16[28,512]{1,0:T(8,128)(2,1)S(1)}, bf16[28,512]{1,0:T(8,128)(2,1)S(1)}, u32[]{:S(2)}, u32[]{:S(2)}) collective-permute-start(bf16[28,512]{1,0:T(8,128)(2,1)S(1)} %get-tuple-element.12), channel_id=1, source_target_pairs={{0,24},{8,16},{16,8},{24,0},{1,25},{9,17},{17,9},{25,1},{2,26},{10... | collective-permute-start | bytes 86024 | tf_op jit(solution)/shard_map/ppermute | solution.py:15
  5.8 9.4 %collective-permute-start.1 = (bf16[28,512]{1,0:T(8,128)(2,1)S(1)}, bf16[28,512]{1,0:T(8,128)(2,1)S(1)}, u32[]{:S(2)}, u32[]{:S(2)}) collective-permute-start(bf16[28,512]{1,0:T(8,128)(2,1)S(1)} %get-tuple-element.12), channel_id=1, source_target_pairs={{0,16},{8,24},{16,0},{24,8},{1,17},{9,25},{17,1},{25,9},{2,18},{10... | collective-permute-start | bytes 86024 | tf_op jit(solution)/shard_map/ppermute | solution.py:15
  5.8 9.4 %collective-permute-start = (bf16[28,512]{1,0:T(8,128)(2,1)S(1)}, bf16[28,512]{1,0:T(8,128)(2,1)S(1)}, u32[]{:S(2)}, u32[]{:S(2)}) collective-permute-start(bf16[28,512]{1,0:T(8,128)(2,1)S(1)} %get-tuple-element.12), channel_id=1, source_target_pairs={{0,8},{8,0},{16,24},{24,16},{1,9},{9,1},{17,25},{25,17},{2,10},{10... | collective-permute-start | bytes 86024 | tf_op jit(solution)/shard_map/ppermute | solution.py:15
  9.7 12.2 %all-to-all-start = ((bf16[8,24,2,2,256]{4,3,2,1,0:T(2,128)(2,1)}), bf16[8,24,2,2,256]{4,3,2,1,0:T(2,128)(2,1)S(1)}, u32[]{:S(2)}, u32[]{:S(2)}) async-start(bf16[8,24,2,2,256]{4,3,2,1,0:T(2,128)(2,1)} %reshape.468), calls=%async_computation | async-start | bytes 786432 | tf_op jit(solution)/shard_map/all_to_all | solution.py:78
  21.9 9.0 %collective-permute-start.5 = (bf16[4,28,512]{2,1,0:T(8,128)(2,1)}, bf16[4,28,512]{2,1,0:T(8,128)(2,1)}, u32[]{:S(2)}, u32[]{:S(2)}) collective-permute-start(bf16[4,28,512]{2,1,0:T(8,128)(2,1)} %pad_maximum_fusion.2), channel_id=1, source_target_pairs={{0,6},{1,7},{2,4},{3,5},{4,2},{5,3},{6,0},{7,1},{8,14},{9,15},{10,... | collective-permute-start | bytes 344072 | tf_op jit(solution)/shard_map/ppermute | solution.py:15
  22.5 8.4 %collective-permute-start.4 = (bf16[4,28,512]{2,1,0:T(8,128)(2,1)}, bf16[4,28,512]{2,1,0:T(8,128)(2,1)}, u32[]{:S(2)}, u32[]{:S(2)}) collective-permute-start(bf16[4,28,512]{2,1,0:T(8,128)(2,1)} %pad_maximum_fusion.2), channel_id=1, source_target_pairs={{0,4},{1,5},{2,6},{3,7},{4,0},{5,1},{6,2},{7,3},{8,12},{9,13},{10,... | collective-permute-start | bytes 344072 | tf_op jit(solution)/shard_map/ppermute | solution.py:15
  23.9 7.0 %collective-permute-start.3 = (bf16[4,28,512]{2,1,0:T(8,128)(2,1)}, bf16[4,28,512]{2,1,0:T(8,128)(2,1)}, u32[]{:S(2)}, u32[]{:S(2)}) collective-permute-start(bf16[4,28,512]{2,1,0:T(8,128)(2,1)} %pad_maximum_fusion.2), channel_id=1, source_target_pairs={{0,2},{1,3},{2,0},{3,1},{4,6},{5,7},{6,4},{7,5},{8,10},{9,11},{10,... | collective-permute-start | bytes 344072 | tf_op jit(solution)/shard_map/ppermute | solution.py:15
  30.9 7.3 %copy-start.3 = (s32[32,1]{0,1:T(1,128)S(1)}, s32[32,1]{0,1:T(1,128)}, u32[]{:S(2)}) copy-start(s32[32,1]{0,1:T(1,128)} %iota.75) | copy-start | bytes 388
  32.1 13.0 %collective-permute-start.6 = (bf16[4,4,28,512]{3,2,1,0:T(8,128)(2,1)S(1)}, bf16[4,4,28,512]{3,2,1,0:T(8,128)(2,1)S(1)}, u32[]{:S(2)}, u32[]{:S(2)}) collective-permute-start(bf16[4,4,28,512]{3,2,1,0:T(8,128)(2,1)S(1)} %get-tuple-element.10), channel_id=1, source_target_pairs={{0,1},{1,0},{2,3},{3,2},{4,5},{5,4},{6,7},{7,6},{8,9},{9,8},{10,11... | collective-permute-start | bytes 1376264 | tf_op jit(solution)/shard_map/ppermute | solution.py:15
  34.7 9.6 %all-to-all-start.1 = ((bf16[8,2,6144]{2,1,0:T(2,128)(2,1)}), bf16[8,2,6144]{2,1,0:T(2,128)(2,1)S(1)}, u32[]{:S(2)}, u32[]{:S(2)}) async-start(bf16[8,2,6144]{2,1,0:T(2,128)(2,1)} %reshape.495), calls=%async_computation.1 | async-start | bytes 393216 | tf_op jit(solution)/shard_map/all_to_all | solution.py:104
  48.1 9.6 %all-to-all-start.2 = ((bf16[8,2,6144]{2,1,0:T(2,128)(2,1)}), bf16[8,2,6144]{2,1,0:T(2,128)(2,1)S(1)}, u32[]{:S(2)}, u32[]{:S(2)}) async-start(bf16[8,2,6144]{2,1,0:T(2,128)(2,1)} %reshape.497), calls=%async_computation.2 | async-start | bytes 393216 | tf_op jit(solution)/shard_map/all_to_all | solution.py:111
  51.5 7.4 %copy-start = (bf16[2,2,64,384]{3,2,1,0:T(8,128)(2,1)S(1)}, bf16[2,2,64,384]{3,2,1,0:T(8,128)(2,1)}, u32[]{:S(2)}) copy-start(bf16[2,2,64,384]{3,2,1,0:T(8,128)(2,1)} %param.13) | copy-start | bytes 589828

commit v12 on v11

--- a/solution.py
+++ b/solution.py
@@ -74,7 +74,7 @@
     packed = jnp.dot(
         one_hot, source_blocks.reshape(held, -1), preferred_element_type=jnp.float32
     ).astype(source_blocks.dtype)
-    packed = packed.reshape(tile_count, capacity, member_count, level_count, block_cells)
+    packed = packed.reshape(tile_count, capacity, -1)
     arrived = lax.all_to_all(packed, "tile", split_axis=0, concat_axis=0, tiled=True)
     x_full, y_full, arrived = gather_operators(x_operator, y_operator, arrived)
     slot_count = columns // block_side * (y_cells // block_side)

time: 60.4 us -> 59.9 us (level)
  local copies, waits for them, and re-layouts: 14.6 us -> 13.3 us
  matrix products: 3.45 us -> 4.2 us
    reshape x1 -> x0, local copies, waits for them, and re-layouts: 1.03 us -> none  [body(): packed.reshape(tile_count, capacity, member_count, level_count, block_cells)]
    dot_general x1, matrix products: 0.31 us -> 1.06 us  [body(): jnp.dot(one_hot, source_blocks.reshape(held, -1), preferred_element_type=...]
  transfers between devices with their start and end apart: 10 -> 10, of which waited for: 3 -> 3; matrix products, arithmetic and copies ran while one was open for 25% -> 24% of each run, Pallas kernels for 0% -> 0%
where the time goes in v12:
time: 59.9 us; the launch traced here: 59.3 us
  starting transfers between devices  19.9 us (33%)
  waiting for transfers between devices  17.5 us (29%)
  local copies, waits for them, and re-layouts  13.3 us (22%)
  matrix products  4.2 us (7%)
  other arithmetic  3.99 us (7%)
    ppermute x7, starting transfers between devices, xor_gather(): lax.ppermute(data, axis_name, [(j, j ^ offset) for j in range(count)])  9.24 us
    all_to_all x1, waiting for transfers between devices, body(): lax.all_to_all(difference, 'tile', split_axis=3, concat_axis=2, tiled=True)  6.12 us
    all_to_all x1, waiting for transfers between devices, body(): lax.all_to_all(packed, 'tile', split_axis=0, concat_axis=0, tiled=True)  6.01 us
    all_to_all x1, waiting for transfers between devices, body(): lax.all_to_all(after_first, 'tile', split_axis=2, concat_axis=3, tiled=True)  5.39 us
    all_to_all x1, starting transfers between devices, body(): lax.all_to_all(packed, 'tile', split_axis=0, concat_axis=0, tiled=True)  3.87 us
    all_to_all x1, starting transfers between devices, body(): lax.all_to_all(difference, 'tile', split_axis=3, concat_axis=2, tiled=True)  3.39 us
    all_to_all x1, starting transfers between devices, body(): lax.all_to_all(after_first, 'tile', split_axis=2, concat_axis=3, tiled=True)  3.39 us
    unnamed x14, local copies, waits for them, and re-layouts  3.24 us
  transfers between devices with their start and end apart: 10, of which 3 were waited for; matrix products, arithmetic and copies ran while one was open for 24% of the time, Pallas kernels for 0%

profile of v12, /device:TPU:0, one launch (start us, length us, event | category | flops | bytes accessed | tf_op | source)
XLA Modules:
  0.0 59.3 jit_solution(7641618039227502146)
XLA Ops:
  0.0 0.8 %fusion.30 = (bf16[1,28,512]{2,1,0:T(8,128)(2,1)S(1)}, bf16[28,512]{1,0:T(8,128)(2,1)S(1)}) fusion(bf16[12,384]{1,0:T(8,128)(2,1)} %param.15, bf16[16,512]{1,0:T(8,128)(2,1)} %param.14), kind=kLoop, calls=%fused_computation.83 | loop fusion | flops 86016 | bytes 82944 | tf_op jit(solution)/shard_map/stack | solution.py:16
  0.8 5.0 %collective-permute-start.2 = (bf16[28,512]{1,0:T(8,128)(2,1)S(1)}, bf16[28,512]{1,0:T(8,128)(2,1)S(1)}, u32[]{:S(2)}, u32[]{:S(2)}) collective-permute-start(bf16[28,512]{1,0:T(8,128)(2,1)S(1)} %get-tuple-element.12), channel_id=1, source_target_pairs={{0,24},{8,16},{16,8},{24,0},{1,25},{9,17},{17,9},{25,1},{2,26},{10... | collective-permute-start | bytes 86024 | tf_op jit(solution)/shard_map/ppermute | solution.py:15
  5.8 0.6 %collective-permute-start = (bf16[28,512]{1,0:T(8,128)(2,1)S(1)}, bf16[28,512]{1,0:T(8,128)(2,1)S(1)}, u32[]{:S(2)}, u32[]{:S(2)}) collective-permute-start(bf16[28,512]{1,0:T(8,128)(2,1)S(1)} %get-tuple-element.12), channel_id=1, source_target_pairs={{0,8},{8,0},{16,24},{24,16},{1,9},{9,1},{17,25},{25,17},{2,10},{10... | collective-permute-start | bytes 86024 | tf_op jit(solution)/shard_map/ppermute | solution.py:15
  6.5 1.1 %reshape.467 = bf16[128,1024]{1,0:T(8,128)(2,1)S(1)} reshape(bf16[128,2,2,256]{3,2,1,0:T(2,128)(2,1)} %param.8) | data formatting | bytes 524288 | tf_op jit(solution)/shard_map/reshape | solution.py:75
  7.6 0.8 %eq.39 = s32[192]{0:T(256)S(1)} reshape(s32[1,8,24]{2,1,0:T(8,128)} %param.9) | data formatting | bytes 1536 | tf_op jit(solution)/shard_map/eq | solution.py:71
  8.4 1.1 %convolution_convert_fusion = bf16[192,1024]{1,0:T(8,128)(2,1)} fusion(bf16[128,1024]{1,0:T(8,128)(2,1)S(1)} %reshape.467, s32[192]{0:T(256)S(1)} %eq.39), kind=kOutput, calls=%fused_computation.3 | convolution fusion | flops 50552832 | bytes 656128 | tf_op jit(solution)/shard_map/dot_general | solution.py:74
  9.4 3.9 %all-to-all-start = ((bf16[8,24,1024]{2,1,0:T(8,128)(2,1)}), bf16[8,24,1024]{2,1,0:T(8,128)(2,1)S(1)}, u32[]{:S(2)}, u32[]{:S(2)}) async-start(bf16[8,24,1024]{2,1,0:T(8,128)(2,1)} %bitcast.7), calls=%async_computation | async-start | bytes 786432 | tf_op jit(solution)/shard_map/all_to_all | solution.py:78
  13.4 0.1 iota_compare_fusion.3
  13.5 0.1 lt.42
  13.6 0.1 squeeze.3
  13.8 0.1 eq.36
  13.9 0.1 select_n.135
  13.9 0.1 iota.83
  14.0 0.1 iota.84
  14.1 0.1 select_n.131
  14.2 0.1 select_n.128
  14.3 0.7 %iota.75 = s32[32,1]{0,1:T(1,128)} reshape(s32[4,8]{1,0:T(4,128)S(1)} %iota.74) | data formatting | bytes 256 | tf_op jit(solution)/shard_map/iota | solution.py:50
  14.9 0.7 %pad_maximum_fusion.2 = bf16[4,28,512]{2,1,0:T(8,128)(2,1)} fusion(bf16[1,28,512]{2,1,0:T(8,128)(2,1)S(1)} %bitcast.78, bf16[1,28,512]{2,1,0:T(8,128)(2,1)S(1)} %bitcast.79, bf16[1,28,512]{2,1,0:T(8,128)(2,1)S(1)} %bitcast.80, bf16[1,28,512]{2,1,0:T(8,128)(2,1)S(1)} %get-tuple-element.11), kind=kLoop, calls=%fused_computation.15 | loop fusion | flops 172032 | bytes 229376 | tf_op jit(solution)/shard_map/stack | solution.py:16
  15.6 6.0 %all-to-all-done = bf16[8,24,1024]{2,1,0:T(8,128)(2,1)S(1)} async-done(((bf16[8,24,1024]{2,1,0:T(8,128)(2,1)}), bf16[8,24,1024]{2,1,0:T(8,128)(2,1)S(1)}, u32[]{:S(2)}, u32[]{:S(2)}) %all-to-all-start) | async-done | bytes 393248 | tf_op jit(solution)/shard_map/all_to_all | solution.py:78
  21.6 0.6 collective-permute-start.5
  22.2 1.5 %collective-permute-start.4 = (bf16[4,28,512]{2,1,0:T(8,128)(2,1)}, bf16[4,28,512]{2,1,0:T(8,128)(2,1)}, u32[]{:S(2)}, u32[]{:S(2)}) collective-permute-start(bf16[4,28,512]{2,1,0:T(8,128)(2,1)} %pad_maximum_fusion.2), channel_id=1, source_target_pairs={{0,4},{1,5},{2,6},{3,7},{4,0},{5,1},{6,2},{7,3},{8,12},{9,13},{10,... | collective-permute-start | bytes 344072 | tf_op jit(solution)/shard_map/ppermute | solution.py:15
  23.7 1.5 %collective-permute-start.3 = (bf16[4,28,512]{2,1,0:T(8,128)(2,1)}, bf16[4,28,512]{2,1,0:T(8,128)(2,1)}, u32[]{:S(2)}, u32[]{:S(2)}) collective-permute-start(bf16[4,28,512]{2,1,0:T(8,128)(2,1)} %pad_maximum_fusion.2), channel_id=1, source_target_pairs={{0,2},{1,3},{2,0},{3,1},{4,6},{5,7},{6,4},{7,5},{8,10},{9,11},{10,... | collective-permute-start | bytes 344072 | tf_op jit(solution)/shard_map/ppermute | solution.py:15
  25.1 0.2 copy.16
  25.3 1.8 %convolution_bitcast_fusion = f32[2,2,4,16,24,16]{4,5,3,1,0,2:T(8,128)} fusion(bf16[2,2,16,16,192,1]{4,3,2,1,0,5:T(8,128)(2,1)S(1)} %bitcast.68, bf16[192]{0:T(256)(128)(2,1)S(1)} %broadcast_select_fusion.3, s32[4,24]{1,0:T(4,128)S(1)} %multiply_add_fusion, s32[192]{0:T(256)S(1)} %eq.36), kind=kOutput, calls=%fused_computation.2 | convolution fusion | flops 37785600 | bytes 787968 | tf_op jit(solution)/shard_map/dot_general | solution.py:87
  27.2 2.2 %copy.17 = f32[2,2,4,16,24,16]{5,4,3,2,1,0:T(8,128)S(1)} copy(f32[2,2,4,16,24,16]{4,5,3,1,0,2:T(8,128)} %convolution_bitcast_fusion) | data formatting | bytes 786432 | tf_op jit(solution)/shard_map/transpose | solution.py:100
  29.4 0.9 %reshape.470 = f32[2,2,64,384]{3,2,1,0:T(8,128)S(1)} reshape(f32[2,2,4,16,24,16]{5,4,3,2,1,0:T(8,128)S(1)} %copy.17) | data formatting | bytes 786432 | tf_op jit(solution)/shard_map/reshape | solution.py:100
  30.3 1.2 %fusion.31 = (bf16[1,4,4,28,512]{4,3,2,1,0:T(8,128)(2,1)S(1)}, bf16[4,4,28,512]{3,2,1,0:T(8,128)(2,1)S(1)}) fusion(bf16[1,4,28,512]{3,2,1,0:T(8,128)(2,1)} %bitcast.19, bf16[1,4,28,512]{3,2,1,0:T(8,128)(2,1)} %bitcast.18, bf16[1,4,28,512]{3,2,1,0:T(8,128)(2,1)} %bitcast.17, bf16[1,4,28,512]{3,2,1,0:T(8,128)(2,1)} %bitcast.16), kind=kLoop, calls=%fused_computation.84 | loop fusion | flops 688128 | bytes 1376256 | tf_op jit(solution)/shard_map/stack | solution.py:16
  31.5 0.1 collective-permute-start.6
  31.6 1.0 %fusion.2 = bf16[2,2,64,384]{3,2,1,0:T(8,128)(2,1)S(1)} fusion(f32[2,2,64,384]{3,2,1,0:T(8,128)S(1)} %reshape.470, bf16[2,2,64,384]{3,2,1,0:T(8,128)(2,1)} %param.13), kind=kLoop, calls=%fused_computation.12 | loop fusion | flops 294912 | bytes 786432 | tf_op jit(solution)/shard_map/convert_element_type | solution.py:103
  32.6 0.6 %copy.18 = bf16[2,2,64,384]{2,1,0,3:T(2,128)(2,1)S(1)} copy(bf16[2,2,64,384]{3,2,1,0:T(8,128)(2,1)S(1)} %fusion.2) | data formatting | bytes 393216 | tf_op jit(solution)/shard_map/convert_element_type | solution.py:103
  33.2 1.0 %reshape.495 = bf16[8,2,6144]{2,1,0:T(2,128)(2,1)} reshape(bf16[384,2,2,64]{3,2,1,0:T(2,128)(2,1)S(1)} %bitcast.74) | data formatting | bytes 393216
  34.2 3.4 %all-to-all-start.1 = ((bf16[8,2,6144]{2,1,0:T(2,128)(2,1)}), bf16[8,2,6144]{2,1,0:T(2,128)(2,1)S(1)}, u32[]{:S(2)}, u32[]{:S(2)}) async-start(bf16[8,2,6144]{2,1,0:T(2,128)(2,1)} %reshape.495), calls=%async_computation.1 | async-start | bytes 393216 | tf_op jit(solution)/shard_map/all_to_all | solution.py:104
  37.6 6.1 %all-to-all-done.1 = bf16[8,2,6144]{2,1,0:T(2,128)(2,1)S(1)} async-done(((bf16[8,2,6144]{2,1,0:T(2,128)(2,1)}), bf16[8,2,6144]{2,1,0:T(2,128)(2,1)S(1)}, u32[]{:S(2)}, u32[]{:S(2)}) %all-to-all-start.1) | async-done | bytes 196640 | tf_op jit(solution)/shard_map/all_to_all | solution.py:104
  43.8 0.3 reshape.496
  44.0 0.3 copy.31
  44.3 0.3 all_to_all.33
  44.6 0.1 pad_maximum_fusion
  44.7 0.6 gather_fusion
  45.3 0.3 fusion.1
  45.7 0.4 copy.21
  46.1 1.4 %reshape.497 = bf16[8,2,6144]{2,1,0:T(2,128)(2,1)} reshape(bf16[512,2,2,48]{3,2,1,0:T(2,128)(2,1)S(1)} %bitcast.70) | data formatting | bytes 393216
  47.5 3.4 %all-to-all-start.2 = ((bf16[8,2,6144]{2,1,0:T(2,128)(2,1)}), bf16[8,2,6144]{2,1,0:T(2,128)(2,1)S(1)}, u32[]{:S(2)}, u32[]{:S(2)}) async-start(bf16[8,2,6144]{2,1,0:T(2,128)(2,1)} %reshape.497), calls=%async_computation.2 | async-start | bytes 393216 | tf_op jit(solution)/shard_map/all_to_all | solution.py:111
  51.0 0.6 %gather_fusion.1 = bf16[32,12,384]{2,1,0:T(8,128)(2,1)S(1)} fusion(bf16[32,12,384]{2,1,0:T(8,128)(2,1)S(1)} %slice.13, s32[1024]{0:T(1024)S(1)} %pad_clamp_fusion), kind=kCustom, calls=%fused_computation.1 | custom fusion | bytes 589952 | tf_op jit(solution)/shard_map/jit(_take)/gather | solution.py:55
  51.7 5.4 %all-to-all-done.2 = bf16[8,2,6144]{2,1,0:T(2,128)(2,1)S(1)} async-done(((bf16[8,2,6144]{2,1,0:T(2,128)(2,1)}), bf16[8,2,6144]{2,1,0:T(2,128)(2,1)S(1)}, u32[]{:S(2)}, u32[]{:S(2)}) %all-to-all-start.2) | async-done | bytes 196640 | tf_op jit(solution)/shard_map/all_to_all | solution.py:111
  57.1 0.5 reshape.498
  57.6 0.3 copy.30
  57.9 0.4 all_to_all.37
  58.3 1.0 %fusion = bf16[2,2,64,384]{3,2,1,0:T(8,128)(2,1)} fusion(bf16[2,2,64,384]{3,2,1,0:T(8,128)(2,1)S(1)} %all_to_all.37, bf16[2,2,64,384]{3,2,1,0:T(8,128)(2,1)S(1)} %copy-done, bf16[384,384,1,1]{1,0,2,3:T(8,128)(2,1)S(1)} %reshape.493), kind=kOutput, calls=%fused_computation.6 | convolution fusion | flops 75792384 | bytes 884736 | tf_op jit(solution)/shard_map/by,mlxy->mlxb/dot_general | solution.py:112
  (36 shorter events, 0.4 us)
Async XLA Ops:
  0.0 13.4 %copy-start.4 = (s32[1,8]{1,0:T(1,128)S(1)}, s32[1,8]{1,0:T(1,128)}, u32[]{:S(2)}) copy-start(s32[1,8]{1,0:T(1,128)} %param.12) | copy-start | bytes 100
  0.0 13.6 %copy-start.2 = (f32[1,8,24]{2,1,0:T(8,128)S(1)}, f32[1,8,24]{2,1,0:T(8,128)}, u32[]{:S(2)}) copy-start(f32[1,8,24]{2,1,0:T(8,128)} %param.11) | copy-start | bytes 2308
  0.0 13.8 %copy-start.1 = (s32[1,8,24]{2,1,0:T(8,128)S(1)}, s32[1,8,24]{2,1,0:T(8,128)}, u32[]{:S(2)}) copy-start(s32[1,8,24]{2,1,0:T(8,128)} %param.10) | copy-start | bytes 2308
  0.8 14.2 %collective-permute-start.2 = (bf16[28,512]{1,0:T(8,128)(2,1)S(1)}, bf16[28,512]{1,0:T(8,128)(2,1)S(1)}, u32[]{:S(2)}, u32[]{:S(2)}) collective-permute-start(bf16[28,512]{1,0:T(8,128)(2,1)S(1)} %get-tuple-element.12), channel_id=1, source_target_pairs={{0,24},{8,16},{16,8},{24,0},{1,25},{9,17},{17,9},{25,1},{2,26},{10... | collective-permute-start | bytes 86024 | tf_op jit(solution)/shard_map/ppermute | solution.py:15
  5.8 9.1 %collective-permute-start.1 = (bf16[28,512]{1,0:T(8,128)(2,1)S(1)}, bf16[28,512]{1,0:T(8,128)(2,1)S(1)}, u32[]{:S(2)}, u32[]{:S(2)}) collective-permute-start(bf16[28,512]{1,0:T(8,128)(2,1)S(1)} %get-tuple-element.12), channel_id=1, source_target_pairs={{0,16},{8,24},{16,0},{24,8},{1,17},{9,25},{17,1},{25,9},{2,18},{10... | collective-permute-start | bytes 86024 | tf_op jit(solution)/shard_map/ppermute | solution.py:15
  5.8 9.1 %collective-permute-start = (bf16[28,512]{1,0:T(8,128)(2,1)S(1)}, bf16[28,512]{1,0:T(8,128)(2,1)S(1)}, u32[]{:S(2)}, u32[]{:S(2)}) collective-permute-start(bf16[28,512]{1,0:T(8,128)(2,1)S(1)} %get-tuple-element.12), channel_id=1, source_target_pairs={{0,8},{8,0},{16,24},{24,16},{1,9},{9,1},{17,25},{25,17},{2,10},{10... | collective-permute-start | bytes 86024 | tf_op jit(solution)/shard_map/ppermute | solution.py:15
  9.4 12.2 %all-to-all-start = ((bf16[8,24,1024]{2,1,0:T(8,128)(2,1)}), bf16[8,24,1024]{2,1,0:T(8,128)(2,1)S(1)}, u32[]{:S(2)}, u32[]{:S(2)}) async-start(bf16[8,24,1024]{2,1,0:T(8,128)(2,1)} %bitcast.7), calls=%async_computation | async-start | bytes 786432 | tf_op jit(solution)/shard_map/all_to_all | solution.py:78
  21.6 8.7 %collective-permute-start.5 = (bf16[4,28,512]{2,1,0:T(8,128)(2,1)}, bf16[4,28,512]{2,1,0:T(8,128)(2,1)}, u32[]{:S(2)}, u32[]{:S(2)}) collective-permute-start(bf16[4,28,512]{2,1,0:T(8,128)(2,1)} %pad_maximum_fusion.2), channel_id=1, source_target_pairs={{0,6},{1,7},{2,4},{3,5},{4,2},{5,3},{6,0},{7,1},{8,14},{9,15},{10,... | collective-permute-start | bytes 344072 | tf_op jit(solution)/shard_map/ppermute | solution.py:15
  22.2 8.1 %collective-permute-start.4 = (bf16[4,28,512]{2,1,0:T(8,128)(2,1)}, bf16[4,28,512]{2,1,0:T(8,128)(2,1)}, u32[]{:S(2)}, u32[]{:S(2)}) collective-permute-start(bf16[4,28,512]{2,1,0:T(8,128)(2,1)} %pad_maximum_fusion.2), channel_id=1, source_target_pairs={{0,4},{1,5},{2,6},{3,7},{4,0},{5,1},{6,2},{7,3},{8,12},{9,13},{10,... | collective-permute-start | bytes 344072 | tf_op jit(solution)/shard_map/ppermute | solution.py:15
  23.7 6.7 %collective-permute-start.3 = (bf16[4,28,512]{2,1,0:T(8,128)(2,1)}, bf16[4,28,512]{2,1,0:T(8,128)(2,1)}, u32[]{:S(2)}, u32[]{:S(2)}) collective-permute-start(bf16[4,28,512]{2,1,0:T(8,128)(2,1)} %pad_maximum_fusion.2), channel_id=1, source_target_pairs={{0,2},{1,3},{2,0},{3,1},{4,6},{5,7},{6,4},{7,5},{8,10},{9,11},{10,... | collective-permute-start | bytes 344072 | tf_op jit(solution)/shard_map/ppermute | solution.py:15
  30.3 7.3 %copy-start.3 = (s32[32,1]{0,1:T(1,128)S(1)}, s32[32,1]{0,1:T(1,128)}, u32[]{:S(2)}) copy-start(s32[32,1]{0,1:T(1,128)} %iota.75) | copy-start | bytes 388
  31.5 13.0 %collective-permute-start.6 = (bf16[4,4,28,512]{3,2,1,0:T(8,128)(2,1)S(1)}, bf16[4,4,28,512]{3,2,1,0:T(8,128)(2,1)S(1)}, u32[]{:S(2)}, u32[]{:S(2)}) collective-permute-start(bf16[4,4,28,512]{3,2,1,0:T(8,128)(2,1)S(1)} %get-tuple-element.10), channel_id=1, source_target_pairs={{0,1},{1,0},{2,3},{3,2},{4,5},{5,4},{6,7},{7,6},{8,9},{9,8},{10,11... | collective-permute-start | bytes 1376264 | tf_op jit(solution)/shard_map/ppermute | solution.py:15
  34.2 9.6 %all-to-all-start.1 = ((bf16[8,2,6144]{2,1,0:T(2,128)(2,1)}), bf16[8,2,6144]{2,1,0:T(2,128)(2,1)S(1)}, u32[]{:S(2)}, u32[]{:S(2)}) async-start(bf16[8,2,6144]{2,1,0:T(2,128)(2,1)} %reshape.495), calls=%async_computation.1 | async-start | bytes 393216 | tf_op jit(solution)/shard_map/all_to_all | solution.py:104
  47.5 9.6 %all-to-all-start.2 = ((bf16[8,2,6144]{2,1,0:T(2,128)(2,1)}), bf16[8,2,6144]{2,1,0:T(2,128)(2,1)S(1)}, u32[]{:S(2)}, u32[]{:S(2)}) async-start(bf16[8,2,6144]{2,1,0:T(2,128)(2,1)} %reshape.497), calls=%async_computation.2 | async-start | bytes 393216 | tf_op jit(solution)/shard_map/all_to_all | solution.py:111
  51.0 7.4 %copy-start = (bf16[2,2,64,384]{3,2,1,0:T(8,128)(2,1)S(1)}, bf16[2,2,64,384]{3,2,1,0:T(8,128)(2,1)}, u32[]{:S(2)}) copy-start(bf16[2,2,64,384]{3,2,1,0:T(8,128)(2,1)} %param.13) | copy-start | bytes 589828

commit v13 on v12

--- a/solution.py
+++ b/solution.py
@@ -97,23 +97,18 @@
         block_side,
         block_side,
     )
-    remapped = remapped.transpose(2, 3, 0, 4, 1, 5).reshape(
-        member_count, level_count, columns, y_cells
+    remapped = remapped.transpose(2, 3, 1, 5, 0, 4).reshape(
+        member_count, level_count, y_cells, columns
     )
-    difference = (remapped - regional.astype(jnp.float32)).astype(jnp.bfloat16)
-    x_lines = lax.all_to_all(difference, "tile", split_axis=3, concat_axis=2, tiled=True)
+    y_major = regional.transpose(0, 1, 3, 2)
+    difference = (remapped - y_major.astype(jnp.float32)).astype(jnp.bfloat16)
+    x_lines = lax.all_to_all(difference, "tile", split_axis=2, concat_axis=3, tiled=True)
     after_first = jnp.einsum(
-        "ax,mlxy->mlay",
-        x_full,
-        x_lines,
-        preferred_element_type=jnp.float32,
+        "mlyx,ax->mlya", x_lines, x_full, preferred_element_type=jnp.float32
     ).astype(jnp.bfloat16)
-    tile_back = lax.all_to_all(after_first, "tile", split_axis=2, concat_axis=3, tiled=True)
+    tile_back = lax.all_to_all(after_first, "tile", split_axis=3, concat_axis=2, tiled=True)
     after_second = jnp.einsum(
-        "by,mlxy->mlxb",
-        y_full,
-        tile_back,
-        preferred_element_type=jnp.float32,
+        "mlyx,by->mlxb", tile_back, y_full, preferred_element_type=jnp.float32
     )
     return (regional.astype(jnp.float32) + after_second).astype(jnp.bfloat16)
 

time: 59.9 us -> 59.9 us (level)
  no operation moved by 1% of the time
where the time goes in v13:
time: 59.9 us; the launch traced here: 59.3 us
  starting transfers between devices  19.9 us (33%)
  waiting for transfers between devices  17.5 us (29%)
  local copies, waits for them, and re-layouts  13.3 us (22%)
  matrix products  4.2 us (7%)
  other arithmetic  3.99 us (7%)
    ppermute x7, starting transfers between devices, xor_gather(): lax.ppermute(data, axis_name, [(j, j ^ offset) for j in range(count)])  9.24 us
    all_to_all x1, waiting for transfers between devices, body(): lax.all_to_all(difference, 'tile', split_axis=2, concat_axis=3, tiled=True)  6.12 us
    all_to_all x1, waiting for transfers between devices, body(): lax.all_to_all(packed, 'tile', split_axis=0, concat_axis=0, tiled=True)  6.01 us
    all_to_all x1, waiting for transfers between devices, body(): lax.all_to_all(after_first, 'tile', split_axis=3, concat_axis=2, tiled=True)  5.39 us
    all_to_all x1, starting transfers between devices, body(): lax.all_to_all(packed, 'tile', split_axis=0, concat_axis=0, tiled=True)  3.87 us
    all_to_all x1, starting transfers between devices, body(): lax.all_to_all(difference, 'tile', split_axis=2, concat_axis=3, tiled=True)  3.39 us
    all_to_all x1, starting transfers between devices, body(): lax.all_to_all(after_first, 'tile', split_axis=3, concat_axis=2, tiled=True)  3.39 us
    unnamed x14, local copies, waits for them, and re-layouts  3.24 us
  transfers between devices with their start and end apart: 10, of which 3 were waited for; matrix products, arithmetic and copies ran while one was open for 24% of the time, Pallas kernels for 0%

profile of v13, /device:TPU:0, one launch (start us, length us, event | category | flops | bytes accessed | tf_op | source)
XLA Modules:
  0.0 59.3 jit_solution(7641618039227502146)
XLA Ops:
  0.0 0.8 %fusion.30 = (bf16[1,28,512]{2,1,0:T(8,128)(2,1)S(1)}, bf16[28,512]{1,0:T(8,128)(2,1)S(1)}) fusion(bf16[12,384]{1,0:T(8,128)(2,1)} %param.15, bf16[16,512]{1,0:T(8,128)(2,1)} %param.14), kind=kLoop, calls=%fused_computation.83 | loop fusion | flops 86016 | bytes 82944 | tf_op jit(solution)/shard_map/stack | solution.py:16
  0.8 5.0 %collective-permute-start.2 = (bf16[28,512]{1,0:T(8,128)(2,1)S(1)}, bf16[28,512]{1,0:T(8,128)(2,1)S(1)}, u32[]{:S(2)}, u32[]{:S(2)}) collective-permute-start(bf16[28,512]{1,0:T(8,128)(2,1)S(1)} %get-tuple-element.12), channel_id=1, source_target_pairs={{0,24},{8,16},{16,8},{24,0},{1,25},{9,17},{17,9},{25,1},{2,26},{10... | collective-permute-start | bytes 86024 | tf_op jit(solution)/shard_map/ppermute | solution.py:15
  5.8 0.6 %collective-permute-start = (bf16[28,512]{1,0:T(8,128)(2,1)S(1)}, bf16[28,512]{1,0:T(8,128)(2,1)S(1)}, u32[]{:S(2)}, u32[]{:S(2)}) collective-permute-start(bf16[28,512]{1,0:T(8,128)(2,1)S(1)} %get-tuple-element.12), channel_id=1, source_target_pairs={{0,8},{8,0},{16,24},{24,16},{1,9},{9,1},{17,25},{25,17},{2,10},{10... | collective-permute-start | bytes 86024 | tf_op jit(solution)/shard_map/ppermute | solution.py:15
  6.5 1.1 %reshape.467 = bf16[128,1024]{1,0:T(8,128)(2,1)S(1)} reshape(bf16[128,2,2,256]{3,2,1,0:T(2,128)(2,1)} %param.8) | data formatting | bytes 524288 | tf_op jit(solution)/shard_map/reshape | solution.py:75
  7.6 0.8 %eq.39 = s32[192]{0:T(256)S(1)} reshape(s32[1,8,24]{2,1,0:T(8,128)} %param.9) | data formatting | bytes 1536 | tf_op jit(solution)/shard_map/eq | solution.py:71
  8.4 1.1 %convolution_convert_fusion = bf16[192,1024]{1,0:T(8,128)(2,1)} fusion(bf16[128,1024]{1,0:T(8,128)(2,1)S(1)} %reshape.467, s32[192]{0:T(256)S(1)} %eq.39), kind=kOutput, calls=%fused_computation.3 | convolution fusion | flops 50552832 | bytes 656128 | tf_op jit(solution)/shard_map/dot_general | solution.py:74
  9.4 3.9 %all-to-all-start = ((bf16[8,24,1024]{2,1,0:T(8,128)(2,1)}), bf16[8,24,1024]{2,1,0:T(8,128)(2,1)S(1)}, u32[]{:S(2)}, u32[]{:S(2)}) async-start(bf16[8,24,1024]{2,1,0:T(8,128)(2,1)} %bitcast.7), calls=%async_computation | async-start | bytes 786432 | tf_op jit(solution)/shard_map/all_to_all | solution.py:78
  13.4 0.1 iota_compare_fusion.3
  13.5 0.1 lt.42
  13.6 0.1 squeeze.3
  13.8 0.1 eq.36
  13.9 0.1 select_n.135
  13.9 0.1 iota.83
  14.0 0.1 iota.84
  14.1 0.1 select_n.131
  14.2 0.1 select_n.128
  14.3 0.7 %iota.75 = s32[32,1]{0,1:T(1,128)} reshape(s32[4,8]{1,0:T(4,128)S(1)} %iota.74) | data formatting | bytes 256 | tf_op jit(solution)/shard_map/iota | solution.py:50
  14.9 0.7 %pad_maximum_fusion.2 = bf16[4,28,512]{2,1,0:T(8,128)(2,1)} fusion(bf16[1,28,512]{2,1,0:T(8,128)(2,1)S(1)} %bitcast.84, bf16[1,28,512]{2,1,0:T(8,128)(2,1)S(1)} %bitcast.85, bf16[1,28,512]{2,1,0:T(8,128)(2,1)S(1)} %bitcast.86, bf16[1,28,512]{2,1,0:T(8,128)(2,1)S(1)} %get-tuple-element.11), kind=kLoop, calls=%fused_computation.15 | loop fusion | flops 172032 | bytes 229376 | tf_op jit(solution)/shard_map/stack | solution.py:16
  15.6 6.0 %all-to-all-done = bf16[8,24,1024]{2,1,0:T(8,128)(2,1)S(1)} async-done(((bf16[8,24,1024]{2,1,0:T(8,128)(2,1)}), bf16[8,24,1024]{2,1,0:T(8,128)(2,1)S(1)}, u32[]{:S(2)}, u32[]{:S(2)}) %all-to-all-start) | async-done | bytes 393248 | tf_op jit(solution)/shard_map/all_to_all | solution.py:78
  21.6 0.6 collective-permute-start.5
  22.2 1.5 %collective-permute-start.4 = (bf16[4,28,512]{2,1,0:T(8,128)(2,1)}, bf16[4,28,512]{2,1,0:T(8,128)(2,1)}, u32[]{:S(2)}, u32[]{:S(2)}) collective-permute-start(bf16[4,28,512]{2,1,0:T(8,128)(2,1)} %pad_maximum_fusion.2), channel_id=1, source_target_pairs={{0,4},{1,5},{2,6},{3,7},{4,0},{5,1},{6,2},{7,3},{8,12},{9,13},{10,... | collective-permute-start | bytes 344072 | tf_op jit(solution)/shard_map/ppermute | solution.py:15
  23.7 1.5 %collective-permute-start.3 = (bf16[4,28,512]{2,1,0:T(8,128)(2,1)}, bf16[4,28,512]{2,1,0:T(8,128)(2,1)}, u32[]{:S(2)}, u32[]{:S(2)}) collective-permute-start(bf16[4,28,512]{2,1,0:T(8,128)(2,1)} %pad_maximum_fusion.2), channel_id=1, source_target_pairs={{0,2},{1,3},{2,0},{3,1},{4,6},{5,7},{6,4},{7,5},{8,10},{9,11},{10,... | collective-permute-start | bytes 344072 | tf_op jit(solution)/shard_map/ppermute | solution.py:15
  25.1 0.2 copy.16
  25.3 1.8 %convolution_bitcast_fusion = f32[2,2,24,16,4,16]{2,3,5,1,0,4:T(8,128)} fusion(bf16[2,2,16,16,192,1]{4,3,2,1,0,5:T(8,128)(2,1)S(1)} %bitcast.74, bf16[192]{0:T(256)(128)(2,1)S(1)} %broadcast_select_fusion.3, s32[4,24]{1,0:T(4,128)S(1)} %multiply_add_fusion, s32[192]{0:T(256)S(1)} %eq.36), kind=kOutput, calls=%fused_computation.2 | convolution fusion | flops 37785600 | bytes 787968 | tf_op jit(solution)/shard_map/dot_general | solution.py:87
  27.2 2.2 %copy.17 = f32[2,2,24,16,4,16]{3,2,5,4,1,0:T(8,128)S(1)} copy(f32[2,2,24,16,4,16]{2,3,5,1,0,4:T(8,128)} %convolution_bitcast_fusion) | data formatting | bytes 786432 | tf_op jit(solution)/shard_map/transpose | solution.py:100
  29.4 0.9 %reshape.470 = f32[2,2,384,64]{2,3,1,0:T(8,128)S(1)} reshape(f32[2,2,24,16,4,16]{3,2,5,4,1,0:T(8,128)S(1)} %copy.17) | data formatting | bytes 786432 | tf_op jit(solution)/shard_map/reshape | solution.py:100
  30.3 1.2 %fusion.31 = (bf16[1,4,4,28,512]{4,3,2,1,0:T(8,128)(2,1)S(1)}, bf16[4,4,28,512]{3,2,1,0:T(8,128)(2,1)S(1)}) fusion(bf16[1,4,28,512]{3,2,1,0:T(8,128)(2,1)} %bitcast.20, bf16[1,4,28,512]{3,2,1,0:T(8,128)(2,1)} %bitcast.19, bf16[1,4,28,512]{3,2,1,0:T(8,128)(2,1)} %bitcast.18, bf16[1,4,28,512]{3,2,1,0:T(8,128)(2,1)} %bitcast.17), kind=kLoop, calls=%fused_computation.84 | loop fusion | flops 688128 | bytes 1376256 | tf_op jit(solution)/shard_map/stack | solution.py:16
  31.5 0.1 collective-permute-start.6
  31.6 1.0 %fusion.2 = bf16[2,2,384,64]{2,3,1,0:T(8,128)(2,1)S(1)} fusion(f32[2,2,384,64]{2,3,1,0:T(8,128)S(1)} %reshape.470, bf16[2,2,64,384]{3,2,1,0:T(8,128)(2,1)} %param.13), kind=kLoop, calls=%fused_computation.12 | loop fusion | flops 294912 | bytes 786432 | tf_op jit(solution)/shard_map/convert_element_type | solution.py:104
  32.6 0.6 %copy.18 = bf16[2,2,384,64]{3,1,0,2:T(2,128)(2,1)S(1)} copy(bf16[2,2,384,64]{2,3,1,0:T(8,128)(2,1)S(1)} %fusion.2) | data formatting | bytes 393216 | tf_op jit(solution)/shard_map/convert_element_type | solution.py:104
  33.2 1.0 %reshape.495 = bf16[8,2,6144]{2,1,0:T(2,128)(2,1)} reshape(bf16[384,2,2,64]{3,2,1,0:T(2,128)(2,1)S(1)} %bitcast.80) | data formatting | bytes 393216
  34.2 3.4 %all-to-all-start.1 = ((bf16[8,2,6144]{2,1,0:T(2,128)(2,1)}), bf16[8,2,6144]{2,1,0:T(2,128)(2,1)S(1)}, u32[]{:S(2)}, u32[]{:S(2)}) async-start(bf16[8,2,6144]{2,1,0:T(2,128)(2,1)} %reshape.495), calls=%async_computation.1 | async-start | bytes 393216 | tf_op jit(solution)/shard_map/all_to_all | solution.py:105
  37.6 6.1 %all-to-all-done.1 = bf16[8,2,6144]{2,1,0:T(2,128)(2,1)S(1)} async-done(((bf16[8,2,6144]{2,1,0:T(2,128)(2,1)}), bf16[8,2,6144]{2,1,0:T(2,128)(2,1)S(1)}, u32[]{:S(2)}, u32[]{:S(2)}) %all-to-all-start.1) | async-done | bytes 196640 | tf_op jit(solution)/shard_map/all_to_all | solution.py:105
  43.8 0.3 reshape.496
  44.0 0.3 copy.31
  44.3 0.3 all_to_all.33
  44.6 0.1 pad_maximum_fusion
  44.7 0.6 gather_fusion
  45.3 0.3 convolution_convert_fusion.1
  45.7 0.4 copy.21
  46.1 1.4 %reshape.497 = bf16[8,2,6144]{2,1,0:T(2,128)(2,1)} reshape(bf16[512,2,2,48]{3,2,1,0:T(2,128)(2,1)S(1)} %bitcast.76) | data formatting | bytes 393216
  47.5 3.4 %all-to-all-start.2 = ((bf16[8,2,6144]{2,1,0:T(2,128)(2,1)}), bf16[8,2,6144]{2,1,0:T(2,128)(2,1)S(1)}, u32[]{:S(2)}, u32[]{:S(2)}) async-start(bf16[8,2,6144]{2,1,0:T(2,128)(2,1)} %reshape.497), calls=%async_computation.2 | async-start | bytes 393216 | tf_op jit(solution)/shard_map/all_to_all | solution.py:109
  51.0 0.6 %gather_fusion.1 = bf16[32,12,384]{2,1,0:T(8,128)(2,1)S(1)} fusion(bf16[32,12,384]{2,1,0:T(8,128)(2,1)S(1)} %slice.13, s32[1024]{0:T(1024)S(1)} %pad_clamp_fusion), kind=kCustom, calls=%fused_computation.1 | custom fusion | bytes 589952 | tf_op jit(solution)/shard_map/jit(_take)/gather | solution.py:55
  51.7 5.4 %all-to-all-done.2 = bf16[8,2,6144]{2,1,0:T(2,128)(2,1)S(1)} async-done(((bf16[8,2,6144]{2,1,0:T(2,128)(2,1)}), bf16[8,2,6144]{2,1,0:T(2,128)(2,1)S(1)}, u32[]{:S(2)}, u32[]{:S(2)}) %all-to-all-start.2) | async-done | bytes 196640 | tf_op jit(solution)/shard_map/all_to_all | solution.py:109
  57.1 0.5 reshape.498
  57.6 0.3 copy.30
  57.9 0.4 all_to_all.37
  58.3 1.0 %fusion = bf16[2,2,64,384]{3,2,1,0:T(8,128)(2,1)} fusion(bf16[2,2,384,64]{2,3,1,0:T(8,128)(2,1)S(1)} %all_to_all.37, bf16[2,2,64,384]{3,2,1,0:T(8,128)(2,1)S(1)} %copy-done, bf16[384,384,1,1]{1,0,2,3:T(8,128)(2,1)S(1)} %reshape.493), kind=kOutput, calls=%fused_computation.6 | convolution fusion | flops 75792384 | bytes 884736 | tf_op jit(solution)/shard_map/mlyx,by->mlxb/dot_general | solution.py:110
  (36 shorter events, 0.4 us)
Async XLA Ops:
  0.0 13.4 %copy-start.4 = (s32[1,8]{1,0:T(1,128)S(1)}, s32[1,8]{1,0:T(1,128)}, u32[]{:S(2)}) copy-start(s32[1,8]{1,0:T(1,128)} %param.12) | copy-start | bytes 100
  0.0 13.6 %copy-start.2 = (f32[1,8,24]{2,1,0:T(8,128)S(1)}, f32[1,8,24]{2,1,0:T(8,128)}, u32[]{:S(2)}) copy-start(f32[1,8,24]{2,1,0:T(8,128)} %param.11) | copy-start | bytes 2308
  0.0 13.8 %copy-start.1 = (s32[1,8,24]{2,1,0:T(8,128)S(1)}, s32[1,8,24]{2,1,0:T(8,128)}, u32[]{:S(2)}) copy-start(s32[1,8,24]{2,1,0:T(8,128)} %param.10) | copy-start | bytes 2308
  0.8 14.2 %collective-permute-start.2 = (bf16[28,512]{1,0:T(8,128)(2,1)S(1)}, bf16[28,512]{1,0:T(8,128)(2,1)S(1)}, u32[]{:S(2)}, u32[]{:S(2)}) collective-permute-start(bf16[28,512]{1,0:T(8,128)(2,1)S(1)} %get-tuple-element.12), channel_id=1, source_target_pairs={{0,24},{8,16},{16,8},{24,0},{1,25},{9,17},{17,9},{25,1},{2,26},{10... | collective-permute-start | bytes 86024 | tf_op jit(solution)/shard_map/ppermute | solution.py:15
  5.8 9.1 %collective-permute-start.1 = (bf16[28,512]{1,0:T(8,128)(2,1)S(1)}, bf16[28,512]{1,0:T(8,128)(2,1)S(1)}, u32[]{:S(2)}, u32[]{:S(2)}) collective-permute-start(bf16[28,512]{1,0:T(8,128)(2,1)S(1)} %get-tuple-element.12), channel_id=1, source_target_pairs={{0,16},{8,24},{16,0},{24,8},{1,17},{9,25},{17,1},{25,9},{2,18},{10... | collective-permute-start | bytes 86024 | tf_op jit(solution)/shard_map/ppermute | solution.py:15
  5.8 9.1 %collective-permute-start = (bf16[28,512]{1,0:T(8,128)(2,1)S(1)}, bf16[28,512]{1,0:T(8,128)(2,1)S(1)}, u32[]{:S(2)}, u32[]{:S(2)}) collective-permute-start(bf16[28,512]{1,0:T(8,128)(2,1)S(1)} %get-tuple-element.12), channel_id=1, source_target_pairs={{0,8},{8,0},{16,24},{24,16},{1,9},{9,1},{17,25},{25,17},{2,10},{10... | collective-permute-start | bytes 86024 | tf_op jit(solution)/shard_map/ppermute | solution.py:15
  9.4 12.2 %all-to-all-start = ((bf16[8,24,1024]{2,1,0:T(8,128)(2,1)}), bf16[8,24,1024]{2,1,0:T(8,128)(2,1)S(1)}, u32[]{:S(2)}, u32[]{:S(2)}) async-start(bf16[8,24,1024]{2,1,0:T(8,128)(2,1)} %bitcast.7), calls=%async_computation | async-start | bytes 786432 | tf_op jit(solution)/shard_map/all_to_all | solution.py:78
  21.6 8.7 %collective-permute-start.5 = (bf16[4,28,512]{2,1,0:T(8,128)(2,1)}, bf16[4,28,512]{2,1,0:T(8,128)(2,1)}, u32[]{:S(2)}, u32[]{:S(2)}) collective-permute-start(bf16[4,28,512]{2,1,0:T(8,128)(2,1)} %pad_maximum_fusion.2), channel_id=1, source_target_pairs={{0,6},{1,7},{2,4},{3,5},{4,2},{5,3},{6,0},{7,1},{8,14},{9,15},{10,... | collective-permute-start | bytes 344072 | tf_op jit(solution)/shard_map/ppermute | solution.py:15
  22.2 8.1 %collective-permute-start.4 = (bf16[4,28,512]{2,1,0:T(8,128)(2,1)}, bf16[4,28,512]{2,1,0:T(8,128)(2,1)}, u32[]{:S(2)}, u32[]{:S(2)}) collective-permute-start(bf16[4,28,512]{2,1,0:T(8,128)(2,1)} %pad_maximum_fusion.2), channel_id=1, source_target_pairs={{0,4},{1,5},{2,6},{3,7},{4,0},{5,1},{6,2},{7,3},{8,12},{9,13},{10,... | collective-permute-start | bytes 344072 | tf_op jit(solution)/shard_map/ppermute | solution.py:15
  23.7 6.7 %collective-permute-start.3 = (bf16[4,28,512]{2,1,0:T(8,128)(2,1)}, bf16[4,28,512]{2,1,0:T(8,128)(2,1)}, u32[]{:S(2)}, u32[]{:S(2)}) collective-permute-start(bf16[4,28,512]{2,1,0:T(8,128)(2,1)} %pad_maximum_fusion.2), channel_id=1, source_target_pairs={{0,2},{1,3},{2,0},{3,1},{4,6},{5,7},{6,4},{7,5},{8,10},{9,11},{10,... | collective-permute-start | bytes 344072 | tf_op jit(solution)/shard_map/ppermute | solution.py:15
  30.3 7.3 %copy-start.3 = (s32[32,1]{0,1:T(1,128)S(1)}, s32[32,1]{0,1:T(1,128)}, u32[]{:S(2)}) copy-start(s32[32,1]{0,1:T(1,128)} %iota.75) | copy-start | bytes 388
  31.5 13.0 %collective-permute-start.6 = (bf16[4,4,28,512]{3,2,1,0:T(8,128)(2,1)S(1)}, bf16[4,4,28,512]{3,2,1,0:T(8,128)(2,1)S(1)}, u32[]{:S(2)}, u32[]{:S(2)}) collective-permute-start(bf16[4,4,28,512]{3,2,1,0:T(8,128)(2,1)S(1)} %get-tuple-element.10), channel_id=1, source_target_pairs={{0,1},{1,0},{2,3},{3,2},{4,5},{5,4},{6,7},{7,6},{8,9},{9,8},{10,11... | collective-permute-start | bytes 1376264 | tf_op jit(solution)/shard_map/ppermute | solution.py:15
  34.2 9.6 %all-to-all-start.1 = ((bf16[8,2,6144]{2,1,0:T(2,128)(2,1)}), bf16[8,2,6144]{2,1,0:T(2,128)(2,1)S(1)}, u32[]{:S(2)}, u32[]{:S(2)}) async-start(bf16[8,2,6144]{2,1,0:T(2,128)(2,1)} %reshape.495), calls=%async_computation.1 | async-start | bytes 393216 | tf_op jit(solution)/shard_map/all_to_all | solution.py:105
  47.5 9.6 %all-to-all-start.2 = ((bf16[8,2,6144]{2,1,0:T(2,128)(2,1)}), bf16[8,2,6144]{2,1,0:T(2,128)(2,1)S(1)}, u32[]{:S(2)}, u32[]{:S(2)}) async-start(bf16[8,2,6144]{2,1,0:T(2,128)(2,1)} %reshape.497), calls=%async_computation.2 | async-start | bytes 393216 | tf_op jit(solution)/shard_map/all_to_all | solution.py:109
  51.0 7.4 %copy-start = (bf16[2,2,64,384]{3,2,1,0:T(8,128)(2,1)S(1)}, bf16[2,2,64,384]{3,2,1,0:T(8,128)(2,1)}, u32[]{:S(2)}) copy-start(bf16[2,2,64,384]{3,2,1,0:T(8,128)(2,1)} %param.13) | copy-start | bytes 589828

commit v14 on v12

--- a/solution.py
+++ b/solution.py
@@ -44,8 +44,11 @@
     mem_bits = bit_groups([1 << k for k in range(mem_count.bit_length() - 1)])
     tile_bits = bit_groups([1 << k for k in range(1, tile_count.bit_length() - 1)]) + [[1]]
     both = xor_gather(both, "mem", mem_bits)
+    both = xor_gather(both, "tile", tile_bits[:-1])
     both, after = lax.optimization_barrier((both, after))
-    both = xor_gather(both, "tile", tile_bits).reshape(mem_count * tile_count, x_rows + y_rows, width)
+    both = xor_gather(both, "tile", tile_bits[-1:]).reshape(
+        mem_count * tile_count, x_rows + y_rows, width
+    )
     mem_of = lax.broadcasted_iota(jnp.int32, (mem_count, tile_count), 0)
     tile_of = lax.broadcasted_iota(jnp.int32, (mem_count, tile_count), 1)
     position = stacked_position(tile_of ^ lax.axis_index("tile"), tile_bits) * mem_count
@@ -76,7 +79,6 @@
     ).astype(source_blocks.dtype)
     packed = packed.reshape(tile_count, capacity, -1)
     arrived = lax.all_to_all(packed, "tile", split_axis=0, concat_axis=0, tiled=True)
-    x_full, y_full, arrived = gather_operators(x_operator, y_operator, arrived)
     slot_count = columns // block_side * (y_cells // block_side)
     live_mask = lax.broadcasted_iota(jnp.int32, (tile_count, capacity), 1) < recv_count[0][:, None]
     weights = jnp.where(live_mask, recv_weight[0], 0.0).reshape(-1)
@@ -101,6 +103,7 @@
         member_count, level_count, columns, y_cells
     )
     difference = (remapped - regional.astype(jnp.float32)).astype(jnp.bfloat16)
+    x_full, y_full, difference = gather_operators(x_operator, y_operator, difference)
     x_lines = lax.all_to_all(difference, "tile", split_axis=3, concat_axis=2, tiled=True)
     after_first = jnp.einsum(
         "ax,mlxy->mlay",

time: 59.9 us -> 62.8 us (1.048)
  other arithmetic: 3.99 us -> 5.87 us
  waiting for transfers between devices: 17.5 us -> 18.3 us
    ppermute x7, waiting for transfers between devices: 0.02 us -> 6.82 us  [xor_gather(): lax.ppermute(data, axis_name, [(j, j ^ offset) for j in range(count)])]
    all_to_all x1, waiting for transfers between devices: 6.01 us -> 0.01 us  [body(): lax.all_to_all(packed, 'tile', split_axis=0, concat_axis=0, tiled=True)]
    another operation x4, other arithmetic: 2.75 us -> 1.75 us  [xor_gather(): data = jnp.stack(parts)]
    squeeze x1, local copies, waits for them, and re-layouts: 0.08 us -> 0.77 us  [body(): weights = jnp.where(live_mask, recv_weight[0], 0.0).reshape(-1)]
    lt x1, other arithmetic: 0.07 us -> 0.73 us  [body(): lax.broadcasted_iota(jnp.int32, (tile_count, capacity), 1)]
    select_n x3, other arithmetic: 0.08 us -> 0.74 us  [stacked_position(): digit = sum((offset // bit % 2 << k for k, bit in enumerate(group)))]
    unnamed x14 -> x10, local copies, waits for them, and re-layouts: 3.24 us -> 3.23 us
  transfers between devices with their start and end apart: 10 -> 10, of which waited for: 3 -> 5; matrix products, arithmetic and copies ran while one was open for 24% -> 18% of each run, Pallas kernels for 0% -> 0%
where the time goes in v14:
time: 62.8 us; the launch traced here: 62.2 us
  starting transfers between devices  20 us (32%)
  waiting for transfers between devices  18.3 us (29%)
  local copies, waits for them, and re-layouts  13.5 us (21%)
  other arithmetic  5.87 us (9%)
  matrix products  4.21 us (7%)
    ppermute x7, starting transfers between devices, xor_gather(): lax.ppermute(data, axis_name, [(j, j ^ offset) for j in range(count)])  9.31 us
    ppermute x7, waiting for transfers between devices, xor_gather(): lax.ppermute(data, axis_name, [(j, j ^ offset) for j in range(count)])  6.82 us
    all_to_all x1, waiting for transfers between devices, body(): lax.all_to_all(difference, 'tile', split_axis=3, concat_axis=2, tiled=True)  6.13 us
    all_to_all x1, waiting for transfers between devices, body(): lax.all_to_all(after_first, 'tile', split_axis=2, concat_axis=3, tiled=True)  5.39 us
    all_to_all x1, starting transfers between devices, body(): lax.all_to_all(packed, 'tile', split_axis=0, concat_axis=0, tiled=True)  3.94 us
    all_to_all x1, starting transfers between devices, body(): lax.all_to_all(difference, 'tile', split_axis=3, concat_axis=2, tiled=True)  3.39 us
    all_to_all x1, starting transfers between devices, body(): lax.all_to_all(after_first, 'tile', split_axis=2, concat_axis=3, tiled=True)  3.39 us
    unnamed x10, local copies, waits for them, and re-layouts  3.23 us
  transfers between devices with their start and end apart: 10, of which 5 were waited for; matrix products, arithmetic and copies ran while one was open for 18% of the time, Pallas kernels for 0%

profile of v14, /device:TPU:0, one launch (start us, length us, event | category | flops | bytes accessed | tf_op | source)
XLA Modules:
  0.0 62.2 jit_solution(15089793718562013962)
XLA Ops:
  0.0 0.8 %fusion.30 = (bf16[1,28,512]{2,1,0:T(8,128)(2,1)S(1)}, bf16[28,512]{1,0:T(8,128)(2,1)S(1)}) fusion(bf16[12,384]{1,0:T(8,128)(2,1)} %param.15, bf16[16,512]{1,0:T(8,128)(2,1)} %param.14), kind=kLoop, calls=%fused_computation.83 | loop fusion | flops 86016 | bytes 82944 | tf_op jit(solution)/shard_map/stack | solution.py:16
  0.8 3.0 %collective-permute-start = (bf16[28,512]{1,0:T(8,128)(2,1)S(1)}, bf16[28,512]{1,0:T(8,128)(2,1)S(1)}, u32[]{:S(2)}, u32[]{:S(2)}) collective-permute-start(bf16[28,512]{1,0:T(8,128)(2,1)S(1)} %get-tuple-element.12), channel_id=1, source_target_pairs={{0,8},{8,0},{16,24},{24,16},{1,9},{9,1},{17,25},{25,17},{2,10},{10... | collective-permute-start | bytes 86024 | tf_op jit(solution)/shard_map/ppermute | solution.py:15
  3.8 2.6 %collective-permute-start.1 = (bf16[28,512]{1,0:T(8,128)(2,1)S(1)}, bf16[28,512]{1,0:T(8,128)(2,1)S(1)}, u32[]{:S(2)}, u32[]{:S(2)}) collective-permute-start(bf16[28,512]{1,0:T(8,128)(2,1)S(1)} %get-tuple-element.12), channel_id=1, source_target_pairs={{0,16},{8,24},{16,0},{24,8},{1,17},{9,25},{17,1},{25,9},{2,18},{10... | collective-permute-start | bytes 86024 | tf_op jit(solution)/shard_map/ppermute | solution.py:15
  6.4 1.1 %reshape.467 = bf16[128,1024]{1,0:T(8,128)(2,1)S(1)} reshape(bf16[128,2,2,256]{3,2,1,0:T(2,128)(2,1)} %param.8) | data formatting | bytes 524288 | tf_op jit(solution)/shard_map/reshape | solution.py:78
  7.5 0.8 %eq.39 = s32[192]{0:T(256)S(1)} reshape(s32[1,8,24]{2,1,0:T(8,128)} %param.9) | data formatting | bytes 1536 | tf_op jit(solution)/shard_map/eq | solution.py:74
  8.3 1.1 %convolution_convert_fusion = bf16[192,1024]{1,0:T(8,128)(2,1)} fusion(bf16[128,1024]{1,0:T(8,128)(2,1)S(1)} %reshape.467, s32[192]{0:T(256)S(1)} %eq.39), kind=kOutput, calls=%fused_computation.3 | convolution fusion | flops 50552832 | bytes 656128 | tf_op jit(solution)/shard_map/dot_general | solution.py:77
  9.3 3.9 %all-to-all-start = ((bf16[8,24,1024]{2,1,0:T(8,128)(2,1)}), bf16[8,24,1024]{2,1,0:T(8,128)(2,1)S(1)}, u32[]{:S(2)}, u32[]{:S(2)}) async-start(bf16[8,24,1024]{2,1,0:T(8,128)(2,1)} %bitcast.11), calls=%async_computation | async-start | bytes 786432 | tf_op jit(solution)/shard_map/all_to_all | solution.py:81
  13.3 0.7 %iota_compare_fusion.3 = pred[8,24]{1,0:T(8,128)(4,1)S(1)} fusion(s32[8]{0:T(128)} %bitcast.85), kind=kLoop, calls=%fused_computation.28 | loop fusion | flops 192 | bytes 224 | tf_op jit(solution)/shard_map/lt | solution.py:83
  14.1 0.1 lt.42
  14.1 0.8 %squeeze.3 = bf16[192]{0:T(256)(128)(2,1)S(1)} reshape(f32[1,8,24]{2,1,0:T(8,128)} %param.11) | data formatting | bytes 1152 | tf_op jit(solution)/shard_map/squeeze | solution.py:84
  14.9 0.5 compare_select_fusion.10
  15.5 0.5 broadcast_add_fusion
  16.0 2.1 %collective-permute-start.3 = (bf16[4,28,512]{2,1,0:T(8,128)(2,1)S(1)}, bf16[4,28,512]{2,1,0:T(8,128)(2,1)S(1)}, u32[]{:S(2)}, u32[]{:S(2)}) collective-permute-start(bf16[4,28,512]{2,1,0:T(8,128)(2,1)S(1)} %get-tuple-element.10), channel_id=1, source_target_pairs={{0,2},{1,3},{2,0},{3,1},{4,6},{5,7},{6,4},{7,5},{8,10},{9,11},{10,... | collective-permute-start | bytes 344072 | tf_op jit(solution)/shard_map/ppermute | solution.py:15
  18.1 1.5 %collective-permute-start.4 = (bf16[4,28,512]{2,1,0:T(8,128)(2,1)S(1)}, bf16[4,28,512]{2,1,0:T(8,128)(2,1)S(1)}, u32[]{:S(2)}, u32[]{:S(2)}) collective-permute-start(bf16[4,28,512]{2,1,0:T(8,128)(2,1)S(1)} %get-tuple-element.10), channel_id=1, source_target_pairs={{0,4},{1,5},{2,6},{3,7},{4,0},{5,1},{6,2},{7,3},{8,12},{9,13},{10,... | collective-permute-start | bytes 344072 | tf_op jit(solution)/shard_map/ppermute | solution.py:15
  19.6 0.5 compare_and_fusion
  20.2 0.1 select_n.131
  20.4 3.6 %collective-permute-done.3 = bf16[4,28,512]{2,1,0:T(8,128)(2,1)S(1)} collective-permute-done((bf16[4,28,512]{2,1,0:T(8,128)(2,1)S(1)}, bf16[4,28,512]{2,1,0:T(8,128)(2,1)S(1)}, u32[]{:S(2)}, u32[]{:S(2)}) %collective-permute-start.3) | collective-permute-done | bytes 114720 | tf_op jit(solution)/shard_map/ppermute | solution.py:15
  24.0 0.4 collective-permute-done.4
  24.4 2.8 %collective-permute-done.5 = bf16[4,28,512]{2,1,0:T(8,128)(2,1)S(1)} collective-permute-done((bf16[4,28,512]{2,1,0:T(8,128)(2,1)S(1)}, bf16[4,28,512]{2,1,0:T(8,128)(2,1)S(1)}, u32[]{:S(2)}, u32[]{:S(2)}) %collective-permute-start.5) | collective-permute-done | bytes 114720 | tf_op jit(solution)/shard_map/ppermute | solution.py:15
  27.2 0.9 %pad_maximum_fusion.1 = bf16[4,4,28,512]{3,2,1,0:T(8,128)(2,1)} fusion(bf16[1,4,28,512]{3,2,1,0:T(8,128)(2,1)S(1)} %bitcast.81, bf16[1,4,28,512]{3,2,1,0:T(8,128)(2,1)S(1)} %bitcast.80, bf16[1,4,28,512]{3,2,1,0:T(8,128)(2,1)S(1)} %bitcast.79, bf16[1,4,28,512]{3,2,1,0:T(8,128)(2,1)S(1)} %get-tuple-element.9), kind=kLoop, calls=%fused_computation.9 | loop fusion | flops 688128 | bytes 917504 | tf_op jit(solution)/shard_map/stack | solution.py:16
  28.1 0.2 copy.16
  28.3 1.9 %convolution_bitcast_fusion = f32[2,2,4,16,24,16]{4,5,3,1,0,2:T(8,128)} fusion(bf16[2,2,16,16,192,1]{4,3,2,1,0,5:T(8,128)(2,1)S(1)} %bitcast.68, bf16[192]{0:T(256)(128)(2,1)S(1)} %broadcast_select_fusion.3, s32[4,24]{1,0:T(4,128)S(1)} %multiply_add_fusion, s32[192]{0:T(256)S(1)} %eq.36), kind=kOutput, calls=%fused_computation.2 | convolution fusion | flops 37785600 | bytes 787968 | tf_op jit(solution)/shard_map/dot_general | solution.py:89
  30.2 2.2 %copy.17 = f32[2,2,4,16,24,16]{5,4,3,2,1,0:T(8,128)S(1)} copy(f32[2,2,4,16,24,16]{4,5,3,1,0,2:T(8,128)} %convolution_bitcast_fusion) | data formatting | bytes 786432 | tf_op jit(solution)/shard_map/transpose | solution.py:102
  32.4 0.9 %reshape.470 = f32[2,2,64,384]{3,2,1,0:T(8,128)S(1)} reshape(f32[2,2,4,16,24,16]{5,4,3,2,1,0:T(8,128)S(1)} %copy.17) | data formatting | bytes 786432 | tf_op jit(solution)/shard_map/reshape | solution.py:102
  33.3 1.0 %fusion.2 = bf16[2,2,64,384]{3,2,1,0:T(8,128)(2,1)S(1)} fusion(f32[2,2,64,384]{3,2,1,0:T(8,128)S(1)} %reshape.470, bf16[2,2,64,384]{3,2,1,0:T(8,128)(2,1)} %param.13), kind=kLoop, calls=%fused_computation.12 | loop fusion | flops 294912 | bytes 786432 | tf_op jit(solution)/shard_map/convert_element_type | solution.py:105
  34.4 0.7 %broadcast_select_fusion = s32[4,8]{1,0:T(4,128)S(1)} fusion(s32[4]{0:T(128)} %get-tuple-element.13, s32[4]{0:T(128)} %broadcast_add_fusion, pred[4]{0:T(512)(128)(4,1)} %compare_and_fusion), kind=kLoop, calls=%fused_computation.51 | loop fusion | flops 32 | bytes 164 | tf_op jit(solution)/shard_map/jit(floor_divide)/jit(_where)/select_n | solution.py:23
  35.1 0.1 select_n.135
  35.2 0.1 iota.75
  35.4 0.1 iota.84
  35.5 0.6 copy.18
  36.1 1.0 %reshape.495 = bf16[8,2,6144]{2,1,0:T(2,128)(2,1)} reshape(bf16[384,2,2,64]{3,2,1,0:T(2,128)(2,1)S(1)} %bitcast.75) | data formatting | bytes 393216
  37.1 3.4 %all-to-all-start.1 = ((bf16[8,2,6144]{2,1,0:T(2,128)(2,1)}), bf16[8,2,6144]{2,1,0:T(2,128)(2,1)S(1)}, u32[]{:S(2)}, u32[]{:S(2)}) async-start(bf16[8,2,6144]{2,1,0:T(2,128)(2,1)} %reshape.495), calls=%async_computation.1 | async-start | bytes 393216 | tf_op jit(solution)/shard_map/all_to_all | solution.py:107
  40.5 6.1 %all-to-all-done.1 = bf16[8,2,6144]{2,1,0:T(2,128)(2,1)S(1)} async-done(((bf16[8,2,6144]{2,1,0:T(2,128)(2,1)}), bf16[8,2,6144]{2,1,0:T(2,128)(2,1)S(1)}, u32[]{:S(2)}, u32[]{:S(2)}) %all-to-all-start.1) | async-done | bytes 196640 | tf_op jit(solution)/shard_map/all_to_all | solution.py:107
  46.6 0.3 reshape.496
  46.9 0.3 copy.31
  47.2 0.3 all_to_all.33
  47.5 0.1 pad_maximum_fusion
  47.6 0.6 gather_fusion
  48.2 0.3 fusion.1
  48.5 0.4 copy.21
  48.9 1.4 %reshape.497 = bf16[8,2,6144]{2,1,0:T(2,128)(2,1)} reshape(bf16[512,2,2,48]{3,2,1,0:T(2,128)(2,1)S(1)} %bitcast.70) | data formatting | bytes 393216
  50.4 3.4 %all-to-all-start.2 = ((bf16[8,2,6144]{2,1,0:T(2,128)(2,1)}), bf16[8,2,6144]{2,1,0:T(2,128)(2,1)S(1)}, u32[]{:S(2)}, u32[]{:S(2)}) async-start(bf16[8,2,6144]{2,1,0:T(2,128)(2,1)} %reshape.497), calls=%async_computation.2 | async-start | bytes 393216 | tf_op jit(solution)/shard_map/all_to_all | solution.py:114
  53.8 0.6 %gather_fusion.1 = bf16[32,12,384]{2,1,0:T(8,128)(2,1)S(1)} fusion(bf16[32,12,384]{2,1,0:T(8,128)(2,1)S(1)} %slice.13, s32[1024]{0:T(1024)S(1)} %pad_clamp_fusion), kind=kCustom, calls=%fused_computation.1 | custom fusion | bytes 589952 | tf_op jit(solution)/shard_map/jit(_take)/gather | solution.py:58
  54.6 5.4 %all-to-all-done.2 = bf16[8,2,6144]{2,1,0:T(2,128)(2,1)S(1)} async-done(((bf16[8,2,6144]{2,1,0:T(2,128)(2,1)}), bf16[8,2,6144]{2,1,0:T(2,128)(2,1)S(1)}, u32[]{:S(2)}, u32[]{:S(2)}) %all-to-all-start.2) | async-done | bytes 196640 | tf_op jit(solution)/shard_map/all_to_all | solution.py:114
  59.9 0.5 reshape.498
  60.5 0.3 copy.30
  60.8 0.4 all_to_all.37
  61.2 1.0 %fusion = bf16[2,2,64,384]{3,2,1,0:T(8,128)(2,1)} fusion(bf16[2,2,64,384]{3,2,1,0:T(8,128)(2,1)S(1)} %all_to_all.37, bf16[2,2,64,384]{3,2,1,0:T(8,128)(2,1)S(1)} %copy-done.1, bf16[384,384,1,1]{1,0,2,3:T(8,128)(2,1)S(1)} %reshape.493), kind=kOutput, calls=%fused_computation.6 | convolution fusion | flops 75792384 | bytes 884736 | tf_op jit(solution)/shard_map/by,mlxy->mlxb/dot_general | solution.py:115
  (32 shorter events, 0.7 us)
Async XLA Ops:
  0.0 20.2 %copy-start.2 = (s32[1,8,24]{2,1,0:T(8,128)S(1)}, s32[1,8,24]{2,1,0:T(8,128)}, u32[]{:S(2)}) copy-start(s32[1,8,24]{2,1,0:T(8,128)} %param.10) | copy-start | bytes 2308
  0.8 15.2 %collective-permute-start = (bf16[28,512]{1,0:T(8,128)(2,1)S(1)}, bf16[28,512]{1,0:T(8,128)(2,1)S(1)}, u32[]{:S(2)}, u32[]{:S(2)}) collective-permute-start(bf16[28,512]{1,0:T(8,128)(2,1)S(1)} %get-tuple-element.12), channel_id=1, source_target_pairs={{0,8},{8,0},{16,24},{24,16},{1,9},{9,1},{17,25},{25,17},{2,10},{10... | collective-permute-start | bytes 86024 | tf_op jit(solution)/shard_map/ppermute | solution.py:15
  3.8 12.2 %collective-permute-start.1 = (bf16[28,512]{1,0:T(8,128)(2,1)S(1)}, bf16[28,512]{1,0:T(8,128)(2,1)S(1)}, u32[]{:S(2)}, u32[]{:S(2)}) collective-permute-start(bf16[28,512]{1,0:T(8,128)(2,1)S(1)} %get-tuple-element.12), channel_id=1, source_target_pairs={{0,16},{8,24},{16,0},{24,8},{1,17},{9,25},{17,1},{25,9},{2,18},{10... | collective-permute-start | bytes 86024 | tf_op jit(solution)/shard_map/ppermute | solution.py:15
  6.4 9.6 %collective-permute-start.2 = (bf16[28,512]{1,0:T(8,128)(2,1)S(1)}, bf16[28,512]{1,0:T(8,128)(2,1)S(1)}, u32[]{:S(2)}, u32[]{:S(2)}) collective-permute-start(bf16[28,512]{1,0:T(8,128)(2,1)S(1)} %get-tuple-element.12), channel_id=1, source_target_pairs={{0,24},{8,16},{16,8},{24,0},{1,25},{9,17},{17,9},{25,1},{2,26},{10... | collective-permute-start | bytes 86024 | tf_op jit(solution)/shard_map/ppermute | solution.py:15
  9.3 18.8 %all-to-all-start = ((bf16[8,24,1024]{2,1,0:T(8,128)(2,1)}), bf16[8,24,1024]{2,1,0:T(8,128)(2,1)S(1)}, u32[]{:S(2)}, u32[]{:S(2)}) async-start(bf16[8,24,1024]{2,1,0:T(8,128)(2,1)} %bitcast.11), calls=%async_computation | async-start | bytes 786432 | tf_op jit(solution)/shard_map/all_to_all | solution.py:81
  16.0 8.0 %collective-permute-start.3 = (bf16[4,28,512]{2,1,0:T(8,128)(2,1)S(1)}, bf16[4,28,512]{2,1,0:T(8,128)(2,1)S(1)}, u32[]{:S(2)}, u32[]{:S(2)}) collective-permute-start(bf16[4,28,512]{2,1,0:T(8,128)(2,1)S(1)} %get-tuple-element.10), channel_id=1, source_target_pairs={{0,2},{1,3},{2,0},{3,1},{4,6},{5,7},{6,4},{7,5},{8,10},{9,11},{10,... | collective-permute-start | bytes 344072 | tf_op jit(solution)/shard_map/ppermute | solution.py:15
  18.1 6.3 %collective-permute-start.4 = (bf16[4,28,512]{2,1,0:T(8,128)(2,1)S(1)}, bf16[4,28,512]{2,1,0:T(8,128)(2,1)S(1)}, u32[]{:S(2)}, u32[]{:S(2)}) collective-permute-start(bf16[4,28,512]{2,1,0:T(8,128)(2,1)S(1)} %get-tuple-element.10), channel_id=1, source_target_pairs={{0,4},{1,5},{2,6},{3,7},{4,0},{5,1},{6,2},{7,3},{8,12},{9,13},{10,... | collective-permute-start | bytes 344072 | tf_op jit(solution)/shard_map/ppermute | solution.py:15
  19.6 7.7 %collective-permute-start.5 = (bf16[4,28,512]{2,1,0:T(8,128)(2,1)S(1)}, bf16[4,28,512]{2,1,0:T(8,128)(2,1)S(1)}, u32[]{:S(2)}, u32[]{:S(2)}) collective-permute-start(bf16[4,28,512]{2,1,0:T(8,128)(2,1)S(1)} %get-tuple-element.10), channel_id=1, source_target_pairs={{0,6},{1,7},{2,4},{3,5},{4,2},{5,3},{6,0},{7,1},{8,14},{9,15},{10,... | collective-permute-start | bytes 344072 | tf_op jit(solution)/shard_map/ppermute | solution.py:15
  33.3 14.2 %copy-start = (bf16[4,4,28,512]{3,2,1,0:T(8,128)(2,1)S(1)}, bf16[4,4,28,512]{3,2,1,0:T(8,128)(2,1)}, u32[]{:S(2)}) copy-start(bf16[4,4,28,512]{3,2,1,0:T(8,128)(2,1)} %pad_maximum_fusion.1) | copy-start | bytes 1376260
  34.3 13.1 %collective-permute-start.6 = (bf16[4,4,28,512]{3,2,1,0:T(8,128)(2,1)}, bf16[4,4,28,512]{3,2,1,0:T(8,128)(2,1)S(1)}, u32[]{:S(2)}, u32[]{:S(2)}) collective-permute-start(bf16[4,4,28,512]{3,2,1,0:T(8,128)(2,1)} %pad_maximum_fusion.1), channel_id=1, source_target_pairs={{0,1},{1,0},{2,3},{3,2},{4,5},{5,4},{6,7},{7,6},{8,9},{9,8},{10,11... | collective-permute-start | bytes 1376264 | tf_op jit(solution)/shard_map/ppermute | solution.py:15
  37.1 9.6 %all-to-all-start.1 = ((bf16[8,2,6144]{2,1,0:T(2,128)(2,1)}), bf16[8,2,6144]{2,1,0:T(2,128)(2,1)S(1)}, u32[]{:S(2)}, u32[]{:S(2)}) async-start(bf16[8,2,6144]{2,1,0:T(2,128)(2,1)} %reshape.495), calls=%async_computation.1 | async-start | bytes 393216 | tf_op jit(solution)/shard_map/all_to_all | solution.py:107
  50.4 9.6 %all-to-all-start.2 = ((bf16[8,2,6144]{2,1,0:T(2,128)(2,1)}), bf16[8,2,6144]{2,1,0:T(2,128)(2,1)S(1)}, u32[]{:S(2)}, u32[]{:S(2)}) async-start(bf16[8,2,6144]{2,1,0:T(2,128)(2,1)} %reshape.497), calls=%async_computation.2 | async-start | bytes 393216 | tf_op jit(solution)/shard_map/all_to_all | solution.py:114
  53.8 7.4 %copy-start.1 = (bf16[2,2,64,384]{3,2,1,0:T(8,128)(2,1)S(1)}, bf16[2,2,64,384]{3,2,1,0:T(8,128)(2,1)}, u32[]{:S(2)}) copy-start(bf16[2,2,64,384]{3,2,1,0:T(8,128)(2,1)} %param.13) | copy-start | bytes 589828

commit v15 on v12

--- a/solution.py
+++ b/solution.py
@@ -108,11 +108,15 @@
         x_lines,
         preferred_element_type=jnp.float32,
     ).astype(jnp.bfloat16)
-    tile_back = lax.all_to_all(after_first, "tile", split_axis=2, concat_axis=3, tiled=True)
+    y_chunk = y_cells // tile_count
+    outgoing = after_first.reshape(
+        member_count, level_count, tile_count, columns, y_chunk
+    ).transpose(2, 0, 1, 3, 4)
+    tile_back = lax.all_to_all(outgoing, "tile", split_axis=0, concat_axis=0, tiled=True)
     after_second = jnp.einsum(
-        "by,mlxy->mlxb",
-        y_full,
+        "tmlxy,bty->mlxb",
         tile_back,
+        y_full.reshape(y_cells, tile_count, y_chunk),
         preferred_element_type=jnp.float32,
     )
     return (regional.astype(jnp.float32) + after_second).astype(jnp.bfloat16)

time: 59.9 us -> 58.6 us (0.978)
  local copies, waits for them, and re-layouts: 13.3 us -> 12.5 us
  other arithmetic: 3.99 us -> 4.71 us
  waiting for transfers between devices: 17.5 us -> 16.9 us
    convert_element_type x0 -> x1, other arithmetic: none -> 0.72 us  [body(): return (regional.astype(jnp.float32) + after_second).astype(jnp.bfloat16)]
    all_to_all x2 -> x0, local copies, waits for them, and re-layouts: 0.72 us -> none  [body(): lax.all_to_all(after_first, 'tile', split_axis=2, concat_axis=3, tiled=True)]
    another operation x0 -> x1, local copies, waits for them, and re-layouts: none -> 0.69 us  [body(): y_full.reshape(y_cells, tile_count, y_chunk)]
    unnamed x14, local copies, waits for them, and re-layouts: 3.24 us -> 2.56 us
    all_to_all x1, waiting for transfers between devices: 5.39 us -> 4.76 us  [body(): lax.all_to_all(outgoing, 'tile', split_axis=0, concat_axis=0, tiled=True)]
  transfers between devices with their start and end apart: 10 -> 10, of which waited for: 3 -> 3; matrix products, arithmetic and copies ran while one was open for 24% -> 26% of each run, Pallas kernels for 0% -> 0%
where the time goes in v15:
time: 58.6 us; the launch traced here: 58.1 us
  starting transfers between devices  19.9 us (34%)
  waiting for transfers between devices  16.9 us (29%)
  local copies, waits for them, and re-layouts  12.5 us (21%)
  other arithmetic  4.71 us (8%)
  matrix products  3.74 us (6%)
    ppermute x7, starting transfers between devices, xor_gather(): lax.ppermute(data, axis_name, [(j, j ^ offset) for j in range(count)])  9.17 us
    all_to_all x1, waiting for transfers between devices, body(): lax.all_to_all(difference, 'tile', split_axis=3, concat_axis=2, tiled=True)  6.12 us
    all_to_all x1, waiting for transfers between devices, body(): lax.all_to_all(packed, 'tile', split_axis=0, concat_axis=0, tiled=True)  6.01 us
    all_to_all x1, waiting for transfers between devices, body(): lax.all_to_all(outgoing, 'tile', split_axis=0, concat_axis=0, tiled=True)  4.76 us
    all_to_all x1, starting transfers between devices, body(): lax.all_to_all(packed, 'tile', split_axis=0, concat_axis=0, tiled=True)  3.94 us
    all_to_all x1, starting transfers between devices, body(): lax.all_to_all(difference, 'tile', split_axis=3, concat_axis=2, tiled=True)  3.39 us
    all_to_all x1, starting transfers between devices, body(): lax.all_to_all(outgoing, 'tile', split_axis=0, concat_axis=0, tiled=True)  3.39 us
    another operation x4, other arithmetic, xor_gather(): data = jnp.stack(parts)  2.75 us
  transfers between devices with their start and end apart: 10, of which 3 were waited for; matrix products, arithmetic and copies ran while one was open for 26% of the time, Pallas kernels for 0%

profile of v15, /device:TPU:0, one launch (start us, length us, event | category | flops | bytes accessed | tf_op | source)
XLA Modules:
  0.0 58.1 jit_solution(13111498339498469465)
XLA Ops:
  0.0 0.8 %fusion.32 = (bf16[1,28,512]{2,1,0:T(8,128)(2,1)S(1)}, bf16[28,512]{1,0:T(8,128)(2,1)S(1)}) fusion(bf16[12,384]{1,0:T(8,128)(2,1)} %param.15, bf16[16,512]{1,0:T(8,128)(2,1)} %param.14), kind=kLoop, calls=%fused_computation.85 | loop fusion | flops 86016 | bytes 82944 | tf_op jit(solution)/shard_map/stack | solution.py:16
  0.8 4.0 %collective-permute-start.1 = (bf16[28,512]{1,0:T(8,128)(2,1)S(1)}, bf16[28,512]{1,0:T(8,128)(2,1)S(1)}, u32[]{:S(2)}, u32[]{:S(2)}) collective-permute-start(bf16[28,512]{1,0:T(8,128)(2,1)S(1)} %get-tuple-element.12), channel_id=1, source_target_pairs={{0,16},{8,24},{16,0},{24,8},{1,17},{9,25},{17,1},{25,9},{2,18},{10... | collective-permute-start | bytes 86024 | tf_op jit(solution)/shard_map/ppermute | solution.py:15
  4.8 1.6 %collective-permute-start = (bf16[28,512]{1,0:T(8,128)(2,1)S(1)}, bf16[28,512]{1,0:T(8,128)(2,1)S(1)}, u32[]{:S(2)}, u32[]{:S(2)}) collective-permute-start(bf16[28,512]{1,0:T(8,128)(2,1)S(1)} %get-tuple-element.12), channel_id=1, source_target_pairs={{0,8},{8,0},{16,24},{24,16},{1,9},{9,1},{17,25},{25,17},{2,10},{10... | collective-permute-start | bytes 86024 | tf_op jit(solution)/shard_map/ppermute | solution.py:15
  6.4 0.8 %eq.39 = s32[192]{0:T(256)S(1)} reshape(s32[1,8,24]{2,1,0:T(8,128)} %param.9) | data formatting | bytes 1536 | tf_op jit(solution)/shard_map/eq | solution.py:71
  7.2 1.1 %reshape.467 = bf16[128,1024]{1,0:T(8,128)(2,1)S(1)} reshape(bf16[128,2,2,256]{3,2,1,0:T(2,128)(2,1)} %param.8) | data formatting | bytes 524288 | tf_op jit(solution)/shard_map/reshape | solution.py:75
  8.3 1.1 %convolution_convert_fusion = bf16[192,1024]{1,0:T(8,128)(2,1)} fusion(bf16[128,1024]{1,0:T(8,128)(2,1)S(1)} %reshape.467, s32[192]{0:T(256)S(1)} %eq.39), kind=kOutput, calls=%fused_computation.3 | convolution fusion | flops 50552832 | bytes 656128 | tf_op jit(solution)/shard_map/dot_general | solution.py:74
  9.3 3.9 %all-to-all-start = ((bf16[8,24,1024]{2,1,0:T(8,128)(2,1)}), bf16[8,24,1024]{2,1,0:T(8,128)(2,1)S(1)}, u32[]{:S(2)}, u32[]{:S(2)}) async-start(bf16[8,24,1024]{2,1,0:T(8,128)(2,1)} %bitcast.7), calls=%async_computation | async-start | bytes 786432 | tf_op jit(solution)/shard_map/all_to_all | solution.py:78
  13.4 0.1 squeeze.3
  13.5 0.1 iota_compare_fusion.3
  13.6 0.1 lt.42
  13.6 0.1 broadcast_select_fusion
  13.8 0.1 select_n.135
  13.9 0.1 eq.36
  13.9 0.1 select_n.131
  14.0 0.1 select_n.128
  14.1 0.1 iota.75
  14.3 0.7 %iota.84 = s32[32,1]{0,1:T(1,128)} reshape(s32[4,8]{1,0:T(4,128)S(1)} %iota.83) | data formatting | bytes 256 | tf_op jit(solution)/shard_map/iota | solution.py:49
  14.9 0.7 %pad_maximum_fusion.2 = bf16[4,28,512]{2,1,0:T(8,128)(2,1)} fusion(bf16[1,28,512]{2,1,0:T(8,128)(2,1)S(1)} %bitcast.86, bf16[1,28,512]{2,1,0:T(8,128)(2,1)S(1)} %bitcast.84, bf16[1,28,512]{2,1,0:T(8,128)(2,1)S(1)} %bitcast.85, bf16[1,28,512]{2,1,0:T(8,128)(2,1)S(1)} %get-tuple-element.11), kind=kLoop, calls=%fused_computation.17 | loop fusion | flops 172032 | bytes 229376 | tf_op jit(solution)/shard_map/stack | solution.py:16
  15.6 6.0 %all-to-all-done = bf16[8,24,1024]{2,1,0:T(8,128)(2,1)S(1)} async-done(((bf16[8,24,1024]{2,1,0:T(8,128)(2,1)}), bf16[8,24,1024]{2,1,0:T(8,128)(2,1)S(1)}, u32[]{:S(2)}, u32[]{:S(2)}) %all-to-all-start) | async-done | bytes 393248 | tf_op jit(solution)/shard_map/all_to_all | solution.py:78
  21.6 0.6 collective-permute-start.5
  22.2 1.5 %collective-permute-start.4 = (bf16[4,28,512]{2,1,0:T(8,128)(2,1)}, bf16[4,28,512]{2,1,0:T(8,128)(2,1)}, u32[]{:S(2)}, u32[]{:S(2)}) collective-permute-start(bf16[4,28,512]{2,1,0:T(8,128)(2,1)} %pad_maximum_fusion.2), channel_id=1, source_target_pairs={{0,4},{1,5},{2,6},{3,7},{4,0},{5,1},{6,2},{7,3},{8,12},{9,13},{10,... | collective-permute-start | bytes 344072 | tf_op jit(solution)/shard_map/ppermute | solution.py:15
  23.7 1.5 %collective-permute-start.3 = (bf16[4,28,512]{2,1,0:T(8,128)(2,1)}, bf16[4,28,512]{2,1,0:T(8,128)(2,1)}, u32[]{:S(2)}, u32[]{:S(2)}) collective-permute-start(bf16[4,28,512]{2,1,0:T(8,128)(2,1)} %pad_maximum_fusion.2), channel_id=1, source_target_pairs={{0,2},{1,3},{2,0},{3,1},{4,6},{5,7},{6,4},{7,5},{8,10},{9,11},{10,... | collective-permute-start | bytes 344072 | tf_op jit(solution)/shard_map/ppermute | solution.py:15
  25.1 0.2 copy.18
  25.3 1.8 %convolution_bitcast_fusion = f32[2,2,4,16,24,16]{4,5,3,1,0,2:T(8,128)} fusion(bf16[2,2,16,16,192,1]{4,3,2,1,0,5:T(8,128)(2,1)S(1)} %bitcast.75, bf16[192]{0:T(256)(128)(2,1)S(1)} %broadcast_select_fusion.3, s32[4,24]{1,0:T(4,128)S(1)} %multiply_add_fusion, s32[192]{0:T(256)S(1)} %eq.36), kind=kOutput, calls=%fused_computation.2 | convolution fusion | flops 37785600 | bytes 787968 | tf_op jit(solution)/shard_map/dot_general | solution.py:87
  27.2 2.2 %copy.19 = f32[2,2,4,16,24,16]{5,4,3,2,1,0:T(8,128)S(1)} copy(f32[2,2,4,16,24,16]{4,5,3,1,0,2:T(8,128)} %convolution_bitcast_fusion) | data formatting | bytes 786432 | tf_op jit(solution)/shard_map/transpose | solution.py:100
  29.4 0.9 %reshape.470 = f32[2,2,64,384]{3,2,1,0:T(8,128)S(1)} reshape(f32[2,2,4,16,24,16]{5,4,3,2,1,0:T(8,128)S(1)} %copy.19) | data formatting | bytes 786432 | tf_op jit(solution)/shard_map/reshape | solution.py:100
  30.3 1.2 %fusion.33 = (bf16[1,4,4,28,512]{4,3,2,1,0:T(8,128)(2,1)S(1)}, bf16[4,4,28,512]{3,2,1,0:T(8,128)(2,1)S(1)}) fusion(bf16[1,4,28,512]{3,2,1,0:T(8,128)(2,1)} %bitcast.19, bf16[1,4,28,512]{3,2,1,0:T(8,128)(2,1)} %bitcast.18, bf16[1,4,28,512]{3,2,1,0:T(8,128)(2,1)} %bitcast.17, bf16[1,4,28,512]{3,2,1,0:T(8,128)(2,1)} %bitcast.16), kind=kLoop, calls=%fused_computation.86 | loop fusion | flops 688128 | bytes 1376256 | tf_op jit(solution)/shard_map/stack | solution.py:16
  31.5 0.1 collective-permute-start.6
  31.6 1.0 %fusion.3 = bf16[2,2,64,384]{3,2,1,0:T(8,128)(2,1)S(1)} fusion(f32[2,2,64,384]{3,2,1,0:T(8,128)S(1)} %reshape.470, bf16[2,2,64,384]{3,2,1,0:T(8,128)(2,1)} %param.13), kind=kLoop, calls=%fused_computation.12 | loop fusion | flops 294912 | bytes 786432 | tf_op jit(solution)/shard_map/convert_element_type | solution.py:103
  32.6 0.6 %copy.20 = bf16[2,2,64,384]{2,1,0,3:T(2,128)(2,1)S(1)} copy(bf16[2,2,64,384]{3,2,1,0:T(8,128)(2,1)S(1)} %fusion.3) | data formatting | bytes 393216 | tf_op jit(solution)/shard_map/convert_element_type | solution.py:103
  33.2 1.0 %reshape.495 = bf16[8,2,6144]{2,1,0:T(2,128)(2,1)} reshape(bf16[384,2,2,64]{3,2,1,0:T(2,128)(2,1)S(1)} %bitcast.78) | data formatting | bytes 393216
  34.2 3.4 %all-to-all-start.1 = ((bf16[8,2,6144]{2,1,0:T(2,128)(2,1)}), bf16[8,2,6144]{2,1,0:T(2,128)(2,1)S(1)}, u32[]{:S(2)}, u32[]{:S(2)}) async-start(bf16[8,2,6144]{2,1,0:T(2,128)(2,1)} %reshape.495), calls=%async_computation.1 | async-start | bytes 393216 | tf_op jit(solution)/shard_map/all_to_all | solution.py:104
  37.6 6.1 %all-to-all-done.1 = bf16[8,2,6144]{2,1,0:T(2,128)(2,1)S(1)} async-done(((bf16[8,2,6144]{2,1,0:T(2,128)(2,1)}), bf16[8,2,6144]{2,1,0:T(2,128)(2,1)S(1)}, u32[]{:S(2)}, u32[]{:S(2)}) %all-to-all-start.1) | async-done | bytes 196640 | tf_op jit(solution)/shard_map/all_to_all | solution.py:104
  43.8 0.3 reshape.496
  44.0 0.3 copy.45
  44.3 0.3 all_to_all.23
  44.6 0.1 pad_maximum_fusion
  44.7 0.6 %gather_fusion = bf16[32,16,512]{2,1,0:T(8,128)(2,1)S(1)} fusion(bf16[32,16,512]{2,1,0:T(8,128)(2,1)S(1)} %slice.12, s32[1024]{0:T(1024)S(1)} %pad_clamp_fusion), kind=kCustom, calls=%fused_computation | custom fusion | bytes 1048704 | tf_op jit(solution)/shard_map/jit(_take)/gather | solution.py:54
  45.3 0.3 fusion
  45.7 0.2 reshape.473
  46.0 1.0 %reshape.497 = bf16[8,2,6144]{2,1,0:T(2,128)(2,1)} reshape(bf16[8,2,2,48,64]{4,3,2,1,0:T(8,128)(2,1)S(1)} %bitcast.81) | data formatting | bytes 393216
  46.9 3.4 %all-to-all-start.2 = ((bf16[8,2,6144]{2,1,0:T(2,128)(2,1)}), bf16[8,2,6144]{2,1,0:T(2,128)(2,1)S(1)}, u32[]{:S(2)}, u32[]{:S(2)}) async-start(bf16[8,2,6144]{2,1,0:T(2,128)(2,1)} %reshape.497), calls=%async_computation.2 | async-start | bytes 393216 | tf_op jit(solution)/shard_map/all_to_all | solution.py:115
  50.4 0.6 %gather_fusion.1 = bf16[32,12,384]{2,1,0:T(8,128)(2,1)S(1)} fusion(bf16[32,12,384]{2,1,0:T(8,128)(2,1)S(1)} %slice.13, s32[1024]{0:T(1024)S(1)} %pad_clamp_fusion), kind=kCustom, calls=%fused_computation.1 | custom fusion | bytes 589952 | tf_op jit(solution)/shard_map/jit(_take)/gather | solution.py:55
  51.0 0.7 %reshape_reshape.3 = bf16[384,8,48]{2,1,0:T(8,128)(2,1)S(1)} reshape(bf16[32,12,384]{2,1,0:T(8,128)(2,1)S(1)} %gather_fusion.1) | data formatting | bytes 589824 | tf_op jit(solution)/shard_map/reshape;reshape | solution.py:119
  51.7 4.8 %all-to-all-done.2 = bf16[8,2,6144]{2,1,0:T(2,128)(2,1)S(1)} async-done(((bf16[8,2,6144]{2,1,0:T(2,128)(2,1)}), bf16[8,2,6144]{2,1,0:T(2,128)(2,1)S(1)}, u32[]{:S(2)}, u32[]{:S(2)}) %all-to-all-start.2) | async-done | bytes 196640 | tf_op jit(solution)/shard_map/all_to_all | solution.py:115
  56.5 0.3 reshape.498
  56.8 0.5 fusion.1
  57.3 0.7 %fusion.4 = bf16[2,2,64,384]{3,2,1,0:T(8,128)(2,1)} fusion(bf16[2,2,64,384]{3,2,1,0:T(8,128)(2,1)S(1)} %copy-done, f32[2,2,64,384,1]{3,2,0,1,4:T(8,128)S(1)} %fusion.1), kind=kLoop, calls=%fused_computation.13 | loop fusion | flops 294912 | bytes 786432 | tf_op jit(solution)/shard_map/convert_element_type | solution.py:122
  (36 shorter events, 0.4 us)
Async XLA Ops:
  0.0 13.4 %copy-start.2 = (f32[1,8,24]{2,1,0:T(8,128)S(1)}, f32[1,8,24]{2,1,0:T(8,128)}, u32[]{:S(2)}) copy-start(f32[1,8,24]{2,1,0:T(8,128)} %param.11) | copy-start | bytes 2308
  0.0 13.5 %copy-start.4 = (s32[1,8]{1,0:T(1,128)S(1)}, s32[1,8]{1,0:T(1,128)}, u32[]{:S(2)}) copy-start(s32[1,8]{1,0:T(1,128)} %param.12) | copy-start | bytes 100
  0.0 13.9 %copy-start.1 = (s32[1,8,24]{2,1,0:T(8,128)S(1)}, s32[1,8,24]{2,1,0:T(8,128)}, u32[]{:S(2)}) copy-start(s32[1,8,24]{2,1,0:T(8,128)} %param.10) | copy-start | bytes 2308
  0.8 14.1 %collective-permute-start.1 = (bf16[28,512]{1,0:T(8,128)(2,1)S(1)}, bf16[28,512]{1,0:T(8,128)(2,1)S(1)}, u32[]{:S(2)}, u32[]{:S(2)}) collective-permute-start(bf16[28,512]{1,0:T(8,128)(2,1)S(1)} %get-tuple-element.12), channel_id=1, source_target_pairs={{0,16},{8,24},{16,0},{24,8},{1,17},{9,25},{17,1},{25,9},{2,18},{10... | collective-permute-start | bytes 86024 | tf_op jit(solution)/shard_map/ppermute | solution.py:15
  4.8 10.1 %collective-permute-start = (bf16[28,512]{1,0:T(8,128)(2,1)S(1)}, bf16[28,512]{1,0:T(8,128)(2,1)S(1)}, u32[]{:S(2)}, u32[]{:S(2)}) collective-permute-start(bf16[28,512]{1,0:T(8,128)(2,1)S(1)} %get-tuple-element.12), channel_id=1, source_target_pairs={{0,8},{8,0},{16,24},{24,16},{1,9},{9,1},{17,25},{25,17},{2,10},{10... | collective-permute-start | bytes 86024 | tf_op jit(solution)/shard_map/ppermute | solution.py:15
  6.4 8.5 %collective-permute-start.2 = (bf16[28,512]{1,0:T(8,128)(2,1)S(1)}, bf16[28,512]{1,0:T(8,128)(2,1)S(1)}, u32[]{:S(2)}, u32[]{:S(2)}) collective-permute-start(bf16[28,512]{1,0:T(8,128)(2,1)S(1)} %get-tuple-element.12), channel_id=1, source_target_pairs={{0,24},{8,16},{16,8},{24,0},{1,25},{9,17},{17,9},{25,1},{2,26},{10... | collective-permute-start | bytes 86024 | tf_op jit(solution)/shard_map/ppermute | solution.py:15
  9.3 12.3 %all-to-all-start = ((bf16[8,24,1024]{2,1,0:T(8,128)(2,1)}), bf16[8,24,1024]{2,1,0:T(8,128)(2,1)S(1)}, u32[]{:S(2)}, u32[]{:S(2)}) async-start(bf16[8,24,1024]{2,1,0:T(8,128)(2,1)} %bitcast.7), calls=%async_computation | async-start | bytes 786432 | tf_op jit(solution)/shard_map/all_to_all | solution.py:78
  21.6 8.7 %collective-permute-start.5 = (bf16[4,28,512]{2,1,0:T(8,128)(2,1)}, bf16[4,28,512]{2,1,0:T(8,128)(2,1)}, u32[]{:S(2)}, u32[]{:S(2)}) collective-permute-start(bf16[4,28,512]{2,1,0:T(8,128)(2,1)} %pad_maximum_fusion.2), channel_id=1, source_target_pairs={{0,6},{1,7},{2,4},{3,5},{4,2},{5,3},{6,0},{7,1},{8,14},{9,15},{10,... | collective-permute-start | bytes 344072 | tf_op jit(solution)/shard_map/ppermute | solution.py:15
  22.2 8.1 %collective-permute-start.4 = (bf16[4,28,512]{2,1,0:T(8,128)(2,1)}, bf16[4,28,512]{2,1,0:T(8,128)(2,1)}, u32[]{:S(2)}, u32[]{:S(2)}) collective-permute-start(bf16[4,28,512]{2,1,0:T(8,128)(2,1)} %pad_maximum_fusion.2), channel_id=1, source_target_pairs={{0,4},{1,5},{2,6},{3,7},{4,0},{5,1},{6,2},{7,3},{8,12},{9,13},{10,... | collective-permute-start | bytes 344072 | tf_op jit(solution)/shard_map/ppermute | solution.py:15
  23.7 6.7 %collective-permute-start.3 = (bf16[4,28,512]{2,1,0:T(8,128)(2,1)}, bf16[4,28,512]{2,1,0:T(8,128)(2,1)}, u32[]{:S(2)}, u32[]{:S(2)}) collective-permute-start(bf16[4,28,512]{2,1,0:T(8,128)(2,1)} %pad_maximum_fusion.2), channel_id=1, source_target_pairs={{0,2},{1,3},{2,0},{3,1},{4,6},{5,7},{6,4},{7,5},{8,10},{9,11},{10,... | collective-permute-start | bytes 344072 | tf_op jit(solution)/shard_map/ppermute | solution.py:15
  30.3 7.3 %copy-start.3 = (s32[32,1]{0,1:T(1,128)S(1)}, s32[32,1]{0,1:T(1,128)}, u32[]{:S(2)}) copy-start(s32[32,1]{0,1:T(1,128)} %iota.84) | copy-start | bytes 388
  31.5 13.0 %collective-permute-start.6 = (bf16[4,4,28,512]{3,2,1,0:T(8,128)(2,1)S(1)}, bf16[4,4,28,512]{3,2,1,0:T(8,128)(2,1)S(1)}, u32[]{:S(2)}, u32[]{:S(2)}) collective-permute-start(bf16[4,4,28,512]{3,2,1,0:T(8,128)(2,1)S(1)} %get-tuple-element.10), channel_id=1, source_target_pairs={{0,1},{1,0},{2,3},{3,2},{4,5},{5,4},{6,7},{7,6},{8,9},{9,8},{10,11... | collective-permute-start | bytes 1376264 | tf_op jit(solution)/shard_map/ppermute | solution.py:15
  34.2 9.6 %all-to-all-start.1 = ((bf16[8,2,6144]{2,1,0:T(2,128)(2,1)}), bf16[8,2,6144]{2,1,0:T(2,128)(2,1)S(1)}, u32[]{:S(2)}, u32[]{:S(2)}) async-start(bf16[8,2,6144]{2,1,0:T(2,128)(2,1)} %reshape.495), calls=%async_computation.1 | async-start | bytes 393216 | tf_op jit(solution)/shard_map/all_to_all | solution.py:104
  46.9 9.6 %all-to-all-start.2 = ((bf16[8,2,6144]{2,1,0:T(2,128)(2,1)}), bf16[8,2,6144]{2,1,0:T(2,128)(2,1)S(1)}, u32[]{:S(2)}, u32[]{:S(2)}) async-start(bf16[8,2,6144]{2,1,0:T(2,128)(2,1)} %reshape.497), calls=%async_computation.2 | async-start | bytes 393216 | tf_op jit(solution)/shard_map/all_to_all | solution.py:115
  50.4 6.9 %copy-start = (bf16[2,2,64,384]{3,2,1,0:T(8,128)(2,1)S(1)}, bf16[2,2,64,384]{3,2,1,0:T(8,128)(2,1)}, u32[]{:S(2)}) copy-start(bf16[2,2,64,384]{3,2,1,0:T(8,128)(2,1)} %param.13) | copy-start | bytes 589828

commit v16 on v15

--- a/solution.py
+++ b/solution.py
@@ -101,17 +101,17 @@
         member_count, level_count, columns, y_cells
     )
     difference = (remapped - regional.astype(jnp.float32)).astype(jnp.bfloat16)
-    x_lines = lax.all_to_all(difference, "tile", split_axis=3, concat_axis=2, tiled=True)
-    after_first = jnp.einsum(
-        "ax,mlxy->mlay",
-        x_full,
+    y_chunk = y_cells // tile_count
+    sending = difference.reshape(
+        member_count, level_count, columns, tile_count, y_chunk
+    ).transpose(3, 0, 1, 2, 4)
+    x_lines = lax.all_to_all(sending, "tile", split_axis=0, concat_axis=0, tiled=True)
+    outgoing = jnp.einsum(
+        "dmlxy,tadx->tmlay",
         x_lines,
+        x_full.reshape(tile_count, columns, tile_count, columns),
         preferred_element_type=jnp.float32,
     ).astype(jnp.bfloat16)
-    y_chunk = y_cells // tile_count
-    outgoing = after_first.reshape(
-        member_count, level_count, tile_count, columns, y_chunk
-    ).transpose(2, 0, 1, 3, 4)
     tile_back = lax.all_to_all(outgoing, "tile", split_axis=0, concat_axis=0, tiled=True)
     after_second = jnp.einsum(
         "tmlxy,bty->mlxb",

time: 58.6 us -> 59 us (level)
  local copies, waits for them, and re-layouts: 12.5 us -> 13.2 us
  other arithmetic: 4.71 us -> 4.04 us
    reshape x1 -> x2, local copies, waits for them, and re-layouts: 0.87 us -> 3.12 us  [body(): remapped.transpose(2, 3, 0, 4, 1, 5)]
    transpose x1, local copies, waits for them, and re-layouts: 2.25 us -> 0.4 us  [body(): sending = difference.reshape(member_count, level_count, columns, tile_cou...]
    convert_element_type x0 -> x2, local copies, waits for them, and re-layouts: none -> 0.73 us  [the longest x1 0.7 us: body(): return (regional.astype(jnp.float32) + after_second).astype(jnp.bfloat16)]
    convert_element_type x1, other arithmetic: 0.72 us -> 0.04 us  [body(): return (regional.astype(jnp.float32) + after_second).astype(jnp.bfloat16)]
  transfers between devices with their start and end apart: 10 -> 10, of which waited for: 3 -> 3; matrix products, arithmetic and copies ran while one was open for 26% -> 25% of each run, Pallas kernels for 0% -> 0%
where the time goes in v16:
time: 59 us; the launch traced here: 58.4 us
  starting transfers between devices  19.9 us (34%)
  waiting for transfers between devices  16.9 us (29%)
  local copies, waits for them, and re-layouts  13.2 us (22%)
  other arithmetic  4.04 us (7%)
  matrix products  4.01 us (7%)
    ppermute x7, starting transfers between devices, xor_gather(): lax.ppermute(data, axis_name, [(j, j ^ offset) for j in range(count)])  9.17 us
    all_to_all x1, waiting for transfers between devices, body(): lax.all_to_all(sending, 'tile', split_axis=0, concat_axis=0, tiled=True)  6.12 us
    all_to_all x1, waiting for transfers between devices, body(): lax.all_to_all(packed, 'tile', split_axis=0, concat_axis=0, tiled=True)  6.01 us
    all_to_all x1, waiting for transfers between devices, body(): lax.all_to_all(outgoing, 'tile', split_axis=0, concat_axis=0, tiled=True)  4.76 us
    all_to_all x1, starting transfers between devices, body(): lax.all_to_all(packed, 'tile', split_axis=0, concat_axis=0, tiled=True)  3.94 us
    all_to_all x1, starting transfers between devices, body(): lax.all_to_all(sending, 'tile', split_axis=0, concat_axis=0, tiled=True)  3.39 us
    all_to_all x1, starting transfers between devices, body(): lax.all_to_all(outgoing, 'tile', split_axis=0, concat_axis=0, tiled=True)  3.39 us
    reshape x2, local copies, waits for them, and re-layouts, body(): remapped.transpose(2, 3, 0, 4, 1, 5)  3.12 us
  transfers between devices with their start and end apart: 10, of which 3 were waited for; matrix products, arithmetic and copies ran while one was open for 25% of the time, Pallas kernels for 0%

profile of v16, /device:TPU:0, one launch (start us, length us, event | category | flops | bytes accessed | tf_op | source)
XLA Modules:
  0.0 58.4 jit_solution(13342149423435899015)
XLA Ops:
  0.0 0.8 %fusion.34 = (bf16[1,28,512]{2,1,0:T(8,128)(2,1)S(1)}, bf16[28,512]{1,0:T(8,128)(2,1)S(1)}) fusion(bf16[12,384]{1,0:T(8,128)(2,1)} %param.15, bf16[16,512]{1,0:T(8,128)(2,1)} %param.14), kind=kLoop, calls=%fused_computation.85 | loop fusion | flops 86016 | bytes 82944 | tf_op jit(solution)/shard_map/stack | solution.py:16
  0.8 4.0 %collective-permute-start.1 = (bf16[28,512]{1,0:T(8,128)(2,1)S(1)}, bf16[28,512]{1,0:T(8,128)(2,1)S(1)}, u32[]{:S(2)}, u32[]{:S(2)}) collective-permute-start(bf16[28,512]{1,0:T(8,128)(2,1)S(1)} %get-tuple-element.12), channel_id=1, source_target_pairs={{0,16},{8,24},{16,0},{24,8},{1,17},{9,25},{17,1},{25,9},{2,18},{10... | collective-permute-start | bytes 86024 | tf_op jit(solution)/shard_map/ppermute | solution.py:15
  4.8 1.6 %collective-permute-start = (bf16[28,512]{1,0:T(8,128)(2,1)S(1)}, bf16[28,512]{1,0:T(8,128)(2,1)S(1)}, u32[]{:S(2)}, u32[]{:S(2)}) collective-permute-start(bf16[28,512]{1,0:T(8,128)(2,1)S(1)} %get-tuple-element.12), channel_id=1, source_target_pairs={{0,8},{8,0},{16,24},{24,16},{1,9},{9,1},{17,25},{25,17},{2,10},{10... | collective-permute-start | bytes 86024 | tf_op jit(solution)/shard_map/ppermute | solution.py:15
  6.4 0.8 %eq.36 = s32[192]{0:T(256)S(1)} reshape(s32[1,8,24]{2,1,0:T(8,128)} %param.9) | data formatting | bytes 1536 | tf_op jit(solution)/shard_map/eq | solution.py:71
  7.2 1.1 %reshape.464 = bf16[128,1024]{1,0:T(8,128)(2,1)S(1)} reshape(bf16[128,2,2,256]{3,2,1,0:T(2,128)(2,1)} %param.8) | data formatting | bytes 524288 | tf_op jit(solution)/shard_map/reshape | solution.py:75
  8.3 1.1 %convolution_convert_fusion = bf16[192,1024]{1,0:T(8,128)(2,1)} fusion(bf16[128,1024]{1,0:T(8,128)(2,1)S(1)} %reshape.464, s32[192]{0:T(256)S(1)} %eq.36), kind=kOutput, calls=%fused_computation.4 | convolution fusion | flops 50552832 | bytes 656128 | tf_op jit(solution)/shard_map/dot_general | solution.py:74
  9.3 3.9 %all-to-all-start = ((bf16[8,24,1024]{2,1,0:T(8,128)(2,1)}), bf16[8,24,1024]{2,1,0:T(8,128)(2,1)S(1)}, u32[]{:S(2)}, u32[]{:S(2)}) async-start(bf16[8,24,1024]{2,1,0:T(8,128)(2,1)} %bitcast.4), calls=%async_computation | async-start | bytes 786432 | tf_op jit(solution)/shard_map/all_to_all | solution.py:78
  13.4 0.1 squeeze.3
  13.5 0.1 iota_compare_fusion.3
  13.6 0.1 lt.47
  13.6 0.1 broadcast_select_fusion
  13.8 0.1 select_n.133
  13.9 0.1 eq.40
  13.9 0.1 select_n.129
  14.0 0.1 select_n.126
  14.1 0.1 iota.68
  14.2 0.1 iota.76
  14.3 0.7 %iota.77 = s32[32,1]{0,1:T(1,128)} reshape(s32[4,8]{1,0:T(4,128)S(1)} %iota.76) | data formatting | bytes 256 | tf_op jit(solution)/shard_map/iota | solution.py:49
  14.9 0.7 %pad_maximum_fusion.2 = bf16[4,28,512]{2,1,0:T(8,128)(2,1)} fusion(bf16[1,28,512]{2,1,0:T(8,128)(2,1)S(1)} %bitcast.79, bf16[1,28,512]{2,1,0:T(8,128)(2,1)S(1)} %bitcast.77, bf16[1,28,512]{2,1,0:T(8,128)(2,1)S(1)} %bitcast.78, bf16[1,28,512]{2,1,0:T(8,128)(2,1)S(1)} %get-tuple-element.11), kind=kLoop, calls=%fused_computation.17 | loop fusion | flops 172032 | bytes 229376 | tf_op jit(solution)/shard_map/stack | solution.py:16
  15.6 6.0 %all-to-all-done = bf16[8,24,1024]{2,1,0:T(8,128)(2,1)S(1)} async-done(((bf16[8,24,1024]{2,1,0:T(8,128)(2,1)}), bf16[8,24,1024]{2,1,0:T(8,128)(2,1)S(1)}, u32[]{:S(2)}, u32[]{:S(2)}) %all-to-all-start) | async-done | bytes 393248 | tf_op jit(solution)/shard_map/all_to_all | solution.py:78
  21.6 0.6 collective-permute-start.5
  22.2 1.5 %collective-permute-start.4 = (bf16[4,28,512]{2,1,0:T(8,128)(2,1)}, bf16[4,28,512]{2,1,0:T(8,128)(2,1)}, u32[]{:S(2)}, u32[]{:S(2)}) collective-permute-start(bf16[4,28,512]{2,1,0:T(8,128)(2,1)} %pad_maximum_fusion.2), channel_id=1, source_target_pairs={{0,4},{1,5},{2,6},{3,7},{4,0},{5,1},{6,2},{7,3},{8,12},{9,13},{10,... | collective-permute-start | bytes 344072 | tf_op jit(solution)/shard_map/ppermute | solution.py:15
  23.7 1.5 %collective-permute-start.3 = (bf16[4,28,512]{2,1,0:T(8,128)(2,1)}, bf16[4,28,512]{2,1,0:T(8,128)(2,1)}, u32[]{:S(2)}, u32[]{:S(2)}) collective-permute-start(bf16[4,28,512]{2,1,0:T(8,128)(2,1)} %pad_maximum_fusion.2), channel_id=1, source_target_pairs={{0,2},{1,3},{2,0},{3,1},{4,6},{5,7},{6,4},{7,5},{8,10},{9,11},{10,... | collective-permute-start | bytes 344072 | tf_op jit(solution)/shard_map/ppermute | solution.py:15
  25.1 0.2 copy.22
  25.3 1.8 %convolution_bitcast_fusion = f32[2,2,4,16,24,16]{4,5,3,1,0,2:T(8,128)} fusion(bf16[2,2,16,16,192,1]{4,3,2,1,0,5:T(8,128)(2,1)S(1)} %bitcast.70, bf16[192]{0:T(256)(128)(2,1)S(1)} %broadcast_select_fusion.3, s32[4,24]{1,0:T(4,128)S(1)} %multiply_add_fusion, s32[192]{0:T(256)S(1)} %eq.40), kind=kOutput, calls=%fused_computation.2 | convolution fusion | flops 37785600 | bytes 787968 | tf_op jit(solution)/shard_map/dot_general | solution.py:87
  27.2 2.2 %copy.42 = f32[2,2,4,16,24,16]{5,4,3,2,0,1:T(8,128)S(1)} copy(f32[2,2,4,16,24,16]{4,5,3,1,0,2:T(8,128)} %convolution_bitcast_fusion) | data formatting | bytes 786432 | tf_op jit(solution)/shard_map/reshape | solution.py:100
  29.4 0.9 %reshape.493 = f32[2,2,64,384]{3,2,0,1:T(8,128)S(1)} reshape(f32[2,2,4,16,24,16]{5,4,3,2,0,1:T(8,128)S(1)} %copy.42) | data formatting | bytes 786432 | tf_op jit(solution)/shard_map/reshape | solution.py:100
  30.3 1.2 %fusion.35 = (bf16[1,4,4,28,512]{4,3,2,1,0:T(8,128)(2,1)S(1)}, bf16[4,4,28,512]{3,2,1,0:T(8,128)(2,1)S(1)}) fusion(bf16[1,4,28,512]{3,2,1,0:T(8,128)(2,1)} %bitcast.8, bf16[1,4,28,512]{3,2,1,0:T(8,128)(2,1)} %bitcast.7, bf16[1,4,28,512]{3,2,1,0:T(8,128)(2,1)} %bitcast.6, bf16[1,4,28,512]{3,2,1,0:T(8,128)(2,1)} %bitcast.5), kind=kLoop, calls=%fused_computation.86 | loop fusion | flops 688128 | bytes 1376256 | tf_op jit(solution)/shard_map/stack | solution.py:16
  31.5 0.1 collective-permute-start.6
  31.6 1.0 %fusion.5 = bf16[2,2,64,384]{3,2,0,1:T(8,128)(2,1)S(1)} fusion(f32[2,2,64,384]{3,2,0,1:T(8,128)S(1)} %reshape.493, bf16[2,2,64,384]{3,2,1,0:T(8,128)(2,1)} %param.13), kind=kLoop, calls=%fused_computation.14 | loop fusion | flops 294912 | bytes 786432 | tf_op jit(solution)/shard_map/convert_element_type | solution.py:103
  32.6 0.4 reshape.469
  33.1 0.4 copy.26
  33.5 1.0 %reshape.494 = bf16[8,2,6144]{2,1,0:T(2,128)(2,1)} reshape(bf16[8,2,2,48,64]{4,3,2,1,0:T(8,128)(2,1)S(1)} %bitcast.72) | data formatting | bytes 393216
  34.5 3.4 %all-to-all-start.1 = ((bf16[8,2,6144]{2,1,0:T(2,128)(2,1)}), bf16[8,2,6144]{2,1,0:T(2,128)(2,1)S(1)}, u32[]{:S(2)}, u32[]{:S(2)}) async-start(bf16[8,2,6144]{2,1,0:T(2,128)(2,1)} %reshape.494), calls=%async_computation.1 | async-start | bytes 393216 | tf_op jit(solution)/shard_map/all_to_all | solution.py:108
  37.9 6.1 %all-to-all-done.1 = bf16[8,2,6144]{2,1,0:T(2,128)(2,1)S(1)} async-done(((bf16[8,2,6144]{2,1,0:T(2,128)(2,1)}), bf16[8,2,6144]{2,1,0:T(2,128)(2,1)S(1)}, u32[]{:S(2)}, u32[]{:S(2)}) %all-to-all-start.1) | async-done | bytes 196640 | tf_op jit(solution)/shard_map/all_to_all | solution.py:108
  44.0 0.3 reshape.495
  44.3 0.1 pad_maximum_fusion
  44.5 0.6 gather_fusion
  45.1 0.5 reshape_reshape.6
  45.6 0.6 %fusion.1 = bf16[8,2,2,64,48]{3,4,0,2,1:T(8,128)(2,1)S(1)} fusion(bf16[8,64,8,64,1,1]{3,2,1,0,5,4:T(8,128)(2,1)S(1)} %bitcast.74, bf16[8,2,2,48,64]{4,3,2,1,0:T(8,128)(2,1)S(1)} %reshape.495), kind=kOutput, calls=%fused_computation.6 | convolution fusion | flops 100761600 | bytes 917504 | tf_op jit(solution)/shard_map/dmlxy,tadx->tmlay/dot_general | solution.py:109
  46.3 1.0 %reshape.496 = bf16[8,2,6144]{2,1,0:T(2,128)(2,1)} reshape(bf16[8,2,2,48,64]{4,3,2,1,0:T(8,128)(2,1)S(1)} %bitcast.73) | data formatting | bytes 393216
  47.2 3.4 %all-to-all-start.2 = ((bf16[8,2,6144]{2,1,0:T(2,128)(2,1)}), bf16[8,2,6144]{2,1,0:T(2,128)(2,1)S(1)}, u32[]{:S(2)}, u32[]{:S(2)}) async-start(bf16[8,2,6144]{2,1,0:T(2,128)(2,1)} %reshape.496), calls=%async_computation.2 | async-start | bytes 393216 | tf_op jit(solution)/shard_map/all_to_all | solution.py:115
  50.7 0.6 %gather_fusion.1 = bf16[32,12,384]{2,1,0:T(8,128)(2,1)S(1)} fusion(bf16[32,12,384]{2,1,0:T(8,128)(2,1)S(1)} %slice.13, s32[1024]{0:T(1024)S(1)} %pad_clamp_fusion), kind=kCustom, calls=%fused_computation.1 | custom fusion | bytes 589952 | tf_op jit(solution)/shard_map/jit(_take)/gather | solution.py:55
  51.3 0.7 %reshape_reshape.7 = bf16[384,8,48]{2,1,0:T(8,128)(2,1)S(1)} reshape(bf16[32,12,384]{2,1,0:T(8,128)(2,1)S(1)} %gather_fusion.1) | data formatting | bytes 589824 | tf_op jit(solution)/shard_map/reshape;reshape | solution.py:119
  52.0 4.8 %all-to-all-done.2 = bf16[8,2,6144]{2,1,0:T(2,128)(2,1)S(1)} async-done(((bf16[8,2,6144]{2,1,0:T(2,128)(2,1)}), bf16[8,2,6144]{2,1,0:T(2,128)(2,1)S(1)}, u32[]{:S(2)}, u32[]{:S(2)}) %all-to-all-start.2) | async-done | bytes 196640 | tf_op jit(solution)/shard_map/all_to_all | solution.py:115
  56.8 0.3 reshape.497
  57.1 0.5 fusion.3
  57.7 0.7 %copy.32 = bf16[2,2,64,384]{3,2,1,0:T(8,128)(2,1)} copy(bf16[2,2,64,384]{3,2,0,1:T(8,128)(2,1)S(1)} %fusion.6) | data formatting | bytes 393216 | tf_op jit(solution)/shard_map/convert_element_type | solution.py:122
  (37 shorter events, 0.3 us)
Async XLA Ops:
  0.0 13.4 %copy-start.2 = (f32[1,8,24]{2,1,0:T(8,128)S(1)}, f32[1,8,24]{2,1,0:T(8,128)}, u32[]{:S(2)}) copy-start(f32[1,8,24]{2,1,0:T(8,128)} %param.11) | copy-start | bytes 2308
  0.0 13.5 %copy-start.4 = (s32[1,8]{1,0:T(1,128)S(1)}, s32[1,8]{1,0:T(1,128)}, u32[]{:S(2)}) copy-start(s32[1,8]{1,0:T(1,128)} %param.12) | copy-start | bytes 100
  0.0 13.9 %copy-start.1 = (s32[1,8,24]{2,1,0:T(8,128)S(1)}, s32[1,8,24]{2,1,0:T(8,128)}, u32[]{:S(2)}) copy-start(s32[1,8,24]{2,1,0:T(8,128)} %param.10) | copy-start | bytes 2308
  0.8 14.1 %collective-permute-start.1 = (bf16[28,512]{1,0:T(8,128)(2,1)S(1)}, bf16[28,512]{1,0:T(8,128)(2,1)S(1)}, u32[]{:S(2)}, u32[]{:S(2)}) collective-permute-start(bf16[28,512]{1,0:T(8,128)(2,1)S(1)} %get-tuple-element.12), channel_id=1, source_target_pairs={{0,16},{8,24},{16,0},{24,8},{1,17},{9,25},{17,1},{25,9},{2,18},{10... | collective-permute-start | bytes 86024 | tf_op jit(solution)/shard_map/ppermute | solution.py:15
  4.8 10.1 %collective-permute-start = (bf16[28,512]{1,0:T(8,128)(2,1)S(1)}, bf16[28,512]{1,0:T(8,128)(2,1)S(1)}, u32[]{:S(2)}, u32[]{:S(2)}) collective-permute-start(bf16[28,512]{1,0:T(8,128)(2,1)S(1)} %get-tuple-element.12), channel_id=1, source_target_pairs={{0,8},{8,0},{16,24},{24,16},{1,9},{9,1},{17,25},{25,17},{2,10},{10... | collective-permute-start | bytes 86024 | tf_op jit(solution)/shard_map/ppermute | solution.py:15
  6.4 8.5 %collective-permute-start.2 = (bf16[28,512]{1,0:T(8,128)(2,1)S(1)}, bf16[28,512]{1,0:T(8,128)(2,1)S(1)}, u32[]{:S(2)}, u32[]{:S(2)}) collective-permute-start(bf16[28,512]{1,0:T(8,128)(2,1)S(1)} %get-tuple-element.12), channel_id=1, source_target_pairs={{0,24},{8,16},{16,8},{24,0},{1,25},{9,17},{17,9},{25,1},{2,26},{10... | collective-permute-start | bytes 86024 | tf_op jit(solution)/shard_map/ppermute | solution.py:15
  9.3 12.3 %all-to-all-start = ((bf16[8,24,1024]{2,1,0:T(8,128)(2,1)}), bf16[8,24,1024]{2,1,0:T(8,128)(2,1)S(1)}, u32[]{:S(2)}, u32[]{:S(2)}) async-start(bf16[8,24,1024]{2,1,0:T(8,128)(2,1)} %bitcast.4), calls=%async_computation | async-start | bytes 786432 | tf_op jit(solution)/shard_map/all_to_all | solution.py:78
  21.6 8.7 %collective-permute-start.5 = (bf16[4,28,512]{2,1,0:T(8,128)(2,1)}, bf16[4,28,512]{2,1,0:T(8,128)(2,1)}, u32[]{:S(2)}, u32[]{:S(2)}) collective-permute-start(bf16[4,28,512]{2,1,0:T(8,128)(2,1)} %pad_maximum_fusion.2), channel_id=1, source_target_pairs={{0,6},{1,7},{2,4},{3,5},{4,2},{5,3},{6,0},{7,1},{8,14},{9,15},{10,... | collective-permute-start | bytes 344072 | tf_op jit(solution)/shard_map/ppermute | solution.py:15
  22.2 8.1 %collective-permute-start.4 = (bf16[4,28,512]{2,1,0:T(8,128)(2,1)}, bf16[4,28,512]{2,1,0:T(8,128)(2,1)}, u32[]{:S(2)}, u32[]{:S(2)}) collective-permute-start(bf16[4,28,512]{2,1,0:T(8,128)(2,1)} %pad_maximum_fusion.2), channel_id=1, source_target_pairs={{0,4},{1,5},{2,6},{3,7},{4,0},{5,1},{6,2},{7,3},{8,12},{9,13},{10,... | collective-permute-start | bytes 344072 | tf_op jit(solution)/shard_map/ppermute | solution.py:15
  23.7 6.7 %collective-permute-start.3 = (bf16[4,28,512]{2,1,0:T(8,128)(2,1)}, bf16[4,28,512]{2,1,0:T(8,128)(2,1)}, u32[]{:S(2)}, u32[]{:S(2)}) collective-permute-start(bf16[4,28,512]{2,1,0:T(8,128)(2,1)} %pad_maximum_fusion.2), channel_id=1, source_target_pairs={{0,2},{1,3},{2,0},{3,1},{4,6},{5,7},{6,4},{7,5},{8,10},{9,11},{10,... | collective-permute-start | bytes 344072 | tf_op jit(solution)/shard_map/ppermute | solution.py:15
  31.5 6.3 %copy-start.3 = (s32[32,1]{0,1:T(1,128)S(1)}, s32[32,1]{0,1:T(1,128)}, u32[]{:S(2)}) copy-start(s32[32,1]{0,1:T(1,128)} %iota.77) | copy-start | bytes 388
  31.5 12.8 %collective-permute-start.6 = (bf16[4,4,28,512]{3,2,1,0:T(8,128)(2,1)S(1)}, bf16[4,4,28,512]{3,2,1,0:T(8,128)(2,1)S(1)}, u32[]{:S(2)}, u32[]{:S(2)}) collective-permute-start(bf16[4,4,28,512]{3,2,1,0:T(8,128)(2,1)S(1)} %get-tuple-element.10), channel_id=1, source_target_pairs={{0,1},{1,0},{2,3},{3,2},{4,5},{5,4},{6,7},{7,6},{8,9},{9,8},{10,11... | collective-permute-start | bytes 1376264 | tf_op jit(solution)/shard_map/ppermute | solution.py:15
  34.5 9.6 %all-to-all-start.1 = ((bf16[8,2,6144]{2,1,0:T(2,128)(2,1)}), bf16[8,2,6144]{2,1,0:T(2,128)(2,1)S(1)}, u32[]{:S(2)}, u32[]{:S(2)}) async-start(bf16[8,2,6144]{2,1,0:T(2,128)(2,1)} %reshape.494), calls=%async_computation.1 | async-start | bytes 393216 | tf_op jit(solution)/shard_map/all_to_all | solution.py:108
  47.2 9.6 %all-to-all-start.2 = ((bf16[8,2,6144]{2,1,0:T(2,128)(2,1)}), bf16[8,2,6144]{2,1,0:T(2,128)(2,1)S(1)}, u32[]{:S(2)}, u32[]{:S(2)}) async-start(bf16[8,2,6144]{2,1,0:T(2,128)(2,1)} %reshape.496), calls=%async_computation.2 | async-start | bytes 393216 | tf_op jit(solution)/shard_map/all_to_all | solution.py:115
  50.7 6.9 %copy-start = (bf16[2,2,64,384]{3,2,1,0:T(8,128)(2,1)S(1)}, bf16[2,2,64,384]{3,2,1,0:T(8,128)(2,1)}, u32[]{:S(2)}) copy-start(bf16[2,2,64,384]{3,2,1,0:T(8,128)(2,1)} %param.13) | copy-start | bytes 589828

commit v17 on v15

--- a/solution.py
+++ b/solution.py
@@ -102,20 +102,14 @@
     )
     difference = (remapped - regional.astype(jnp.float32)).astype(jnp.bfloat16)
     x_lines = lax.all_to_all(difference, "tile", split_axis=3, concat_axis=2, tiled=True)
-    after_first = jnp.einsum(
-        "ax,mlxy->mlay",
-        x_full,
-        x_lines,
-        preferred_element_type=jnp.float32,
-    ).astype(jnp.bfloat16)
     y_chunk = y_cells // tile_count
-    outgoing = after_first.reshape(
-        member_count, level_count, tile_count, columns, y_chunk
-    ).transpose(2, 0, 1, 3, 4)
+    lines = x_lines.transpose(2, 0, 1, 3).reshape(tile_count * columns, -1)
+    after_first = jnp.dot(x_full, lines, preferred_element_type=jnp.float32).astype(jnp.bfloat16)
+    outgoing = after_first.reshape(tile_count, columns, -1)
     tile_back = lax.all_to_all(outgoing, "tile", split_axis=0, concat_axis=0, tiled=True)
     after_second = jnp.einsum(
-        "tmlxy,bty->mlxb",
-        tile_back,
+        "txmly,bty->mlxb",
+        tile_back.reshape(tile_count, columns, member_count, level_count, y_chunk),
         y_full.reshape(y_cells, tile_count, y_chunk),
         preferred_element_type=jnp.float32,
     )

time: 58.6 us -> 58.8 us (level)
  other arithmetic: 4.71 us -> 3.99 us
  waiting for transfers between devices: 16.9 us -> 17.6 us
  matrix products: 3.74 us -> 4.4 us
    unnamed x14 -> x12, local copies, waits for them, and re-layouts: 2.56 us -> 1.29 us
    convert_element_type x0 -> x1, local copies, waits for them, and re-layouts: none -> 0.84 us  [body(): jnp.dot(x_full, lines, preferred_element_type=jnp.float32)]
    convert_element_type x1 -> x0, other arithmetic: 0.72 us -> none  [body(): return (regional.astype(jnp.float32) + after_second).astype(jnp.bfloat16)]
    all_to_all x1, waiting for transfers between devices: 4.76 us -> 5.48 us  [body(): lax.all_to_all(outgoing, 'tile', split_axis=0, concat_axis=0, tiled=True)]
    dot_general x2, matrix products: 0.84 us -> 1.5 us  [the longest x1 1.17 us: body(): jnp.einsum('txmly,bty->mlxb', tile_back.reshape(tile_count, columns, memb...]
  transfers between devices with their start and end apart: 10 -> 10, of which waited for: 3 -> 3; matrix products, arithmetic and copies ran while one was open for 26% -> 25% of each run, Pallas kernels for 0% -> 0%
where the time goes in v17:
time: 58.8 us; the launch traced here: 58.2 us
  starting transfers between devices  19.9 us (34%)
  waiting for transfers between devices  17.6 us (30%)
  local copies, waits for them, and re-layouts  12 us (20%)
  matrix products  4.4 us (7%)
  other arithmetic  3.99 us (7%)
    ppermute x7, starting transfers between devices, xor_gather(): lax.ppermute(data, axis_name, [(j, j ^ offset) for j in range(count)])  9.17 us
    all_to_all x1, waiting for transfers between devices, body(): lax.all_to_all(difference, 'tile', split_axis=3, concat_axis=2, tiled=True)  6.12 us
    all_to_all x1, waiting for transfers between devices, body(): lax.all_to_all(packed, 'tile', split_axis=0, concat_axis=0, tiled=True)  6.01 us
    all_to_all x1, waiting for transfers between devices, body(): lax.all_to_all(outgoing, 'tile', split_axis=0, concat_axis=0, tiled=True)  5.48 us
    all_to_all x1, starting transfers between devices, body(): lax.all_to_all(packed, 'tile', split_axis=0, concat_axis=0, tiled=True)  3.94 us
    all_to_all x1, starting transfers between devices, body(): lax.all_to_all(outgoing, 'tile', split_axis=0, concat_axis=0, tiled=True)  3.41 us
    all_to_all x1, starting transfers between devices, body(): lax.all_to_all(difference, 'tile', split_axis=3, concat_axis=2, tiled=True)  3.39 us
    another operation x4, other arithmetic, xor_gather(): data = jnp.stack(parts)  2.75 us
  transfers between devices with their start and end apart: 10, of which 3 were waited for; matrix products, arithmetic and copies ran while one was open for 25% of the time, Pallas kernels for 0%

profile of v17, /device:TPU:0, one launch (start us, length us, event | category | flops | bytes accessed | tf_op | source)
XLA Modules:
  0.0 58.2 jit_solution(972652208913009863)
XLA Ops:
  0.0 0.8 %fusion.31 = (bf16[1,28,512]{2,1,0:T(8,128)(2,1)S(1)}, bf16[28,512]{1,0:T(8,128)(2,1)S(1)}) fusion(bf16[12,384]{1,0:T(8,128)(2,1)} %param.15, bf16[16,512]{1,0:T(8,128)(2,1)} %param.14), kind=kLoop, calls=%fused_computation.83 | loop fusion | flops 86016 | bytes 82944 | tf_op jit(solution)/shard_map/stack | solution.py:16
  0.8 4.0 %collective-permute-start.1 = (bf16[28,512]{1,0:T(8,128)(2,1)S(1)}, bf16[28,512]{1,0:T(8,128)(2,1)S(1)}, u32[]{:S(2)}, u32[]{:S(2)}) collective-permute-start(bf16[28,512]{1,0:T(8,128)(2,1)S(1)} %get-tuple-element.12), channel_id=1, source_target_pairs={{0,16},{8,24},{16,0},{24,8},{1,17},{9,25},{17,1},{25,9},{2,18},{10... | collective-permute-start | bytes 86024 | tf_op jit(solution)/shard_map/ppermute | solution.py:15
  4.8 1.6 %collective-permute-start = (bf16[28,512]{1,0:T(8,128)(2,1)S(1)}, bf16[28,512]{1,0:T(8,128)(2,1)S(1)}, u32[]{:S(2)}, u32[]{:S(2)}) collective-permute-start(bf16[28,512]{1,0:T(8,128)(2,1)S(1)} %get-tuple-element.12), channel_id=1, source_target_pairs={{0,8},{8,0},{16,24},{24,16},{1,9},{9,1},{17,25},{25,17},{2,10},{10... | collective-permute-start | bytes 86024 | tf_op jit(solution)/shard_map/ppermute | solution.py:15
  6.4 0.8 %eq.36 = s32[192]{0:T(256)S(1)} reshape(s32[1,8,24]{2,1,0:T(8,128)} %param.9) | data formatting | bytes 1536 | tf_op jit(solution)/shard_map/eq | solution.py:71
  7.2 1.1 %reshape.473 = bf16[128,1024]{1,0:T(8,128)(2,1)S(1)} reshape(bf16[128,2,2,256]{3,2,1,0:T(2,128)(2,1)} %param.8) | data formatting | bytes 524288 | tf_op jit(solution)/shard_map/reshape | solution.py:75
  8.3 1.1 %convolution_convert_fusion = bf16[192,1024]{1,0:T(8,128)(2,1)} fusion(bf16[128,1024]{1,0:T(8,128)(2,1)S(1)} %reshape.473, s32[192]{0:T(256)S(1)} %eq.36), kind=kOutput, calls=%fused_computation.3 | convolution fusion | flops 50552832 | bytes 656128 | tf_op jit(solution)/shard_map/dot_general | solution.py:74
  9.3 3.9 %all-to-all-start = ((bf16[8,24,1024]{2,1,0:T(8,128)(2,1)}), bf16[8,24,1024]{2,1,0:T(8,128)(2,1)S(1)}, u32[]{:S(2)}, u32[]{:S(2)}) async-start(bf16[8,24,1024]{2,1,0:T(8,128)(2,1)} %bitcast.4), calls=%async_computation | async-start | bytes 786432 | tf_op jit(solution)/shard_map/all_to_all | solution.py:78
  13.4 0.1 squeeze.3
  13.5 0.1 iota_compare_fusion.3
  13.6 0.1 lt.47
  13.6 0.1 broadcast_select_fusion
  13.8 0.1 select_n.133
  13.9 0.1 eq.40
  13.9 0.1 select_n.129
  14.0 0.1 select_n.126
  14.1 0.1 iota.68
  14.2 0.1 iota.76
  14.3 0.7 %iota.77 = s32[32,1]{0,1:T(1,128)} reshape(s32[4,8]{1,0:T(4,128)S(1)} %iota.76) | data formatting | bytes 256 | tf_op jit(solution)/shard_map/iota | solution.py:49
  14.9 0.7 %pad_maximum_fusion.2 = bf16[4,28,512]{2,1,0:T(8,128)(2,1)} fusion(bf16[1,28,512]{2,1,0:T(8,128)(2,1)S(1)} %bitcast.77, bf16[1,28,512]{2,1,0:T(8,128)(2,1)S(1)} %bitcast.75, bf16[1,28,512]{2,1,0:T(8,128)(2,1)S(1)} %bitcast.76, bf16[1,28,512]{2,1,0:T(8,128)(2,1)S(1)} %get-tuple-element.11), kind=kLoop, calls=%fused_computation.15 | loop fusion | flops 172032 | bytes 229376 | tf_op jit(solution)/shard_map/stack | solution.py:16
  15.6 6.0 %all-to-all-done = bf16[8,24,1024]{2,1,0:T(8,128)(2,1)S(1)} async-done(((bf16[8,24,1024]{2,1,0:T(8,128)(2,1)}), bf16[8,24,1024]{2,1,0:T(8,128)(2,1)S(1)}, u32[]{:S(2)}, u32[]{:S(2)}) %all-to-all-start) | async-done | bytes 393248 | tf_op jit(solution)/shard_map/all_to_all | solution.py:78
  21.6 0.6 collective-permute-start.5
  22.2 1.5 %collective-permute-start.4 = (bf16[4,28,512]{2,1,0:T(8,128)(2,1)}, bf16[4,28,512]{2,1,0:T(8,128)(2,1)}, u32[]{:S(2)}, u32[]{:S(2)}) collective-permute-start(bf16[4,28,512]{2,1,0:T(8,128)(2,1)} %pad_maximum_fusion.2), channel_id=1, source_target_pairs={{0,4},{1,5},{2,6},{3,7},{4,0},{5,1},{6,2},{7,3},{8,12},{9,13},{10,... | collective-permute-start | bytes 344072 | tf_op jit(solution)/shard_map/ppermute | solution.py:15
  23.7 1.5 %collective-permute-start.3 = (bf16[4,28,512]{2,1,0:T(8,128)(2,1)}, bf16[4,28,512]{2,1,0:T(8,128)(2,1)}, u32[]{:S(2)}, u32[]{:S(2)}) collective-permute-start(bf16[4,28,512]{2,1,0:T(8,128)(2,1)} %pad_maximum_fusion.2), channel_id=1, source_target_pairs={{0,2},{1,3},{2,0},{3,1},{4,6},{5,7},{6,4},{7,5},{8,10},{9,11},{10,... | collective-permute-start | bytes 344072 | tf_op jit(solution)/shard_map/ppermute | solution.py:15
  25.1 0.2 copy.18
  25.3 1.8 %convolution_bitcast_fusion = f32[2,2,4,16,24,16]{4,5,3,1,0,2:T(8,128)} fusion(bf16[2,2,16,16,192,1]{4,3,2,1,0,5:T(8,128)(2,1)S(1)} %bitcast.65, bf16[192]{0:T(256)(128)(2,1)S(1)} %broadcast_select_fusion.3, s32[4,24]{1,0:T(4,128)S(1)} %multiply_add_fusion, s32[192]{0:T(256)S(1)} %eq.40), kind=kOutput, calls=%fused_computation.2 | convolution fusion | flops 37785600 | bytes 787968 | tf_op jit(solution)/shard_map/dot_general | solution.py:87
  27.2 2.2 %copy.19 = f32[2,2,4,16,24,16]{5,4,3,2,1,0:T(8,128)S(1)} copy(f32[2,2,4,16,24,16]{4,5,3,1,0,2:T(8,128)} %convolution_bitcast_fusion) | data formatting | bytes 786432 | tf_op jit(solution)/shard_map/transpose | solution.py:100
  29.4 0.9 %reshape.478 = f32[2,2,64,384]{3,2,1,0:T(8,128)S(1)} reshape(f32[2,2,4,16,24,16]{5,4,3,2,1,0:T(8,128)S(1)} %copy.19) | data formatting | bytes 786432 | tf_op jit(solution)/shard_map/reshape | solution.py:100
  30.3 1.2 %fusion.32 = (bf16[1,4,4,28,512]{4,3,2,1,0:T(8,128)(2,1)S(1)}, bf16[4,4,28,512]{3,2,1,0:T(8,128)(2,1)S(1)}) fusion(bf16[1,4,28,512]{3,2,1,0:T(8,128)(2,1)} %bitcast.8, bf16[1,4,28,512]{3,2,1,0:T(8,128)(2,1)} %bitcast.7, bf16[1,4,28,512]{3,2,1,0:T(8,128)(2,1)} %bitcast.6, bf16[1,4,28,512]{3,2,1,0:T(8,128)(2,1)} %bitcast.5), kind=kLoop, calls=%fused_computation.84 | loop fusion | flops 688128 | bytes 1376256 | tf_op jit(solution)/shard_map/stack | solution.py:16
  31.5 0.1 collective-permute-start.6
  31.6 1.0 %fusion.3 = bf16[2,2,64,384]{3,2,1,0:T(8,128)(2,1)S(1)} fusion(f32[2,2,64,384]{3,2,1,0:T(8,128)S(1)} %reshape.478, bf16[2,2,64,384]{3,2,1,0:T(8,128)(2,1)} %param.13), kind=kLoop, calls=%fused_computation.12 | loop fusion | flops 294912 | bytes 786432 | tf_op jit(solution)/shard_map/convert_element_type | solution.py:103
  32.6 0.6 %copy.20 = bf16[2,2,64,384]{2,1,0,3:T(2,128)(2,1)S(1)} copy(bf16[2,2,64,384]{3,2,1,0:T(8,128)(2,1)S(1)} %fusion.3) | data formatting | bytes 393216 | tf_op jit(solution)/shard_map/convert_element_type | solution.py:103
  33.2 1.0 %reshape.502 = bf16[8,2,6144]{2,1,0:T(2,128)(2,1)} reshape(bf16[384,2,2,64]{3,2,1,0:T(2,128)(2,1)S(1)} %bitcast.68) | data formatting | bytes 393216
  34.2 3.4 %all-to-all-start.1 = ((bf16[8,2,6144]{2,1,0:T(2,128)(2,1)}), bf16[8,2,6144]{2,1,0:T(2,128)(2,1)S(1)}, u32[]{:S(2)}, u32[]{:S(2)}) async-start(bf16[8,2,6144]{2,1,0:T(2,128)(2,1)} %reshape.502), calls=%async_computation.1 | async-start | bytes 393216 | tf_op jit(solution)/shard_map/all_to_all | solution.py:104
  37.6 6.1 %all-to-all-done.1 = bf16[8,2,6144]{2,1,0:T(2,128)(2,1)S(1)} async-done(((bf16[8,2,6144]{2,1,0:T(2,128)(2,1)}), bf16[8,2,6144]{2,1,0:T(2,128)(2,1)S(1)}, u32[]{:S(2)}, u32[]{:S(2)}) %all-to-all-start.1) | async-done | bytes 196640 | tf_op jit(solution)/shard_map/all_to_all | solution.py:104
  43.8 0.3 reshape.503
  44.0 0.3 copy.39
  44.3 0.3 all_to_all.23
  44.6 0.1 pad_maximum_fusion
  44.7 0.6 gather_fusion.1
  45.3 0.3 convolution_convert_fusion.1
  45.7 0.0 copy-start
  45.7 0.8 %copy.23 = bf16[512,192]{1,0:T(8,128)(2,1)} copy(bf16[512,192]{0,1:T(8,128)(2,1)S(1)} %convolution_convert_fusion.1) | data formatting | bytes 393216 | tf_op jit(solution)/shard_map/convert_element_type | solution.py:107
  46.5 3.4 %all-to-all-start.2 = ((bf16[8,64,192]{2,1,0:T(8,128)(2,1)}), bf16[8,64,192]{2,1,0:T(8,128)(2,1)S(1)}, u32[]{:S(2)}, u32[]{:S(2)}) async-start(bf16[8,64,192]{2,1,0:T(8,128)(2,1)} %bitcast.28), calls=%async_computation.2 | async-start | bytes 524288 | tf_op jit(solution)/shard_map/all_to_all | solution.py:109
  50.0 0.6 %gather_fusion = bf16[32,12,384]{2,1,0:T(8,128)(2,1)S(1)} fusion(bf16[32,12,384]{2,1,0:T(8,128)(2,1)S(1)} %slice.12, s32[1024]{0:T(1024)S(1)} %pad_clamp_fusion), kind=kCustom, calls=%fused_computation | custom fusion | bytes 589952 | tf_op jit(solution)/shard_map/jit(_take)/gather | solution.py:55
  50.6 0.7 %reshape_reshape.3 = bf16[384,8,48]{2,1,0:T(8,128)(2,1)S(1)} reshape(bf16[32,12,384]{2,1,0:T(8,128)(2,1)S(1)} %gather_fusion) | data formatting | bytes 589824 | tf_op jit(solution)/shard_map/reshape;reshape | solution.py:113
  51.3 5.5 %all-to-all-done.2 = bf16[8,64,192]{2,1,0:T(8,128)(2,1)S(1)} async-done(((bf16[8,64,192]{2,1,0:T(8,128)(2,1)}), bf16[8,64,192]{2,1,0:T(8,128)(2,1)S(1)}, u32[]{:S(2)}, u32[]{:S(2)}) %all-to-all-start.2) | async-done | bytes 196640 | tf_op jit(solution)/shard_map/all_to_all | solution.py:109
  56.8 0.2 copy.24
  57.0 1.2 %fusion.1 = bf16[2,2,64,384]{3,2,1,0:T(8,128)(2,1)} fusion(bf16[384,8,48,1,1]{2,1,0,4,3:T(8,128)(2,1)S(1)} %bitcast.71, bf16[2,2,64,384]{3,2,1,0:T(8,128)(2,1)S(1)} %copy-done, bf16[8,64,2,2,48]{1,4,3,2,0:T(8,128)(2,1)S(1)} %bitcast.74), kind=kOutput, calls=%fused_computation.6 | convolution fusion | flops 75792384 | bytes 884736 | tf_op jit(solution)/shard_map/txmly,bty->mlxb/dot_general | solution.py:110
  (33 shorter events, 0.2 us)
Async XLA Ops:
  0.0 13.4 %copy-start.2 = (f32[1,8,24]{2,1,0:T(8,128)S(1)}, f32[1,8,24]{2,1,0:T(8,128)}, u32[]{:S(2)}) copy-start(f32[1,8,24]{2,1,0:T(8,128)} %param.11) | copy-start | bytes 2308
  0.0 13.5 %copy-start.4 = (s32[1,8]{1,0:T(1,128)S(1)}, s32[1,8]{1,0:T(1,128)}, u32[]{:S(2)}) copy-start(s32[1,8]{1,0:T(1,128)} %param.12) | copy-start | bytes 100
  0.0 13.9 %copy-start.1 = (s32[1,8,24]{2,1,0:T(8,128)S(1)}, s32[1,8,24]{2,1,0:T(8,128)}, u32[]{:S(2)}) copy-start(s32[1,8,24]{2,1,0:T(8,128)} %param.10) | copy-start | bytes 2308
  0.8 14.1 %collective-permute-start.1 = (bf16[28,512]{1,0:T(8,128)(2,1)S(1)}, bf16[28,512]{1,0:T(8,128)(2,1)S(1)}, u32[]{:S(2)}, u32[]{:S(2)}) collective-permute-start(bf16[28,512]{1,0:T(8,128)(2,1)S(1)} %get-tuple-element.12), channel_id=1, source_target_pairs={{0,16},{8,24},{16,0},{24,8},{1,17},{9,25},{17,1},{25,9},{2,18},{10... | collective-permute-start | bytes 86024 | tf_op jit(solution)/shard_map/ppermute | solution.py:15
  4.8 10.1 %collective-permute-start = (bf16[28,512]{1,0:T(8,128)(2,1)S(1)}, bf16[28,512]{1,0:T(8,128)(2,1)S(1)}, u32[]{:S(2)}, u32[]{:S(2)}) collective-permute-start(bf16[28,512]{1,0:T(8,128)(2,1)S(1)} %get-tuple-element.12), channel_id=1, source_target_pairs={{0,8},{8,0},{16,24},{24,16},{1,9},{9,1},{17,25},{25,17},{2,10},{10... | collective-permute-start | bytes 86024 | tf_op jit(solution)/shard_map/ppermute | solution.py:15
  6.4 8.5 %collective-permute-start.2 = (bf16[28,512]{1,0:T(8,128)(2,1)S(1)}, bf16[28,512]{1,0:T(8,128)(2,1)S(1)}, u32[]{:S(2)}, u32[]{:S(2)}) collective-permute-start(bf16[28,512]{1,0:T(8,128)(2,1)S(1)} %get-tuple-element.12), channel_id=1, source_target_pairs={{0,24},{8,16},{16,8},{24,0},{1,25},{9,17},{17,9},{25,1},{2,26},{10... | collective-permute-start | bytes 86024 | tf_op jit(solution)/shard_map/ppermute | solution.py:15
  9.3 12.3 %all-to-all-start = ((bf16[8,24,1024]{2,1,0:T(8,128)(2,1)}), bf16[8,24,1024]{2,1,0:T(8,128)(2,1)S(1)}, u32[]{:S(2)}, u32[]{:S(2)}) async-start(bf16[8,24,1024]{2,1,0:T(8,128)(2,1)} %bitcast.4), calls=%async_computation | async-start | bytes 786432 | tf_op jit(solution)/shard_map/all_to_all | solution.py:78
  21.6 8.7 %collective-permute-start.5 = (bf16[4,28,512]{2,1,0:T(8,128)(2,1)}, bf16[4,28,512]{2,1,0:T(8,128)(2,1)}, u32[]{:S(2)}, u32[]{:S(2)}) collective-permute-start(bf16[4,28,512]{2,1,0:T(8,128)(2,1)} %pad_maximum_fusion.2), channel_id=1, source_target_pairs={{0,6},{1,7},{2,4},{3,5},{4,2},{5,3},{6,0},{7,1},{8,14},{9,15},{10,... | collective-permute-start | bytes 344072 | tf_op jit(solution)/shard_map/ppermute | solution.py:15
  22.2 8.1 %collective-permute-start.4 = (bf16[4,28,512]{2,1,0:T(8,128)(2,1)}, bf16[4,28,512]{2,1,0:T(8,128)(2,1)}, u32[]{:S(2)}, u32[]{:S(2)}) collective-permute-start(bf16[4,28,512]{2,1,0:T(8,128)(2,1)} %pad_maximum_fusion.2), channel_id=1, source_target_pairs={{0,4},{1,5},{2,6},{3,7},{4,0},{5,1},{6,2},{7,3},{8,12},{9,13},{10,... | collective-permute-start | bytes 344072 | tf_op jit(solution)/shard_map/ppermute | solution.py:15
  23.7 6.7 %collective-permute-start.3 = (bf16[4,28,512]{2,1,0:T(8,128)(2,1)}, bf16[4,28,512]{2,1,0:T(8,128)(2,1)}, u32[]{:S(2)}, u32[]{:S(2)}) collective-permute-start(bf16[4,28,512]{2,1,0:T(8,128)(2,1)} %pad_maximum_fusion.2), channel_id=1, source_target_pairs={{0,2},{1,3},{2,0},{3,1},{4,6},{5,7},{6,4},{7,5},{8,10},{9,11},{10,... | collective-permute-start | bytes 344072 | tf_op jit(solution)/shard_map/ppermute | solution.py:15
  30.3 7.3 %copy-start.3 = (s32[32,1]{0,1:T(1,128)S(1)}, s32[32,1]{0,1:T(1,128)}, u32[]{:S(2)}) copy-start(s32[32,1]{0,1:T(1,128)} %iota.77) | copy-start | bytes 388
  31.5 13.0 %collective-permute-start.6 = (bf16[4,4,28,512]{3,2,1,0:T(8,128)(2,1)S(1)}, bf16[4,4,28,512]{3,2,1,0:T(8,128)(2,1)S(1)}, u32[]{:S(2)}, u32[]{:S(2)}) collective-permute-start(bf16[4,4,28,512]{3,2,1,0:T(8,128)(2,1)S(1)} %get-tuple-element.10), channel_id=1, source_target_pairs={{0,1},{1,0},{2,3},{3,2},{4,5},{5,4},{6,7},{7,6},{8,9},{9,8},{10,11... | collective-permute-start | bytes 1376264 | tf_op jit(solution)/shard_map/ppermute | solution.py:15
  34.2 9.6 %all-to-all-start.1 = ((bf16[8,2,6144]{2,1,0:T(2,128)(2,1)}), bf16[8,2,6144]{2,1,0:T(2,128)(2,1)S(1)}, u32[]{:S(2)}, u32[]{:S(2)}) async-start(bf16[8,2,6144]{2,1,0:T(2,128)(2,1)} %reshape.502), calls=%async_computation.1 | async-start | bytes 393216 | tf_op jit(solution)/shard_map/all_to_all | solution.py:104
  45.7 11.4 %copy-start = (bf16[2,2,64,384]{3,2,1,0:T(8,128)(2,1)S(1)}, bf16[2,2,64,384]{3,2,1,0:T(8,128)(2,1)}, u32[]{:S(2)}) copy-start(bf16[2,2,64,384]{3,2,1,0:T(8,128)(2,1)} %param.13) | copy-start | bytes 589828
  46.5 10.3 %all-to-all-start.2 = ((bf16[8,64,192]{2,1,0:T(8,128)(2,1)}), bf16[8,64,192]{2,1,0:T(8,128)(2,1)S(1)}, u32[]{:S(2)}, u32[]{:S(2)}) async-start(bf16[8,64,192]{2,1,0:T(8,128)(2,1)} %bitcast.28), calls=%async_computation.2 | async-start | bytes 524288 | tf_op jit(solution)/shard_map/all_to_all | solution.py:109

commit v18 on v15

--- a/solution.py
+++ b/solution.py
@@ -43,8 +43,8 @@
     )
     mem_bits = bit_groups([1 << k for k in range(mem_count.bit_length() - 1)])
     tile_bits = bit_groups([1 << k for k in range(1, tile_count.bit_length() - 1)]) + [[1]]
+    both, after = lax.optimization_barrier((both, after))
     both = xor_gather(both, "mem", mem_bits)
-    both, after = lax.optimization_barrier((both, after))
     both = xor_gather(both, "tile", tile_bits).reshape(mem_count * tile_count, x_rows + y_rows, width)
     mem_of = lax.broadcasted_iota(jnp.int32, (mem_count, tile_count), 0)
     tile_of = lax.broadcasted_iota(jnp.int32, (mem_count, tile_count), 1)

time: 58.6 us -> 62.5 us (1.067)
  waiting for transfers between devices: 16.9 us -> 19.5 us
  other arithmetic: 4.71 us -> 5.38 us
    ppermute x7, waiting for transfers between devices: 0.02 us -> 2.76 us  [xor_gather(): lax.ppermute(data, axis_name, [(j, j ^ offset) for j in range(count)])]
    ppermute x7, starting transfers between devices: 9.17 us -> 7.95 us  [xor_gather(): lax.ppermute(data, axis_name, [(j, j ^ offset) for j in range(count)])]
    all_to_all x1, starting transfers between devices: 3.94 us -> 5.17 us  [body(): lax.all_to_all(packed, 'tile', split_axis=0, concat_axis=0, tiled=True)]
    concatenate x0 -> x1, other arithmetic: none -> 0.74 us  [gather_operators(): jnp.concatenate([jnp.pad(x_operator, ((0, 0), (0, width - x_cols))), jnp....]
    another operation x4 -> x3, other arithmetic: 2.75 us -> 2.02 us  [xor_gather(): data = jnp.stack(parts)]
    squeeze x1, local copies, waits for them, and re-layouts: 0.08 us -> 0.76 us  [body(): weights = jnp.where(live_mask, recv_weight[0], 0.0).reshape(-1)]
    lt x1, other arithmetic: 0.07 us -> 0.73 us  [body(): lax.broadcasted_iota(jnp.int32, (tile_count, capacity), 1)]
    unnamed x14 -> x10, local copies, waits for them, and re-layouts: 2.56 us -> 2.55 us
  transfers between devices with their start and end apart: 10 -> 10, of which waited for: 3 -> 4; matrix products, arithmetic and copies ran while one was open for 26% -> 21% of each run, Pallas kernels for 0% -> 0%
where the time goes in v18:
time: 62.5 us; the launch traced here: 61.8 us
  starting transfers between devices  19.9 us (32%)
  waiting for transfers between devices  19.5 us (31%)
  local copies, waits for them, and re-layouts  13.1 us (21%)
  other arithmetic  5.38 us (9%)
  matrix products  3.74 us (6%)
    ppermute x7, starting transfers between devices, xor_gather(): lax.ppermute(data, axis_name, [(j, j ^ offset) for j in range(count)])  7.95 us
    all_to_all x1, waiting for transfers between devices, body(): lax.all_to_all(difference, 'tile', split_axis=3, concat_axis=2, tiled=True)  6.12 us
    all_to_all x1, waiting for transfers between devices, body(): lax.all_to_all(packed, 'tile', split_axis=0, concat_axis=0, tiled=True)  5.81 us
    all_to_all x1, starting transfers between devices, body(): lax.all_to_all(packed, 'tile', split_axis=0, concat_axis=0, tiled=True)  5.17 us
    all_to_all x1, waiting for transfers between devices, body(): lax.all_to_all(outgoing, 'tile', split_axis=0, concat_axis=0, tiled=True)  4.76 us
    all_to_all x1, starting transfers between devices, body(): lax.all_to_all(difference, 'tile', split_axis=3, concat_axis=2, tiled=True)  3.39 us
    all_to_all x1, starting transfers between devices, body(): lax.all_to_all(outgoing, 'tile', split_axis=0, concat_axis=0, tiled=True)  3.39 us
    ppermute x7, waiting for transfers between devices, xor_gather(): lax.ppermute(data, axis_name, [(j, j ^ offset) for j in range(count)])  2.76 us
  transfers between devices with their start and end apart: 10, of which 4 were waited for; matrix products, arithmetic and copies ran while one was open for 21% of the time, Pallas kernels for 0%

profile of v18, /device:TPU:0, one launch (start us, length us, event | category | flops | bytes accessed | tf_op | source)
XLA Modules:
  0.0 61.8 jit_solution(10473568419531535232)
XLA Ops:
  0.0 0.8 %eq.39 = s32[192]{0:T(256)S(1)} reshape(s32[1,8,24]{2,1,0:T(8,128)} %param.9) | data formatting | bytes 1536 | tf_op jit(solution)/shard_map/eq | solution.py:71
  0.8 1.1 %reshape.467 = bf16[128,1024]{1,0:T(8,128)(2,1)S(1)} reshape(bf16[128,2,2,256]{3,2,1,0:T(2,128)(2,1)} %param.8) | data formatting | bytes 524288 | tf_op jit(solution)/shard_map/reshape | solution.py:75
  1.9 1.1 %convolution_convert_fusion = bf16[192,1024]{1,0:T(8,128)(2,1)} fusion(bf16[128,1024]{1,0:T(8,128)(2,1)S(1)} %reshape.467, s32[192]{0:T(256)S(1)} %eq.39), kind=kOutput, calls=%fused_computation.3 | convolution fusion | flops 50552832 | bytes 656128 | tf_op jit(solution)/shard_map/dot_general | solution.py:74
  3.0 5.2 %all-to-all-start = ((bf16[8,24,1024]{2,1,0:T(8,128)(2,1)}), bf16[8,24,1024]{2,1,0:T(8,128)(2,1)S(1)}, u32[]{:S(2)}, u32[]{:S(2)}) async-start(bf16[8,24,1024]{2,1,0:T(8,128)(2,1)} %bitcast.3), calls=%async_computation | async-start | bytes 786432 | tf_op jit(solution)/shard_map/all_to_all | solution.py:78
  8.2 0.8 %squeeze.3 = bf16[192]{0:T(256)(128)(2,1)S(1)} reshape(f32[1,8,24]{2,1,0:T(8,128)} %param.11) | data formatting | bytes 1152 | tf_op jit(solution)/shard_map/squeeze | solution.py:82
  9.0 0.7 %iota_compare_fusion.3 = pred[8,24]{1,0:T(8,128)(4,1)S(1)} fusion(s32[8]{0:T(128)} %bitcast.88), kind=kLoop, calls=%fused_computation.30 | loop fusion | flops 192 | bytes 224 | tf_op jit(solution)/shard_map/lt | solution.py:81
  9.7 0.1 lt.42
  9.9 0.7 %fusion.14 = bf16[28,512]{1,0:T(8,128)(2,1)S(1)} fusion(bf16[12,384]{1,0:T(8,128)(2,1)} %param.15, bf16[16,512]{1,0:T(8,128)(2,1)} %param.14), kind=kLoop, calls=%fused_computation.28 | loop fusion | flops 86016 | bytes 54272 | tf_op jit(solution)/shard_map/concatenate | solution.py:38
  10.7 5.8 %all-to-all-done = bf16[8,24,1024]{2,1,0:T(8,128)(2,1)S(1)} async-done(((bf16[8,24,1024]{2,1,0:T(8,128)(2,1)}), bf16[8,24,1024]{2,1,0:T(8,128)(2,1)S(1)}, u32[]{:S(2)}, u32[]{:S(2)}) %all-to-all-start) | async-done | bytes 393248 | tf_op jit(solution)/shard_map/all_to_all | solution.py:78
  16.5 3.6 %collective-permute-start.2 = (bf16[28,512]{1,0:T(8,128)(2,1)S(1)}, bf16[28,512]{1,0:T(8,128)(2,1)S(1)}, u32[]{:S(2)}, u32[]{:S(2)}) collective-permute-start(bf16[28,512]{1,0:T(8,128)(2,1)S(1)} %fusion.14), channel_id=1, source_target_pairs={{0,24},{8,16},{16,8},{24,0},{1,25},{9,17},{17,9},{25,1},{2,26},{10... | collective-permute-start | bytes 86024 | tf_op jit(solution)/shard_map/ppermute | solution.py:15
  20.1 0.8 %collective-permute-start = (bf16[28,512]{1,0:T(8,128)(2,1)S(1)}, bf16[28,512]{1,0:T(8,128)(2,1)S(1)}, u32[]{:S(2)}, u32[]{:S(2)}) collective-permute-start(bf16[28,512]{1,0:T(8,128)(2,1)S(1)} %fusion.14), channel_id=1, source_target_pairs={{0,8},{8,0},{16,24},{24,16},{1,9},{9,1},{17,25},{25,17},{2,10},{10... | collective-permute-start | bytes 86024 | tf_op jit(solution)/shard_map/ppermute | solution.py:15
  20.9 0.1 select_n.135
  21.0 0.1 eq.36
  21.0 0.1 select_n.131
  21.1 0.1 select_n.128
  21.2 0.1 iota.75
  21.4 0.6 iota.84
  21.9 0.2 copy.18
  22.2 2.7 %collective-permute-done.1 = bf16[28,512]{1,0:T(8,128)(2,1)S(1)} collective-permute-done((bf16[28,512]{1,0:T(8,128)(2,1)S(1)}, bf16[28,512]{1,0:T(8,128)(2,1)S(1)}, u32[]{:S(2)}, u32[]{:S(2)}) %collective-permute-start.1) | collective-permute-done | bytes 28704 | tf_op jit(solution)/shard_map/ppermute | solution.py:15
  24.9 0.7 %fusion.32 = (bf16[1,4,28,512]{3,2,1,0:T(8,128)(2,1)}, bf16[4,28,512]{2,1,0:T(8,128)(2,1)}) fusion(bf16[1,28,512]{2,1,0:T(8,128)(2,1)S(1)} %bitcast.85, bf16[1,28,512]{2,1,0:T(8,128)(2,1)S(1)} %bitcast.86, bf16[1,28,512]{2,1,0:T(8,128)(2,1)S(1)} %bitcast.87, bf16[1,28,512]{2,1,0:T(8,128)(2,1)S(1)} %bitcast.84), kind=kLoop, calls=%fused_computation.85 | loop fusion | flops 172032 | bytes 344064 | tf_op jit(solution)/shard_map/stack | solution.py:16
  25.6 0.6 collective-permute-start.4
  26.2 0.6 collective-permute-start.3
  26.7 2.4 %collective-permute-start.5 = (bf16[4,28,512]{2,1,0:T(8,128)(2,1)}, bf16[4,28,512]{2,1,0:T(8,128)(2,1)}, u32[]{:S(2)}, u32[]{:S(2)}) collective-permute-start(bf16[4,28,512]{2,1,0:T(8,128)(2,1)} %get-tuple-element.12), channel_id=1, source_target_pairs={{0,6},{1,7},{2,4},{3,5},{4,2},{5,3},{6,0},{7,1},{8,14},{9,15},{10,... | collective-permute-start | bytes 344072 | tf_op jit(solution)/shard_map/ppermute | solution.py:15
  29.1 1.9 %convolution_bitcast_fusion = f32[2,2,4,16,24,16]{4,5,3,1,0,2:T(8,128)} fusion(bf16[2,2,16,16,192,1]{4,3,2,1,0,5:T(8,128)(2,1)S(1)} %bitcast.75, bf16[192]{0:T(256)(128)(2,1)S(1)} %broadcast_select_fusion.3, s32[4,24]{1,0:T(4,128)S(1)} %multiply_add_fusion, s32[192]{0:T(256)S(1)} %eq.36), kind=kOutput, calls=%fused_computation.2 | convolution fusion | flops 37785600 | bytes 787968 | tf_op jit(solution)/shard_map/dot_general | solution.py:87
  31.0 2.2 %copy.19 = f32[2,2,4,16,24,16]{5,4,3,2,1,0:T(8,128)S(1)} copy(f32[2,2,4,16,24,16]{4,5,3,1,0,2:T(8,128)} %convolution_bitcast_fusion) | data formatting | bytes 786432 | tf_op jit(solution)/shard_map/transpose | solution.py:100
  33.2 0.9 %reshape.470 = f32[2,2,64,384]{3,2,1,0:T(8,128)S(1)} reshape(f32[2,2,4,16,24,16]{5,4,3,2,1,0:T(8,128)S(1)} %copy.19) | data formatting | bytes 786432 | tf_op jit(solution)/shard_map/reshape | solution.py:100
  34.1 1.2 %fusion.33 = (bf16[1,4,4,28,512]{4,3,2,1,0:T(8,128)(2,1)S(1)}, bf16[4,4,28,512]{3,2,1,0:T(8,128)(2,1)S(1)}) fusion(bf16[1,4,28,512]{3,2,1,0:T(8,128)(2,1)} %bitcast.19, bf16[1,4,28,512]{3,2,1,0:T(8,128)(2,1)} %bitcast.18, bf16[1,4,28,512]{3,2,1,0:T(8,128)(2,1)} %bitcast.17, bf16[1,4,28,512]{3,2,1,0:T(8,128)(2,1)} %get-tuple-element.11), kind=kLoop, calls=%fused_computation.86 | loop fusion | flops 688128 | bytes 1376256 | tf_op jit(solution)/shard_map/stack | solution.py:16
  35.3 0.1 collective-permute-start.6
  35.4 1.0 %fusion.3 = bf16[2,2,64,384]{3,2,1,0:T(8,128)(2,1)S(1)} fusion(f32[2,2,64,384]{3,2,1,0:T(8,128)S(1)} %reshape.470, bf16[2,2,64,384]{3,2,1,0:T(8,128)(2,1)} %param.13), kind=kLoop, calls=%fused_computation.12 | loop fusion | flops 294912 | bytes 786432 | tf_op jit(solution)/shard_map/convert_element_type | solution.py:103
  36.4 0.6 copy.20
  37.0 1.0 %reshape.495 = bf16[8,2,6144]{2,1,0:T(2,128)(2,1)} reshape(bf16[384,2,2,64]{3,2,1,0:T(2,128)(2,1)S(1)} %bitcast.78) | data formatting | bytes 393216
  38.0 3.4 %all-to-all-start.1 = ((bf16[8,2,6144]{2,1,0:T(2,128)(2,1)}), bf16[8,2,6144]{2,1,0:T(2,128)(2,1)S(1)}, u32[]{:S(2)}, u32[]{:S(2)}) async-start(bf16[8,2,6144]{2,1,0:T(2,128)(2,1)} %reshape.495), calls=%async_computation.1 | async-start | bytes 393216 | tf_op jit(solution)/shard_map/all_to_all | solution.py:104
  41.4 6.1 %all-to-all-done.1 = bf16[8,2,6144]{2,1,0:T(2,128)(2,1)S(1)} async-done(((bf16[8,2,6144]{2,1,0:T(2,128)(2,1)}), bf16[8,2,6144]{2,1,0:T(2,128)(2,1)S(1)}, u32[]{:S(2)}, u32[]{:S(2)}) %all-to-all-start.1) | async-done | bytes 196640 | tf_op jit(solution)/shard_map/all_to_all | solution.py:104
  47.5 0.3 reshape.496
  47.8 0.3 copy.45
  48.1 0.3 all_to_all.23
  48.4 0.1 pad_maximum_fusion
  48.5 0.6 gather_fusion
  49.1 0.3 fusion
  49.4 0.2 reshape.473
  49.7 1.0 %reshape.497 = bf16[8,2,6144]{2,1,0:T(2,128)(2,1)} reshape(bf16[8,2,2,48,64]{4,3,2,1,0:T(8,128)(2,1)S(1)} %bitcast.81) | data formatting | bytes 393216
  50.7 3.4 %all-to-all-start.2 = ((bf16[8,2,6144]{2,1,0:T(2,128)(2,1)}), bf16[8,2,6144]{2,1,0:T(2,128)(2,1)S(1)}, u32[]{:S(2)}, u32[]{:S(2)}) async-start(bf16[8,2,6144]{2,1,0:T(2,128)(2,1)} %reshape.497), calls=%async_computation.2 | async-start | bytes 393216 | tf_op jit(solution)/shard_map/all_to_all | solution.py:115
  54.2 0.6 %gather_fusion.1 = bf16[32,12,384]{2,1,0:T(8,128)(2,1)S(1)} fusion(bf16[32,12,384]{2,1,0:T(8,128)(2,1)S(1)} %slice.13, s32[1024]{0:T(1024)S(1)} %pad_clamp_fusion), kind=kCustom, calls=%fused_computation.1 | custom fusion | bytes 589952 | tf_op jit(solution)/shard_map/jit(_take)/gather | solution.py:55
  54.8 0.7 %reshape_reshape.3 = bf16[384,8,48]{2,1,0:T(8,128)(2,1)S(1)} reshape(bf16[32,12,384]{2,1,0:T(8,128)(2,1)S(1)} %gather_fusion.1) | data formatting | bytes 589824 | tf_op jit(solution)/shard_map/reshape;reshape | solution.py:119
  55.5 4.8 %all-to-all-done.2 = bf16[8,2,6144]{2,1,0:T(2,128)(2,1)S(1)} async-done(((bf16[8,2,6144]{2,1,0:T(2,128)(2,1)}), bf16[8,2,6144]{2,1,0:T(2,128)(2,1)S(1)}, u32[]{:S(2)}, u32[]{:S(2)}) %all-to-all-start.2) | async-done | bytes 196640 | tf_op jit(solution)/shard_map/all_to_all | solution.py:115
  60.3 0.3 reshape.498
  60.6 0.5 fusion.1
  61.1 0.7 %fusion.4 = bf16[2,2,64,384]{3,2,1,0:T(8,128)(2,1)} fusion(bf16[2,2,64,384]{3,2,1,0:T(8,128)(2,1)S(1)} %copy-done, f32[2,2,64,384,1]{3,2,0,1,4:T(8,128)S(1)} %fusion.1), kind=kLoop, calls=%fused_computation.13 | loop fusion | flops 294912 | bytes 786432 | tf_op jit(solution)/shard_map/convert_element_type | solution.py:122
  (32 shorter events, 0.5 us)
Async XLA Ops:
  0.0 21.0 %copy-start.1 = (s32[1,8,24]{2,1,0:T(8,128)S(1)}, s32[1,8,24]{2,1,0:T(8,128)}, u32[]{:S(2)}) copy-start(s32[1,8,24]{2,1,0:T(8,128)} %param.10) | copy-start | bytes 2308
  3.0 13.5 %all-to-all-start = ((bf16[8,24,1024]{2,1,0:T(8,128)(2,1)}), bf16[8,24,1024]{2,1,0:T(8,128)(2,1)S(1)}, u32[]{:S(2)}, u32[]{:S(2)}) async-start(bf16[8,24,1024]{2,1,0:T(8,128)(2,1)} %bitcast.3), calls=%async_computation | async-start | bytes 786432 | tf_op jit(solution)/shard_map/all_to_all | solution.py:78
  16.5 5.7 %collective-permute-start.2 = (bf16[28,512]{1,0:T(8,128)(2,1)S(1)}, bf16[28,512]{1,0:T(8,128)(2,1)S(1)}, u32[]{:S(2)}, u32[]{:S(2)}) collective-permute-start(bf16[28,512]{1,0:T(8,128)(2,1)S(1)} %fusion.14), channel_id=1, source_target_pairs={{0,24},{8,16},{16,8},{24,0},{1,25},{9,17},{17,9},{25,1},{2,26},{10... | collective-permute-start | bytes 86024 | tf_op jit(solution)/shard_map/ppermute | solution.py:15
  20.1 4.8 %collective-permute-start.1 = (bf16[28,512]{1,0:T(8,128)(2,1)S(1)}, bf16[28,512]{1,0:T(8,128)(2,1)S(1)}, u32[]{:S(2)}, u32[]{:S(2)}) collective-permute-start(bf16[28,512]{1,0:T(8,128)(2,1)S(1)} %fusion.14), channel_id=1, source_target_pairs={{0,16},{8,24},{16,0},{24,8},{1,17},{9,25},{17,1},{25,9},{2,18},{10... | collective-permute-start | bytes 86024 | tf_op jit(solution)/shard_map/ppermute | solution.py:15
  20.1 4.8 %collective-permute-start = (bf16[28,512]{1,0:T(8,128)(2,1)S(1)}, bf16[28,512]{1,0:T(8,128)(2,1)S(1)}, u32[]{:S(2)}, u32[]{:S(2)}) collective-permute-start(bf16[28,512]{1,0:T(8,128)(2,1)S(1)} %fusion.14), channel_id=1, source_target_pairs={{0,8},{8,0},{16,24},{24,16},{1,9},{9,1},{17,25},{25,17},{2,10},{10... | collective-permute-start | bytes 86024 | tf_op jit(solution)/shard_map/ppermute | solution.py:15
  25.6 8.5 %collective-permute-start.4 = (bf16[4,28,512]{2,1,0:T(8,128)(2,1)}, bf16[4,28,512]{2,1,0:T(8,128)(2,1)}, u32[]{:S(2)}, u32[]{:S(2)}) collective-permute-start(bf16[4,28,512]{2,1,0:T(8,128)(2,1)} %get-tuple-element.12), channel_id=1, source_target_pairs={{0,4},{1,5},{2,6},{3,7},{4,0},{5,1},{6,2},{7,3},{8,12},{9,13},{10,... | collective-permute-start | bytes 344072 | tf_op jit(solution)/shard_map/ppermute | solution.py:15
  26.2 7.9 %collective-permute-start.3 = (bf16[4,28,512]{2,1,0:T(8,128)(2,1)}, bf16[4,28,512]{2,1,0:T(8,128)(2,1)}, u32[]{:S(2)}, u32[]{:S(2)}) collective-permute-start(bf16[4,28,512]{2,1,0:T(8,128)(2,1)} %get-tuple-element.12), channel_id=1, source_target_pairs={{0,2},{1,3},{2,0},{3,1},{4,6},{5,7},{6,4},{7,5},{8,10},{9,11},{10,... | collective-permute-start | bytes 344072 | tf_op jit(solution)/shard_map/ppermute | solution.py:15
  26.7 7.4 %collective-permute-start.5 = (bf16[4,28,512]{2,1,0:T(8,128)(2,1)}, bf16[4,28,512]{2,1,0:T(8,128)(2,1)}, u32[]{:S(2)}, u32[]{:S(2)}) collective-permute-start(bf16[4,28,512]{2,1,0:T(8,128)(2,1)} %get-tuple-element.12), channel_id=1, source_target_pairs={{0,6},{1,7},{2,4},{3,5},{4,2},{5,3},{6,0},{7,1},{8,14},{9,15},{10,... | collective-permute-start | bytes 344072 | tf_op jit(solution)/shard_map/ppermute | solution.py:15
  34.1 7.3 %copy-start.2 = (s32[32,1]{0,1:T(1,128)S(1)}, s32[32,1]{0,1:T(1,128)}, u32[]{:S(2)}) copy-start(s32[32,1]{0,1:T(1,128)} %iota.84) | copy-start | bytes 388
  35.3 13.0 %collective-permute-start.6 = (bf16[4,4,28,512]{3,2,1,0:T(8,128)(2,1)S(1)}, bf16[4,4,28,512]{3,2,1,0:T(8,128)(2,1)S(1)}, u32[]{:S(2)}, u32[]{:S(2)}) collective-permute-start(bf16[4,4,28,512]{3,2,1,0:T(8,128)(2,1)S(1)} %get-tuple-element.10), channel_id=1, source_target_pairs={{0,1},{1,0},{2,3},{3,2},{4,5},{5,4},{6,7},{7,6},{8,9},{9,8},{10,11... | collective-permute-start | bytes 1376264 | tf_op jit(solution)/shard_map/ppermute | solution.py:15
  38.0 9.6 %all-to-all-start.1 = ((bf16[8,2,6144]{2,1,0:T(2,128)(2,1)}), bf16[8,2,6144]{2,1,0:T(2,128)(2,1)S(1)}, u32[]{:S(2)}, u32[]{:S(2)}) async-start(bf16[8,2,6144]{2,1,0:T(2,128)(2,1)} %reshape.495), calls=%async_computation.1 | async-start | bytes 393216 | tf_op jit(solution)/shard_map/all_to_all | solution.py:104
  50.7 9.6 %all-to-all-start.2 = ((bf16[8,2,6144]{2,1,0:T(2,128)(2,1)}), bf16[8,2,6144]{2,1,0:T(2,128)(2,1)S(1)}, u32[]{:S(2)}, u32[]{:S(2)}) async-start(bf16[8,2,6144]{2,1,0:T(2,128)(2,1)} %reshape.497), calls=%async_computation.2 | async-start | bytes 393216 | tf_op jit(solution)/shard_map/all_to_all | solution.py:115
  54.2 6.9 %copy-start = (bf16[2,2,64,384]{3,2,1,0:T(8,128)(2,1)S(1)}, bf16[2,2,64,384]{3,2,1,0:T(8,128)(2,1)}, u32[]{:S(2)}) copy-start(bf16[2,2,64,384]{3,2,1,0:T(8,128)(2,1)} %param.13) | copy-start | bytes 589828

commit v19 on v15

--- a/solution.py
+++ b/solution.py
@@ -66,7 +66,8 @@
     capacity = send_blocks.shape[2]
     block_cells = source_blocks.shape[3]
     block_side = math.isqrt(block_cells)
-    picked = send_blocks[0].reshape(-1)
+    order = jnp.arange(tile_count, dtype=jnp.int32) ^ lax.axis_index("tile")
+    picked = jnp.take(send_blocks[0], order, axis=0, mode="clip").reshape(-1)
     held = source_blocks.shape[0]
     one_hot = (picked[:, None] == lax.broadcasted_iota(jnp.int32, (1, held), 1)).astype(
         source_blocks.dtype
@@ -75,12 +76,22 @@
         one_hot, source_blocks.reshape(held, -1), preferred_element_type=jnp.float32
     ).astype(source_blocks.dtype)
     packed = packed.reshape(tile_count, capacity, -1)
-    arrived = lax.all_to_all(packed, "tile", split_axis=0, concat_axis=0, tiled=True)
+    outgoing = packed
+    arrived = jnp.stack(
+        [outgoing[0]]
+        + [
+            lax.ppermute(outgoing[o], "tile", [(j, j ^ o) for j in range(tile_count)])
+            for o in range(1, tile_count)
+        ]
+    )
     x_full, y_full, arrived = gather_operators(x_operator, y_operator, arrived)
     slot_count = columns // block_side * (y_cells // block_side)
-    live_mask = lax.broadcasted_iota(jnp.int32, (tile_count, capacity), 1) < recv_count[0][:, None]
-    weights = jnp.where(live_mask, recv_weight[0], 0.0).reshape(-1)
-    slot_match = recv_slot[0].reshape(-1)[None, :] == lax.broadcasted_iota(
+    count_of = jnp.take(recv_count[0], order, axis=0, mode="clip")
+    weight_of = jnp.take(recv_weight[0], order, axis=0, mode="clip")
+    slot_of = jnp.take(recv_slot[0], order, axis=0, mode="clip")
+    live_mask = lax.broadcasted_iota(jnp.int32, (tile_count, capacity), 1) < count_of[:, None]
+    weights = jnp.where(live_mask, weight_of, 0.0).reshape(-1)
+    slot_match = slot_of.reshape(-1)[None, :] == lax.broadcasted_iota(
         jnp.int32, (slot_count, tile_count * capacity), 0
     )
     remap_weights = jnp.where(slot_match, weights[None, :], 0.0).astype(jnp.bfloat16)

time: 58.6 us -> 64.4 us (1.099)
  starting transfers between devices: 19.9 us -> 22.7 us
  local copies, waits for them, and re-layouts: 12.5 us -> 14.6 us
  waiting for transfers between devices: 16.9 us -> 18.5 us
  matrix products: 3.74 us -> 3.01 us
    ppermute x0 -> x7, starting transfers between devices: none -> 6.68 us  [body(): lax.ppermute(outgoing[o], 'tile', [(j, j ^ o) for j in range(tile_count)])]
    ppermute x0 -> x7, waiting for transfers between devices: none -> 6.36 us  [body(): lax.ppermute(outgoing[o], 'tile', [(j, j ^ o) for j in range(tile_count)])]
    all_to_all x1 -> x0, waiting for transfers between devices: 6.01 us -> none  [body(): lax.all_to_all(packed, 'tile', split_axis=0, concat_axis=0, tiled=True)]
    all_to_all x1 -> x0, starting transfers between devices: 3.94 us -> none  [body(): lax.all_to_all(packed, 'tile', split_axis=0, concat_axis=0, tiled=True)]
    gather x0 -> x4, local copies, waits for them, and re-layouts: none -> 2.32 us  [the longest x1 0.64 us: body(): count_of = jnp.take(recv_count[0], order, axis=0, mode='clip')]
    ppermute x7, waiting for transfers between devices: 0.02 us -> 1.26 us  [xor_gather(): lax.ppermute(data, axis_name, [(j, j ^ offset) for j in range(count)])]
    dot_general x1, matrix products: 1.05 us -> 0.3 us  [body(): jnp.dot(one_hot, source_blocks.reshape(held, -1), preferred_element_type=...]
    eq x1, local copies, waits for them, and re-layouts: 0.76 us -> 0.08 us  [body(): picked[:, None] == lax.broadcasted_iota(jnp.int32, (1, held), 1)]
  transfers between devices with their start and end apart: 10 -> 16, of which waited for: 3 -> 7; matrix products, arithmetic and copies ran while one was open for 26% -> 25% of each run, Pallas kernels for 0% -> 0%
where the time goes in v19:
time: 64.4 us; the launch traced here: 64 us
  starting transfers between devices  22.7 us (35%)
  waiting for transfers between devices  18.5 us (29%)
  local copies, waits for them, and re-layouts  14.6 us (23%)
  other arithmetic  4.72 us (7%)
  matrix products  3.01 us (5%)
    ppermute x7, starting transfers between devices, xor_gather(): lax.ppermute(data, axis_name, [(j, j ^ offset) for j in range(count)])  9.24 us
    ppermute x7, starting transfers between devices, body(): lax.ppermute(outgoing[o], 'tile', [(j, j ^ o) for j in range(tile_count)])  6.68 us
    ppermute x7, waiting for transfers between devices, body(): lax.ppermute(outgoing[o], 'tile', [(j, j ^ o) for j in range(tile_count)])  6.36 us
    all_to_all x1, waiting for transfers between devices, body(): lax.all_to_all(difference, 'tile', split_axis=3, concat_axis=2, tiled=True)  6.11 us
    all_to_all x1, waiting for transfers between devices, body(): lax.all_to_all(outgoing, 'tile', split_axis=0, concat_axis=0, tiled=True)  4.76 us
    all_to_all x1, starting transfers between devices, body(): lax.all_to_all(difference, 'tile', split_axis=3, concat_axis=2, tiled=True)  3.39 us
    all_to_all x1, starting transfers between devices, body(): lax.all_to_all(outgoing, 'tile', split_axis=0, concat_axis=0, tiled=True)  3.39 us
    another operation x4, other arithmetic, xor_gather(): data = jnp.stack(parts)  2.76 us
  transfers between devices with their start and end apart: 16, of which 7 were waited for; matrix products, arithmetic and copies ran while one was open for 25% of the time, Pallas kernels for 0%

profile of v19, /device:TPU:0, one launch (start us, length us, event | category | flops | bytes accessed | tf_op | source)
XLA Modules:
  0.0 64.0 jit_solution(1886344838061096398)
XLA Ops:
  0.0 0.8 %fusion.34 = (bf16[1,28,512]{2,1,0:T(8,128)(2,1)S(1)}, bf16[28,512]{1,0:T(8,128)(2,1)S(1)}) fusion(bf16[12,384]{1,0:T(8,128)(2,1)} %param.15, bf16[16,512]{1,0:T(8,128)(2,1)} %param.14), kind=kLoop, calls=%fused_computation.100 | loop fusion | flops 86016 | bytes 82944 | tf_op jit(solution)/shard_map/stack | solution.py:16
  0.8 4.0 %collective-permute-start.1 = (bf16[28,512]{1,0:T(8,128)(2,1)S(1)}, bf16[28,512]{1,0:T(8,128)(2,1)S(1)}, u32[]{:S(2)}, u32[]{:S(2)}) collective-permute-start(bf16[28,512]{1,0:T(8,128)(2,1)S(1)} %get-tuple-element.19), channel_id=1, source_target_pairs={{0,16},{8,24},{16,0},{24,8},{1,17},{9,25},{17,1},{25,9},{2,18},{10... | collective-permute-start | bytes 86024 | tf_op jit(solution)/shard_map/ppermute | solution.py:15
  4.8 1.6 %collective-permute-start = (bf16[28,512]{1,0:T(8,128)(2,1)S(1)}, bf16[28,512]{1,0:T(8,128)(2,1)S(1)}, u32[]{:S(2)}, u32[]{:S(2)}) collective-permute-start(bf16[28,512]{1,0:T(8,128)(2,1)S(1)} %get-tuple-element.19), channel_id=1, source_target_pairs={{0,8},{8,0},{16,24},{24,16},{1,9},{9,1},{17,25},{25,17},{2,10},{10... | collective-permute-start | bytes 86024 | tf_op jit(solution)/shard_map/ppermute | solution.py:15
  6.4 0.6 gather_fusion.3
  7.1 1.1 %reshape.489 = bf16[128,1024]{1,0:T(8,128)(2,1)S(1)} reshape(bf16[128,2,2,256]{3,2,1,0:T(2,128)(2,1)} %param.8) | data formatting | bytes 524288 | tf_op jit(solution)/shard_map/reshape | solution.py:76
  8.2 0.3 convolution_convert_fusion
  8.5 1.4 %collective-permute-start.9 = (bf16[24,1024]{1,0:T(8,128)(2,1)S(1)}, bf16[24,1024]{1,0:T(8,128)(2,1)S(1)}, u32[]{:S(2)}, u32[]{:S(2)}) collective-permute-start(bf16[24,1024]{1,0:T(8,128)(2,1)S(1)} %get-tuple-element.11), channel_id=1, source_target_pairs={{0,7},{1,6},{2,5},{3,4},{4,3},{5,2},{6,1},{7,0},{8,15},{9,14},{10,... | collective-permute-start | bytes 147464 | tf_op jit(solution)/shard_map/ppermute | solution.py:83
  9.9 1.4 %collective-permute-start.8 = (bf16[24,1024]{1,0:T(8,128)(2,1)S(1)}, bf16[24,1024]{1,0:T(8,128)(2,1)S(1)}, u32[]{:S(2)}, u32[]{:S(2)}) collective-permute-start(bf16[24,1024]{1,0:T(8,128)(2,1)S(1)} %get-tuple-element.12), channel_id=1, source_target_pairs={{0,6},{1,7},{2,4},{3,5},{4,2},{5,3},{6,0},{7,1},{8,14},{9,15},{10,... | collective-permute-start | bytes 147464 | tf_op jit(solution)/shard_map/ppermute | solution.py:83
  11.5 0.6 %gather_fusion.1 = s32[8]{0:T(128)S(1)} fusion(s32[8]{0:T(128)S(1)} %bitcast.96, s32[1024]{0:T(1024)S(1)} %pad_clamp_fusion.1), kind=kCustom, calls=%fused_computation.1 | custom fusion | bytes 96 | tf_op jit(solution)/shard_map/jit(_take)/gather | solution.py:89
  12.1 0.6 gather_fusion.2
  13.1 0.6 iota.80
  13.8 0.7 %iota.89 = s32[32,1]{0,1:T(1,128)} reshape(s32[4,8]{1,0:T(4,128)S(1)} %iota.88) | data formatting | bytes 256 | tf_op jit(solution)/shard_map/iota | solution.py:49
  14.5 0.6 gather_fusion
  15.2 1.4 %collective-permute-start.7 = (bf16[24,1024]{1,0:T(8,128)(2,1)S(1)}, bf16[24,1024]{1,0:T(8,128)(2,1)S(1)}, u32[]{:S(2)}, u32[]{:S(2)}) collective-permute-start(bf16[24,1024]{1,0:T(8,128)(2,1)S(1)} %get-tuple-element.13), channel_id=1, source_target_pairs={{0,5},{1,4},{2,7},{3,6},{4,1},{5,0},{6,3},{7,2},{8,13},{9,12},{10,... | collective-permute-start | bytes 147464 | tf_op jit(solution)/shard_map/ppermute | solution.py:83
  16.6 0.3 collective-permute-start.6
  17.1 0.7 %pad_maximum_fusion.2 = bf16[4,28,512]{2,1,0:T(8,128)(2,1)} fusion(bf16[1,28,512]{2,1,0:T(8,128)(2,1)S(1)} %bitcast.112, bf16[1,28,512]{2,1,0:T(8,128)(2,1)S(1)} %bitcast.110, bf16[1,28,512]{2,1,0:T(8,128)(2,1)S(1)} %bitcast.111, bf16[1,28,512]{2,1,0:T(8,128)(2,1)S(1)} %get-tuple-element.18), kind=kLoop, calls=%fused_computation.21 | loop fusion | flops 172032 | bytes 229376 | tf_op jit(solution)/shard_map/stack | solution.py:16
  17.8 0.4 collective-permute-done.3
  18.2 1.7 %collective-permute-start.4 = (bf16[24,1024]{1,0:T(8,128)(2,1)S(1)}, bf16[24,1024]{1,0:T(8,128)(2,1)S(1)}, u32[]{:S(2)}, u32[]{:S(2)}) collective-permute-start(bf16[24,1024]{1,0:T(8,128)(2,1)S(1)} %get-tuple-element.16), channel_id=1, source_target_pairs={{0,2},{1,3},{2,0},{3,1},{4,6},{5,7},{6,4},{7,5},{8,10},{9,11},{10,... | collective-permute-start | bytes 147464 | tf_op jit(solution)/shard_map/ppermute | solution.py:83
  19.8 2.4 %collective-permute-done.4 = bf16[24,1024]{1,0:T(8,128)(2,1)S(1)} collective-permute-done((bf16[24,1024]{1,0:T(8,128)(2,1)S(1)}, bf16[24,1024]{1,0:T(8,128)(2,1)S(1)}, u32[]{:S(2)}, u32[]{:S(2)}) %collective-permute-start.4) | collective-permute-done | bytes 49184 | tf_op jit(solution)/shard_map/ppermute | solution.py:83
  22.3 0.3 collective-permute-start.5
  22.6 3.5 %collective-permute-done.5 = bf16[24,1024]{1,0:T(8,128)(2,1)S(1)} collective-permute-done((bf16[24,1024]{1,0:T(8,128)(2,1)S(1)}, bf16[24,1024]{1,0:T(8,128)(2,1)S(1)}, u32[]{:S(2)}, u32[]{:S(2)}) %collective-permute-start.5) | collective-permute-done | bytes 49184 | tf_op jit(solution)/shard_map/ppermute | solution.py:83
  26.2 2.4 %collective-permute-start.12 = (bf16[4,28,512]{2,1,0:T(8,128)(2,1)}, bf16[4,28,512]{2,1,0:T(8,128)(2,1)}, u32[]{:S(2)}, u32[]{:S(2)}) collective-permute-start(bf16[4,28,512]{2,1,0:T(8,128)(2,1)} %pad_maximum_fusion.2), channel_id=1, source_target_pairs={{0,6},{1,7},{2,4},{3,5},{4,2},{5,3},{6,0},{7,1},{8,14},{9,15},{10,... | collective-permute-start | bytes 344072 | tf_op jit(solution)/shard_map/ppermute | solution.py:15
  28.6 0.5 collective-permute-start.11
  29.1 0.7 %collective-permute-start.10 = (bf16[4,28,512]{2,1,0:T(8,128)(2,1)}, bf16[4,28,512]{2,1,0:T(8,128)(2,1)}, u32[]{:S(2)}, u32[]{:S(2)}) collective-permute-start(bf16[4,28,512]{2,1,0:T(8,128)(2,1)} %pad_maximum_fusion.2), channel_id=1, source_target_pairs={{0,2},{1,3},{2,0},{3,1},{4,6},{5,7},{6,4},{7,5},{8,10},{9,11},{10,... | collective-permute-start | bytes 344072 | tf_op jit(solution)/shard_map/ppermute | solution.py:15
  30.0 1.9 %convolution_bitcast_fusion = f32[2,2,4,16,24,16]{4,5,3,1,0,2:T(8,128)} fusion(bf16[2,2,16,16,192,1]{4,3,2,1,0,5:T(8,128)(2,1)S(1)} %bitcast.99, bf16[192]{0:T(256)(128)(2,1)S(1)} %select_n.128, s32[4,24]{1,0:T(4,128)S(1)} %multiply_add_fusion, s32[192]{0:T(256)S(1)} %eq.36), kind=kOutput, calls=%fused_computation.6 | convolution fusion | flops 37785600 | bytes 787968 | tf_op jit(solution)/shard_map/dot_general | solution.py:98
  31.8 2.2 %copy.19 = f32[2,2,4,16,24,16]{5,4,3,2,1,0:T(8,128)S(1)} copy(f32[2,2,4,16,24,16]{4,5,3,1,0,2:T(8,128)} %convolution_bitcast_fusion) | data formatting | bytes 786432 | tf_op jit(solution)/shard_map/transpose | solution.py:111
  34.1 0.9 %reshape.491 = f32[2,2,64,384]{3,2,1,0:T(8,128)S(1)} reshape(f32[2,2,4,16,24,16]{5,4,3,2,1,0:T(8,128)S(1)} %copy.19) | data formatting | bytes 786432 | tf_op jit(solution)/shard_map/reshape | solution.py:111
  35.0 0.8 %collective-permute-done.11 = bf16[4,28,512]{2,1,0:T(8,128)(2,1)} collective-permute-done((bf16[4,28,512]{2,1,0:T(8,128)(2,1)}, bf16[4,28,512]{2,1,0:T(8,128)(2,1)}, u32[]{:S(2)}, u32[]{:S(2)}) %collective-permute-start.11) | collective-permute-done | bytes 114720 | tf_op jit(solution)/shard_map/ppermute | solution.py:15
  35.8 0.4 collective-permute-done.10
  36.2 1.2 %fusion.35 = (bf16[1,4,4,28,512]{4,3,2,1,0:T(8,128)(2,1)S(1)}, bf16[4,4,28,512]{3,2,1,0:T(8,128)(2,1)S(1)}) fusion(bf16[1,4,28,512]{3,2,1,0:T(8,128)(2,1)} %bitcast.30, bf16[1,4,28,512]{3,2,1,0:T(8,128)(2,1)} %bitcast.29, bf16[1,4,28,512]{3,2,1,0:T(8,128)(2,1)} %bitcast.28, bf16[1,4,28,512]{3,2,1,0:T(8,128)(2,1)} %bitcast.27), kind=kLoop, calls=%fused_computation.101 | loop fusion | flops 688128 | bytes 1376256 | tf_op jit(solution)/shard_map/stack | solution.py:16
  37.5 1.0 %fusion.3 = bf16[2,2,64,384]{3,2,1,0:T(8,128)(2,1)S(1)} fusion(f32[2,2,64,384]{3,2,1,0:T(8,128)S(1)} %reshape.491, bf16[2,2,64,384]{3,2,1,0:T(8,128)(2,1)} %param.13), kind=kLoop, calls=%fused_computation.16 | loop fusion | flops 294912 | bytes 786432 | tf_op jit(solution)/shard_map/convert_element_type | solution.py:114
  38.5 0.6 copy.20
  39.1 1.0 %reshape.548 = bf16[8,2,6144]{2,1,0:T(2,128)(2,1)} reshape(bf16[384,2,2,64]{3,2,1,0:T(2,128)(2,1)S(1)} %bitcast.101) | data formatting | bytes 393216
  40.1 3.4 %all-to-all-start = ((bf16[8,2,6144]{2,1,0:T(2,128)(2,1)}), bf16[8,2,6144]{2,1,0:T(2,128)(2,1)S(1)}, u32[]{:S(2)}, u32[]{:S(2)}) async-start(bf16[8,2,6144]{2,1,0:T(2,128)(2,1)} %reshape.548), calls=%async_computation | async-start | bytes 393216 | tf_op jit(solution)/shard_map/all_to_all | solution.py:115
  43.5 6.1 %all-to-all-done = bf16[8,2,6144]{2,1,0:T(2,128)(2,1)S(1)} async-done(((bf16[8,2,6144]{2,1,0:T(2,128)(2,1)}), bf16[8,2,6144]{2,1,0:T(2,128)(2,1)S(1)}, u32[]{:S(2)}, u32[]{:S(2)}) %all-to-all-start) | async-done | bytes 196640 | tf_op jit(solution)/shard_map/all_to_all | solution.py:115
  49.6 0.3 reshape.549
  49.9 0.3 copy.45
  50.2 0.3 all_to_all.19
  50.6 0.6 gather_fusion.4
  51.2 0.3 fusion
  51.9 1.0 %reshape.550 = bf16[8,2,6144]{2,1,0:T(2,128)(2,1)} reshape(bf16[8,2,2,48,64]{4,3,2,1,0:T(8,128)(2,1)S(1)} %bitcast.104) | data formatting | bytes 393216
  52.8 3.4 %all-to-all-start.1 = ((bf16[8,2,6144]{2,1,0:T(2,128)(2,1)}), bf16[8,2,6144]{2,1,0:T(2,128)(2,1)S(1)}, u32[]{:S(2)}, u32[]{:S(2)}) async-start(bf16[8,2,6144]{2,1,0:T(2,128)(2,1)} %reshape.550), calls=%async_computation.1 | async-start | bytes 393216 | tf_op jit(solution)/shard_map/all_to_all | solution.py:126
  56.3 0.6 gather_fusion.5
  56.9 0.7 %reshape_reshape.3 = bf16[384,8,48]{2,1,0:T(8,128)(2,1)S(1)} reshape(bf16[32,12,384]{2,1,0:T(8,128)(2,1)S(1)} %gather_fusion.5) | data formatting | bytes 589824 | tf_op jit(solution)/shard_map/reshape;reshape | solution.py:130
  57.6 4.8 %all-to-all-done.1 = bf16[8,2,6144]{2,1,0:T(2,128)(2,1)S(1)} async-done(((bf16[8,2,6144]{2,1,0:T(2,128)(2,1)}), bf16[8,2,6144]{2,1,0:T(2,128)(2,1)S(1)}, u32[]{:S(2)}, u32[]{:S(2)}) %all-to-all-start.1) | async-done | bytes 196640 | tf_op jit(solution)/shard_map/all_to_all | solution.py:126
  62.4 0.3 reshape.551
  62.7 0.5 fusion.1
  63.2 0.7 %fusion.4 = bf16[2,2,64,384]{3,2,1,0:T(8,128)(2,1)} fusion(bf16[2,2,64,384]{3,2,1,0:T(8,128)(2,1)S(1)} %copy-done.2, f32[2,2,64,384,1]{3,2,0,1,4:T(8,128)S(1)} %fusion.1), kind=kLoop, calls=%fused_computation.17 | loop fusion | flops 294912 | bytes 786432 | tf_op jit(solution)/shard_map/convert_element_type | solution.py:133
  (65 shorter events, 1.8 us)
Async XLA Ops:
  0.0 6.4 %copy-start = (s32[1,8,24]{2,1,0:T(8,128)S(1)}, s32[1,8,24]{2,1,0:T(8,128)}, u32[]{:S(2)}) copy-start(s32[1,8,24]{2,1,0:T(8,128)} %param.9) | copy-start | bytes 2308
  0.0 11.5 %copy-start.1 = (s32[1,8]{1,0:T(1,128)S(1)}, s32[1,8]{1,0:T(1,128)}, u32[]{:S(2)}) copy-start(s32[1,8]{1,0:T(1,128)} %param.12) | copy-start | bytes 100
  0.0 12.1 %copy-start.4 = (f32[1,8,24]{2,1,0:T(8,128)S(1)}, f32[1,8,24]{2,1,0:T(8,128)}, u32[]{:S(2)}) copy-start(f32[1,8,24]{2,1,0:T(8,128)} %param.11) | copy-start | bytes 2308
  0.0 14.5 %copy-start.3 = (s32[1,8,24]{2,1,0:T(8,128)S(1)}, s32[1,8,24]{2,1,0:T(8,128)}, u32[]{:S(2)}) copy-start(s32[1,8,24]{2,1,0:T(8,128)} %param.10) | copy-start | bytes 2308
  0.8 14.4 %collective-permute-start.1 = (bf16[28,512]{1,0:T(8,128)(2,1)S(1)}, bf16[28,512]{1,0:T(8,128)(2,1)S(1)}, u32[]{:S(2)}, u32[]{:S(2)}) collective-permute-start(bf16[28,512]{1,0:T(8,128)(2,1)S(1)} %get-tuple-element.19), channel_id=1, source_target_pairs={{0,16},{8,24},{16,0},{24,8},{1,17},{9,25},{17,1},{25,9},{2,18},{10... | collective-permute-start | bytes 86024 | tf_op jit(solution)/shard_map/ppermute | solution.py:15
  4.8 11.8 %collective-permute-start = (bf16[28,512]{1,0:T(8,128)(2,1)S(1)}, bf16[28,512]{1,0:T(8,128)(2,1)S(1)}, u32[]{:S(2)}, u32[]{:S(2)}) collective-permute-start(bf16[28,512]{1,0:T(8,128)(2,1)S(1)} %get-tuple-element.19), channel_id=1, source_target_pairs={{0,8},{8,0},{16,24},{24,16},{1,9},{9,1},{17,25},{25,17},{2,10},{10... | collective-permute-start | bytes 86024 | tf_op jit(solution)/shard_map/ppermute | solution.py:15
  6.4 10.5 %collective-permute-start.2 = (bf16[28,512]{1,0:T(8,128)(2,1)S(1)}, bf16[28,512]{1,0:T(8,128)(2,1)S(1)}, u32[]{:S(2)}, u32[]{:S(2)}) collective-permute-start(bf16[28,512]{1,0:T(8,128)(2,1)S(1)} %get-tuple-element.19), channel_id=1, source_target_pairs={{0,24},{8,16},{16,8},{24,0},{1,25},{9,17},{17,9},{25,1},{2,26},{10... | collective-permute-start | bytes 86024 | tf_op jit(solution)/shard_map/ppermute | solution.py:15
  8.5 17.6 %collective-permute-start.9 = (bf16[24,1024]{1,0:T(8,128)(2,1)S(1)}, bf16[24,1024]{1,0:T(8,128)(2,1)S(1)}, u32[]{:S(2)}, u32[]{:S(2)}) collective-permute-start(bf16[24,1024]{1,0:T(8,128)(2,1)S(1)} %get-tuple-element.11), channel_id=1, source_target_pairs={{0,7},{1,6},{2,5},{3,4},{4,3},{5,2},{6,1},{7,0},{8,15},{9,14},{10,... | collective-permute-start | bytes 147464 | tf_op jit(solution)/shard_map/ppermute | solution.py:83
  9.9 16.2 %collective-permute-start.8 = (bf16[24,1024]{1,0:T(8,128)(2,1)S(1)}, bf16[24,1024]{1,0:T(8,128)(2,1)S(1)}, u32[]{:S(2)}, u32[]{:S(2)}) collective-permute-start(bf16[24,1024]{1,0:T(8,128)(2,1)S(1)} %get-tuple-element.12), channel_id=1, source_target_pairs={{0,6},{1,7},{2,4},{3,5},{4,2},{5,3},{6,0},{7,1},{8,14},{9,15},{10,... | collective-permute-start | bytes 147464 | tf_op jit(solution)/shard_map/ppermute | solution.py:83
  15.2 10.9 %collective-permute-start.7 = (bf16[24,1024]{1,0:T(8,128)(2,1)S(1)}, bf16[24,1024]{1,0:T(8,128)(2,1)S(1)}, u32[]{:S(2)}, u32[]{:S(2)}) collective-permute-start(bf16[24,1024]{1,0:T(8,128)(2,1)S(1)} %get-tuple-element.13), channel_id=1, source_target_pairs={{0,5},{1,4},{2,7},{3,6},{4,1},{5,0},{6,3},{7,2},{8,13},{9,12},{10,... | collective-permute-start | bytes 147464 | tf_op jit(solution)/shard_map/ppermute | solution.py:83
  16.6 9.5 %collective-permute-start.6 = (bf16[24,1024]{1,0:T(8,128)(2,1)S(1)}, bf16[24,1024]{1,0:T(8,128)(2,1)S(1)}, u32[]{:S(2)}, u32[]{:S(2)}) collective-permute-start(bf16[24,1024]{1,0:T(8,128)(2,1)S(1)} %get-tuple-element.14), channel_id=1, source_target_pairs={{0,4},{1,5},{2,6},{3,7},{4,0},{5,1},{6,2},{7,3},{8,12},{9,13},{10,... | collective-permute-start | bytes 147464 | tf_op jit(solution)/shard_map/ppermute | solution.py:83
  16.9 1.2 %collective-permute-start.3 = (bf16[24,1024]{1,0:T(8,128)(2,1)S(1)}, bf16[24,1024]{1,0:T(8,128)(2,1)S(1)}, u32[]{:S(2)}, u32[]{:S(2)}) collective-permute-start(bf16[24,1024]{1,0:T(8,128)(2,1)S(1)} %get-tuple-element.17), channel_id=1, source_target_pairs={{0,1},{1,0},{2,3},{3,2},{4,5},{5,4},{6,7},{7,6},{8,9},{9,8},{10,11... | collective-permute-start | bytes 147464 | tf_op jit(solution)/shard_map/ppermute | solution.py:83
  18.2 4.1 %collective-permute-start.4 = (bf16[24,1024]{1,0:T(8,128)(2,1)S(1)}, bf16[24,1024]{1,0:T(8,128)(2,1)S(1)}, u32[]{:S(2)}, u32[]{:S(2)}) collective-permute-start(bf16[24,1024]{1,0:T(8,128)(2,1)S(1)} %get-tuple-element.16), channel_id=1, source_target_pairs={{0,2},{1,3},{2,0},{3,1},{4,6},{5,7},{6,4},{7,5},{8,10},{9,11},{10,... | collective-permute-start | bytes 147464 | tf_op jit(solution)/shard_map/ppermute | solution.py:83
  22.3 3.8 %collective-permute-start.5 = (bf16[24,1024]{1,0:T(8,128)(2,1)S(1)}, bf16[24,1024]{1,0:T(8,128)(2,1)S(1)}, u32[]{:S(2)}, u32[]{:S(2)}) collective-permute-start(bf16[24,1024]{1,0:T(8,128)(2,1)S(1)} %get-tuple-element.15), channel_id=1, source_target_pairs={{0,3},{1,2},{2,1},{3,0},{4,7},{5,6},{6,5},{7,4},{8,11},{9,10},{10,... | collective-permute-start | bytes 147464 | tf_op jit(solution)/shard_map/ppermute | solution.py:83
  26.2 8.8 %collective-permute-start.12 = (bf16[4,28,512]{2,1,0:T(8,128)(2,1)}, bf16[4,28,512]{2,1,0:T(8,128)(2,1)}, u32[]{:S(2)}, u32[]{:S(2)}) collective-permute-start(bf16[4,28,512]{2,1,0:T(8,128)(2,1)} %pad_maximum_fusion.2), channel_id=1, source_target_pairs={{0,6},{1,7},{2,4},{3,5},{4,2},{5,3},{6,0},{7,1},{8,14},{9,15},{10,... | collective-permute-start | bytes 344072 | tf_op jit(solution)/shard_map/ppermute | solution.py:15
  28.6 7.2 %collective-permute-start.11 = (bf16[4,28,512]{2,1,0:T(8,128)(2,1)}, bf16[4,28,512]{2,1,0:T(8,128)(2,1)}, u32[]{:S(2)}, u32[]{:S(2)}) collective-permute-start(bf16[4,28,512]{2,1,0:T(8,128)(2,1)} %pad_maximum_fusion.2), channel_id=1, source_target_pairs={{0,4},{1,5},{2,6},{3,7},{4,0},{5,1},{6,2},{7,3},{8,12},{9,13},{10,... | collective-permute-start | bytes 344072 | tf_op jit(solution)/shard_map/ppermute | solution.py:15
  29.1 7.2 %collective-permute-start.10 = (bf16[4,28,512]{2,1,0:T(8,128)(2,1)}, bf16[4,28,512]{2,1,0:T(8,128)(2,1)}, u32[]{:S(2)}, u32[]{:S(2)}) collective-permute-start(bf16[4,28,512]{2,1,0:T(8,128)(2,1)} %pad_maximum_fusion.2), channel_id=1, source_target_pairs={{0,2},{1,3},{2,0},{3,1},{4,6},{5,7},{6,4},{7,5},{8,10},{9,11},{10,... | collective-permute-start | bytes 344072 | tf_op jit(solution)/shard_map/ppermute | solution.py:15
  35.0 8.5 %copy-start.5 = (s32[32,1]{0,1:T(1,128)S(1)}, s32[32,1]{0,1:T(1,128)}, u32[]{:S(2)}) copy-start(s32[32,1]{0,1:T(1,128)} %iota.80) | copy-start | bytes 388
  35.0 8.5 %copy-start.6 = (s32[32,1]{0,1:T(1,128)S(1)}, s32[32,1]{0,1:T(1,128)}, u32[]{:S(2)}) copy-start(s32[32,1]{0,1:T(1,128)} %iota.89) | copy-start | bytes 388
  37.4 13.1 %collective-permute-start.13 = (bf16[4,4,28,512]{3,2,1,0:T(8,128)(2,1)S(1)}, bf16[4,4,28,512]{3,2,1,0:T(8,128)(2,1)S(1)}, u32[]{:S(2)}, u32[]{:S(2)}) collective-permute-start(bf16[4,4,28,512]{3,2,1,0:T(8,128)(2,1)S(1)} %get-tuple-element.10), channel_id=1, source_target_pairs={{0,1},{1,0},{2,3},{3,2},{4,5},{5,4},{6,7},{7,6},{8,9},{9,8},{10,11... | collective-permute-start | bytes 1376264 | tf_op jit(solution)/shard_map/ppermute | solution.py:15
  40.1 9.6 %all-to-all-start = ((bf16[8,2,6144]{2,1,0:T(2,128)(2,1)}), bf16[8,2,6144]{2,1,0:T(2,128)(2,1)S(1)}, u32[]{:S(2)}, u32[]{:S(2)}) async-start(bf16[8,2,6144]{2,1,0:T(2,128)(2,1)} %reshape.548), calls=%async_computation | async-start | bytes 393216 | tf_op jit(solution)/shard_map/all_to_all | solution.py:115
  52.8 9.6 %all-to-all-start.1 = ((bf16[8,2,6144]{2,1,0:T(2,128)(2,1)}), bf16[8,2,6144]{2,1,0:T(2,128)(2,1)S(1)}, u32[]{:S(2)}, u32[]{:S(2)}) async-start(bf16[8,2,6144]{2,1,0:T(2,128)(2,1)} %reshape.550), calls=%async_computation.1 | async-start | bytes 393216 | tf_op jit(solution)/shard_map/all_to_all | solution.py:126
  56.3 6.9 %copy-start.2 = (bf16[2,2,64,384]{3,2,1,0:T(8,128)(2,1)S(1)}, bf16[2,2,64,384]{3,2,1,0:T(8,128)(2,1)}, u32[]{:S(2)}) copy-start(bf16[2,2,64,384]{3,2,1,0:T(8,128)(2,1)} %param.13) | copy-start | bytes 589828

commit v20 on v15

--- a/solution.py
+++ b/solution.py
@@ -15,6 +15,15 @@
             parts.append(lax.ppermute(data, axis_name, [(j, j ^ offset) for j in range(count)]))
         data = jnp.stack(parts)
     return data
+
+
+def xor_parts(data, axis_name, group):
+    count = lax.axis_size(axis_name)
+    parts = [data]
+    for code in range(1, 1 << len(group)):
+        offset = sum(bit for k, bit in enumerate(group) if code >> k & 1)
+        parts.append(lax.ppermute(data, axis_name, [(j, j ^ offset) for j in range(count)]))
+    return parts
 
 
 def stacked_position(offset, groups):
@@ -45,7 +54,12 @@
     tile_bits = bit_groups([1 << k for k in range(1, tile_count.bit_length() - 1)]) + [[1]]
     both = xor_gather(both, "mem", mem_bits)
     both, after = lax.optimization_barrier((both, after))
-    both = xor_gather(both, "tile", tile_bits).reshape(mem_count * tile_count, x_rows + y_rows, width)
+    chip_groups = tile_bits[:-1]
+    both = xor_gather(both, "tile", chip_groups[:-1])
+    parts = xor_parts(both, "tile", chip_groups[-1]) if chip_groups else [both]
+    swapped = [lax.ppermute(part, "tile", [(j, j ^ 1) for j in range(tile_count)]) for part in parts]
+    both = jnp.stack([jnp.stack(parts), jnp.stack(swapped)])
+    both = both.reshape(mem_count * tile_count, x_rows + y_rows, width)
     mem_of = lax.broadcasted_iota(jnp.int32, (mem_count, tile_count), 0)
     tile_of = lax.broadcasted_iota(jnp.int32, (mem_count, tile_count), 1)
     position = stacked_position(tile_of ^ lax.axis_index("tile"), tile_bits) * mem_count

time: 58.6 us -> 57.4 us (0.980)
  waiting for transfers between devices: 16.9 us -> 15.2 us
  starting transfers between devices: 19.9 us -> 20.9 us
  local copies, waits for them, and re-layouts: 12.5 us -> 11.9 us
    ppermute x0 -> x7, starting transfers between devices: none -> 4.58 us  [the longest x3 3.49 us: xor_parts(): lax.ppermute(data, axis_name, [(j, j ^ offset) for j in range(count)])]
    ppermute x7 -> x3, starting transfers between devices: 9.17 us -> 5.62 us  [xor_gather(): lax.ppermute(data, axis_name, [(j, j ^ offset) for j in range(count)])]
    all_to_all x1, waiting for transfers between devices: 6.12 us -> 3.88 us  [body(): lax.all_to_all(difference, 'tile', split_axis=3, concat_axis=2, tiled=True)]
    another operation x0 -> x3, other arithmetic: none -> 1.35 us  [gather_operators(): both = jnp.stack([jnp.stack(parts), jnp.stack(swapped)])]
    another operation x4 -> x2, other arithmetic: 2.75 us -> 1.47 us  [xor_gather(): data = jnp.stack(parts)]
    unnamed x14 -> x12, local copies, waits for them, and re-layouts: 2.56 us -> 2.56 us
  transfers between devices with their start and end apart: 10 -> 13, of which waited for: 3 -> 3; matrix products, arithmetic and copies ran while one was open for 26% -> 27% of each run, Pallas kernels for 0% -> 0%
where the time goes in v20:
time: 57.4 us; the launch traced here: 56.9 us
  starting transfers between devices  20.9 us (36%)
  waiting for transfers between devices  15.2 us (26%)
  local copies, waits for them, and re-layouts  11.9 us (21%)
  other arithmetic  4.78 us (8%)
  matrix products  3.75 us (7%)
    all_to_all x1, waiting for transfers between devices, body(): lax.all_to_all(packed, 'tile', split_axis=0, concat_axis=0, tiled=True)  6.53 us
    ppermute x3, starting transfers between devices, xor_gather(): lax.ppermute(data, axis_name, [(j, j ^ offset) for j in range(count)])  5.62 us
    all_to_all x1, waiting for transfers between devices, body(): lax.all_to_all(outgoing, 'tile', split_axis=0, concat_axis=0, tiled=True)  4.76 us
    all_to_all x1, starting transfers between devices, body(): lax.all_to_all(packed, 'tile', split_axis=0, concat_axis=0, tiled=True)  3.94 us
    all_to_all x1, waiting for transfers between devices, body(): lax.all_to_all(difference, 'tile', split_axis=3, concat_axis=2, tiled=True)  3.88 us
    ppermute x3, starting transfers between devices, xor_parts(): lax.ppermute(data, axis_name, [(j, j ^ offset) for j in range(count)])  3.49 us
    all_to_all x1, starting transfers between devices, body(): lax.all_to_all(difference, 'tile', split_axis=3, concat_axis=2, tiled=True)  3.39 us
    all_to_all x1, starting transfers between devices, body(): lax.all_to_all(outgoing, 'tile', split_axis=0, concat_axis=0, tiled=True)  3.39 us
  transfers between devices with their start and end apart: 13, of which 3 were waited for; matrix products, arithmetic and copies ran while one was open for 27% of the time, Pallas kernels for 0%

profile of v20, /device:TPU:0, one launch (start us, length us, event | category | flops | bytes accessed | tf_op | source)
XLA Modules:
  0.0 56.9 jit_solution(2981279868217659312)
XLA Ops:
  0.0 0.8 %fusion.32 = (bf16[1,28,512]{2,1,0:T(8,128)(2,1)S(1)}, bf16[28,512]{1,0:T(8,128)(2,1)S(1)}) fusion(bf16[12,384]{1,0:T(8,128)(2,1)} %param.15, bf16[16,512]{1,0:T(8,128)(2,1)} %param.14), kind=kLoop, calls=%fused_computation.86 | loop fusion | flops 86016 | bytes 82944 | tf_op jit(solution)/shard_map/stack | solution.py:16
  0.8 4.0 %collective-permute-start.1 = (bf16[28,512]{1,0:T(8,128)(2,1)S(1)}, bf16[28,512]{1,0:T(8,128)(2,1)S(1)}, u32[]{:S(2)}, u32[]{:S(2)}) collective-permute-start(bf16[28,512]{1,0:T(8,128)(2,1)S(1)} %get-tuple-element.10), channel_id=1, source_target_pairs={{0,16},{8,24},{16,0},{24,8},{1,17},{9,25},{17,1},{25,9},{2,18},{10... | collective-permute-start | bytes 86024 | tf_op jit(solution)/shard_map/ppermute | solution.py:15
  4.8 1.6 %collective-permute-start = (bf16[28,512]{1,0:T(8,128)(2,1)S(1)}, bf16[28,512]{1,0:T(8,128)(2,1)S(1)}, u32[]{:S(2)}, u32[]{:S(2)}) collective-permute-start(bf16[28,512]{1,0:T(8,128)(2,1)S(1)} %get-tuple-element.10), channel_id=1, source_target_pairs={{0,8},{8,0},{16,24},{24,16},{1,9},{9,1},{17,25},{25,17},{2,10},{10... | collective-permute-start | bytes 86024 | tf_op jit(solution)/shard_map/ppermute | solution.py:15
  6.4 0.8 %eq.39 = s32[192]{0:T(256)S(1)} reshape(s32[1,8,24]{2,1,0:T(8,128)} %param.9) | data formatting | bytes 1536 | tf_op jit(solution)/shard_map/eq | solution.py:85
  7.2 1.1 %reshape.467 = bf16[128,1024]{1,0:T(8,128)(2,1)S(1)} reshape(bf16[128,2,2,256]{3,2,1,0:T(2,128)(2,1)} %param.8) | data formatting | bytes 524288 | tf_op jit(solution)/shard_map/reshape | solution.py:89
  8.3 1.1 %convolution_convert_fusion = bf16[192,1024]{1,0:T(8,128)(2,1)} fusion(bf16[128,1024]{1,0:T(8,128)(2,1)S(1)} %reshape.467, s32[192]{0:T(256)S(1)} %eq.39), kind=kOutput, calls=%fused_computation.3 | convolution fusion | flops 50552832 | bytes 656128 | tf_op jit(solution)/shard_map/dot_general | solution.py:88
  9.3 3.9 %all-to-all-start = ((bf16[8,24,1024]{2,1,0:T(8,128)(2,1)}), bf16[8,24,1024]{2,1,0:T(8,128)(2,1)S(1)}, u32[]{:S(2)}, u32[]{:S(2)}) async-start(bf16[8,24,1024]{2,1,0:T(8,128)(2,1)} %bitcast.7), calls=%async_computation | async-start | bytes 786432 | tf_op jit(solution)/shard_map/all_to_all | solution.py:92
  13.4 0.1 squeeze.3
  13.6 0.1 select_n.135
  13.7 0.1 lt.42
  13.8 0.1 select_n.131
  13.9 0.1 select_n.128
  14.0 0.1 iota.75
  14.2 0.1 iota.84
  14.4 0.7 %pad_maximum_fusion.1 = bf16[4,28,512]{2,1,0:T(8,128)(2,1)} fusion(bf16[1,28,512]{2,1,0:T(8,128)(2,1)S(1)} %bitcast.94, bf16[1,28,512]{2,1,0:T(8,128)(2,1)S(1)} %bitcast.92, bf16[1,28,512]{2,1,0:T(8,128)(2,1)S(1)} %bitcast.93, bf16[1,28,512]{2,1,0:T(8,128)(2,1)S(1)} %get-tuple-element.9), kind=kLoop, calls=%fused_computation.18 | loop fusion | flops 172032 | bytes 229376 | tf_op jit(solution)/shard_map/stack | solution.py:16
  15.1 6.5 %all-to-all-done = bf16[8,24,1024]{2,1,0:T(8,128)(2,1)S(1)} async-done(((bf16[8,24,1024]{2,1,0:T(8,128)(2,1)}), bf16[8,24,1024]{2,1,0:T(8,128)(2,1)S(1)}, u32[]{:S(2)}, u32[]{:S(2)}) %all-to-all-start) | async-done | bytes 393248 | tf_op jit(solution)/shard_map/all_to_all | solution.py:92
  21.6 0.6 collective-permute-start.5
  22.2 1.5 %collective-permute-start.4 = (bf16[4,28,512]{2,1,0:T(8,128)(2,1)}, bf16[4,28,512]{2,1,0:T(8,128)(2,1)}, u32[]{:S(2)}, u32[]{:S(2)}) collective-permute-start(bf16[4,28,512]{2,1,0:T(8,128)(2,1)} %pad_maximum_fusion.1), channel_id=1, source_target_pairs={{0,4},{1,5},{2,6},{3,7},{4,0},{5,1},{6,2},{7,3},{8,12},{9,13},{10,... | collective-permute-start | bytes 344072 | tf_op jit(solution)/shard_map/ppermute | solution.py:25
  23.7 1.5 %collective-permute-start.3 = (bf16[4,28,512]{2,1,0:T(8,128)(2,1)}, bf16[4,28,512]{2,1,0:T(8,128)(2,1)}, u32[]{:S(2)}, u32[]{:S(2)}) collective-permute-start(bf16[4,28,512]{2,1,0:T(8,128)(2,1)} %pad_maximum_fusion.1), channel_id=1, source_target_pairs={{0,2},{1,3},{2,0},{3,1},{4,6},{5,7},{6,4},{7,5},{8,10},{9,11},{10,... | collective-permute-start | bytes 344072 | tf_op jit(solution)/shard_map/ppermute | solution.py:25
  25.1 0.2 copy.18
  25.3 1.9 %convolution_bitcast_fusion = f32[2,2,4,16,24,16]{4,5,3,1,0,2:T(8,128)} fusion(bf16[2,2,16,16,192,1]{4,3,2,1,0,5:T(8,128)(2,1)S(1)} %bitcast.80, bf16[192]{0:T(256)(128)(2,1)S(1)} %broadcast_select_fusion.3, s32[4,24]{1,0:T(4,128)S(1)} %multiply_add_fusion, s32[192]{0:T(256)S(1)} %eq.36), kind=kOutput, calls=%fused_computation.2 | convolution fusion | flops 37785600 | bytes 787968 | tf_op jit(solution)/shard_map/dot_general | solution.py:101
  27.2 2.2 %copy.19 = f32[2,2,4,16,24,16]{5,4,3,2,1,0:T(8,128)S(1)} copy(f32[2,2,4,16,24,16]{4,5,3,1,0,2:T(8,128)} %convolution_bitcast_fusion) | data formatting | bytes 786432 | tf_op jit(solution)/shard_map/transpose | solution.py:114
  29.4 0.9 %reshape.470 = f32[2,2,64,384]{3,2,1,0:T(8,128)S(1)} reshape(f32[2,2,4,16,24,16]{5,4,3,2,1,0:T(8,128)S(1)} %copy.19) | data formatting | bytes 786432 | tf_op jit(solution)/shard_map/reshape | solution.py:114
  30.3 1.0 %fusion.3 = bf16[2,2,64,384]{3,2,1,0:T(8,128)(2,1)S(1)} fusion(f32[2,2,64,384]{3,2,1,0:T(8,128)S(1)} %reshape.470, bf16[2,2,64,384]{3,2,1,0:T(8,128)(2,1)} %param.13), kind=kLoop, calls=%fused_computation.13 | loop fusion | flops 294912 | bytes 786432 | tf_op jit(solution)/shard_map/convert_element_type | solution.py:117
  31.3 0.6 %copy.20 = bf16[2,2,64,384]{2,1,0,3:T(2,128)(2,1)S(1)} copy(bf16[2,2,64,384]{3,2,1,0:T(8,128)(2,1)S(1)} %fusion.3) | data formatting | bytes 393216 | tf_op jit(solution)/shard_map/convert_element_type | solution.py:117
  31.9 1.0 %reshape.495 = bf16[8,2,6144]{2,1,0:T(2,128)(2,1)} reshape(bf16[384,2,2,64]{3,2,1,0:T(2,128)(2,1)S(1)} %bitcast.83) | data formatting | bytes 393216
  32.9 3.4 %all-to-all-start.1 = ((bf16[8,2,6144]{2,1,0:T(2,128)(2,1)}), bf16[8,2,6144]{2,1,0:T(2,128)(2,1)S(1)}, u32[]{:S(2)}, u32[]{:S(2)}) async-start(bf16[8,2,6144]{2,1,0:T(2,128)(2,1)} %reshape.495), calls=%async_computation.1 | async-start | bytes 393216 | tf_op jit(solution)/shard_map/all_to_all | solution.py:118
  36.3 0.5 collective-permute-start.6
  36.8 0.1 collective-permute-start.9
  36.9 0.4 collective-permute-start.8
  37.3 0.1 collective-permute-start.7
  37.4 1.2 %maximum_bitcast_fusion = bf16[1,4,4,28,512]{4,3,2,1,0:T(8,128)(2,1)S(1)} fusion(bf16[1,4,28,512]{3,2,1,0:T(8,128)(2,1)} %bitcast.19, bf16[1,4,28,512]{3,2,1,0:T(8,128)(2,1)} %bitcast.18, bf16[1,4,28,512]{3,2,1,0:T(8,128)(2,1)} %bitcast.17, bf16[1,4,28,512]{3,2,1,0:T(8,128)(2,1)} %bitcast.16), kind=kLoop, calls=%fused_computation.9 | loop fusion | flops 688128 | bytes 917504 | tf_op jit(solution)/shard_map/stack | solution.py:61
  38.6 3.9 %all-to-all-done.1 = bf16[8,2,6144]{2,1,0:T(2,128)(2,1)S(1)} async-done(((bf16[8,2,6144]{2,1,0:T(2,128)(2,1)}), bf16[8,2,6144]{2,1,0:T(2,128)(2,1)S(1)}, u32[]{:S(2)}, u32[]{:S(2)}) %all-to-all-start.1) | async-done | bytes 196640 | tf_op jit(solution)/shard_map/all_to_all | solution.py:118
  42.5 0.3 reshape.496
  42.7 0.3 copy.45
  43.0 0.3 all_to_all.23
  43.4 0.1 pad_maximum_fusion
  43.6 0.6 %gather_fusion = bf16[32,16,512]{2,1,0:T(8,128)(2,1)S(1)} fusion(bf16[32,16,512]{2,1,0:T(8,128)(2,1)S(1)} %slice.12, s32[1024]{0:T(1024)S(1)} %pad_clamp_fusion), kind=kCustom, calls=%fused_computation | custom fusion | bytes 1048704 | tf_op jit(solution)/shard_map/jit(_take)/gather | solution.py:68
  44.2 0.3 fusion
  44.5 0.2 reshape.473
  44.8 1.0 %reshape.497 = bf16[8,2,6144]{2,1,0:T(2,128)(2,1)} reshape(bf16[8,2,2,48,64]{4,3,2,1,0:T(8,128)(2,1)S(1)} %bitcast.86) | data formatting | bytes 393216
  45.8 3.4 %all-to-all-start.2 = ((bf16[8,2,6144]{2,1,0:T(2,128)(2,1)}), bf16[8,2,6144]{2,1,0:T(2,128)(2,1)S(1)}, u32[]{:S(2)}, u32[]{:S(2)}) async-start(bf16[8,2,6144]{2,1,0:T(2,128)(2,1)} %reshape.497), calls=%async_computation.2 | async-start | bytes 393216 | tf_op jit(solution)/shard_map/all_to_all | solution.py:129
  49.2 0.6 %gather_fusion.1 = bf16[32,12,384]{2,1,0:T(8,128)(2,1)S(1)} fusion(bf16[32,12,384]{2,1,0:T(8,128)(2,1)S(1)} %slice.13, s32[1024]{0:T(1024)S(1)} %pad_clamp_fusion), kind=kCustom, calls=%fused_computation.1 | custom fusion | bytes 589952 | tf_op jit(solution)/shard_map/jit(_take)/gather | solution.py:69
  49.9 0.7 %reshape_reshape.3 = bf16[384,8,48]{2,1,0:T(8,128)(2,1)S(1)} reshape(bf16[32,12,384]{2,1,0:T(8,128)(2,1)S(1)} %gather_fusion.1) | data formatting | bytes 589824 | tf_op jit(solution)/shard_map/reshape;reshape | solution.py:133
  50.6 4.8 %all-to-all-done.2 = bf16[8,2,6144]{2,1,0:T(2,128)(2,1)S(1)} async-done(((bf16[8,2,6144]{2,1,0:T(2,128)(2,1)}), bf16[8,2,6144]{2,1,0:T(2,128)(2,1)S(1)}, u32[]{:S(2)}, u32[]{:S(2)}) %all-to-all-start.2) | async-done | bytes 196640 | tf_op jit(solution)/shard_map/all_to_all | solution.py:129
  55.3 0.3 reshape.498
  55.6 0.5 fusion.1
  56.1 0.7 %fusion.4 = bf16[2,2,64,384]{3,2,1,0:T(8,128)(2,1)} fusion(bf16[2,2,64,384]{3,2,1,0:T(8,128)(2,1)S(1)} %copy-done, f32[2,2,64,384,1]{3,2,0,1,4:T(8,128)S(1)} %fusion.1), kind=kLoop, calls=%fused_computation.14 | loop fusion | flops 294912 | bytes 786432 | tf_op jit(solution)/shard_map/convert_element_type | solution.py:136
  (41 shorter events, 0.7 us)
Async XLA Ops:
  0.0 13.4 %copy-start.2 = (f32[1,8,24]{2,1,0:T(8,128)S(1)}, f32[1,8,24]{2,1,0:T(8,128)}, u32[]{:S(2)}) copy-start(f32[1,8,24]{2,1,0:T(8,128)} %param.11) | copy-start | bytes 2308
  0.0 13.6 %copy-start.3 = (s32[1,8]{1,0:T(1,128)S(1)}, s32[1,8]{1,0:T(1,128)}, u32[]{:S(2)}) copy-start(s32[1,8]{1,0:T(1,128)} %param.12) | copy-start | bytes 100
  0.0 14.3 %copy-start.1 = (s32[1,8,24]{2,1,0:T(8,128)S(1)}, s32[1,8,24]{2,1,0:T(8,128)}, u32[]{:S(2)}) copy-start(s32[1,8,24]{2,1,0:T(8,128)} %param.10) | copy-start | bytes 2308
  0.8 13.6 %collective-permute-start.1 = (bf16[28,512]{1,0:T(8,128)(2,1)S(1)}, bf16[28,512]{1,0:T(8,128)(2,1)S(1)}, u32[]{:S(2)}, u32[]{:S(2)}) collective-permute-start(bf16[28,512]{1,0:T(8,128)(2,1)S(1)} %get-tuple-element.10), channel_id=1, source_target_pairs={{0,16},{8,24},{16,0},{24,8},{1,17},{9,25},{17,1},{25,9},{2,18},{10... | collective-permute-start | bytes 86024 | tf_op jit(solution)/shard_map/ppermute | solution.py:15
  4.8 9.6 %collective-permute-start = (bf16[28,512]{1,0:T(8,128)(2,1)S(1)}, bf16[28,512]{1,0:T(8,128)(2,1)S(1)}, u32[]{:S(2)}, u32[]{:S(2)}) collective-permute-start(bf16[28,512]{1,0:T(8,128)(2,1)S(1)} %get-tuple-element.10), channel_id=1, source_target_pairs={{0,8},{8,0},{16,24},{24,16},{1,9},{9,1},{17,25},{25,17},{2,10},{10... | collective-permute-start | bytes 86024 | tf_op jit(solution)/shard_map/ppermute | solution.py:15
  6.4 8.0 %collective-permute-start.2 = (bf16[28,512]{1,0:T(8,128)(2,1)S(1)}, bf16[28,512]{1,0:T(8,128)(2,1)S(1)}, u32[]{:S(2)}, u32[]{:S(2)}) collective-permute-start(bf16[28,512]{1,0:T(8,128)(2,1)S(1)} %get-tuple-element.10), channel_id=1, source_target_pairs={{0,24},{8,16},{16,8},{24,0},{1,25},{9,17},{17,9},{25,1},{2,26},{10... | collective-permute-start | bytes 86024 | tf_op jit(solution)/shard_map/ppermute | solution.py:15
  9.3 12.3 %all-to-all-start = ((bf16[8,24,1024]{2,1,0:T(8,128)(2,1)}), bf16[8,24,1024]{2,1,0:T(8,128)(2,1)S(1)}, u32[]{:S(2)}, u32[]{:S(2)}) async-start(bf16[8,24,1024]{2,1,0:T(8,128)(2,1)} %bitcast.7), calls=%async_computation | async-start | bytes 786432 | tf_op jit(solution)/shard_map/all_to_all | solution.py:92
  21.6 15.1 %collective-permute-start.5 = (bf16[4,28,512]{2,1,0:T(8,128)(2,1)}, bf16[4,28,512]{2,1,0:T(8,128)(2,1)}, u32[]{:S(2)}, u32[]{:S(2)}) collective-permute-start(bf16[4,28,512]{2,1,0:T(8,128)(2,1)} %pad_maximum_fusion.1), channel_id=1, source_target_pairs={{0,6},{1,7},{2,4},{3,5},{4,2},{5,3},{6,0},{7,1},{8,14},{9,15},{10,... | collective-permute-start | bytes 344072 | tf_op jit(solution)/shard_map/ppermute | solution.py:25
  22.2 14.7 %collective-permute-start.4 = (bf16[4,28,512]{2,1,0:T(8,128)(2,1)}, bf16[4,28,512]{2,1,0:T(8,128)(2,1)}, u32[]{:S(2)}, u32[]{:S(2)}) collective-permute-start(bf16[4,28,512]{2,1,0:T(8,128)(2,1)} %pad_maximum_fusion.1), channel_id=1, source_target_pairs={{0,4},{1,5},{2,6},{3,7},{4,0},{5,1},{6,2},{7,3},{8,12},{9,13},{10,... | collective-permute-start | bytes 344072 | tf_op jit(solution)/shard_map/ppermute | solution.py:25
  23.7 13.6 %collective-permute-start.3 = (bf16[4,28,512]{2,1,0:T(8,128)(2,1)}, bf16[4,28,512]{2,1,0:T(8,128)(2,1)}, u32[]{:S(2)}, u32[]{:S(2)}) collective-permute-start(bf16[4,28,512]{2,1,0:T(8,128)(2,1)} %pad_maximum_fusion.1), channel_id=1, source_target_pairs={{0,2},{1,3},{2,0},{3,1},{4,6},{5,7},{6,4},{7,5},{8,10},{9,11},{10,... | collective-permute-start | bytes 344072 | tf_op jit(solution)/shard_map/ppermute | solution.py:25
  32.9 9.6 %all-to-all-start.1 = ((bf16[8,2,6144]{2,1,0:T(2,128)(2,1)}), bf16[8,2,6144]{2,1,0:T(2,128)(2,1)S(1)}, u32[]{:S(2)}, u32[]{:S(2)}) async-start(bf16[8,2,6144]{2,1,0:T(2,128)(2,1)} %reshape.495), calls=%async_computation.1 | async-start | bytes 393216 | tf_op jit(solution)/shard_map/all_to_all | solution.py:118
  36.3 7.0 %collective-permute-start.6 = (bf16[4,28,512]{2,1,0:T(8,128)(2,1)}, bf16[4,28,512]{2,1,0:T(8,128)(2,1)S(1)}, u32[]{:S(2)}, u32[]{:S(2)}) collective-permute-start(bf16[4,28,512]{2,1,0:T(8,128)(2,1)} %pad_maximum_fusion.1), channel_id=1, source_target_pairs={{0,1},{1,0},{2,3},{3,2},{4,5},{5,4},{6,7},{7,6},{8,9},{9,8},{10,11... | collective-permute-start | bytes 344072 | tf_op jit(solution)/shard_map/ppermute | solution.py:60
  36.8 6.5 %collective-permute-start.9 = (bf16[4,28,512]{2,1,0:T(8,128)(2,1)}, bf16[4,28,512]{2,1,0:T(8,128)(2,1)S(1)}, u32[]{:S(2)}, u32[]{:S(2)}) collective-permute-start(bf16[4,28,512]{2,1,0:T(8,128)(2,1)} %collective-permute-done.5), channel_id=1, source_target_pairs={{0,1},{1,0},{2,3},{3,2},{4,5},{5,4},{6,7},{7,6},{8,9},{9,8},{10,11... | collective-permute-start | bytes 344072 | tf_op jit(solution)/shard_map/ppermute | solution.py:60
  36.9 6.4 %collective-permute-start.8 = (bf16[4,28,512]{2,1,0:T(8,128)(2,1)}, bf16[4,28,512]{2,1,0:T(8,128)(2,1)S(1)}, u32[]{:S(2)}, u32[]{:S(2)}) collective-permute-start(bf16[4,28,512]{2,1,0:T(8,128)(2,1)} %collective-permute-done.4), channel_id=1, source_target_pairs={{0,1},{1,0},{2,3},{3,2},{4,5},{5,4},{6,7},{7,6},{8,9},{9,8},{10,11... | collective-permute-start | bytes 344072 | tf_op jit(solution)/shard_map/ppermute | solution.py:60
  37.3 6.0 %collective-permute-start.7 = (bf16[4,28,512]{2,1,0:T(8,128)(2,1)}, bf16[4,28,512]{2,1,0:T(8,128)(2,1)S(1)}, u32[]{:S(2)}, u32[]{:S(2)}) collective-permute-start(bf16[4,28,512]{2,1,0:T(8,128)(2,1)} %collective-permute-done.3), channel_id=1, source_target_pairs={{0,1},{1,0},{2,3},{3,2},{4,5},{5,4},{6,7},{7,6},{8,9},{9,8},{10,11... | collective-permute-start | bytes 344072 | tf_op jit(solution)/shard_map/ppermute | solution.py:60
  45.8 9.6 %all-to-all-start.2 = ((bf16[8,2,6144]{2,1,0:T(2,128)(2,1)}), bf16[8,2,6144]{2,1,0:T(2,128)(2,1)S(1)}, u32[]{:S(2)}, u32[]{:S(2)}) async-start(bf16[8,2,6144]{2,1,0:T(2,128)(2,1)} %reshape.497), calls=%async_computation.2 | async-start | bytes 393216 | tf_op jit(solution)/shard_map/all_to_all | solution.py:129
  49.2 6.9 %copy-start = (bf16[2,2,64,384]{3,2,1,0:T(8,128)(2,1)S(1)}, bf16[2,2,64,384]{3,2,1,0:T(8,128)(2,1)}, u32[]{:S(2)}) copy-start(bf16[2,2,64,384]{3,2,1,0:T(8,128)(2,1)} %param.13) | copy-start | bytes 589828

commit v21 on v20

--- a/solution.py
+++ b/solution.py
@@ -53,10 +53,10 @@
     mem_bits = bit_groups([1 << k for k in range(mem_count.bit_length() - 1)])
     tile_bits = bit_groups([1 << k for k in range(1, tile_count.bit_length() - 1)]) + [[1]]
     both = xor_gather(both, "mem", mem_bits)
-    both, after = lax.optimization_barrier((both, after))
     chip_groups = tile_bits[:-1]
     both = xor_gather(both, "tile", chip_groups[:-1])
     parts = xor_parts(both, "tile", chip_groups[-1]) if chip_groups else [both]
+    parts, after = lax.optimization_barrier((parts, after))
     swapped = [lax.ppermute(part, "tile", [(j, j ^ 1) for j in range(tile_count)]) for part in parts]
     both = jnp.stack([jnp.stack(parts), jnp.stack(swapped)])
     both = both.reshape(mem_count * tile_count, x_rows + y_rows, width)
@@ -90,7 +90,6 @@
     ).astype(source_blocks.dtype)
     packed = packed.reshape(tile_count, capacity, -1)
     arrived = lax.all_to_all(packed, "tile", split_axis=0, concat_axis=0, tiled=True)
-    x_full, y_full, arrived = gather_operators(x_operator, y_operator, arrived)
     slot_count = columns // block_side * (y_cells // block_side)
     live_mask = lax.broadcasted_iota(jnp.int32, (tile_count, capacity), 1) < recv_count[0][:, None]
     weights = jnp.where(live_mask, recv_weight[0], 0.0).reshape(-1)
@@ -115,6 +114,7 @@
         member_count, level_count, columns, y_cells
     )
     difference = (remapped - regional.astype(jnp.float32)).astype(jnp.bfloat16)
+    x_full, y_full, difference = gather_operators(x_operator, y_operator, difference)
     x_lines = lax.all_to_all(difference, "tile", split_axis=3, concat_axis=2, tiled=True)
     after_first = jnp.einsum(
         "ax,mlxy->mlay",

time: 57.4 us -> 54.7 us (0.953)
  waiting for transfers between devices: 15.2 us -> 12.4 us
    all_to_all x1, waiting for transfers between devices: 6.53 us -> 3.5 us  [body(): lax.all_to_all(packed, 'tile', split_axis=0, concat_axis=0, tiled=True)]
    convert_element_type x1 -> x0, local copies, waits for them, and re-layouts: 0.6 us -> none  [body(): difference = (remapped - regional.astype(jnp.float32)).astype(jnp.bfloat16)]
    optimization_barrier x0 -> x1, local copies, waits for them, and re-layouts: none -> 0.59 us  [gather_operators(): parts, after = lax.optimization_barrier((parts, after))]
  transfers between devices with their start and end apart: 13 -> 13, of which waited for: 3 -> 3; matrix products, arithmetic and copies ran while one was open for 27% -> 29% of each run, Pallas kernels for 0% -> 0%
where the time goes in v21:
time: 54.7 us; the launch traced here: 54.1 us
  starting transfers between devices  20.9 us (38%)
  waiting for transfers between devices  12.4 us (23%)
  local copies, waits for them, and re-layouts  11.9 us (22%)
  other arithmetic  4.78 us (9%)
  matrix products  3.76 us (7%)
    ppermute x3, starting transfers between devices, xor_gather(): lax.ppermute(data, axis_name, [(j, j ^ offset) for j in range(count)])  5.62 us
    all_to_all x1, waiting for transfers between devices, body(): lax.all_to_all(outgoing, 'tile', split_axis=0, concat_axis=0, tiled=True)  4.76 us
    all_to_all x1, waiting for transfers between devices, body(): lax.all_to_all(difference, 'tile', split_axis=3, concat_axis=2, tiled=True)  4.11 us
    all_to_all x1, starting transfers between devices, body(): lax.all_to_all(packed, 'tile', split_axis=0, concat_axis=0, tiled=True)  3.94 us
    all_to_all x1, waiting for transfers between devices, body(): lax.all_to_all(packed, 'tile', split_axis=0, concat_axis=0, tiled=True)  3.5 us
    ppermute x3, starting transfers between devices, xor_parts(): lax.ppermute(data, axis_name, [(j, j ^ offset) for j in range(count)])  3.49 us
    all_to_all x1, starting transfers between devices, body(): lax.all_to_all(difference, 'tile', split_axis=3, concat_axis=2, tiled=True)  3.39 us
    all_to_all x1, starting transfers between devices, body(): lax.all_to_all(outgoing, 'tile', split_axis=0, concat_axis=0, tiled=True)  3.39 us
  transfers between devices with their start and end apart: 13, of which 3 were waited for; matrix products, arithmetic and copies ran while one was open for 29% of the time, Pallas kernels for 0%

profile of v21, /device:TPU:0, one launch (start us, length us, event | category | flops | bytes accessed | tf_op | source)
XLA Modules:
  0.0 54.1 jit_solution(3132020845288126406)
XLA Ops:
  0.0 0.8 %fusion.32 = (bf16[1,28,512]{2,1,0:T(8,128)(2,1)S(1)}, bf16[28,512]{1,0:T(8,128)(2,1)S(1)}) fusion(bf16[12,384]{1,0:T(8,128)(2,1)} %param.15, bf16[16,512]{1,0:T(8,128)(2,1)} %param.14), kind=kLoop, calls=%fused_computation.86 | loop fusion | flops 86016 | bytes 82944 | tf_op jit(solution)/shard_map/stack | solution.py:16
  0.8 3.0 %collective-permute-start = (bf16[28,512]{1,0:T(8,128)(2,1)S(1)}, bf16[28,512]{1,0:T(8,128)(2,1)S(1)}, u32[]{:S(2)}, u32[]{:S(2)}) collective-permute-start(bf16[28,512]{1,0:T(8,128)(2,1)S(1)} %get-tuple-element.16), channel_id=1, source_target_pairs={{0,8},{8,0},{16,24},{24,16},{1,9},{9,1},{17,25},{25,17},{2,10},{10... | collective-permute-start | bytes 86024 | tf_op jit(solution)/shard_map/ppermute | solution.py:15
  3.8 2.6 %collective-permute-start.1 = (bf16[28,512]{1,0:T(8,128)(2,1)S(1)}, bf16[28,512]{1,0:T(8,128)(2,1)S(1)}, u32[]{:S(2)}, u32[]{:S(2)}) collective-permute-start(bf16[28,512]{1,0:T(8,128)(2,1)S(1)} %get-tuple-element.16), channel_id=1, source_target_pairs={{0,16},{8,24},{16,0},{24,8},{1,17},{9,25},{17,1},{25,9},{2,18},{10... | collective-permute-start | bytes 86024 | tf_op jit(solution)/shard_map/ppermute | solution.py:15
  6.4 1.1 %reshape.467 = bf16[128,1024]{1,0:T(8,128)(2,1)S(1)} reshape(bf16[128,2,2,256]{3,2,1,0:T(2,128)(2,1)} %param.8) | data formatting | bytes 524288 | tf_op jit(solution)/shard_map/reshape | solution.py:89
  7.5 0.8 %eq.39 = s32[192]{0:T(256)S(1)} reshape(s32[1,8,24]{2,1,0:T(8,128)} %param.9) | data formatting | bytes 1536 | tf_op jit(solution)/shard_map/eq | solution.py:85
  8.3 1.1 %convolution_convert_fusion = bf16[192,1024]{1,0:T(8,128)(2,1)} fusion(bf16[128,1024]{1,0:T(8,128)(2,1)S(1)} %reshape.467, s32[192]{0:T(256)S(1)} %eq.39), kind=kOutput, calls=%fused_computation.3 | convolution fusion | flops 50552832 | bytes 656128 | tf_op jit(solution)/shard_map/dot_general | solution.py:88
  9.4 3.9 %all-to-all-start = ((bf16[8,24,1024]{2,1,0:T(8,128)(2,1)}), bf16[8,24,1024]{2,1,0:T(8,128)(2,1)S(1)}, u32[]{:S(2)}, u32[]{:S(2)}) async-start(bf16[8,24,1024]{2,1,0:T(8,128)(2,1)} %bitcast.7), calls=%async_computation | async-start | bytes 786432 | tf_op jit(solution)/shard_map/all_to_all | solution.py:92
  13.5 0.1 lt.42
  13.6 0.1 squeeze.3
  13.7 0.1 select_n.131
  13.8 0.1 select_n.128
  13.9 0.1 select_n.135
  14.0 0.1 iota.75
  14.2 0.1 iota.84
  14.3 0.1 eq.36
  14.4 0.7 %pad_maximum_fusion.1 = bf16[4,28,512]{2,1,0:T(8,128)(2,1)} fusion(bf16[1,28,512]{2,1,0:T(8,128)(2,1)S(1)} %bitcast.94, bf16[1,28,512]{2,1,0:T(8,128)(2,1)S(1)} %bitcast.93, bf16[1,28,512]{2,1,0:T(8,128)(2,1)S(1)} %bitcast.92, bf16[1,28,512]{2,1,0:T(8,128)(2,1)S(1)} %get-tuple-element.15), kind=kLoop, calls=%fused_computation.18 | loop fusion | flops 172032 | bytes 229376 | tf_op jit(solution)/shard_map/stack | solution.py:16
  15.1 2.0 %collective-permute-start.3 = (bf16[4,28,512]{2,1,0:T(8,128)(2,1)}, bf16[4,28,512]{2,1,0:T(8,128)(2,1)}, u32[]{:S(2)}, u32[]{:S(2)}) collective-permute-start(bf16[4,28,512]{2,1,0:T(8,128)(2,1)} %pad_maximum_fusion.1), channel_id=1, source_target_pairs={{0,2},{1,3},{2,0},{3,1},{4,6},{5,7},{6,4},{7,5},{8,10},{9,11},{10,... | collective-permute-start | bytes 344072 | tf_op jit(solution)/shard_map/ppermute | solution.py:25
  17.1 1.5 %collective-permute-start.4 = (bf16[4,28,512]{2,1,0:T(8,128)(2,1)}, bf16[4,28,512]{2,1,0:T(8,128)(2,1)}, u32[]{:S(2)}, u32[]{:S(2)}) collective-permute-start(bf16[4,28,512]{2,1,0:T(8,128)(2,1)} %pad_maximum_fusion.1), channel_id=1, source_target_pairs={{0,4},{1,5},{2,6},{3,7},{4,0},{5,1},{6,2},{7,3},{8,12},{9,13},{10,... | collective-permute-start | bytes 344072 | tf_op jit(solution)/shard_map/ppermute | solution.py:25
  18.6 3.5 %all-to-all-done = bf16[8,24,1024]{2,1,0:T(8,128)(2,1)S(1)} async-done(((bf16[8,24,1024]{2,1,0:T(8,128)(2,1)}), bf16[8,24,1024]{2,1,0:T(8,128)(2,1)S(1)}, u32[]{:S(2)}, u32[]{:S(2)}) %all-to-all-start) | async-done | bytes 393248 | tf_op jit(solution)/shard_map/all_to_all | solution.py:92
  22.1 0.2 copy.18
  22.3 1.9 %convolution_bitcast_fusion = f32[2,2,4,16,24,16]{4,5,3,1,0,2:T(8,128)} fusion(bf16[2,2,16,16,192,1]{4,3,2,1,0,5:T(8,128)(2,1)S(1)} %bitcast.81, bf16[192]{0:T(256)(128)(2,1)S(1)} %broadcast_select_fusion.3, s32[4,24]{1,0:T(4,128)S(1)} %multiply_add_fusion, s32[192]{0:T(256)S(1)} %eq.36), kind=kOutput, calls=%fused_computation.2 | convolution fusion | flops 37785600 | bytes 787968 | tf_op jit(solution)/shard_map/dot_general | solution.py:100
  24.2 2.2 %copy.19 = f32[2,2,4,16,24,16]{5,4,3,2,1,0:T(8,128)S(1)} copy(f32[2,2,4,16,24,16]{4,5,3,1,0,2:T(8,128)} %convolution_bitcast_fusion) | data formatting | bytes 786432 | tf_op jit(solution)/shard_map/transpose | solution.py:113
  26.4 0.9 %reshape.470 = f32[2,2,64,384]{3,2,1,0:T(8,128)S(1)} reshape(f32[2,2,4,16,24,16]{5,4,3,2,1,0:T(8,128)S(1)} %copy.19) | data formatting | bytes 786432 | tf_op jit(solution)/shard_map/reshape | solution.py:113
  27.3 1.0 %fusion.3 = bf16[2,2,64,384]{3,2,1,0:T(8,128)(2,1)S(1)} fusion(f32[2,2,64,384]{3,2,1,0:T(8,128)S(1)} %reshape.470, bf16[2,2,64,384]{3,2,1,0:T(8,128)(2,1)} %param.13), kind=kLoop, calls=%fused_computation.13 | loop fusion | flops 294912 | bytes 786432 | tf_op jit(solution)/shard_map/convert_element_type | solution.py:116
  28.4 0.5 collective-permute-start.7
  28.9 0.1 collective-permute-start.8
  29.0 0.4 collective-permute-start.9
  29.4 0.6 %copy.20 = bf16[2,2,64,384]{2,1,0,3:T(2,128)(2,1)S(1)} copy(bf16[2,2,64,384]{3,2,1,0:T(8,128)(2,1)S(1)} %fusion.3) | data formatting | bytes 393216 | tf_op jit(solution)/shard_map/optimization_barrier | solution.py:59
  30.0 1.0 %reshape.495 = bf16[8,2,6144]{2,1,0:T(2,128)(2,1)} reshape(bf16[384,2,2,64]{3,2,1,0:T(2,128)(2,1)S(1)} %bitcast.83) | data formatting | bytes 393216
  31.0 3.4 %all-to-all-start.1 = ((bf16[8,2,6144]{2,1,0:T(2,128)(2,1)}), bf16[8,2,6144]{2,1,0:T(2,128)(2,1)S(1)}, u32[]{:S(2)}, u32[]{:S(2)}) async-start(bf16[8,2,6144]{2,1,0:T(2,128)(2,1)} %reshape.495), calls=%async_computation.1 | async-start | bytes 393216 | tf_op jit(solution)/shard_map/all_to_all | solution.py:118
  34.4 1.2 %maximum_bitcast_fusion = bf16[1,4,4,28,512]{4,3,2,1,0:T(8,128)(2,1)S(1)} fusion(bf16[1,4,28,512]{3,2,1,0:T(8,128)(2,1)} %bitcast.19, bf16[1,4,28,512]{3,2,1,0:T(8,128)(2,1)} %bitcast.18, bf16[1,4,28,512]{3,2,1,0:T(8,128)(2,1)} %bitcast.17, bf16[1,4,28,512]{3,2,1,0:T(8,128)(2,1)} %bitcast.16), kind=kLoop, calls=%fused_computation.9 | loop fusion | flops 688128 | bytes 917504 | tf_op jit(solution)/shard_map/stack | solution.py:61
  35.6 0.1 maximum_bitcast_fusion.1
  35.7 0.1 pad_maximum_fusion
  35.8 0.6 %gather_fusion = bf16[32,16,512]{2,1,0:T(8,128)(2,1)S(1)} fusion(bf16[32,16,512]{2,1,0:T(8,128)(2,1)S(1)} %slice.12, s32[1024]{0:T(1024)S(1)} %pad_clamp_fusion), kind=kCustom, calls=%fused_computation | custom fusion | bytes 1048704 | tf_op jit(solution)/shard_map/jit(_take)/gather | solution.py:68
  36.4 4.1 %all-to-all-done.1 = bf16[8,2,6144]{2,1,0:T(2,128)(2,1)S(1)} async-done(((bf16[8,2,6144]{2,1,0:T(2,128)(2,1)}), bf16[8,2,6144]{2,1,0:T(2,128)(2,1)S(1)}, u32[]{:S(2)}, u32[]{:S(2)}) %all-to-all-start.1) | async-done | bytes 196640 | tf_op jit(solution)/shard_map/all_to_all | solution.py:118
  40.5 0.3 reshape.496
  40.8 0.3 copy.45
  41.1 0.3 all_to_all.23
  41.4 0.3 fusion
  41.7 0.2 reshape.473
  42.0 1.0 %reshape.497 = bf16[8,2,6144]{2,1,0:T(2,128)(2,1)} reshape(bf16[8,2,2,48,64]{4,3,2,1,0:T(8,128)(2,1)S(1)} %bitcast.86) | data formatting | bytes 393216
  43.0 3.4 %all-to-all-start.2 = ((bf16[8,2,6144]{2,1,0:T(2,128)(2,1)}), bf16[8,2,6144]{2,1,0:T(2,128)(2,1)S(1)}, u32[]{:S(2)}, u32[]{:S(2)}) async-start(bf16[8,2,6144]{2,1,0:T(2,128)(2,1)} %reshape.497), calls=%async_computation.2 | async-start | bytes 393216 | tf_op jit(solution)/shard_map/all_to_all | solution.py:129
  46.4 0.6 %gather_fusion.1 = bf16[32,12,384]{2,1,0:T(8,128)(2,1)S(1)} fusion(bf16[32,12,384]{2,1,0:T(8,128)(2,1)S(1)} %slice.13, s32[1024]{0:T(1024)S(1)} %pad_clamp_fusion), kind=kCustom, calls=%fused_computation.1 | custom fusion | bytes 589952 | tf_op jit(solution)/shard_map/jit(_take)/gather | solution.py:69
  47.1 0.7 %reshape_reshape.3 = bf16[384,8,48]{2,1,0:T(8,128)(2,1)S(1)} reshape(bf16[32,12,384]{2,1,0:T(8,128)(2,1)S(1)} %gather_fusion.1) | data formatting | bytes 589824 | tf_op jit(solution)/shard_map/reshape;reshape | solution.py:133
  47.8 4.8 %all-to-all-done.2 = bf16[8,2,6144]{2,1,0:T(2,128)(2,1)S(1)} async-done(((bf16[8,2,6144]{2,1,0:T(2,128)(2,1)}), bf16[8,2,6144]{2,1,0:T(2,128)(2,1)S(1)}, u32[]{:S(2)}, u32[]{:S(2)}) %all-to-all-start.2) | async-done | bytes 196640 | tf_op jit(solution)/shard_map/all_to_all | solution.py:129
  52.5 0.3 reshape.498
  52.8 0.5 fusion.1
  53.4 0.7 %fusion.4 = bf16[2,2,64,384]{3,2,1,0:T(8,128)(2,1)} fusion(bf16[2,2,64,384]{3,2,1,0:T(8,128)(2,1)S(1)} %copy-done, f32[2,2,64,384,1]{3,2,0,1,4:T(8,128)S(1)} %fusion.1), kind=kLoop, calls=%fused_computation.14 | loop fusion | flops 294912 | bytes 786432 | tf_op jit(solution)/shard_map/convert_element_type | solution.py:136
  (41 shorter events, 0.6 us)
Async XLA Ops:
  0.0 13.4 %copy-start.3 = (s32[1,8]{1,0:T(1,128)S(1)}, s32[1,8]{1,0:T(1,128)}, u32[]{:S(2)}) copy-start(s32[1,8]{1,0:T(1,128)} %param.12) | copy-start | bytes 100
  0.0 13.6 %copy-start.2 = (f32[1,8,24]{2,1,0:T(8,128)S(1)}, f32[1,8,24]{2,1,0:T(8,128)}, u32[]{:S(2)}) copy-start(f32[1,8,24]{2,1,0:T(8,128)} %param.11) | copy-start | bytes 2308
  0.0 14.3 %copy-start.1 = (s32[1,8,24]{2,1,0:T(8,128)S(1)}, s32[1,8,24]{2,1,0:T(8,128)}, u32[]{:S(2)}) copy-start(s32[1,8,24]{2,1,0:T(8,128)} %param.10) | copy-start | bytes 2308
  0.8 13.6 %collective-permute-start = (bf16[28,512]{1,0:T(8,128)(2,1)S(1)}, bf16[28,512]{1,0:T(8,128)(2,1)S(1)}, u32[]{:S(2)}, u32[]{:S(2)}) collective-permute-start(bf16[28,512]{1,0:T(8,128)(2,1)S(1)} %get-tuple-element.16), channel_id=1, source_target_pairs={{0,8},{8,0},{16,24},{24,16},{1,9},{9,1},{17,25},{25,17},{2,10},{10... | collective-permute-start | bytes 86024 | tf_op jit(solution)/shard_map/ppermute | solution.py:15
  3.8 10.6 %collective-permute-start.1 = (bf16[28,512]{1,0:T(8,128)(2,1)S(1)}, bf16[28,512]{1,0:T(8,128)(2,1)S(1)}, u32[]{:S(2)}, u32[]{:S(2)}) collective-permute-start(bf16[28,512]{1,0:T(8,128)(2,1)S(1)} %get-tuple-element.16), channel_id=1, source_target_pairs={{0,16},{8,24},{16,0},{24,8},{1,17},{9,25},{17,1},{25,9},{2,18},{10... | collective-permute-start | bytes 86024 | tf_op jit(solution)/shard_map/ppermute | solution.py:15
  6.4 8.0 %collective-permute-start.2 = (bf16[28,512]{1,0:T(8,128)(2,1)S(1)}, bf16[28,512]{1,0:T(8,128)(2,1)S(1)}, u32[]{:S(2)}, u32[]{:S(2)}) collective-permute-start(bf16[28,512]{1,0:T(8,128)(2,1)S(1)} %get-tuple-element.16), channel_id=1, source_target_pairs={{0,24},{8,16},{16,8},{24,0},{1,25},{9,17},{17,9},{25,1},{2,26},{10... | collective-permute-start | bytes 86024 | tf_op jit(solution)/shard_map/ppermute | solution.py:15
  9.4 12.8 %all-to-all-start = ((bf16[8,24,1024]{2,1,0:T(8,128)(2,1)}), bf16[8,24,1024]{2,1,0:T(8,128)(2,1)S(1)}, u32[]{:S(2)}, u32[]{:S(2)}) async-start(bf16[8,24,1024]{2,1,0:T(8,128)(2,1)} %bitcast.7), calls=%async_computation | async-start | bytes 786432 | tf_op jit(solution)/shard_map/all_to_all | solution.py:92
  15.1 13.2 %collective-permute-start.3 = (bf16[4,28,512]{2,1,0:T(8,128)(2,1)}, bf16[4,28,512]{2,1,0:T(8,128)(2,1)}, u32[]{:S(2)}, u32[]{:S(2)}) collective-permute-start(bf16[4,28,512]{2,1,0:T(8,128)(2,1)} %pad_maximum_fusion.1), channel_id=1, source_target_pairs={{0,2},{1,3},{2,0},{3,1},{4,6},{5,7},{6,4},{7,5},{8,10},{9,11},{10,... | collective-permute-start | bytes 344072 | tf_op jit(solution)/shard_map/ppermute | solution.py:25
  17.1 11.2 %collective-permute-start.4 = (bf16[4,28,512]{2,1,0:T(8,128)(2,1)}, bf16[4,28,512]{2,1,0:T(8,128)(2,1)}, u32[]{:S(2)}, u32[]{:S(2)}) collective-permute-start(bf16[4,28,512]{2,1,0:T(8,128)(2,1)} %pad_maximum_fusion.1), channel_id=1, source_target_pairs={{0,4},{1,5},{2,6},{3,7},{4,0},{5,1},{6,2},{7,3},{8,12},{9,13},{10,... | collective-permute-start | bytes 344072 | tf_op jit(solution)/shard_map/ppermute | solution.py:25
  18.6 9.7 %collective-permute-start.5 = (bf16[4,28,512]{2,1,0:T(8,128)(2,1)}, bf16[4,28,512]{2,1,0:T(8,128)(2,1)}, u32[]{:S(2)}, u32[]{:S(2)}) collective-permute-start(bf16[4,28,512]{2,1,0:T(8,128)(2,1)} %pad_maximum_fusion.1), channel_id=1, source_target_pairs={{0,6},{1,7},{2,4},{3,5},{4,2},{5,3},{6,0},{7,1},{8,14},{9,15},{10,... | collective-permute-start | bytes 344072 | tf_op jit(solution)/shard_map/ppermute | solution.py:25
  28.3 7.3 %collective-permute-start.6 = (bf16[4,28,512]{2,1,0:T(8,128)(2,1)}, bf16[4,28,512]{2,1,0:T(8,128)(2,1)S(1)}, u32[]{:S(2)}, u32[]{:S(2)}) collective-permute-start(bf16[4,28,512]{2,1,0:T(8,128)(2,1)} %pad_maximum_fusion.1), channel_id=1, source_target_pairs={{0,1},{1,0},{2,3},{3,2},{4,5},{5,4},{6,7},{7,6},{8,9},{9,8},{10,11... | collective-permute-start | bytes 344072 | tf_op jit(solution)/shard_map/ppermute | solution.py:60
  28.4 7.2 %collective-permute-start.7 = (bf16[4,28,512]{2,1,0:T(8,128)(2,1)}, bf16[4,28,512]{2,1,0:T(8,128)(2,1)S(1)}, u32[]{:S(2)}, u32[]{:S(2)}) collective-permute-start(bf16[4,28,512]{2,1,0:T(8,128)(2,1)} %collective-permute-done.3), channel_id=1, source_target_pairs={{0,1},{1,0},{2,3},{3,2},{4,5},{5,4},{6,7},{7,6},{8,9},{9,8},{10,11... | collective-permute-start | bytes 344072 | tf_op jit(solution)/shard_map/ppermute | solution.py:60
  28.9 6.7 %collective-permute-start.8 = (bf16[4,28,512]{2,1,0:T(8,128)(2,1)}, bf16[4,28,512]{2,1,0:T(8,128)(2,1)S(1)}, u32[]{:S(2)}, u32[]{:S(2)}) collective-permute-start(bf16[4,28,512]{2,1,0:T(8,128)(2,1)} %collective-permute-done.4), channel_id=1, source_target_pairs={{0,1},{1,0},{2,3},{3,2},{4,5},{5,4},{6,7},{7,6},{8,9},{9,8},{10,11... | collective-permute-start | bytes 344072 | tf_op jit(solution)/shard_map/ppermute | solution.py:60
  29.0 6.6 %collective-permute-start.9 = (bf16[4,28,512]{2,1,0:T(8,128)(2,1)}, bf16[4,28,512]{2,1,0:T(8,128)(2,1)S(1)}, u32[]{:S(2)}, u32[]{:S(2)}) collective-permute-start(bf16[4,28,512]{2,1,0:T(8,128)(2,1)} %collective-permute-done.5), channel_id=1, source_target_pairs={{0,1},{1,0},{2,3},{3,2},{4,5},{5,4},{6,7},{7,6},{8,9},{9,8},{10,11... | collective-permute-start | bytes 344072 | tf_op jit(solution)/shard_map/ppermute | solution.py:60
  31.0 9.6 %all-to-all-start.1 = ((bf16[8,2,6144]{2,1,0:T(2,128)(2,1)}), bf16[8,2,6144]{2,1,0:T(2,128)(2,1)S(1)}, u32[]{:S(2)}, u32[]{:S(2)}) async-start(bf16[8,2,6144]{2,1,0:T(2,128)(2,1)} %reshape.495), calls=%async_computation.1 | async-start | bytes 393216 | tf_op jit(solution)/shard_map/all_to_all | solution.py:118
  43.0 9.6 %all-to-all-start.2 = ((bf16[8,2,6144]{2,1,0:T(2,128)(2,1)}), bf16[8,2,6144]{2,1,0:T(2,128)(2,1)S(1)}, u32[]{:S(2)}, u32[]{:S(2)}) async-start(bf16[8,2,6144]{2,1,0:T(2,128)(2,1)} %reshape.497), calls=%async_computation.2 | async-start | bytes 393216 | tf_op jit(solution)/shard_map/all_to_all | solution.py:129
  46.4 6.9 %copy-start = (bf16[2,2,64,384]{3,2,1,0:T(8,128)(2,1)S(1)}, bf16[2,2,64,384]{3,2,1,0:T(8,128)(2,1)}, u32[]{:S(2)}) copy-start(bf16[2,2,64,384]{3,2,1,0:T(8,128)(2,1)} %param.13) | copy-start | bytes 589828
